TPU v7x, 256 devices: a whole 4x4x8 slice. The times are simulated.
256 devices in a mesh: seg: 64 (over z, y, x_hi), frm: 2 (over core), rec: 2 (over x_lo).
Axes of the slice: x: 4 (x_hi: 2, x_lo: 2; x = x_hi * 2 + x_lo), y: 4, z: 8, core: 2. Of those that a mesh axis runs over, the one named last changes fastest.
Arguments:
- frames_in: bfloat16 [2, 32768, 1024], P('rec', ('seg', 'frm')), may hold values from -12 to 12
- w_qkv: bfloat16 [1024, 3072], replicated, may hold values from -0.1875 to 0.1875
- w_out: bfloat16 [1024, 1024], replicated, may hold values from -0.1875 to 0.1875
Outputs:
- attended: bfloat16 [2, 32768, 1024], P('rec', ('seg', 'frm'))
All inputs are finite; a program needn't handle non-finite values.
Results may differ from a plain program's by a relative error of at most 0.0051.
Values may be sent and summed in bfloat16 or wider, within the bound.
No kernel may reach another device: no remote copies, remote signals or barrier semaphores. Data moves between devices by JAX's collectives and lax.ppermute only.
A program may use at most 192 MiB of HBM per device.

v0:
```python
import jax
import jax.numpy as jnp
from jax import lax
from jax.sharding import PartitionSpec as P

HEADS = 16
SPAN = 256


def entering(shard, axis, combine, identity):
    size, mine = (lax.axis_size(axis), lax.axis_index(axis))
    everything = jax.tree.map(lambda part: lax.all_gather(part, axis), shard)
    start = jax.tree.map(
        lambda part, zero: jnp.broadcast_to(jnp.asarray(zero, part.dtype), part.shape),
        shard,
        identity,
    )

    def turn(k, before):
        reached = k < mine
        new = combine(before, jax.tree.map(lambda part: part[k], everything))
        return jax.tree.map(lambda a, b: jnp.where(reached, a, b), new, before)

    return lax.fori_loop(0, size, turn, start)


def features(t):
    return jnp.where(t > 0.0, t + 1.0, jnp.exp(jnp.minimum(t, 0.0)))


def block_terms(phi_q, phi_k, values, span):
    rows, length, heads, dim = phi_q.shape
    count = length // span
    pq = phi_q.reshape(rows, count, span, heads, dim)
    pk = phi_k.reshape(rows, count, span, heads, dim)
    vv = values.reshape(rows, count, span, heads, dim)
    scores = jnp.einsum("rnihd,rnjhd->rnhij", pq, pk, preferred_element_type=jnp.float32)
    causal = jnp.arange(span)[:, None] >= jnp.arange(span)[None, :]
    scores = jnp.where(causal, scores, 0.0)
    den_local = jnp.sum(scores, axis=-1)
    weights = scores.astype(jnp.bfloat16)
    num_local = jnp.einsum("rnhij,rnjhd->rnihd", weights, vv, preferred_element_type=jnp.float32)
    kv_blocks = jnp.einsum("rnjhd,rnjhe->rnhde", pk, vv, preferred_element_type=jnp.float32)
    k_blocks = jnp.sum(pk, axis=2, dtype=jnp.float32)
    return (pq, num_local, den_local, kv_blocks, k_blocks)


def finish(pq, num_local, den_local, kv_blocks, k_blocks, prior_kv, prior_k):
    rows, count, span, heads, dim = pq.shape
    before_kv = jnp.cumsum(kv_blocks, axis=1) - kv_blocks + prior_kv[:, None]
    before_k = jnp.cumsum(k_blocks, axis=1) - k_blocks + prior_k[:, None]
    pq32 = pq.astype(jnp.float32)
    num = num_local + jnp.einsum(
        "rnihd,rnhde->rnihe", pq32, before_kv, precision=lax.Precision.HIGHEST
    )
    den = jnp.transpose(den_local, (0, 1, 3, 2)) + jnp.einsum(
        "rnihd,rnhd->rnih", pq32, before_k, precision=lax.Precision.HIGHEST
    )
    result = (num / den[..., None]).astype(jnp.bfloat16)
    return result.reshape(rows, count * span, heads * dim)


def add_pair(earlier, later):
    return (earlier[0] + later[0], earlier[1] + later[1])


def split_qkv(qkv):
    phi_q = features(qkv[:, :, 0].astype(jnp.float32)).astype(jnp.bfloat16)
    phi_k = features(qkv[:, :, 1].astype(jnp.float32)).astype(jnp.bfloat16)
    return (phi_q, phi_k, qkv[:, :, 2])


def shards(frames_in, w_qkv, w_out):
    rows, tok_local, width = frames_in.shape
    head_dim = width // HEADS
    qkv = jnp.einsum("rtd,de->rte", frames_in, w_qkv, preferred_element_type=jnp.float32).astype(
        jnp.bfloat16
    )
    parts = qkv.reshape(rows, tok_local, 3, HEADS, head_dim)
    phi_q, phi_k, values = split_qkv(parts)
    pq, num_local, den_local, kv_blocks, k_blocks = block_terms(phi_q, phi_k, values, SPAN)
    total_kv = jnp.sum(kv_blocks, axis=1)
    total_k = jnp.sum(k_blocks, axis=1)
    zeros = (jnp.zeros_like(total_kv), jnp.zeros_like(total_k))
    prior_kv, prior_k = entering((total_kv, total_k), ("seg", "frm"), add_pair, zeros)
    heads_out = finish(pq, num_local, den_local, kv_blocks, k_blocks, prior_kv, prior_k)
    return jnp.einsum("rtd,de->rte", heads_out, w_out, preferred_element_type=jnp.float32).astype(
        jnp.bfloat16
    )


def solution(mesh):
    in_specs = (P("rec", ("seg", "frm"), None), P(), P())
    out_specs = P("rec", ("seg", "frm"), None)
    return jax.shard_map(shards, mesh=mesh, in_specs=in_specs, out_specs=out_specs, check_vma=False)
```

profile of v0, /device:TPU:1, one launch (start us, length us, event | category | flops | bytes accessed | tf_op | source)
XLA Modules:
  0.0 630.6 jit_solution(16531211193574491094)
XLA Ops:
  6.5 6.1 convolution_convert_fusion
  12.6 2.6 copy.16
  15.2 2.4 fusion.14
  17.6 1.4 convert_reduce_fusion
  19.0 204.8 %all-gather.1 = f32[2048,64]{1,0:T(8,128)} all-gather(f32[16,64]{1,0:T(8,128)S(1)} %convert_reduce_fusion), channel_id=3, replica_groups=mesh['seg'=64,'frm'=2,'rec'=2] {'seg','frm'}, dimensions={0}, use_global_device_ids=true | all-gather | bytes 528384 | tf_op jit(solution)/shard_map/all_gather | solution.py:12
  223.9 3.6 select_reduce_fusion
  227.5 144.2 %all-gather.4.cloned.1.call-done = f32[2048,64,64]{2,1,0:T(8,128)} async-done(((f32[16,64,64]{2,1,0:T(8,128)}), f32[2048,64,64]{2,1,0:T(8,128)}) %all-gather.4.cloned.1.call-update) | async-done | bytes 33554448 | tf_op jit(solution)/shard_map/all_gather | solution.py:12
  371.7 247.4 %while.16 = (s32[]{:T(128)}, f32[1,16,64,64]{3,2,1,0:T(8,128)S(1)}, f32[1,16,64]{2,1,0:T(8,128)S(1)}, s32[]{:T(128)}, f32[128,1,16,64,64]{4,3,2,1,0:T(8,128)}, /...) while((s32[]{:T(128)}, f32[1,16,64,64]{3,2,1,0:T(8,128)S(1)}, f32[1,16,64]{2,1,0:T(8,128)S(1)}, ...), condition=%wide.region_2.3_spmd.clone, body=%wide.region_1.2_spmd.clone.sunk | while | flops 199684 | bytes 798835 | solution.py:24
  371.7 1.3 add_select_fusion.4
  375.7 1.2 add_select_fusion.4
  377.6 1.2 add_select_fusion.4
  381.4 1.2 add_select_fusion.4
  385.3 1.2 add_select_fusion.4
  389.2 1.2 add_select_fusion.4
  391.1 1.2 add_select_fusion.4
  395.0 1.2 add_select_fusion.4
  398.8 1.2 add_select_fusion.4
  400.8 1.2 add_select_fusion.4
  402.7 1.2 add_select_fusion.4
  404.6 1.2 add_select_fusion.4
  408.5 1.2 add_select_fusion.4
  412.4 1.2 add_select_fusion.4
  414.3 1.2 add_select_fusion.4
  418.2 1.2 add_select_fusion.4
  422.0 1.2 add_select_fusion.4
  425.9 1.2 add_select_fusion.4
  427.8 1.2 add_select_fusion.4
  431.7 1.2 add_select_fusion.4
  435.6 1.2 add_select_fusion.4
  437.5 1.2 add_select_fusion.4
  439.4 1.2 add_select_fusion.4
  441.4 1.2 add_select_fusion.4
  445.2 1.2 add_select_fusion.4
  449.1 1.2 add_select_fusion.4
  451.0 1.2 add_select_fusion.4
  454.9 1.2 add_select_fusion.4
  458.8 1.2 add_select_fusion.4
  462.6 1.2 add_select_fusion.4
  464.6 1.2 add_select_fusion.4
  468.4 1.2 add_select_fusion.4
  472.3 1.2 add_select_fusion.4
  474.2 1.2 add_select_fusion.4
  476.1 1.2 add_select_fusion.4
  478.1 1.2 add_select_fusion.4
  481.9 1.2 add_select_fusion.4
  485.8 1.2 add_select_fusion.4
  619.2 1.7 fusion.24
  622.2 1.5 fusion.5
  (235 shorter events, 201.8 us)
Async XLA Ops:
  6.5 615.7 %copy-start = (bf16[1024,1024]{1,0:T(8,128)(2,1)S(1)}, bf16[1024,1024]{1,0:T(8,128)(2,1)}, u32[]{:S(2)}) copy-start(bf16[1024,1024]{1,0:T(8,128)(2,1)} %param.7) | copy-start | bytes 6291460
  6.5 365.2 %all-gather.4.cloned.1.call-start = ((), (), s32[]{:S(2)}) async-start(), calls=%async_computation | async-start | bytes 67633152 | tf_op jit(solution)/shard_map/all_gather | solution.py:12
  371.7 249.2 %copy-start.2 = (f32[16,64,64]{2,1,0:T(8,128)S(1)}, f32[16,64,64]{2,1,0:T(8,128)}, u32[]{:S(2)}) copy-start(f32[16,64,64]{2,1,0:T(8,128)} %fusion.14) | copy-start | bytes 786436
  619.2 1.7 copy-start.1
  619.2 2.6 copy-start.3
Sparse Core Ops, SparseCore 0:
  17.7 353.9 all-gather.3
where the time goes:
time: 642 us; the launch traced here: 631 us
  other arithmetic  248 us (39%)
  blocking collectives  205 us (32%)
  waiting for transfers between devices  144 us (22%)
  matrix products  16.6 us (3%)
  between operations  13.5 us (2%)
    select_n x256, other arithmetic, turn(): return jax.tree.map(lambda a, b: jnp.where(reached, a, b), new, before)  247 us
    all_gather x1, blocking collectives, entering(): everything = jax.tree.map(lambda part: lax.all_gather(part, axis), shard)  205 us
    all_gather x1, waiting for transfers between devices, entering(): everything = jax.tree.map(lambda part: lax.all_gather(part, axis), shard)  144 us
  transfers between devices with their start and end apart: 1, of which 1 were waited for; matrix products, arithmetic and copies ran while one was open for 1% of the time, Pallas kernels for 0%

commit v1 on v0

--- a/solution.py
+++ b/solution.py
@@ -1,31 +1,75 @@
 import jax
 import jax.numpy as jnp
 from jax import lax
-from jax.sharding import PartitionSpec as P
+from jax.sharding import Mesh, PartitionSpec as P
 
 HEADS = 16
 SPAN = 256
 
-
-def entering(shard, axis, combine, identity):
-    size, mine = (lax.axis_size(axis), lax.axis_index(axis))
-    everything = jax.tree.map(lambda part: lax.all_gather(part, axis), shard)
-    start = jax.tree.map(
-        lambda part, zero: jnp.broadcast_to(jnp.asarray(zero, part.dtype), part.shape),
-        shard,
-        identity,
-    )
-
-    def turn(k, before):
-        reached = k < mine
-        new = combine(before, jax.tree.map(lambda part: part[k], everything))
-        return jax.tree.map(lambda a, b: jnp.where(reached, a, b), new, before)
-
-    return lax.fori_loop(0, size, turn, start)
+SEG_SPLIT = (("seg_z", 8), ("seg_y", 4), ("seg_x", 2))
+SCAN_AXES = ("seg_z", "seg_y", "seg_x", "frm")
 
 
 def features(t):
     return jnp.where(t > 0.0, t + 1.0, jnp.exp(jnp.minimum(t, 0.0)))
+
+
+def tmap(f, *trees):
+    return jax.tree.map(f, *trees)
+
+
+def swap(tree, axis):
+    return tmap(lambda t: lax.ppermute(t, axis, perm=[(0, 1), (1, 0)]), tree)
+
+
+def part(tree, index, count):
+    def one(t):
+        size = t.shape[0] // count
+        return lax.dynamic_slice_in_dim(t, index * size, size, axis=0)
+
+    return tmap(one, tree)
+
+
+def gather(tree, axis, tiled):
+    return tmap(lambda t: lax.all_gather(t, axis, axis=0, tiled=tiled), tree)
+
+
+def before_and_total(stack, mine):
+    def one(s):
+        n = s.shape[0]
+        idx = lax.broadcasted_iota(jnp.int32, s.shape, 0)
+        before = jnp.sum(jnp.where(idx < mine, s, 0.0), axis=0)
+        return before, jnp.sum(s, axis=0)
+
+    pairs = tmap(one, stack)
+    is_pair = lambda x: isinstance(x, tuple) and len(x) == 2 and not isinstance(x[0], tuple)
+    before = jax.tree.map(lambda p: p[0], pairs, is_leaf=is_pair)
+    total = jax.tree.map(lambda p: p[1], pairs, is_leaf=is_pair)
+    return before, total
+
+
+def ordered(mine, other, first):
+    lo = tmap(lambda a, b: jnp.where(first, a, b), mine, other)
+    hi = tmap(lambda a, b: jnp.where(first, b, a), mine, other)
+    return lo, hi
+
+
+def entering(total):
+    core = lax.axis_index("frm")
+    xh = lax.axis_index("seg_x")
+    y = lax.axis_index("seg_y")
+    z = lax.axis_index("seg_z")
+    lo, hi = ordered(total, swap(total, "frm"), core == 0)
+    own_core = tmap(lambda a: jnp.where(core == 1, a, 0.0), lo)
+    chip = part(tmap(jnp.add, lo, hi), core, 2)
+    lo, hi = ordered(chip, swap(chip, "seg_x"), xh == 0)
+    own_x = tmap(lambda a: jnp.where(xh == 1, a, 0.0), lo)
+    row = part(tmap(jnp.add, lo, hi), xh, 2)
+    own_y, plane = before_and_total(gather(row, "seg_y", False), y)
+    own_z, _ = before_and_total(gather(part(plane, y, 4), "seg_z", False), z)
+    quarter = tmap(jnp.add, gather(own_z, "seg_y", True), own_y)
+    half = tmap(jnp.add, gather(quarter, "seg_x", True), own_x)
+    return tmap(jnp.add, gather(half, "frm", True), own_core)
 
 
 def block_terms(phi_q, phi_k, values, span):
@@ -60,10 +104,6 @@
     return result.reshape(rows, count * span, heads * dim)
 
 
-def add_pair(earlier, later):
-    return (earlier[0] + later[0], earlier[1] + later[1])
-
-
 def split_qkv(qkv):
     phi_q = features(qkv[:, :, 0].astype(jnp.float32)).astype(jnp.bfloat16)
     phi_k = features(qkv[:, :, 1].astype(jnp.float32)).astype(jnp.bfloat16)
@@ -79,17 +119,23 @@
     parts = qkv.reshape(rows, tok_local, 3, HEADS, head_dim)
     phi_q, phi_k, values = split_qkv(parts)
     pq, num_local, den_local, kv_blocks, k_blocks = block_terms(phi_q, phi_k, values, SPAN)
-    total_kv = jnp.sum(kv_blocks, axis=1)
-    total_k = jnp.sum(k_blocks, axis=1)
-    zeros = (jnp.zeros_like(total_kv), jnp.zeros_like(total_k))
-    prior_kv, prior_k = entering((total_kv, total_k), ("seg", "frm"), add_pair, zeros)
-    heads_out = finish(pq, num_local, den_local, kv_blocks, k_blocks, prior_kv, prior_k)
+    total_kv = jnp.sum(kv_blocks, axis=1)[0]
+    total_k = jnp.sum(k_blocks, axis=1)[0]
+    prior_kv, prior_k = entering((total_kv, total_k))
+    heads_out = finish(
+        pq, num_local, den_local, kv_blocks, k_blocks, prior_kv[None], prior_k[None]
+    )
     return jnp.einsum("rtd,de->rte", heads_out, w_out, preferred_element_type=jnp.float32).astype(
         jnp.bfloat16
     )
 
 
 def solution(mesh):
-    in_specs = (P("rec", ("seg", "frm"), None), P(), P())
-    out_specs = P("rec", ("seg", "frm"), None)
-    return jax.shard_map(shards, mesh=mesh, in_specs=in_specs, out_specs=out_specs, check_vma=False)
+    sizes = [n for _, n in SEG_SPLIT]
+    devices = mesh.devices.reshape(
+        *sizes, mesh.shape["frm"], mesh.shape["rec"]
+    )
+    fine = Mesh(devices, tuple(name for name, _ in SEG_SPLIT) + ("frm", "rec"))
+    in_specs = (P("rec", SCAN_AXES, None), P(), P())
+    out_specs = P("rec", SCAN_AXES, None)
+    return jax.shard_map(shards, mesh=fine, in_specs=in_specs, out_specs=out_specs, check_vma=False)

time: 642 us -> 145 us (0.23); the launches traced: 631 us -> 144 us
  other arithmetic: 248 us -> 2.21 us
  waiting for transfers between devices: 144 us -> 7.95 us
  blocking collectives: 205 us -> 107 us
  between operations: 13.5 us -> 0.81 us
  starting transfers between devices: 0.01 us -> 7.34 us
    select_n x256 -> x3, other arithmetic: 247 us -> 0.09 us  [ordered(): lo = tmap(lambda a, b: jnp.where(first, a, b), mine, other)]
    all_gather x1 -> x0, waiting for transfers between devices: 144 us -> none  [entering(): everything = jax.tree.map(lambda part: lax.all_gather(part, axis), shard)]
    all_gather x1 -> x9, blocking collectives: 205 us -> 100 us  [gather(): return tmap(lambda t: lax.all_gather(t, axis, axis=0, tiled=tiled), tree)]
    ppermute x0 -> x4, waiting for transfers between devices: none -> 7.95 us  [swap(): return tmap(lambda t: lax.ppermute(t, axis, perm=[(0, 1), (1, 0)]), tree)]
    unnamed x0 -> x1, blocking collectives: none -> 7.35 us
    ppermute x0 -> x4, starting transfers between devices: none -> 7.34 us  [swap(): return tmap(lambda t: lax.ppermute(t, axis, perm=[(0, 1), (1, 0)]), tree)]
  transfers between devices with their start and end apart: 1 -> 4, of which waited for: 1 -> 2; matrix products, arithmetic and copies ran while one was open for 1% -> 5% of each run, Pallas kernels for 0% -> 0%
where the time goes in v1:
time: 145 us; the launch traced here: 144 us
  blocking collectives  107 us (74%)
  matrix products  15.2 us (10%)
  waiting for transfers between devices  7.95 us (5%)
  starting transfers between devices  7.34 us (5%)
  local copies, waits for them, and re-layouts  3.55 us (2%)
  other arithmetic  2.21 us (2%)
    all_gather x9, blocking collectives, gather(): return tmap(lambda t: lax.all_gather(t, axis, axis=0, tiled=tiled), tree)  100 us
    ppermute x4, waiting for transfers between devices, swap(): return tmap(lambda t: lax.ppermute(t, axis, perm=[(0, 1), (1, 0)]), tree)  7.95 us
    unnamed x1, blocking collectives  7.35 us
    ppermute x4, starting transfers between devices, swap(): return tmap(lambda t: lax.ppermute(t, axis, perm=[(0, 1), (1, 0)]), tree)  7.34 us
    dot_general x1, matrix products, shards(): jnp.einsum('rtd,de->rte', frames_in, w_qkv, preferred_element_type=jnp.fl...  6.03 us
  transfers between devices with their start and end apart: 4, of which 2 were waited for; matrix products, arithmetic and copies ran while one was open for 5% of the time, Pallas kernels for 0%

profile of v1, /device:TPU:1, one launch (start us, length us, event | category | flops | bytes accessed | tf_op | source)
XLA Modules:
  0.0 144.5 jit_solution(18073540168264908960)
XLA Ops:
  0.0 0.0 copy-start
  0.0 6.0 %convolution_convert_fusion = bf16[256,3072]{1,0:T(8,128)(2,1)} fusion(bf16[1024,3072]{1,0:T(8,128)(2,1)} %param.4, bf16[1,256,1024]{2,1,0:T(8,128)(2,1)} %param.3), kind=kOutput, calls=%fused_computation.2 | convolution fusion | flops 1611399168 | bytes 8388608 | tf_op jit(solution)/shard_map/rtd,de->rte/dot_general | solution.py:116
  6.0 2.6 %copy.12 = bf16[256,3072]{0,1:T(8,128)(2,1)} copy(bf16[256,3072]{1,0:T(8,128)(2,1)} %convolution_convert_fusion) | data formatting | bytes 3145728 | tf_op jit(solution)/shard_map/convert_element_type | solution.py:116
  8.6 0.0 copy-start.1
  8.6 1.5 %convert_reduce_fusion = f32[16,64]{1,0:T(8,128)S(1)} fusion(bf16[1,256,3,16,64]{1,4,3,2,0:T(8,128)(2,1)} %bitcast.62), kind=kLoop, calls=%fused_computation.22 | loop fusion | flops 2096128 | bytes 528384 | tf_op jit(solution)/shard_map/reduce_sum | solution.py:88
  10.1 3.3 %collective-permute-start.2 = (f32[16,64]{1,0:T(8,128)S(1)}, f32[16,64]{1,0:T(8,128)S(1)}, u32[]{:S(2)}, u32[]{:S(2)}) collective-permute-start(f32[16,64]{1,0:T(8,128)S(1)} %convert_reduce_fusion), channel_id=1, source_target_pairs={{0,2},{2,0},{1,3},{3,1},{4,6},{6,4},{5,7},{7,5},{8,10},{10,8},{9,1... | collective-permute-start | bytes 12296 | tf_op jit(solution)/shard_map/ppermute | solution.py:22
  13.4 1.6 %fusion.12 = f32[16,64,64]{2,1,0:T(8,128)S(1)} fusion(bf16[1,256,3,16,64]{1,4,3,2,0:T(8,128)(2,1)} %bitcast.63), kind=kOutput, calls=%fused_computation.26 | convolution fusion | flops 35127296 | bytes 1310720 | tf_op jit(solution)/shard_map/rnjhd,rnjhe->rnhde/dot_general | solution.py:87
  15.0 0.1 collective-permute-start
  15.1 0.0 copy-done.1
  15.2 1.1 select_reduce_fusion
  16.3 0.0 copy-start.2
  16.3 1.4 fusion
  17.8 0.0 collective-permute-done.2
  17.8 1.1 collective-permute-start.3
  18.9 0.0 copy-done.2
  18.9 0.6 dynamic-slice
  20.2 1.7 %collective-permute-done.3 = f32[8,64]{1,0:T(8,128)S(1)} collective-permute-done((f32[8,64]{1,0:T(8,128)S(1)}, f32[8,64]{1,0:T(8,128)S(1)}, u32[]{:S(2)}, u32[]{:S(2)}) %collective-permute-start.3) | collective-permute-done | bytes 2080 | tf_op jit(solution)/shard_map/ppermute | solution.py:22
  21.8 8.1 %all-gather.6 = f32[4,4,64]{2,1,0:T(4,128)S(1)} all-gather(f32[1,4,64]{2,1,0:T(4,128)S(1)} %fusion.26), channel_id=5, replica_groups=mesh['seg_z'=8,'seg_y'=4,'seg_x'=2,'frm'=2,'rec'=2] {'seg_y'}, dimensions={0}, use_global_device_ids=true | all-gather | bytes 5120 | tf_op jit(solution)/shard_map/all_gather | solution.py:34
  30.0 0.1 select_reduce_fusion.2
  30.1 14.3 %all-gather.7 = f32[8,1,64]{2,1,0:T(1,128)S(1)} all-gather(f32[1,1,64]{2,1,0:T(1,128)S(1)} %fusion.27), channel_id=6, replica_groups=mesh['seg_z'=8,'seg_y'=4,'seg_x'=2,'frm'=2,'rec'=2] {'seg_z'}, dimensions={0}, use_global_device_ids=true | all-gather | bytes 2304 | tf_op jit(solution)/shard_map/all_gather | solution.py:34
  44.3 0.1 fusion.25
  44.4 0.2 dynamic-update-slice
  44.7 7.3 %all-reduce = f32[256]{0:T(256)S(1)} all-reduce(f32[256]{0:T(256)S(1)} %dynamic-update-slice), channel_id=7, replica_groups=mesh['seg_z'=8,'seg_y'=4,'seg_x'=2,'frm'=2,'rec'=2] {'seg_y'}, use_global_device_ids=true, to_apply=%add | all-reduce | flops 256 | bytes 2048
  52.0 0.1 reshape.167
  52.1 4.7 %all-gather.8 = f32[2,4,64]{2,1,0:T(4,128)S(1)} all-gather(f32[1,4,64]{2,1,0:T(4,128)S(1)} %add_bitcast_fusion), channel_id=1, replica_groups=mesh['seg_z'=8,'seg_y'=4,'seg_x'=2,'frm'=2,'rec'=2] {'seg_x'}, dimensions={0}, use_global_device_ids=true | all-gather | bytes 3072 | tf_op jit(solution)/shard_map/all_gather | solution.py:34
  56.8 12.9 %all_gather.55 = f32[16,64]{1,0:T(8,128)S(1)} all-gather(f32[8,64]{1,0:T(8,128)S(1)} %select_add_fusion.1), channel_id=1, replica_groups=mesh['seg_z'=8,'seg_y'=4,'seg_x'=2,'frm'=2,'rec'=2] {'frm'}, dimensions={0}, use_global_device_ids=true | all-gather | bytes 6144 | tf_op jit(solution)/shard_map/all_gather | solution.py:34
  69.7 1.6 %fusion.32 = f32[16,1,256]{2,1,0:T(1,128)S(1)} fusion(f32[16,64,1]{1,2,0:T(1,128)S(1)} %bitcast.72, bf16[1,256,3,16,64]{1,4,3,2,0:T(8,128)(2,1)} %bitcast.64), kind=kOutput, calls=%fused_computation.70 | convolution fusion | flops 4718592 | bytes 544768 | tf_op jit(solution)/shard_map/rnihd,rnhd->rnih/dot_general | solution.py:100
  71.3 0.0 collective-permute-done
  71.3 0.1 broadcast_select_fusion
  71.3 0.1 dynamic-slice_add_fusion
  71.4 2.8 %collective-permute-start.1 = (f32[8,64,64]{2,1,0:T(8,128)S(1)}, f32[8,64,64]{2,1,0:T(8,128)S(1)}, u32[]{:S(2)}, u32[]{:S(2)}) collective-permute-start(f32[8,64,64]{2,1,0:T(8,128)S(1)} %dynamic-slice_add_fusion), channel_id=1, source_target_pairs={{0,4},{4,0},{1,5},{5,1},{2,6},{6,2},{3,7},{7,3},{8,12},{12,8},{9,1... | collective-permute-start | bytes 393224 | tf_op jit(solution)/shard_map/ppermute | solution.py:22
  74.2 6.3 %collective-permute-done.1 = f32[8,64,64]{2,1,0:T(8,128)S(1)} collective-permute-done((f32[8,64,64]{2,1,0:T(8,128)S(1)}, f32[8,64,64]{2,1,0:T(8,128)S(1)}, u32[]{:S(2)}, u32[]{:S(2)}) %collective-permute-start.1) | collective-permute-done | bytes 131104 | tf_op jit(solution)/shard_map/ppermute | solution.py:22
  80.6 9.9 %all-gather = f32[16,64,64]{2,1,0:T(8,128)S(1)} all-gather(f32[4,64,64]{2,1,0:T(8,128)S(1)} %dynamic-slice_add_fusion.1), channel_id=2, replica_groups=mesh['seg_z'=8,'seg_y'=4,'seg_x'=2,'frm'=2,'rec'=2] {'seg_y'}, dimensions={0}, use_global_device_ids=true | all-gather | bytes 327680 | tf_op jit(solution)/shard_map/all_gather | solution.py:34
  90.5 0.0 copy-start.3
  90.5 0.1 select_reduce_fusion.1
  90.6 19.0 %all-gather.1 = f32[8,64,64]{2,1,0:T(8,128)S(1)} all-gather(f32[1,64,64]{2,1,0:T(8,128)S(1)} %constant_dynamic-slice_fusion.2), channel_id=3, replica_groups=mesh['seg_z'=8,'seg_y'=4,'seg_x'=2,'frm'=2,'rec'=2] {'seg_z'}, dimensions={0}, use_global_device_ids=true | all-gather | bytes 147456 | tf_op jit(solution)/shard_map/all_gather | solution.py:34
  109.6 0.1 fusion.21
  109.7 9.1 %all-gather.2 = f32[256,64]{1,0:T(8,128)S(1)} all-gather(f32[64,64]{1,0:T(8,128)S(1)} %fusion.21), channel_id=4, replica_groups=mesh['seg_z'=8,'seg_y'=4,'seg_x'=2,'frm'=2,'rec'=2] {'seg_y'}, dimensions={0}, use_global_device_ids=true | all-gather | bytes 81920 | tf_op jit(solution)/shard_map/all_gather | solution.py:34
  118.8 6.0 %all_gather.47 = f32[8,64,64]{2,1,0:T(8,128)S(1)} all-gather(f32[4,64,64]{2,1,0:T(8,128)S(1)} %add.107), channel_id=1, replica_groups=mesh['seg_z'=8,'seg_y'=4,'seg_x'=2,'frm'=2,'rec'=2] {'seg_x'}, dimensions={0}, use_global_device_ids=true | all-gather | bytes 196608 | tf_op jit(solution)/shard_map/all_gather | solution.py:34
  124.8 16.2 %all_gather.48 = f32[16,64,64]{2,1,0:T(8,128)S(1)} all-gather(f32[8,64,64]{2,1,0:T(8,128)S(1)} %select_add_fusion), channel_id=1, replica_groups=mesh['seg_z'=8,'seg_y'=4,'seg_x'=2,'frm'=2,'rec'=2] {'frm'}, dimensions={0}, use_global_device_ids=true | all-gather | bytes 393216 | tf_op jit(solution)/shard_map/all_gather | solution.py:34
  141.0 0.0 copy-done.3
  141.0 1.9 %divide_convert_fusion = bf16[1,1,256,16,64]{2,4,3,1,0:T(8,128)(2,1)S(1)} fusion(f32[16,64,256]{2,1,0:T(8,128)S(1)} %copy-done.3, f32[256,16]{0,1:T(8,128)S(1)} %fusion.24, f32[16,64,64]{2,1,0:T(8,128)S(1)} %all_gather.48, f32[16,64,64]{2,1,0:T(8,128)S(1)} %broadcast_select_fusion, f32[16,64,64]{2,1,0:T(8,128)S(1)} %fusion.12, pred[]{:T(512)S(6)} %eq.17, ...), kind=kOutput, calls=%fused_computation.23 | convolution fusion | flops 203948032 | bytes 2899969 | tf_op jit(solution)/shard_map/rnihd,rnhde->rnihe/dot_general | solution.py:97
  143.0 0.0 copy-done
  143.0 1.5 %fusion.4 = bf16[1,256,1024]{2,1,0:T(8,128)(2,1)} fusion(bf16[256,1024]{0,1:T(8,128)(2,1)S(1)} %bitcast.70, bf16[1024,1024]{1,0:T(8,128)(2,1)S(1)} %copy-done), kind=kOutput, calls=%fused_computation.15 | convolution fusion | flops 537133056 | bytes 3145728 | tf_op jit(solution)/shard_map/rtd,de->rte/dot_general | solution.py:128
  (18 shorter events, 0.2 us)
Async XLA Ops:
  0.0 143.0 %copy-start = (bf16[1024,1024]{1,0:T(8,128)(2,1)S(1)}, bf16[1024,1024]{1,0:T(8,128)(2,1)}, u32[]{:S(2)}) copy-start(bf16[1024,1024]{1,0:T(8,128)(2,1)} %param.5) | copy-start | bytes 6291460
  8.6 6.5 %copy-start.1 = (bf16[256,3072]{0,1:T(8,128)(2,1)S(1)}, bf16[256,3072]{0,1:T(8,128)(2,1)}, u32[]{:S(2)}) copy-start(bf16[256,3072]{0,1:T(8,128)(2,1)} %copy.12) | copy-start | bytes 4718596
  10.1 7.6 %collective-permute-start.2 = (f32[16,64]{1,0:T(8,128)S(1)}, f32[16,64]{1,0:T(8,128)S(1)}, u32[]{:S(2)}, u32[]{:S(2)}) collective-permute-start(f32[16,64]{1,0:T(8,128)S(1)} %convert_reduce_fusion), channel_id=1, source_target_pairs={{0,2},{2,0},{1,3},{3,1},{4,6},{6,4},{5,7},{7,5},{8,10},{10,8},{9,1... | collective-permute-start | bytes 12296 | tf_op jit(solution)/shard_map/ppermute | solution.py:22
  15.0 56.3 %collective-permute-start = (f32[16,64,64]{2,1,0:T(8,128)S(1)}, f32[16,64,64]{2,1,0:T(8,128)S(1)}, u32[]{:S(2)}, u32[]{:S(2)}) collective-permute-start(f32[16,64,64]{2,1,0:T(8,128)S(1)} %fusion.12), channel_id=1, source_target_pairs={{0,2},{2,0},{1,3},{3,1},{4,6},{6,4},{5,7},{7,5},{8,10},{10,8},{9,1... | collective-permute-start | bytes 786440 | tf_op jit(solution)/shard_map/ppermute | solution.py:22
  16.3 2.6 %copy-start.2 = (u32[256]{0:T(256)S(1)}, u32[256]{0:T(256)}, u32[]{:S(2)}) copy-start(u32[256]{0:T(256)} %constant.41) | copy-start | bytes 3076
  17.8 4.0 %collective-permute-start.3 = (f32[8,64]{1,0:T(8,128)S(1)}, f32[8,64]{1,0:T(8,128)S(1)}, u32[]{:S(2)}, u32[]{:S(2)}) collective-permute-start(f32[8,64]{1,0:T(8,128)S(1)} %dynamic-slice_add_fusion.2), channel_id=1, source_target_pairs={{0,4},{4,0},{1,5},{5,1},{2,6},{6,2},{3,7},{7,3},{8,12},{12,8},{9,1... | collective-permute-start | bytes 6152 | tf_op jit(solution)/shard_map/ppermute | solution.py:22
  71.4 9.1 %collective-permute-start.1 = (f32[8,64,64]{2,1,0:T(8,128)S(1)}, f32[8,64,64]{2,1,0:T(8,128)S(1)}, u32[]{:S(2)}, u32[]{:S(2)}) collective-permute-start(f32[8,64,64]{2,1,0:T(8,128)S(1)} %dynamic-slice_add_fusion), channel_id=1, source_target_pairs={{0,4},{4,0},{1,5},{5,1},{2,6},{6,2},{3,7},{7,3},{8,12},{12,8},{9,1... | collective-permute-start | bytes 393224 | tf_op jit(solution)/shard_map/ppermute | solution.py:22
  90.5 50.6 %copy-start.3 = (f32[16,64,256]{2,1,0:T(8,128)S(1)}, f32[16,64,256]{2,1,0:T(8,128)}, u32[]{:S(2)}) copy-start(f32[16,64,256]{2,1,0:T(8,128)} %fusion) | copy-start | bytes 3145732

commit v2 on v1

--- a/solution.py
+++ b/solution.py
@@ -18,8 +18,16 @@
     return jax.tree.map(f, *trees)
 
 
+def send(tree, axis, pairs):
+    return tmap(lambda t: lax.ppermute(t, axis, perm=pairs), tree)
+
+
 def swap(tree, axis):
-    return tmap(lambda t: lax.ppermute(t, axis, perm=[(0, 1), (1, 0)]), tree)
+    return send(tree, axis, [(0, 1), (1, 0)])
+
+
+def forward(n, s):
+    return [(i, i + s) for i in range(n - s)]
 
 
 def part(tree, index, count):
@@ -30,28 +38,18 @@
     return tmap(one, tree)
 
 
-def gather(tree, axis, tiled):
-    return tmap(lambda t: lax.all_gather(t, axis, axis=0, tiled=tiled), tree)
-
-
-def before_and_total(stack, mine):
-    def one(s):
-        n = s.shape[0]
-        idx = lax.broadcasted_iota(jnp.int32, s.shape, 0)
-        before = jnp.sum(jnp.where(idx < mine, s, 0.0), axis=0)
-        return before, jnp.sum(s, axis=0)
-
-    pairs = tmap(one, stack)
-    is_pair = lambda x: isinstance(x, tuple) and len(x) == 2 and not isinstance(x[0], tuple)
-    before = jax.tree.map(lambda p: p[0], pairs, is_leaf=is_pair)
-    total = jax.tree.map(lambda p: p[1], pairs, is_leaf=is_pair)
-    return before, total
-
-
 def ordered(mine, other, first):
     lo = tmap(lambda a, b: jnp.where(first, a, b), mine, other)
     hi = tmap(lambda a, b: jnp.where(first, b, a), mine, other)
     return lo, hi
+
+
+def keep(tree, cond):
+    return tmap(lambda a: jnp.where(cond, a, jnp.zeros_like(a)), tree)
+
+
+def joined(lo, hi):
+    return tmap(lambda a, b: jnp.concatenate([a, b], axis=0), lo, hi)
 
 
 def entering(total):
@@ -59,17 +57,40 @@
     xh = lax.axis_index("seg_x")
     y = lax.axis_index("seg_y")
     z = lax.axis_index("seg_z")
+    n_y = lax.axis_size("seg_y")
+    n_z = lax.axis_size("seg_z")
     lo, hi = ordered(total, swap(total, "frm"), core == 0)
-    own_core = tmap(lambda a: jnp.where(core == 1, a, 0.0), lo)
+    own_core = keep(lo, core == 1)
     chip = part(tmap(jnp.add, lo, hi), core, 2)
     lo, hi = ordered(chip, swap(chip, "seg_x"), xh == 0)
-    own_x = tmap(lambda a: jnp.where(xh == 1, a, 0.0), lo)
+    own_x = keep(lo, xh == 1)
     row = part(tmap(jnp.add, lo, hi), xh, 2)
-    own_y, plane = before_and_total(gather(row, "seg_y", False), y)
-    own_z, _ = before_and_total(gather(part(plane, y, 4), "seg_z", False), z)
-    quarter = tmap(jnp.add, gather(own_z, "seg_y", True), own_y)
-    half = tmap(jnp.add, gather(quarter, "seg_x", True), own_x)
-    return tmap(jnp.add, gather(half, "frm", True), own_core)
+    own_y = tmap(jnp.zeros_like, row)
+    plane = part(row, y, n_y)
+    for s in range(1, n_y):
+        early = send(row, "seg_y", forward(n_y, s))
+        own_y = tmap(jnp.add, own_y, early)
+        plane = tmap(jnp.add, plane, part(early, y, n_y))
+        late = send(part(row, jnp.maximum(y - s, 0), n_y), "seg_y", [(i + s, i) for i in range(n_y - s)])
+        plane = tmap(jnp.add, plane, late)
+    own_z = tmap(jnp.zeros_like, plane)
+    for s in range(1, n_z):
+        own_z = tmap(jnp.add, own_z, send(plane, "seg_z", forward(n_z, s)))
+    pieces = [own_z] + [
+        send(own_z, "seg_y", [(i, (i + s) % n_y) for i in range(n_y)]) for s in range(1, n_y)
+    ]
+    order = (y - jnp.arange(n_y)) % n_y
+    quarter = tmap(
+        lambda *p: jnp.stack(p)[order].reshape(
+            (-1,) + p[0].shape[1:]
+        ),
+        *pieces,
+    )
+    quarter = tmap(jnp.add, quarter, own_y)
+    lo, hi = ordered(quarter, swap(quarter, "seg_x"), xh == 0)
+    half = tmap(jnp.add, joined(lo, hi), own_x)
+    lo, hi = ordered(half, swap(half, "frm"), core == 0)
+    return tmap(jnp.add, joined(lo, hi), own_core)
 
 
 def block_terms(phi_q, phi_k, values, span):
@@ -121,7 +142,9 @@
     pq, num_local, den_local, kv_blocks, k_blocks = block_terms(phi_q, phi_k, values, SPAN)
     total_kv = jnp.sum(kv_blocks, axis=1)[0]
     total_k = jnp.sum(k_blocks, axis=1)[0]
-    prior_kv, prior_k = entering((total_kv, total_k))
+    dense = total_kv.reshape(HEADS, -1, 128)
+    prior_kv, prior_k = entering((dense, total_k))
+    prior_kv = prior_kv.reshape(total_kv.shape)
     heads_out = finish(
         pq, num_local, den_local, kv_blocks, k_blocks, prior_kv[None], prior_k[None]
     )

time: 145 us -> 136 us (0.938)
  blocking collectives: 107 us -> 0 us
  starting transfers between devices: 7.34 us -> 83.1 us
  waiting for transfers between devices: 7.95 us -> 26.2 us
  other arithmetic: 2.21 us -> 4.37 us
  matrix products: 15.2 us -> 16.7 us
    all_gather x9 -> x0, blocking collectives: 100 us -> none  [gather(): return tmap(lambda t: lax.all_gather(t, axis, axis=0, tiled=tiled), tree)]
    ppermute x4 -> x40, starting transfers between devices: 7.34 us -> 83.1 us  [send(): return tmap(lambda t: lax.ppermute(t, axis, perm=pairs), tree)]
    ppermute x4 -> x40, waiting for transfers between devices: 7.95 us -> 26.2 us  [send(): return tmap(lambda t: lax.ppermute(t, axis, perm=pairs), tree)]
    unnamed x1 -> x0, blocking collectives: 7.35 us -> none
  transfers between devices with their start and end apart: 4 -> 40, of which waited for: 2 -> 16; matrix products, arithmetic and copies ran while one was open for 5% -> 7% of each run, Pallas kernels for 0% -> 0%
where the time goes in v2:
time: 136 us; the launch traced here: 135 us
  starting transfers between devices  83.1 us (61%)
  waiting for transfers between devices  26.2 us (19%)
  matrix products  16.7 us (12%)
  other arithmetic  4.37 us (3%)
  local copies, waits for them, and re-layouts  4.18 us (3%)
    ppermute x40, starting transfers between devices, send(): return tmap(lambda t: lax.ppermute(t, axis, perm=pairs), tree)  83.1 us
    ppermute x40, waiting for transfers between devices, send(): return tmap(lambda t: lax.ppermute(t, axis, perm=pairs), tree)  26.2 us
    dot_general x1, matrix products, shards(): jnp.einsum('rtd,de->rte', frames_in, w_qkv, preferred_element_type=jnp.fl...  6.07 us
  transfers between devices with their start and end apart: 40, of which 16 were waited for; matrix products, arithmetic and copies ran while one was open for 7% of the time, Pallas kernels for 0%

profile of v2, /device:TPU:1, one launch (start us, length us, event | category | flops | bytes accessed | tf_op | source)
XLA Modules:
  0.0 135.2 jit_solution(13118325237623407719)
XLA Ops:
  0.0 6.1 %convolution_convert_fusion = bf16[256,3072]{1,0:T(8,128)(2,1)} fusion(bf16[1024,3072]{1,0:T(8,128)(2,1)} %param.4, bf16[1,256,1024]{2,1,0:T(8,128)(2,1)} %param.3), kind=kOutput, calls=%fused_computation.4 | convolution fusion | flops 1611399168 | bytes 8388608 | tf_op jit(solution)/shard_map/rtd,de->rte/dot_general | solution.py:137
  6.1 2.6 %copy.13 = bf16[256,3072]{0,1:T(8,128)(2,1)} copy(bf16[256,3072]{1,0:T(8,128)(2,1)} %convolution_convert_fusion) | data formatting | bytes 3145728 | tf_op jit(solution)/shard_map/convert_element_type | solution.py:137
  8.7 1.4 %convert_reduce_fusion = f32[16,64]{1,0:T(8,128)S(1)} fusion(bf16[1,256,3,16,64]{1,4,3,2,0:T(8,128)(2,1)} %bitcast.70), kind=kLoop, calls=%fused_computation.24 | loop fusion | flops 2096128 | bytes 528384 | tf_op jit(solution)/shard_map/reduce_sum | solution.py:109
  10.0 3.3 %collective-permute-start.20 = (f32[16,64]{1,0:T(8,128)S(1)}, f32[16,64]{1,0:T(8,128)S(1)}, u32[]{:S(2)}, u32[]{:S(2)}) collective-permute-start(f32[16,64]{1,0:T(8,128)S(1)} %convert_reduce_fusion), channel_id=1, source_target_pairs={{0,2},{2,0},{1,3},{3,1},{4,6},{6,4},{5,7},{7,5},{8,10},{10,8},{9,1... | collective-permute-start | bytes 12296 | tf_op jit(solution)/shard_map/ppermute | solution.py:22
  13.3 1.6 %fusion.13 = f32[16,64,64]{2,1,0:T(8,128)S(1)} fusion(bf16[1,256,3,16,64]{1,4,3,2,0:T(8,128)(2,1)} %bitcast.71), kind=kOutput, calls=%fused_computation.28 | convolution fusion | flops 35127296 | bytes 1310720 | tf_op jit(solution)/shard_map/rnjhd,rnjhe->rnhde/dot_general | solution.py:108
  16.8 2.3 %collective-permute-done.21 = f32[8,64]{1,0:T(8,128)S(1)} collective-permute-done((f32[8,64]{1,0:T(8,128)S(1)}, f32[8,64]{1,0:T(8,128)S(1)}, u32[]{:S(2)}, u32[]{:S(2)}) %collective-permute-start.21) | collective-permute-done | bytes 2080 | tf_op jit(solution)/shard_map/ppermute | solution.py:22
  19.0 2.9 %collective-permute-start.26 = (f32[4,64]{1,0:T(4,128)S(1)}, f32[4,64]{1,0:T(4,128)S(1)}, u32[]{:S(2)}, u32[]{:S(2)}) collective-permute-start(f32[4,64]{1,0:T(4,128)S(1)} %constant_dynamic-slice_fusion.5), channel_id=1, source_target_pairs={{0,24},{1,25},{2,26},{3,27},{4,28},{5,29},{6,30},{7,31},{32,56},{3... | collective-permute-start | bytes 3080 | tf_op jit(solution)/shard_map/ppermute | solution.py:22
  22.0 1.3 collective-permute-start.24
  23.3 2.5 %collective-permute-start.22 = (f32[4,64]{1,0:T(4,128)S(1)}, f32[4,64]{1,0:T(4,128)S(1)}, u32[]{:S(2)}, u32[]{:S(2)}) collective-permute-start(f32[4,64]{1,0:T(4,128)S(1)} %constant_dynamic-slice_fusion.5), channel_id=1, source_target_pairs={{0,8},{8,16},{16,24},{1,9},{9,17},{17,25},{2,10},{10,18},{18,26},{... | collective-permute-start | bytes 3080 | tf_op jit(solution)/shard_map/ppermute | solution.py:22
  25.8 1.3 collective-permute-start.23
  27.1 1.3 collective-permute-start.27
  28.4 1.7 %collective-permute-done.23 = f32[1,64]{1,0:T(1,128)S(1)} collective-permute-done((f32[1,64]{1,0:T(1,128)S(1)}, f32[1,64]{1,0:T(1,128)S(1)}, u32[]{:S(2)}, u32[]{:S(2)}) %collective-permute-start.23) | collective-permute-done | bytes 288 | tf_op jit(solution)/shard_map/ppermute | solution.py:22
  32.6 3.3 %collective-permute-done.25 = f32[1,64]{1,0:T(1,128)S(1)} collective-permute-done((f32[1,64]{1,0:T(1,128)S(1)}, f32[1,64]{1,0:T(1,128)S(1)}, u32[]{:S(2)}, u32[]{:S(2)}) %collective-permute-start.25) | collective-permute-done | bytes 288 | tf_op jit(solution)/shard_map/ppermute | solution.py:22
  35.9 7.5 %collective-permute-start.34 = (f32[1,64]{1,0:T(1,128)S(1)}, f32[1,64]{1,0:T(1,128)S(1)}, u32[]{:S(2)}, u32[]{:S(2)}) collective-permute-start(f32[1,64]{1,0:T(1,128)S(1)} %fusion.31), channel_id=1, source_target_pairs={{0,224},{1,225},{2,226},{3,227},{4,228},{5,229},{6,230},{7,231},{8... | collective-permute-start | bytes 776 | tf_op jit(solution)/shard_map/ppermute | solution.py:22
  43.6 1.3 collective-permute-start.33
  44.9 1.3 collective-permute-start.32
  46.2 1.3 collective-permute-start.31
  47.5 4.9 %collective-permute-start.30 = (f32[1,64]{1,0:T(1,128)S(1)}, f32[1,64]{1,0:T(1,128)S(1)}, u32[]{:S(2)}, u32[]{:S(2)}) collective-permute-start(f32[1,64]{1,0:T(1,128)S(1)} %fusion.31), channel_id=1, source_target_pairs={{0,96},{32,128},{64,160},{96,192},{128,224},{1,97},{33,129},{65,16... | collective-permute-start | bytes 776 | tf_op jit(solution)/shard_map/ppermute | solution.py:22
  52.4 1.3 collective-permute-start.29
  53.7 2.8 %collective-permute-start.28 = (f32[1,64]{1,0:T(1,128)S(1)}, f32[1,64]{1,0:T(1,128)S(1)}, u32[]{:S(2)}, u32[]{:S(2)}) collective-permute-start(f32[1,64]{1,0:T(1,128)S(1)} %fusion.31), channel_id=1, source_target_pairs={{0,32},{32,64},{64,96},{96,128},{128,160},{160,192},{192,224},{1,3... | collective-permute-start | bytes 776 | tf_op jit(solution)/shard_map/ppermute | solution.py:22
  56.5 5.0 %collective-permute-start = (f32[16,32,128]{2,1,0:T(8,128)S(1)}, f32[16,32,128]{2,1,0:T(8,128)S(1)}, u32[]{:S(2)}, u32[]{:S(2)}) collective-permute-start(f32[16,32,128]{2,1,0:T(8,128)S(1)} %reshape_squeeze.4), channel_id=1, source_target_pairs={{0,2},{2,0},{1,3},{3,1},{4,6},{6,4},{5,7},{7,5},{8,10},{10,8},{9,1... | collective-permute-start | bytes 786440 | tf_op jit(solution)/shard_map/ppermute | solution.py:22
  61.6 1.5 %collective-permute-start.36 = (f32[1,64]{1,0:T(1,128)S(1)}, f32[1,64]{1,0:T(1,128)S(1)}, u32[]{:S(2)}, u32[]{:S(2)}) collective-permute-start(f32[1,64]{1,0:T(1,128)S(1)} %add_add_fusion.4), channel_id=1, source_target_pairs={{0,16},{8,24},{16,0},{24,8},{1,17},{9,25},{17,1},{25,9},{2,18},{10... | collective-permute-start | bytes 776 | tf_op jit(solution)/shard_map/ppermute | solution.py:22
  64.0 1.6 %collective-permute-done.36 = f32[1,64]{1,0:T(1,128)S(1)} collective-permute-done((f32[1,64]{1,0:T(1,128)S(1)}, f32[1,64]{1,0:T(1,128)S(1)}, u32[]{:S(2)}, u32[]{:S(2)}) %collective-permute-start.36) | collective-permute-done | bytes 288 | tf_op jit(solution)/shard_map/ppermute | solution.py:22
  67.4 2.8 %collective-permute-start.38 = (f32[4,64]{1,0:T(4,128)S(1)}, f32[4,64]{1,0:T(4,128)S(1)}, u32[]{:S(2)}, u32[]{:S(2)}) collective-permute-start(f32[4,64]{1,0:T(4,128)S(1)} %add_add_fusion.3), channel_id=1, source_target_pairs={{0,4},{4,0},{1,5},{5,1},{2,6},{6,2},{3,7},{7,3},{8,12},{12,8},{9,1... | collective-permute-start | bytes 3080 | tf_op jit(solution)/shard_map/ppermute | solution.py:22
  71.4 4.3 %collective-permute-done.1 = f32[8,32,128]{2,1,0:T(8,128)S(1)} collective-permute-done((f32[8,32,128]{2,1,0:T(8,128)S(1)}, f32[8,32,128]{2,1,0:T(8,128)S(1)}, u32[]{:S(2)}, u32[]{:S(2)}) %collective-permute-start.1) | collective-permute-done | bytes 131104 | tf_op jit(solution)/shard_map/ppermute | solution.py:22
  75.8 1.3 collective-permute-start.3
  77.1 3.4 %collective-permute-start.6 = (f32[4,32,128]{2,1,0:T(8,128)S(1)}, f32[4,32,128]{2,1,0:T(8,128)S(1)}, u32[]{:S(2)}, u32[]{:S(2)}) collective-permute-start(f32[4,32,128]{2,1,0:T(8,128)S(1)} %constant_dynamic-slice_fusion.13), channel_id=1, source_target_pairs={{0,24},{1,25},{2,26},{3,27},{4,28},{5,29},{6,30},{7,31},{32,56},{3... | collective-permute-start | bytes 196616 | tf_op jit(solution)/shard_map/ppermute | solution.py:22
  80.5 1.8 %collective-permute-start.4 = (f32[4,32,128]{2,1,0:T(8,128)S(1)}, f32[4,32,128]{2,1,0:T(8,128)S(1)}, u32[]{:S(2)}, u32[]{:S(2)}) collective-permute-start(f32[4,32,128]{2,1,0:T(8,128)S(1)} %constant_dynamic-slice_fusion.13), channel_id=1, source_target_pairs={{0,16},{8,24},{1,17},{9,25},{2,18},{10,26},{3,19},{11,27},{4,20},{... | collective-permute-start | bytes 196616 | tf_op jit(solution)/shard_map/ppermute | solution.py:22
  82.3 2.0 %collective-permute-start.2 = (f32[4,32,128]{2,1,0:T(8,128)S(1)}, f32[4,32,128]{2,1,0:T(8,128)S(1)}, u32[]{:S(2)}, u32[]{:S(2)}) collective-permute-start(f32[4,32,128]{2,1,0:T(8,128)S(1)} %constant_dynamic-slice_fusion.13), channel_id=1, source_target_pairs={{0,8},{8,16},{16,24},{1,9},{9,17},{17,25},{2,10},{10,18},{18,26},{... | collective-permute-start | bytes 196616 | tf_op jit(solution)/shard_map/ppermute | solution.py:22
  84.3 1.3 collective-permute-start.7
  85.6 1.3 collective-permute-start.5
  86.9 1.3 maximum_add_fusion.3
  88.2 1.8 %collective-permute-done.7 = f32[1,32,128]{2,1,0:T(8,128)S(1)} collective-permute-done((f32[1,32,128]{2,1,0:T(8,128)S(1)}, f32[1,32,128]{2,1,0:T(8,128)S(1)}, u32[]{:S(2)}, u32[]{:S(2)}) %collective-permute-start.7) | collective-permute-done | bytes 16416 | tf_op jit(solution)/shard_map/ppermute | solution.py:22
  90.0 5.9 %collective-permute-start.39 = (f32[8,64]{1,0:T(8,128)}, f32[8,64]{1,0:T(8,128)}, u32[]{:S(2)}, u32[]{:S(2)}) collective-permute-start(f32[8,64]{1,0:T(8,128)} %maximum_add_fusion.3), channel_id=1, source_target_pairs={{0,2},{2,0},{1,3},{3,1},{4,6},{6,4},{5,7},{7,5},{8,10},{10,8},{9,1... | collective-permute-start | bytes 6152 | tf_op jit(solution)/shard_map/ppermute | solution.py:22
  95.9 1.3 collective-permute-start.14
  97.2 1.3 collective-permute-start.13
  98.5 2.5 %select_reduce_fusion = (f32[16,256]{1,0:T(8,128)S(1)}, bf16[16,256,256]{1,2,0:T(8,128)(2,1)}) fusion(pred[256,256]{0,1:T(8,128)(4,1)S(1)} %copy-done.2, bf16[1,256,3,16,64]{1,4,3,2,0:T(8,128)(2,1)S(1)} %bitcast.75), kind=kOutput, calls=%fused_computation.2 | convolution fusion | flops 140505088 | bytes 3227648 | tf_op jit(solution)/shard_map/rnihd,rnjhd->rnhij/dot_general | solution.py:102
  102.3 2.1 %collective-permute-start.11 = (f32[1,32,128]{2,1,0:T(8,128)S(1)}, f32[1,32,128]{2,1,0:T(8,128)S(1)}, u32[]{:S(2)}, u32[]{:S(2)}) collective-permute-start(f32[1,32,128]{2,1,0:T(8,128)S(1)} %add_add_fusion.2), channel_id=1, source_target_pairs={{0,128},{32,160},{64,192},{96,224},{1,129},{33,161},{65,193},{97,2... | collective-permute-start | bytes 49160 | tf_op jit(solution)/shard_map/ppermute | solution.py:22
  104.4 2.0 %collective-permute-start.10 = (f32[1,32,128]{2,1,0:T(8,128)S(1)}, f32[1,32,128]{2,1,0:T(8,128)S(1)}, u32[]{:S(2)}, u32[]{:S(2)}) collective-permute-start(f32[1,32,128]{2,1,0:T(8,128)S(1)} %add_add_fusion.2), channel_id=1, source_target_pairs={{0,96},{32,128},{64,160},{96,192},{128,224},{1,97},{33,129},{65,16... | collective-permute-start | bytes 49160 | tf_op jit(solution)/shard_map/ppermute | solution.py:22
  106.5 1.3 collective-permute-start.9
  107.8 2.8 %collective-permute-start.8 = (f32[1,32,128]{2,1,0:T(8,128)S(1)}, f32[1,32,128]{2,1,0:T(8,128)S(1)}, u32[]{:S(2)}, u32[]{:S(2)}) collective-permute-start(f32[1,32,128]{2,1,0:T(8,128)S(1)} %add_add_fusion.2), channel_id=1, source_target_pairs={{0,32},{32,64},{64,96},{96,128},{128,160},{160,192},{192,224},{1,3... | collective-permute-start | bytes 49160 | tf_op jit(solution)/shard_map/ppermute | solution.py:22
  114.2 2.1 %collective-permute-done.16 = f32[1,32,128]{2,1,0:T(8,128)S(1)} collective-permute-done((f32[1,32,128]{2,1,0:T(8,128)S(1)}, f32[1,32,128]{2,1,0:T(8,128)S(1)}, u32[]{:S(2)}, u32[]{:S(2)}) %collective-permute-start.16) | collective-permute-done | bytes 16416 | tf_op jit(solution)/shard_map/ppermute | solution.py:22
  117.6 1.6 %fusion.35 = f32[16,1,256]{2,1,0:T(1,128)S(1)} fusion(f32[16,64,1]{1,2,0:T(1,128)S(1)} %bitcast.81, bf16[1,256,3,16,64]{1,4,3,2,0:T(8,128)(2,1)} %bitcast.72), kind=kOutput, calls=%fused_computation.97 | convolution fusion | flops 4718592 | bytes 544768 | tf_op jit(solution)/shard_map/rnihd,rnhd->rnih/dot_general | solution.py:121
  119.2 2.8 %collective-permute-done.18 = f32[4,32,128]{2,1,0:T(8,128)S(1)} collective-permute-done((f32[4,32,128]{2,1,0:T(8,128)S(1)}, f32[4,32,128]{2,1,0:T(8,128)S(1)}, u32[]{:S(2)}, u32[]{:S(2)}) %collective-permute-start.18) | collective-permute-done | bytes 65568 | tf_op jit(solution)/shard_map/ppermute | solution.py:22
  122.0 6.8 %collective-permute-start.19 = (f32[8,32,128]{2,1,0:T(8,128)S(1)}, f32[8,32,128]{2,1,0:T(8,128)S(1)}, u32[]{:S(2)}, u32[]{:S(2)}) collective-permute-start(f32[8,32,128]{2,1,0:T(8,128)S(1)} %maximum_add_fusion.1), channel_id=1, source_target_pairs={{0,2},{2,0},{1,3},{3,1},{4,6},{6,4},{5,7},{7,5},{8,10},{10,8},{9,1... | collective-permute-start | bytes 393224 | tf_op jit(solution)/shard_map/ppermute | solution.py:22
  130.1 2.0 %fusion.18 = f32[16,64,256]{2,1,0:T(8,128)S(1)} fusion(f32[16,64,64]{2,1,0:T(8,128)S(1)} %broadcast_in_dim_broadcast_in_dim_reshape.3, f32[16,64,64]{2,1,0:T(8,128)S(1)} %fusion.13, bf16[1,256,3,16,64]{1,4,3,2,0:T(8,128)(2,1)} %bitcast.73), kind=kOutput, calls=%fused_computation.33 | convolution fusion | flops 203030528 | bytes 2097152 | tf_op jit(solution)/shard_map/rnihd,rnhde->rnihe/dot_general | solution.py:118
  132.1 1.5 %divide_convert_fusion = bf16[1,1,256,16,64]{2,4,3,1,0:T(8,128)(2,1)S(1)} fusion(f32[16,64,256]{2,1,0:T(8,128)S(1)} %fusion.18, bf16[16,256,256]{1,2,0:T(8,128)(2,1)S(1)} %copy-done.7, pred[256,256]{0,1:T(8,128)(4,1)S(1)} %copy-done.3, f32[256,16]{0,1:T(8,128)S(1)} %fusion.21, bf16[1,256,3,16,64]{1,4,3,2,0:T(8,128)(2,1)} %bitcast.74), kind=kOutput, calls=%fused_computation.25 | convolution fusion | flops 136052736 | bytes 4276224 | tf_op jit(solution)/shard_map/rnhij,rnjhd->rnihd/dot_general | solution.py:107
  133.6 1.5 %fusion.5 = bf16[1,256,1024]{2,1,0:T(8,128)(2,1)} fusion(bf16[256,1024]{0,1:T(8,128)(2,1)S(1)} %bitcast.76, bf16[1024,1024]{1,0:T(8,128)(2,1)S(1)} %copy-done), kind=kOutput, calls=%fused_computation.17 | convolution fusion | flops 537133056 | bytes 3145728 | tf_op jit(solution)/shard_map/rtd,de->rte/dot_general | solution.py:151
  (91 shorter events, 15.8 us)
Async XLA Ops:
  0.0 133.6 %copy-start = (bf16[1024,1024]{1,0:T(8,128)(2,1)S(1)}, bf16[1024,1024]{1,0:T(8,128)(2,1)}, u32[]{:S(2)}) copy-start(bf16[1024,1024]{1,0:T(8,128)(2,1)} %param.5) | copy-start | bytes 6291460
  10.0 4.9 %collective-permute-start.20 = (f32[16,64]{1,0:T(8,128)S(1)}, f32[16,64]{1,0:T(8,128)S(1)}, u32[]{:S(2)}, u32[]{:S(2)}) collective-permute-start(f32[16,64]{1,0:T(8,128)S(1)} %convert_reduce_fusion), channel_id=1, source_target_pairs={{0,2},{2,0},{1,3},{3,1},{4,6},{6,4},{5,7},{7,5},{8,10},{10,8},{9,1... | collective-permute-start | bytes 12296 | tf_op jit(solution)/shard_map/ppermute | solution.py:22
  15.0 55.2 %copy-start.4 = (f32[8,64]{1,0:T(8,128)}, f32[8,64]{1,0:T(8,128)S(1)}, u32[]{:S(2)}) copy-start(f32[8,64]{1,0:T(8,128)S(1)} %fusion.24) | copy-start | bytes 6148
  15.0 4.0 %collective-permute-start.21 = (f32[8,64]{1,0:T(8,128)S(1)}, f32[8,64]{1,0:T(8,128)S(1)}, u32[]{:S(2)}, u32[]{:S(2)}) collective-permute-start(f32[8,64]{1,0:T(8,128)S(1)} %fusion.24), channel_id=1, source_target_pairs={{0,4},{4,0},{1,5},{5,1},{2,6},{6,2},{3,7},{7,3},{8,12},{12,8},{9,1... | collective-permute-start | bytes 6152 | tf_op jit(solution)/shard_map/ppermute | solution.py:22
  19.0 51.2 %copy-start.5 = (f32[8,64]{1,0:T(8,128)}, f32[8,64]{1,0:T(8,128)S(1)}, u32[]{:S(2)}) copy-start(f32[8,64]{1,0:T(8,128)S(1)} %collective-permute-done.21) | copy-start | bytes 6148
  19.0 16.9 %collective-permute-start.26 = (f32[4,64]{1,0:T(4,128)S(1)}, f32[4,64]{1,0:T(4,128)S(1)}, u32[]{:S(2)}, u32[]{:S(2)}) collective-permute-start(f32[4,64]{1,0:T(4,128)S(1)} %constant_dynamic-slice_fusion.5), channel_id=1, source_target_pairs={{0,24},{1,25},{2,26},{3,27},{4,28},{5,29},{6,30},{7,31},{32,56},{3... | collective-permute-start | bytes 3080 | tf_op jit(solution)/shard_map/ppermute | solution.py:22
  22.0 13.9 %collective-permute-start.24 = (f32[4,64]{1,0:T(4,128)S(1)}, f32[4,64]{1,0:T(4,128)S(1)}, u32[]{:S(2)}, u32[]{:S(2)}) collective-permute-start(f32[4,64]{1,0:T(4,128)S(1)} %constant_dynamic-slice_fusion.5), channel_id=1, source_target_pairs={{0,16},{8,24},{1,17},{9,25},{2,18},{10,26},{3,19},{11,27},{4,20},{... | collective-permute-start | bytes 3080 | tf_op jit(solution)/shard_map/ppermute | solution.py:22
  23.3 12.6 %collective-permute-start.22 = (f32[4,64]{1,0:T(4,128)S(1)}, f32[4,64]{1,0:T(4,128)S(1)}, u32[]{:S(2)}, u32[]{:S(2)}) collective-permute-start(f32[4,64]{1,0:T(4,128)S(1)} %constant_dynamic-slice_fusion.5), channel_id=1, source_target_pairs={{0,8},{8,16},{16,24},{1,9},{9,17},{17,25},{2,10},{10,18},{18,26},{... | collective-permute-start | bytes 3080 | tf_op jit(solution)/shard_map/ppermute | solution.py:22
  25.8 4.3 %collective-permute-start.23 = (f32[1,64]{1,0:T(1,128)S(1)}, f32[1,64]{1,0:T(1,128)S(1)}, u32[]{:S(2)}, u32[]{:S(2)}) collective-permute-start(f32[1,64]{1,0:T(1,128)S(1)} %get-tuple-element.16), channel_id=1, source_target_pairs={{8,0},{16,8},{24,16},{9,1},{17,9},{25,17},{10,2},{18,10},{26,18},{... | collective-permute-start | bytes 776 | tf_op jit(solution)/shard_map/ppermute | solution.py:22
  27.1 5.5 %collective-permute-start.27 = (f32[1,64]{1,0:T(1,128)S(1)}, f32[1,64]{1,0:T(1,128)S(1)}, u32[]{:S(2)}, u32[]{:S(2)}) collective-permute-start(f32[1,64]{1,0:T(1,128)S(1)} %get-tuple-element.17), channel_id=1, source_target_pairs={{24,0},{25,1},{26,2},{27,3},{28,4},{29,5},{30,6},{31,7},{56,32},{5... | collective-permute-start | bytes 776 | tf_op jit(solution)/shard_map/ppermute | solution.py:22
  30.1 5.8 %collective-permute-start.25 = (f32[1,64]{1,0:T(1,128)S(1)}, f32[1,64]{1,0:T(1,128)S(1)}, u32[]{:S(2)}, u32[]{:S(2)}) collective-permute-start(f32[1,64]{1,0:T(1,128)S(1)} %get-tuple-element.18), channel_id=1, source_target_pairs={{16,0},{24,8},{17,1},{25,9},{18,2},{26,10},{19,3},{27,11},{20,4},{... | collective-permute-start | bytes 776 | tf_op jit(solution)/shard_map/ppermute | solution.py:22
  35.9 16.4 %collective-permute-start.34 = (f32[1,64]{1,0:T(1,128)S(1)}, f32[1,64]{1,0:T(1,128)S(1)}, u32[]{:S(2)}, u32[]{:S(2)}) collective-permute-start(f32[1,64]{1,0:T(1,128)S(1)} %fusion.31), channel_id=1, source_target_pairs={{0,224},{1,225},{2,226},{3,227},{4,228},{5,229},{6,230},{7,231},{8... | collective-permute-start | bytes 776 | tf_op jit(solution)/shard_map/ppermute | solution.py:22
  43.6 10.1 %collective-permute-start.33 = (f32[1,64]{1,0:T(1,128)S(1)}, f32[1,64]{1,0:T(1,128)S(1)}, u32[]{:S(2)}, u32[]{:S(2)}) collective-permute-start(f32[1,64]{1,0:T(1,128)S(1)} %fusion.31), channel_id=1, source_target_pairs={{0,192},{32,224},{1,193},{33,225},{2,194},{34,226},{3,195},{35,227... | collective-permute-start | bytes 776 | tf_op jit(solution)/shard_map/ppermute | solution.py:22
  44.9 11.6 %collective-permute-start.32 = (f32[1,64]{1,0:T(1,128)S(1)}, f32[1,64]{1,0:T(1,128)S(1)}, u32[]{:S(2)}, u32[]{:S(2)}) collective-permute-start(f32[1,64]{1,0:T(1,128)S(1)} %fusion.31), channel_id=1, source_target_pairs={{0,160},{32,192},{64,224},{1,161},{33,193},{65,225},{2,162},{34,19... | collective-permute-start | bytes 776 | tf_op jit(solution)/shard_map/ppermute | solution.py:22
  46.2 15.3 %collective-permute-start.31 = (f32[1,64]{1,0:T(1,128)S(1)}, f32[1,64]{1,0:T(1,128)S(1)}, u32[]{:S(2)}, u32[]{:S(2)}) collective-permute-start(f32[1,64]{1,0:T(1,128)S(1)} %fusion.31), channel_id=1, source_target_pairs={{0,128},{32,160},{64,192},{96,224},{1,129},{33,161},{65,193},{97,2... | collective-permute-start | bytes 776 | tf_op jit(solution)/shard_map/ppermute | solution.py:22
  47.5 14.0 %collective-permute-start.30 = (f32[1,64]{1,0:T(1,128)S(1)}, f32[1,64]{1,0:T(1,128)S(1)}, u32[]{:S(2)}, u32[]{:S(2)}) collective-permute-start(f32[1,64]{1,0:T(1,128)S(1)} %fusion.31), channel_id=1, source_target_pairs={{0,96},{32,128},{64,160},{96,192},{128,224},{1,97},{33,129},{65,16... | collective-permute-start | bytes 776 | tf_op jit(solution)/shard_map/ppermute | solution.py:22
  52.4 9.1 %collective-permute-start.29 = (f32[1,64]{1,0:T(1,128)S(1)}, f32[1,64]{1,0:T(1,128)S(1)}, u32[]{:S(2)}, u32[]{:S(2)}) collective-permute-start(f32[1,64]{1,0:T(1,128)S(1)} %fusion.31), channel_id=1, source_target_pairs={{0,64},{32,96},{64,128},{96,160},{128,192},{160,224},{1,65},{33,97... | collective-permute-start | bytes 776 | tf_op jit(solution)/shard_map/ppermute | solution.py:22
  53.7 7.8 %collective-permute-start.28 = (f32[1,64]{1,0:T(1,128)S(1)}, f32[1,64]{1,0:T(1,128)S(1)}, u32[]{:S(2)}, u32[]{:S(2)}) collective-permute-start(f32[1,64]{1,0:T(1,128)S(1)} %fusion.31), channel_id=1, source_target_pairs={{0,32},{32,64},{64,96},{96,128},{128,160},{160,192},{192,224},{1,3... | collective-permute-start | bytes 776 | tf_op jit(solution)/shard_map/ppermute | solution.py:22
  56.5 13.7 %collective-permute-start = (f32[16,32,128]{2,1,0:T(8,128)S(1)}, f32[16,32,128]{2,1,0:T(8,128)S(1)}, u32[]{:S(2)}, u32[]{:S(2)}) collective-permute-start(f32[16,32,128]{2,1,0:T(8,128)S(1)} %reshape_squeeze.4), channel_id=1, source_target_pairs={{0,2},{2,0},{1,3},{3,1},{4,6},{6,4},{5,7},{7,5},{8,10},{10,8},{9,1... | collective-permute-start | bytes 786440 | tf_op jit(solution)/shard_map/ppermute | solution.py:22
  61.5 2.5 %collective-permute-start.37 = (f32[1,64]{1,0:T(1,128)S(1)}, f32[1,64]{1,0:T(1,128)S(1)}, u32[]{:S(2)}, u32[]{:S(2)}) collective-permute-start(f32[1,64]{1,0:T(1,128)S(1)} %add_add_fusion.4), channel_id=1, source_target_pairs={{0,24},{8,0},{16,8},{24,16},{1,25},{9,1},{17,9},{25,17},{2,26},{10... | collective-permute-start | bytes 776 | tf_op jit(solution)/shard_map/ppermute | solution.py:22
  61.6 4.0 %collective-permute-start.36 = (f32[1,64]{1,0:T(1,128)S(1)}, f32[1,64]{1,0:T(1,128)S(1)}, u32[]{:S(2)}, u32[]{:S(2)}) collective-permute-start(f32[1,64]{1,0:T(1,128)S(1)} %add_add_fusion.4), channel_id=1, source_target_pairs={{0,16},{8,24},{16,0},{24,8},{1,17},{9,25},{17,1},{25,9},{2,18},{10... | collective-permute-start | bytes 776 | tf_op jit(solution)/shard_map/ppermute | solution.py:22
  63.1 3.6 %collective-permute-start.35 = (f32[1,64]{1,0:T(1,128)S(1)}, f32[1,64]{1,0:T(1,128)S(1)}, u32[]{:S(2)}, u32[]{:S(2)}) collective-permute-start(f32[1,64]{1,0:T(1,128)S(1)} %add_add_fusion.4), channel_id=1, source_target_pairs={{0,8},{8,16},{16,24},{24,0},{1,9},{9,17},{17,25},{25,1},{2,10},{10... | collective-permute-start | bytes 776 | tf_op jit(solution)/shard_map/ppermute | solution.py:22
  63.1 7.1 %copy-start.6 = (s32[1024]{0:T(1024)}, s32[1024]{0:T(1024)S(1)}, u32[]{:S(2)}) copy-start(s32[1024]{0:T(1024)S(1)} %pad_clamp_fusion) | copy-start | bytes 12292
  67.3 31.2 %copy-start.1 = (bf16[256,3072]{0,1:T(8,128)(2,1)S(1)}, bf16[256,3072]{0,1:T(8,128)(2,1)}, u32[]{:S(2)}) copy-start(bf16[256,3072]{0,1:T(8,128)(2,1)} %copy.13) | copy-start | bytes 4718596
  67.3 31.2 %copy-start.2 = (pred[256,256]{0,1:T(8,128)(4,1)S(1)}, pred[256,256]{0,1:T(8,128)(4,1)}, u32[]{:S(2)}) copy-start(pred[256,256]{0,1:T(8,128)(4,1)} %iota_compare_fusion) | copy-start | bytes 196612
  67.4 4.0 %collective-permute-start.38 = (f32[4,64]{1,0:T(4,128)S(1)}, f32[4,64]{1,0:T(4,128)S(1)}, u32[]{:S(2)}, u32[]{:S(2)}) collective-permute-start(f32[4,64]{1,0:T(4,128)S(1)} %add_add_fusion.3), channel_id=1, source_target_pairs={{0,4},{4,0},{1,5},{5,1},{2,6},{6,2},{3,7},{7,3},{8,12},{12,8},{9,1... | collective-permute-start | bytes 3080 | tf_op jit(solution)/shard_map/ppermute | solution.py:22
  70.3 5.4 %collective-permute-start.1 = (f32[8,32,128]{2,1,0:T(8,128)S(1)}, f32[8,32,128]{2,1,0:T(8,128)S(1)}, u32[]{:S(2)}, u32[]{:S(2)}) collective-permute-start(f32[8,32,128]{2,1,0:T(8,128)S(1)} %dynamic-slice_add_fusion), channel_id=1, source_target_pairs={{0,4},{4,0},{1,5},{5,1},{2,6},{6,2},{3,7},{7,3},{8,12},{12,8},{9,1... | collective-permute-start | bytes 393224 | tf_op jit(solution)/shard_map/ppermute | solution.py:22
  75.8 9.8 %collective-permute-start.3 = (f32[1,32,128]{2,1,0:T(8,128)S(1)}, f32[1,32,128]{2,1,0:T(8,128)S(1)}, u32[]{:S(2)}, u32[]{:S(2)}) collective-permute-start(f32[1,32,128]{2,1,0:T(8,128)S(1)} %get-tuple-element.9), channel_id=1, source_target_pairs={{8,0},{16,8},{24,16},{9,1},{17,9},{25,17},{10,2},{18,10},{26,18},{... | collective-permute-start | bytes 49160 | tf_op jit(solution)/shard_map/ppermute | solution.py:22
  77.1 18.8 %collective-permute-start.6 = (f32[4,32,128]{2,1,0:T(8,128)S(1)}, f32[4,32,128]{2,1,0:T(8,128)S(1)}, u32[]{:S(2)}, u32[]{:S(2)}) collective-permute-start(f32[4,32,128]{2,1,0:T(8,128)S(1)} %constant_dynamic-slice_fusion.13), channel_id=1, source_target_pairs={{0,24},{1,25},{2,26},{3,27},{4,28},{5,29},{6,30},{7,31},{32,56},{3... | collective-permute-start | bytes 196616 | tf_op jit(solution)/shard_map/ppermute | solution.py:22
  80.5 15.4 %collective-permute-start.4 = (f32[4,32,128]{2,1,0:T(8,128)S(1)}, f32[4,32,128]{2,1,0:T(8,128)S(1)}, u32[]{:S(2)}, u32[]{:S(2)}) collective-permute-start(f32[4,32,128]{2,1,0:T(8,128)S(1)} %constant_dynamic-slice_fusion.13), channel_id=1, source_target_pairs={{0,16},{8,24},{1,17},{9,25},{2,18},{10,26},{3,19},{11,27},{4,20},{... | collective-permute-start | bytes 196616 | tf_op jit(solution)/shard_map/ppermute | solution.py:22
  82.3 13.6 %collective-permute-start.2 = (f32[4,32,128]{2,1,0:T(8,128)S(1)}, f32[4,32,128]{2,1,0:T(8,128)S(1)}, u32[]{:S(2)}, u32[]{:S(2)}) collective-permute-start(f32[4,32,128]{2,1,0:T(8,128)S(1)} %constant_dynamic-slice_fusion.13), channel_id=1, source_target_pairs={{0,8},{8,16},{16,24},{1,9},{9,17},{17,25},{2,10},{10,18},{18,26},{... | collective-permute-start | bytes 196616 | tf_op jit(solution)/shard_map/ppermute | solution.py:22
  84.3 5.7 %collective-permute-start.7 = (f32[1,32,128]{2,1,0:T(8,128)S(1)}, f32[1,32,128]{2,1,0:T(8,128)S(1)}, u32[]{:S(2)}, u32[]{:S(2)}) collective-permute-start(f32[1,32,128]{2,1,0:T(8,128)S(1)} %get-tuple-element.10), channel_id=1, source_target_pairs={{24,0},{25,1},{26,2},{27,3},{28,4},{29,5},{30,6},{31,7},{56,32},{5... | collective-permute-start | bytes 49160 | tf_op jit(solution)/shard_map/ppermute | solution.py:22
  85.6 10.3 %collective-permute-start.5 = (f32[1,32,128]{2,1,0:T(8,128)S(1)}, f32[1,32,128]{2,1,0:T(8,128)S(1)}, u32[]{:S(2)}, u32[]{:S(2)}) collective-permute-start(f32[1,32,128]{2,1,0:T(8,128)S(1)} %get-tuple-element.11), channel_id=1, source_target_pairs={{16,0},{24,8},{17,1},{25,9},{18,2},{26,10},{19,3},{27,11},{20,4},{... | collective-permute-start | bytes 49160 | tf_op jit(solution)/shard_map/ppermute | solution.py:22
  90.0 14.4 %collective-permute-start.39 = (f32[8,64]{1,0:T(8,128)}, f32[8,64]{1,0:T(8,128)}, u32[]{:S(2)}, u32[]{:S(2)}) collective-permute-start(f32[8,64]{1,0:T(8,128)} %maximum_add_fusion.3), channel_id=1, source_target_pairs={{0,2},{2,0},{1,3},{3,1},{4,6},{6,4},{5,7},{7,5},{8,10},{10,8},{9,1... | collective-permute-start | bytes 6152 | tf_op jit(solution)/shard_map/ppermute | solution.py:22
  95.9 10.5 %collective-permute-start.14 = (f32[1,32,128]{2,1,0:T(8,128)S(1)}, f32[1,32,128]{2,1,0:T(8,128)S(1)}, u32[]{:S(2)}, u32[]{:S(2)}) collective-permute-start(f32[1,32,128]{2,1,0:T(8,128)S(1)} %add_add_fusion.2), channel_id=1, source_target_pairs={{0,224},{1,225},{2,226},{3,227},{4,228},{5,229},{6,230},{7,231},{8... | collective-permute-start | bytes 49160 | tf_op jit(solution)/shard_map/ppermute | solution.py:22
  97.2 10.6 %collective-permute-start.13 = (f32[1,32,128]{2,1,0:T(8,128)S(1)}, f32[1,32,128]{2,1,0:T(8,128)S(1)}, u32[]{:S(2)}, u32[]{:S(2)}) collective-permute-start(f32[1,32,128]{2,1,0:T(8,128)S(1)} %add_add_fusion.2), channel_id=1, source_target_pairs={{0,192},{32,224},{1,193},{33,225},{2,194},{34,226},{3,195},{35,227... | collective-permute-start | bytes 49160 | tf_op jit(solution)/shard_map/ppermute | solution.py:22
  101.0 10.3 %collective-permute-start.12 = (f32[1,32,128]{2,1,0:T(8,128)S(1)}, f32[1,32,128]{2,1,0:T(8,128)S(1)}, u32[]{:S(2)}, u32[]{:S(2)}) collective-permute-start(f32[1,32,128]{2,1,0:T(8,128)S(1)} %add_add_fusion.2), channel_id=1, source_target_pairs={{0,160},{32,192},{64,224},{1,161},{33,193},{65,225},{2,162},{34,19... | collective-permute-start | bytes 49160 | tf_op jit(solution)/shard_map/ppermute | solution.py:22
  102.3 9.0 %collective-permute-start.11 = (f32[1,32,128]{2,1,0:T(8,128)S(1)}, f32[1,32,128]{2,1,0:T(8,128)S(1)}, u32[]{:S(2)}, u32[]{:S(2)}) collective-permute-start(f32[1,32,128]{2,1,0:T(8,128)S(1)} %add_add_fusion.2), channel_id=1, source_target_pairs={{0,128},{32,160},{64,192},{96,224},{1,129},{33,161},{65,193},{97,2... | collective-permute-start | bytes 49160 | tf_op jit(solution)/shard_map/ppermute | solution.py:22
  104.4 6.9 %collective-permute-start.10 = (f32[1,32,128]{2,1,0:T(8,128)S(1)}, f32[1,32,128]{2,1,0:T(8,128)S(1)}, u32[]{:S(2)}, u32[]{:S(2)}) collective-permute-start(f32[1,32,128]{2,1,0:T(8,128)S(1)} %add_add_fusion.2), channel_id=1, source_target_pairs={{0,96},{32,128},{64,160},{96,192},{128,224},{1,97},{33,129},{65,16... | collective-permute-start | bytes 49160 | tf_op jit(solution)/shard_map/ppermute | solution.py:22
  106.5 4.8 %collective-permute-start.9 = (f32[1,32,128]{2,1,0:T(8,128)S(1)}, f32[1,32,128]{2,1,0:T(8,128)S(1)}, u32[]{:S(2)}, u32[]{:S(2)}) collective-permute-start(f32[1,32,128]{2,1,0:T(8,128)S(1)} %add_add_fusion.2), channel_id=1, source_target_pairs={{0,64},{32,96},{64,128},{96,160},{128,192},{160,224},{1,65},{33,97... | collective-permute-start | bytes 49160 | tf_op jit(solution)/shard_map/ppermute | solution.py:22
  107.8 3.7 %collective-permute-start.8 = (f32[1,32,128]{2,1,0:T(8,128)S(1)}, f32[1,32,128]{2,1,0:T(8,128)S(1)}, u32[]{:S(2)}, u32[]{:S(2)}) collective-permute-start(f32[1,32,128]{2,1,0:T(8,128)S(1)} %add_add_fusion.2), channel_id=1, source_target_pairs={{0,32},{32,64},{64,96},{96,128},{128,160},{160,192},{192,224},{1,3... | collective-permute-start | bytes 49160 | tf_op jit(solution)/shard_map/ppermute | solution.py:22
  111.5 2.7 %collective-permute-start.17 = (f32[1,32,128]{2,1,0:T(8,128)S(1)}, f32[1,32,128]{2,1,0:T(8,128)S(1)}, u32[]{:S(2)}, u32[]{:S(2)}) collective-permute-start(f32[1,32,128]{2,1,0:T(8,128)S(1)} %add_add_fusion.1), channel_id=1, source_target_pairs={{0,24},{8,0},{16,8},{24,16},{1,25},{9,1},{17,9},{25,17},{2,26},{10... | collective-permute-start | bytes 49160 | tf_op jit(solution)/shard_map/ppermute | solution.py:22
  112.2 4.1 %collective-permute-start.16 = (f32[1,32,128]{2,1,0:T(8,128)S(1)}, f32[1,32,128]{2,1,0:T(8,128)S(1)}, u32[]{:S(2)}, u32[]{:S(2)}) collective-permute-start(f32[1,32,128]{2,1,0:T(8,128)S(1)} %add_add_fusion.1), channel_id=1, source_target_pairs={{0,16},{8,24},{16,0},{24,8},{1,17},{9,25},{17,1},{25,9},{2,18},{10... | collective-permute-start | bytes 49160 | tf_op jit(solution)/shard_map/ppermute | solution.py:22
  112.8 3.8 %collective-permute-start.15 = (f32[1,32,128]{2,1,0:T(8,128)S(1)}, f32[1,32,128]{2,1,0:T(8,128)S(1)}, u32[]{:S(2)}, u32[]{:S(2)}) collective-permute-start(f32[1,32,128]{2,1,0:T(8,128)S(1)} %add_add_fusion.1), channel_id=1, source_target_pairs={{0,8},{8,16},{16,24},{24,0},{1,9},{9,17},{17,25},{25,1},{2,10},{10... | collective-permute-start | bytes 49160 | tf_op jit(solution)/shard_map/ppermute | solution.py:22
  117.3 4.7 %collective-permute-start.18 = (f32[4,32,128]{2,1,0:T(8,128)S(1)}, f32[4,32,128]{2,1,0:T(8,128)S(1)}, u32[]{:S(2)}, u32[]{:S(2)}) collective-permute-start(f32[4,32,128]{2,1,0:T(8,128)S(1)} %add_add_fusion), channel_id=1, source_target_pairs={{0,4},{4,0},{1,5},{5,1},{2,6},{6,2},{3,7},{7,3},{8,12},{12,8},{9,1... | collective-permute-start | bytes 196616 | tf_op jit(solution)/shard_map/ppermute | solution.py:22
  122.0 7.8 %collective-permute-start.19 = (f32[8,32,128]{2,1,0:T(8,128)S(1)}, f32[8,32,128]{2,1,0:T(8,128)S(1)}, u32[]{:S(2)}, u32[]{:S(2)}) collective-permute-start(f32[8,32,128]{2,1,0:T(8,128)S(1)} %maximum_add_fusion.1), channel_id=1, source_target_pairs={{0,2},{2,0},{1,3},{3,1},{4,6},{6,4},{5,7},{7,5},{8,10},{10,8},{9,1... | collective-permute-start | bytes 393224 | tf_op jit(solution)/shard_map/ppermute | solution.py:22
  129.9 2.2 %copy-start.3 = (pred[256,256]{0,1:T(8,128)(4,1)S(1)}, pred[256,256]{0,1:T(8,128)(4,1)}, u32[]{:S(2)}) copy-start(pred[256,256]{0,1:T(8,128)(4,1)} %iota_compare_fusion) | copy-start | bytes 196612
  130.1 2.0 %copy-start.7 = (bf16[16,256,256]{1,2,0:T(8,128)(2,1)S(1)}, bf16[16,256,256]{1,2,0:T(8,128)(2,1)}, u32[]{:S(2)}) copy-start(bf16[16,256,256]{1,2,0:T(8,128)(2,1)} %get-tuple-element.20) | copy-start | bytes 6291460

commit v3 on v2

--- a/solution.py
+++ b/solution.py
@@ -68,11 +68,9 @@
     own_y = tmap(jnp.zeros_like, row)
     plane = part(row, y, n_y)
     for s in range(1, n_y):
-        early = send(row, "seg_y", forward(n_y, s))
-        own_y = tmap(jnp.add, own_y, early)
-        plane = tmap(jnp.add, plane, part(early, y, n_y))
-        late = send(part(row, jnp.maximum(y - s, 0), n_y), "seg_y", [(i + s, i) for i in range(n_y - s)])
-        plane = tmap(jnp.add, plane, late)
+        came = send(row, "seg_y", [(i, (i + s) % n_y) for i in range(n_y)])
+        own_y = tmap(lambda a, b: a + jnp.where(y >= s, b, jnp.zeros_like(b)), own_y, came)
+        plane = tmap(jnp.add, plane, part(came, y, n_y))
     own_z = tmap(jnp.zeros_like, plane)
     for s in range(1, n_z):
         own_z = tmap(jnp.add, own_z, send(plane, "seg_z", forward(n_z, s)))
@@ -142,9 +140,13 @@
     pq, num_local, den_local, kv_blocks, k_blocks = block_terms(phi_q, phi_k, values, SPAN)
     total_kv = jnp.sum(kv_blocks, axis=1)[0]
     total_k = jnp.sum(k_blocks, axis=1)[0]
-    dense = total_kv.reshape(HEADS, -1, 128)
-    prior_kv, prior_k = entering((dense, total_k))
-    prior_kv = prior_kv.reshape(total_kv.shape)
+    lanes = 128
+    dense = total_kv.reshape(HEADS, -1, lanes)
+    rows_kv = dense.shape[1]
+    norm = jnp.pad(total_k, ((0, 0), (0, lanes - total_k.shape[1])))[:, None]
+    prior = entering(jnp.concatenate([dense, norm], axis=1))
+    prior_kv = prior[:, :rows_kv].reshape(total_kv.shape)
+    prior_k = prior[:, rows_kv, : total_k.shape[1]]
     heads_out = finish(
         pq, num_local, den_local, kv_blocks, k_blocks, prior_kv[None], prior_k[None]
     )

time: 136 us -> 84.9 us (0.62)
  starting transfers between devices: 83.1 us -> 36.3 us
  waiting for transfers between devices: 26.2 us -> 20.8 us
  matrix products: 16.7 us -> 18.5 us
    ppermute x40 -> x17, starting transfers between devices: 83.1 us -> 36.3 us  [send(): return tmap(lambda t: lax.ppermute(t, axis, perm=pairs), tree)]
    ppermute x40 -> x17, waiting for transfers between devices: 26.2 us -> 20.8 us  [send(): return tmap(lambda t: lax.ppermute(t, axis, perm=pairs), tree)]
    dot_general x1, matrix products: 2.46 us -> 4.25 us  [block_terms(): jnp.einsum('rnihd,rnjhd->rnhij', pq, pk, preferred_element_type=jnp.float32)]
  transfers between devices with their start and end apart: 40 -> 17, of which waited for: 16 -> 10; matrix products, arithmetic and copies ran while one was open for 7% -> 5% of each run, Pallas kernels for 0% -> 0%
where the time goes in v3:
time: 84.9 us; the launch traced here: 84.4 us
  starting transfers between devices  36.3 us (43%)
  waiting for transfers between devices  20.8 us (24%)
  matrix products  18.5 us (22%)
  other arithmetic  4.37 us (5%)
  local copies, waits for them, and re-layouts  4.12 us (5%)
    ppermute x17, starting transfers between devices, send(): return tmap(lambda t: lax.ppermute(t, axis, perm=pairs), tree)  36.3 us
    ppermute x17, waiting for transfers between devices, send(): return tmap(lambda t: lax.ppermute(t, axis, perm=pairs), tree)  20.8 us
    dot_general x1, matrix products, shards(): jnp.einsum('rtd,de->rte', frames_in, w_qkv, preferred_element_type=jnp.fl...  6.06 us
    dot_general x1, matrix products, block_terms(): jnp.einsum('rnihd,rnjhd->rnhij', pq, pk, preferred_element_type=jnp.float32)  4.25 us
    convert_element_type x1, local copies, waits for them, and re-layouts, shards(): jnp.einsum('rtd,de->rte', frames_in, w_qkv, preferred_element_type=jnp.fl...  2.57 us
    dot_general x1, matrix products, finish(): jnp.einsum('rnihd,rnhde->rnihe', pq32, before_kv, precision=lax.Precision...  1.98 us
    add x7, other arithmetic, tmap(): return jax.tree.map(f, *trees)  1.86 us
  transfers between devices with their start and end apart: 17, of which 10 were waited for; matrix products, arithmetic and copies ran while one was open for 5% of the time, Pallas kernels for 0%

profile of v3, /device:TPU:1, one launch (start us, length us, event | category | flops | bytes accessed | tf_op | source)
XLA Modules:
  0.0 84.4 jit_solution(6860056412427030823)
XLA Ops:
  0.0 6.1 %convolution_convert_fusion = bf16[256,3072]{1,0:T(8,128)(2,1)} fusion(bf16[1024,3072]{1,0:T(8,128)(2,1)} %param.4, bf16[1,256,1024]{2,1,0:T(8,128)(2,1)} %param.3), kind=kOutput, calls=%fused_computation.3 | convolution fusion | flops 1611399168 | bytes 8388608 | tf_op jit(solution)/shard_map/rtd,de->rte/dot_general | solution.py:135
  6.1 2.6 %copy.10 = bf16[256,3072]{0,1:T(8,128)(2,1)} copy(bf16[256,3072]{1,0:T(8,128)(2,1)} %convolution_convert_fusion) | data formatting | bytes 3145728 | tf_op jit(solution)/shard_map/convert_element_type | solution.py:135
  8.6 1.4 %convert_reduce_fusion = f32[16,64]{1,0:T(8,128)S(1)} fusion(bf16[1,256,3,16,64]{1,4,3,2,0:T(8,128)(2,1)} %bitcast.60), kind=kLoop, calls=%fused_computation.23 | loop fusion | flops 2096128 | bytes 528384 | tf_op jit(solution)/shard_map/reduce_sum | solution.py:107
  10.0 1.6 %fusion.13 = f32[16,64,64]{2,1,0:T(8,128)S(1)} fusion(bf16[1,256,3,16,64]{1,4,3,2,0:T(8,128)(2,1)} %bitcast.61), kind=kOutput, calls=%fused_computation.27 | convolution fusion | flops 35127296 | bytes 1310720 | tf_op jit(solution)/shard_map/rnjhd,rnjhe->rnhde/dot_general | solution.py:106
  11.6 0.1 reshape_squeeze.4
  11.8 3.3 %collective-permute-start = (f32[16,33,128]{2,1,0:T(8,128)S(1)}, f32[16,33,128]{2,1,0:T(8,128)}, u32[]{:S(2)}, u32[]{:S(2)}) collective-permute-start(f32[16,33,128]{2,1,0:T(8,128)S(1)} %pad_maximum_fusion), channel_id=1, source_target_pairs={{0,2},{2,0},{1,3},{3,1},{4,6},{6,4},{5,7},{7,5},{8,10},{10,8},{9,1... | collective-permute-start | bytes 811016 | tf_op jit(solution)/shard_map/ppermute | solution.py:22
  15.1 1.4 %collective-permute-done = f32[16,33,128]{2,1,0:T(8,128)} collective-permute-done((f32[16,33,128]{2,1,0:T(8,128)S(1)}, f32[16,33,128]{2,1,0:T(8,128)}, u32[]{:S(2)}, u32[]{:S(2)}) %collective-permute-start) | collective-permute-done | bytes 270368 | tf_op jit(solution)/shard_map/ppermute | solution.py:22
  16.5 1.0 %broadcast_select_fusion = f32[16,33,128]{2,1,0:T(8,128)S(1)} fusion(f32[16,33,128]{2,1,0:T(8,128)} %collective-permute-done, pred[]{:T(512)S(6)} %eq.16, f32[16,1,128]{2,1,0:T(1,128)S(1)} %bitcast.68, f32[16,32,128]{2,1,0:T(8,128)S(1)} %reshape_squeeze.4), kind=kLoop, calls=%fused_computation.45 | loop fusion | flops 135168 | bytes 811009 | tf_op jit(solution)/shard_map/jit(_where)/select_n | solution.py:42
  17.5 1.0 %fusion.23 = f32[8,33,128]{2,1,0:T(8,128)S(1)} fusion(s32[]{:T(128)S(6)} %select_n.168, f32[16,32,128]{2,1,0:T(8,128)S(1)} %reshape_squeeze.4, f32[16,1,128]{2,1,0:T(1,128)S(1)} %bitcast.69, f32[16,33,128]{2,1,0:T(8,128)S(1)} %broadcast_select_fusion, f32[16,33,128]{2,1,0:T(8,128)} %collective-permute-done, pred[]{:T(512)S(6)} %eq.16), kind=kLoop, calls=%fused_computation.42 | loop fusion | flops 101376 | bytes 675845 | tf_op jit(solution)/shard_map/add | solution.py:18
  18.4 1.1 %collective-permute-start.1 = (f32[8,33,128]{2,1,0:T(8,128)S(1)}, f32[8,33,128]{2,1,0:T(8,128)S(1)}, u32[]{:S(2)}, u32[]{:S(2)}) collective-permute-start(f32[8,33,128]{2,1,0:T(8,128)S(1)} %fusion.23), channel_id=1, source_target_pairs={{0,4},{4,0},{1,5},{5,1},{2,6},{6,2},{3,7},{7,3},{8,12},{12,8},{9,1... | collective-permute-start | bytes 405512 | tf_op jit(solution)/shard_map/ppermute | solution.py:22
  19.6 6.4 %collective-permute-done.1 = f32[8,33,128]{2,1,0:T(8,128)S(1)} collective-permute-done((f32[8,33,128]{2,1,0:T(8,128)S(1)}, f32[8,33,128]{2,1,0:T(8,128)S(1)}, u32[]{:S(2)}, u32[]{:S(2)}) %collective-permute-start.1) | collective-permute-done | bytes 135200 | tf_op jit(solution)/shard_map/ppermute | solution.py:22
  26.0 0.6 constant_dynamic-slice_fusion
  26.6 1.0 %collective-permute-start.4 = (f32[4,33,128]{2,1,0:T(8,128)}, f32[4,33,128]{2,1,0:T(8,128)S(1)}, u32[]{:S(2)}, u32[]{:S(2)}) collective-permute-start(f32[4,33,128]{2,1,0:T(8,128)} %constant_dynamic-slice_fusion), channel_id=1, source_target_pairs={{0,24},{8,0},{16,8},{24,16},{1,25},{9,1},{17,9},{25,17},{2,26},{10... | collective-permute-start | bytes 202760 | tf_op jit(solution)/shard_map/ppermute | solution.py:22
  27.7 0.3 collective-permute-start.3
  28.0 0.7 collective-permute-start.2
  28.7 1.8 %collective-permute-done.4 = f32[4,33,128]{2,1,0:T(8,128)S(1)} collective-permute-done((f32[4,33,128]{2,1,0:T(8,128)}, f32[4,33,128]{2,1,0:T(8,128)S(1)}, u32[]{:S(2)}, u32[]{:S(2)}) %collective-permute-start.4) | collective-permute-done | bytes 67616 | tf_op jit(solution)/shard_map/ppermute | solution.py:22
  30.5 2.4 %collective-permute-done.3 = f32[4,33,128]{2,1,0:T(8,128)} collective-permute-done((f32[4,33,128]{2,1,0:T(8,128)}, f32[4,33,128]{2,1,0:T(8,128)}, u32[]{:S(2)}, u32[]{:S(2)}) %collective-permute-start.3) | collective-permute-done | bytes 67616 | tf_op jit(solution)/shard_map/ppermute | solution.py:22
  32.9 2.4 %collective-permute-done.2 = f32[4,33,128]{2,1,0:T(8,128)} collective-permute-done((f32[4,33,128]{2,1,0:T(8,128)}, f32[4,33,128]{2,1,0:T(8,128)}, u32[]{:S(2)}, u32[]{:S(2)}) %collective-permute-start.2) | collective-permute-done | bytes 67616 | tf_op jit(solution)/shard_map/ppermute | solution.py:22
  35.3 0.8 dynamic-slice_add_fusion
  36.0 7.5 %collective-permute-start.11 = (f32[1,33,128]{2,1,0:T(8,128)S(1)}, f32[1,33,128]{2,1,0:T(8,128)S(1)}, u32[]{:S(2)}, u32[]{:S(2)}) collective-permute-start(f32[1,33,128]{2,1,0:T(8,128)S(1)} %dynamic-slice_add_fusion), channel_id=1, source_target_pairs={{0,224},{1,225},{2,226},{3,227},{4,228},{5,229},{6,230},{7,231},{8... | collective-permute-start | bytes 50696 | tf_op jit(solution)/shard_map/ppermute | solution.py:22
  43.5 1.3 %collective-permute-start.10 = (f32[1,33,128]{2,1,0:T(8,128)S(1)}, f32[1,33,128]{2,1,0:T(8,128)S(1)}, u32[]{:S(2)}, u32[]{:S(2)}) collective-permute-start(f32[1,33,128]{2,1,0:T(8,128)S(1)} %dynamic-slice_add_fusion), channel_id=1, source_target_pairs={{0,192},{32,224},{1,193},{33,225},{2,194},{34,226},{3,195},{35,227... | collective-permute-start | bytes 50696 | tf_op jit(solution)/shard_map/ppermute | solution.py:22
  44.8 1.3 %collective-permute-start.9 = (f32[1,33,128]{2,1,0:T(8,128)S(1)}, f32[1,33,128]{2,1,0:T(8,128)S(1)}, u32[]{:S(2)}, u32[]{:S(2)}) collective-permute-start(f32[1,33,128]{2,1,0:T(8,128)S(1)} %dynamic-slice_add_fusion), channel_id=1, source_target_pairs={{0,160},{32,192},{64,224},{1,161},{33,193},{65,225},{2,162},{34,19... | collective-permute-start | bytes 50696 | tf_op jit(solution)/shard_map/ppermute | solution.py:22
  46.1 1.3 %collective-permute-start.8 = (f32[1,33,128]{2,1,0:T(8,128)S(1)}, f32[1,33,128]{2,1,0:T(8,128)S(1)}, u32[]{:S(2)}, u32[]{:S(2)}) collective-permute-start(f32[1,33,128]{2,1,0:T(8,128)S(1)} %dynamic-slice_add_fusion), channel_id=1, source_target_pairs={{0,128},{32,160},{64,192},{96,224},{1,129},{33,161},{65,193},{97,2... | collective-permute-start | bytes 50696 | tf_op jit(solution)/shard_map/ppermute | solution.py:22
  47.4 4.9 %collective-permute-start.7 = (f32[1,33,128]{2,1,0:T(8,128)S(1)}, f32[1,33,128]{2,1,0:T(8,128)S(1)}, u32[]{:S(2)}, u32[]{:S(2)}) collective-permute-start(f32[1,33,128]{2,1,0:T(8,128)S(1)} %dynamic-slice_add_fusion), channel_id=1, source_target_pairs={{0,96},{32,128},{64,160},{96,192},{128,224},{1,97},{33,129},{65,16... | collective-permute-start | bytes 50696 | tf_op jit(solution)/shard_map/ppermute | solution.py:22
  52.3 0.0 collective-permute-done.11
  52.3 1.3 %collective-permute-start.6 = (f32[1,33,128]{2,1,0:T(8,128)S(1)}, f32[1,33,128]{2,1,0:T(8,128)S(1)}, u32[]{:S(2)}, u32[]{:S(2)}) collective-permute-start(f32[1,33,128]{2,1,0:T(8,128)S(1)} %dynamic-slice_add_fusion), channel_id=1, source_target_pairs={{0,64},{32,96},{64,128},{96,160},{128,192},{160,224},{1,65},{33,97... | collective-permute-start | bytes 50696 | tf_op jit(solution)/shard_map/ppermute | solution.py:22
  53.6 2.8 %collective-permute-start.5 = (f32[1,33,128]{2,1,0:T(8,128)S(1)}, f32[1,33,128]{2,1,0:T(8,128)S(1)}, u32[]{:S(2)}, u32[]{:S(2)}) collective-permute-start(f32[1,33,128]{2,1,0:T(8,128)S(1)} %dynamic-slice_add_fusion), channel_id=1, source_target_pairs={{0,32},{32,64},{64,96},{96,128},{128,160},{160,192},{192,224},{1,3... | collective-permute-start | bytes 50696 | tf_op jit(solution)/shard_map/ppermute | solution.py:22
  56.5 0.0 collective-permute-done.9
  56.5 0.0 collective-permute-done.8
  56.5 0.8 collective-permute-done.5
  57.4 0.1 collective-permute-start.14
  57.5 0.4 collective-permute-start.13
  57.8 1.1 %collective-permute-start.12 = (f32[1,33,128]{2,1,0:T(8,128)S(1)}, f32[1,33,128]{2,1,0:T(8,128)S(1)}, u32[]{:S(2)}, u32[]{:S(2)}) collective-permute-start(f32[1,33,128]{2,1,0:T(8,128)S(1)} %add_add_fusion.1), channel_id=1, source_target_pairs={{0,8},{8,16},{16,24},{24,0},{1,9},{9,17},{17,25},{25,1},{2,10},{10... | collective-permute-start | bytes 50696 | tf_op jit(solution)/shard_map/ppermute | solution.py:22
  58.9 1.2 %collective-permute-done.14 = f32[1,33,128]{2,1,0:T(8,128)S(1)} collective-permute-done((f32[1,33,128]{2,1,0:T(8,128)S(1)}, f32[1,33,128]{2,1,0:T(8,128)S(1)}, u32[]{:S(2)}, u32[]{:S(2)}) %collective-permute-start.14) | collective-permute-done | bytes 16928 | tf_op jit(solution)/shard_map/ppermute | solution.py:22
  60.1 1.6 %collective-permute-done.13 = f32[1,33,128]{2,1,0:T(8,128)S(1)} collective-permute-done((f32[1,33,128]{2,1,0:T(8,128)S(1)}, f32[1,33,128]{2,1,0:T(8,128)S(1)}, u32[]{:S(2)}, u32[]{:S(2)}) %collective-permute-start.13) | collective-permute-done | bytes 16928 | tf_op jit(solution)/shard_map/ppermute | solution.py:22
  61.7 0.8 collective-permute-done.12
  62.5 0.6 gather_fusion
  63.1 2.8 %collective-permute-start.15 = (f32[4,33,128]{2,1,0:T(8,128)S(1)}, f32[4,33,128]{2,1,0:T(8,128)S(1)}, u32[]{:S(2)}, u32[]{:S(2)}) collective-permute-start(f32[4,33,128]{2,1,0:T(8,128)S(1)} %add_add_fusion), channel_id=1, source_target_pairs={{0,4},{4,0},{1,5},{5,1},{2,6},{6,2},{3,7},{7,3},{8,12},{12,8},{9,1... | collective-permute-start | bytes 202760 | tf_op jit(solution)/shard_map/ppermute | solution.py:22
  66.0 0.0 copy-start.2
  66.0 2.0 %collective-permute-done.15 = f32[4,33,128]{2,1,0:T(8,128)S(1)} collective-permute-done((f32[4,33,128]{2,1,0:T(8,128)S(1)}, f32[4,33,128]{2,1,0:T(8,128)S(1)}, u32[]{:S(2)}, u32[]{:S(2)}) %collective-permute-start.15) | collective-permute-done | bytes 67616 | tf_op jit(solution)/shard_map/ppermute | solution.py:22
  68.0 5.1 %collective-permute-start.16 = (f32[8,33,128]{2,1,0:T(8,128)S(1)}, f32[8,33,128]{2,1,0:T(8,128)S(1)}, u32[]{:S(2)}, u32[]{:S(2)}) collective-permute-start(f32[8,33,128]{2,1,0:T(8,128)S(1)} %maximum_add_fusion.1), channel_id=1, source_target_pairs={{0,2},{2,0},{1,3},{3,1},{4,6},{6,4},{5,7},{7,5},{8,10},{10,8},{9,1... | collective-permute-start | bytes 405512 | tf_op jit(solution)/shard_map/ppermute | solution.py:22
  73.1 4.2 %select_reduce_fusion = (f32[16,256]{1,0:T(8,128)}, bf16[16,256,256]{1,2,0:T(8,128)(2,1)}) fusion(pred[256,256]{0,1:T(8,128)(4,1)S(1)} %iota_compare_fusion, bf16[1,256,3,16,64]{1,4,3,2,0:T(8,128)(2,1)} %bitcast.62), kind=kOutput, calls=%fused_computation.1 | convolution fusion | flops 140505088 | bytes 3227648 | tf_op jit(solution)/shard_map/rnihd,rnjhd->rnhij/dot_general | solution.py:100
  77.5 1.6 %fusion.30 = f32[16,1,256]{2,1,0:T(1,128)S(1)} fusion(f32[16,64,1]{1,2,0:T(1,128)S(1)} %bitcast.75, bf16[1,256,3,16,64]{1,4,3,2,0:T(8,128)(2,1)} %bitcast.63), kind=kOutput, calls=%fused_computation.67 | convolution fusion | flops 4718592 | bytes 544768 | tf_op jit(solution)/shard_map/rnihd,rnhd->rnih/dot_general | solution.py:119
  79.1 0.0 copy-start.3
  79.1 0.2 broadcast_in_dim_broadcast_in_dim_reshape.3
  79.3 2.0 %fusion.18 = f32[16,64,256]{2,1,0:T(8,128)S(1)} fusion(f32[16,64,64]{2,1,0:T(8,128)S(1)} %broadcast_in_dim_broadcast_in_dim_reshape.3, f32[16,64,64]{2,1,0:T(8,128)S(1)} %fusion.13, bf16[1,256,3,16,64]{1,4,3,2,0:T(8,128)(2,1)} %bitcast.64), kind=kOutput, calls=%fused_computation.32 | convolution fusion | flops 203030528 | bytes 2097152 | tf_op jit(solution)/shard_map/rnihd,rnhde->rnihe/dot_general | solution.py:116
  81.3 1.5 %divide_convert_fusion = bf16[1,1,256,16,64]{2,4,3,1,0:T(8,128)(2,1)S(1)} fusion(f32[16,64,256]{2,1,0:T(8,128)S(1)} %fusion.18, bf16[16,256,256]{1,2,0:T(8,128)(2,1)S(1)} %copy-done.5, pred[256,256]{0,1:T(8,128)(4,1)S(1)} %copy-done.3, f32[256,16]{0,1:T(8,128)S(1)} %fusion.24, bf16[1,256,3,16,64]{1,4,3,2,0:T(8,128)(2,1)} %bitcast.65), kind=kOutput, calls=%fused_computation.24 | convolution fusion | flops 136052736 | bytes 4276224 | tf_op jit(solution)/shard_map/rnhij,rnjhd->rnihd/dot_general | solution.py:105
  82.8 1.5 %fusion.5 = bf16[1,256,1024]{2,1,0:T(8,128)(2,1)} fusion(bf16[256,1024]{0,1:T(8,128)(2,1)S(1)} %bitcast.66, bf16[1024,1024]{1,0:T(8,128)(2,1)S(1)} %copy-done), kind=kOutput, calls=%fused_computation.16 | convolution fusion | flops 537133056 | bytes 3145728 | tf_op jit(solution)/shard_map/rtd,de->rte/dot_general | solution.py:153
  (31 shorter events, 0.3 us)
Async XLA Ops:
  0.0 82.8 %copy-start = (bf16[1024,1024]{1,0:T(8,128)(2,1)S(1)}, bf16[1024,1024]{1,0:T(8,128)(2,1)}, u32[]{:S(2)}) copy-start(bf16[1024,1024]{1,0:T(8,128)(2,1)} %param.5) | copy-start | bytes 6291460
  11.8 4.7 %collective-permute-start = (f32[16,33,128]{2,1,0:T(8,128)S(1)}, f32[16,33,128]{2,1,0:T(8,128)}, u32[]{:S(2)}, u32[]{:S(2)}) collective-permute-start(f32[16,33,128]{2,1,0:T(8,128)S(1)} %pad_maximum_fusion), channel_id=1, source_target_pairs={{0,2},{2,0},{1,3},{3,1},{4,6},{6,4},{5,7},{7,5},{8,10},{10,8},{9,1... | collective-permute-start | bytes 811016 | tf_op jit(solution)/shard_map/ppermute | solution.py:22
  18.4 7.5 %collective-permute-start.1 = (f32[8,33,128]{2,1,0:T(8,128)S(1)}, f32[8,33,128]{2,1,0:T(8,128)S(1)}, u32[]{:S(2)}, u32[]{:S(2)}) collective-permute-start(f32[8,33,128]{2,1,0:T(8,128)S(1)} %fusion.23), channel_id=1, source_target_pairs={{0,4},{4,0},{1,5},{5,1},{2,6},{6,2},{3,7},{7,3},{8,12},{12,8},{9,1... | collective-permute-start | bytes 405512 | tf_op jit(solution)/shard_map/ppermute | solution.py:22
  26.6 3.8 %collective-permute-start.4 = (f32[4,33,128]{2,1,0:T(8,128)}, f32[4,33,128]{2,1,0:T(8,128)S(1)}, u32[]{:S(2)}, u32[]{:S(2)}) collective-permute-start(f32[4,33,128]{2,1,0:T(8,128)} %constant_dynamic-slice_fusion), channel_id=1, source_target_pairs={{0,24},{8,0},{16,8},{24,16},{1,25},{9,1},{17,9},{25,17},{2,26},{10... | collective-permute-start | bytes 202760 | tf_op jit(solution)/shard_map/ppermute | solution.py:22
  27.7 5.2 %collective-permute-start.3 = (f32[4,33,128]{2,1,0:T(8,128)}, f32[4,33,128]{2,1,0:T(8,128)}, u32[]{:S(2)}, u32[]{:S(2)}) collective-permute-start(f32[4,33,128]{2,1,0:T(8,128)} %constant_dynamic-slice_fusion), channel_id=1, source_target_pairs={{0,16},{8,24},{16,0},{24,8},{1,17},{9,25},{17,1},{25,9},{2,18},{10... | collective-permute-start | bytes 202760 | tf_op jit(solution)/shard_map/ppermute | solution.py:22
  28.0 7.3 %collective-permute-start.2 = (f32[4,33,128]{2,1,0:T(8,128)}, f32[4,33,128]{2,1,0:T(8,128)}, u32[]{:S(2)}, u32[]{:S(2)}) collective-permute-start(f32[4,33,128]{2,1,0:T(8,128)} %constant_dynamic-slice_fusion), channel_id=1, source_target_pairs={{0,8},{8,16},{16,24},{24,0},{1,9},{9,17},{17,25},{25,1},{2,10},{10... | collective-permute-start | bytes 202760 | tf_op jit(solution)/shard_map/ppermute | solution.py:22
  30.5 32.0 %copy-start.1 = (f32[4,33,128]{2,1,0:T(8,128)}, f32[4,33,128]{2,1,0:T(8,128)S(1)}, u32[]{:S(2)}) copy-start(f32[4,33,128]{2,1,0:T(8,128)S(1)} %collective-permute-done.4) | copy-start | bytes 202756
  36.0 16.3 %collective-permute-start.11 = (f32[1,33,128]{2,1,0:T(8,128)S(1)}, f32[1,33,128]{2,1,0:T(8,128)S(1)}, u32[]{:S(2)}, u32[]{:S(2)}) collective-permute-start(f32[1,33,128]{2,1,0:T(8,128)S(1)} %dynamic-slice_add_fusion), channel_id=1, source_target_pairs={{0,224},{1,225},{2,226},{3,227},{4,228},{5,229},{6,230},{7,231},{8... | collective-permute-start | bytes 50696 | tf_op jit(solution)/shard_map/ppermute | solution.py:22
  43.5 10.1 %collective-permute-start.10 = (f32[1,33,128]{2,1,0:T(8,128)S(1)}, f32[1,33,128]{2,1,0:T(8,128)S(1)}, u32[]{:S(2)}, u32[]{:S(2)}) collective-permute-start(f32[1,33,128]{2,1,0:T(8,128)S(1)} %dynamic-slice_add_fusion), channel_id=1, source_target_pairs={{0,192},{32,224},{1,193},{33,225},{2,194},{34,226},{3,195},{35,227... | collective-permute-start | bytes 50696 | tf_op jit(solution)/shard_map/ppermute | solution.py:22
  44.8 11.7 %collective-permute-start.9 = (f32[1,33,128]{2,1,0:T(8,128)S(1)}, f32[1,33,128]{2,1,0:T(8,128)S(1)}, u32[]{:S(2)}, u32[]{:S(2)}) collective-permute-start(f32[1,33,128]{2,1,0:T(8,128)S(1)} %dynamic-slice_add_fusion), channel_id=1, source_target_pairs={{0,160},{32,192},{64,224},{1,161},{33,193},{65,225},{2,162},{34,19... | collective-permute-start | bytes 50696 | tf_op jit(solution)/shard_map/ppermute | solution.py:22
  46.1 10.4 %collective-permute-start.8 = (f32[1,33,128]{2,1,0:T(8,128)S(1)}, f32[1,33,128]{2,1,0:T(8,128)S(1)}, u32[]{:S(2)}, u32[]{:S(2)}) collective-permute-start(f32[1,33,128]{2,1,0:T(8,128)S(1)} %dynamic-slice_add_fusion), channel_id=1, source_target_pairs={{0,128},{32,160},{64,192},{96,224},{1,129},{33,161},{65,193},{97,2... | collective-permute-start | bytes 50696 | tf_op jit(solution)/shard_map/ppermute | solution.py:22
  47.4 9.1 %collective-permute-start.7 = (f32[1,33,128]{2,1,0:T(8,128)S(1)}, f32[1,33,128]{2,1,0:T(8,128)S(1)}, u32[]{:S(2)}, u32[]{:S(2)}) collective-permute-start(f32[1,33,128]{2,1,0:T(8,128)S(1)} %dynamic-slice_add_fusion), channel_id=1, source_target_pairs={{0,96},{32,128},{64,160},{96,192},{128,224},{1,97},{33,129},{65,16... | collective-permute-start | bytes 50696 | tf_op jit(solution)/shard_map/ppermute | solution.py:22
  52.3 4.2 %collective-permute-start.6 = (f32[1,33,128]{2,1,0:T(8,128)S(1)}, f32[1,33,128]{2,1,0:T(8,128)S(1)}, u32[]{:S(2)}, u32[]{:S(2)}) collective-permute-start(f32[1,33,128]{2,1,0:T(8,128)S(1)} %dynamic-slice_add_fusion), channel_id=1, source_target_pairs={{0,64},{32,96},{64,128},{96,160},{128,192},{160,224},{1,65},{33,97... | collective-permute-start | bytes 50696 | tf_op jit(solution)/shard_map/ppermute | solution.py:22
  53.6 3.7 %collective-permute-start.5 = (f32[1,33,128]{2,1,0:T(8,128)S(1)}, f32[1,33,128]{2,1,0:T(8,128)S(1)}, u32[]{:S(2)}, u32[]{:S(2)}) collective-permute-start(f32[1,33,128]{2,1,0:T(8,128)S(1)} %dynamic-slice_add_fusion), channel_id=1, source_target_pairs={{0,32},{32,64},{64,96},{96,128},{128,160},{160,192},{192,224},{1,3... | collective-permute-start | bytes 50696 | tf_op jit(solution)/shard_map/ppermute | solution.py:22
  57.4 2.7 %collective-permute-start.14 = (f32[1,33,128]{2,1,0:T(8,128)S(1)}, f32[1,33,128]{2,1,0:T(8,128)S(1)}, u32[]{:S(2)}, u32[]{:S(2)}) collective-permute-start(f32[1,33,128]{2,1,0:T(8,128)S(1)} %add_add_fusion.1), channel_id=1, source_target_pairs={{0,24},{8,0},{16,8},{24,16},{1,25},{9,1},{17,9},{25,17},{2,26},{10... | collective-permute-start | bytes 50696 | tf_op jit(solution)/shard_map/ppermute | solution.py:22
  57.5 4.2 %collective-permute-start.13 = (f32[1,33,128]{2,1,0:T(8,128)S(1)}, f32[1,33,128]{2,1,0:T(8,128)S(1)}, u32[]{:S(2)}, u32[]{:S(2)}) collective-permute-start(f32[1,33,128]{2,1,0:T(8,128)S(1)} %add_add_fusion.1), channel_id=1, source_target_pairs={{0,16},{8,24},{16,0},{24,8},{1,17},{9,25},{17,1},{25,9},{2,18},{10... | collective-permute-start | bytes 50696 | tf_op jit(solution)/shard_map/ppermute | solution.py:22
  57.8 4.7 %collective-permute-start.12 = (f32[1,33,128]{2,1,0:T(8,128)S(1)}, f32[1,33,128]{2,1,0:T(8,128)S(1)}, u32[]{:S(2)}, u32[]{:S(2)}) collective-permute-start(f32[1,33,128]{2,1,0:T(8,128)S(1)} %add_add_fusion.1), channel_id=1, source_target_pairs={{0,8},{8,16},{16,24},{24,0},{1,9},{9,17},{17,25},{25,1},{2,10},{10... | collective-permute-start | bytes 50696 | tf_op jit(solution)/shard_map/ppermute | solution.py:22
  63.1 4.9 %collective-permute-start.15 = (f32[4,33,128]{2,1,0:T(8,128)S(1)}, f32[4,33,128]{2,1,0:T(8,128)S(1)}, u32[]{:S(2)}, u32[]{:S(2)}) collective-permute-start(f32[4,33,128]{2,1,0:T(8,128)S(1)} %add_add_fusion), channel_id=1, source_target_pairs={{0,4},{4,0},{1,5},{5,1},{2,6},{6,2},{3,7},{7,3},{8,12},{12,8},{9,1... | collective-permute-start | bytes 202760 | tf_op jit(solution)/shard_map/ppermute | solution.py:22
  66.0 7.2 %copy-start.2 = (pred[256,256]{0,1:T(8,128)(4,1)}, pred[256,256]{0,1:T(8,128)(4,1)S(1)}, u32[]{:S(2)}) copy-start(pred[256,256]{0,1:T(8,128)(4,1)S(1)} %iota_compare_fusion) | copy-start | bytes 196612
  68.0 9.3 %collective-permute-start.16 = (f32[8,33,128]{2,1,0:T(8,128)S(1)}, f32[8,33,128]{2,1,0:T(8,128)S(1)}, u32[]{:S(2)}, u32[]{:S(2)}) collective-permute-start(f32[8,33,128]{2,1,0:T(8,128)S(1)} %maximum_add_fusion.1), channel_id=1, source_target_pairs={{0,2},{2,0},{1,3},{3,1},{4,6},{6,4},{5,7},{7,5},{8,10},{10,8},{9,1... | collective-permute-start | bytes 405512 | tf_op jit(solution)/shard_map/ppermute | solution.py:22
  79.1 2.2 %copy-start.4 = (f32[16,256]{1,0:T(8,128)S(1)}, f32[16,256]{1,0:T(8,128)}, u32[]{:S(2)}) copy-start(f32[16,256]{1,0:T(8,128)} %get-tuple-element.9) | copy-start | bytes 49156
  79.1 2.2 %copy-start.3 = (pred[256,256]{0,1:T(8,128)(4,1)S(1)}, pred[256,256]{0,1:T(8,128)(4,1)}, u32[]{:S(2)}) copy-start(pred[256,256]{0,1:T(8,128)(4,1)} %copy-done.2) | copy-start | bytes 196612
  79.2 2.0 %copy-start.5 = (bf16[16,256,256]{1,2,0:T(8,128)(2,1)S(1)}, bf16[16,256,256]{1,2,0:T(8,128)(2,1)}, u32[]{:S(2)}) copy-start(bf16[16,256,256]{1,2,0:T(8,128)(2,1)} %get-tuple-element.10) | copy-start | bytes 6291460

commit v4 on v3

--- a/solution.py
+++ b/solution.py
@@ -52,43 +52,60 @@
     return tmap(lambda a, b: jnp.concatenate([a, b], axis=0), lo, hi)
 
 
+def cyclic(n, s):
+    return [(i, (i + s) % n) for i in range(n)]
+
+
 def entering(total):
     core = lax.axis_index("frm")
     xh = lax.axis_index("seg_x")
     y = lax.axis_index("seg_y")
-    z = lax.axis_index("seg_z")
     n_y = lax.axis_size("seg_y")
     n_z = lax.axis_size("seg_z")
-    lo, hi = ordered(total, swap(total, "frm"), core == 0)
-    own_core = keep(lo, core == 1)
-    chip = part(tmap(jnp.add, lo, hi), core, 2)
-    lo, hi = ordered(chip, swap(chip, "seg_x"), xh == 0)
-    own_x = keep(lo, xh == 1)
-    row = part(tmap(jnp.add, lo, hi), xh, 2)
-    own_y = tmap(jnp.zeros_like, row)
-    plane = part(row, y, n_y)
-    for s in range(1, n_y):
-        came = send(row, "seg_y", [(i, (i + s) % n_y) for i in range(n_y)])
-        own_y = tmap(lambda a, b: a + jnp.where(y >= s, b, jnp.zeros_like(b)), own_y, came)
-        plane = tmap(jnp.add, plane, part(came, y, n_y))
-    own_z = tmap(jnp.zeros_like, plane)
-    for s in range(1, n_z):
-        own_z = tmap(jnp.add, own_z, send(plane, "seg_z", forward(n_z, s)))
-    pieces = [own_z] + [
-        send(own_z, "seg_y", [(i, (i + s) % n_y) for i in range(n_y)]) for s in range(1, n_y)
+    add = lambda a, b: tmap(jnp.add, a, b)
+    own_c = part(total, core, 2)
+    got_c = swap(part(total, 1 - core, 2), "frm")
+    lo, hi = ordered(own_c, got_c, core == 0)
+    chip = add(lo, hi)
+    own_x = part(chip, xh, 2)
+    got_x = swap(part(chip, 1 - xh, 2), "seg_x")
+    lo, hi = ordered(own_x, got_x, xh == 0)
+    row = add(lo, hi)
+    came = [part(row, y, n_y)] + [
+        send(part(row, (y + s) % n_y, n_y), "seg_y", cyclic(n_y, s)) for s in range(1, n_y)
+    ]
+    plane = came[0]
+    for c in came[1:]:
+        plane = add(plane, c)
+    upto = plane
+    s = 1
+    while s < n_z:
+        upto = add(upto, send(upto, "seg_z", forward(n_z, s)))
+        s *= 2
+    before_z = tmap(jnp.subtract, upto, plane)
+
+    def for_row(t):
+        out = before_z
+        for s, c in enumerate(came):
+            out = add(out, keep(c, (y - s) % n_y < t))
+        return out
+
+    pieces = [for_row(y)] + [
+        send(for_row((y + s) % n_y), "seg_y", cyclic(n_y, s)) for s in range(1, n_y)
     ]
     order = (y - jnp.arange(n_y)) % n_y
     quarter = tmap(
-        lambda *p: jnp.stack(p)[order].reshape(
-            (-1,) + p[0].shape[1:]
-        ),
+        lambda *p: jnp.stack(p)[order].reshape((-1,) + p[0].shape[1:]),
         *pieces,
     )
-    quarter = tmap(jnp.add, quarter, own_y)
-    lo, hi = ordered(quarter, swap(quarter, "seg_x"), xh == 0)
-    half = tmap(jnp.add, joined(lo, hi), own_x)
-    lo, hi = ordered(half, swap(half, "frm"), core == 0)
-    return tmap(jnp.add, joined(lo, hi), own_core)
+    got = swap(add(quarter, keep(own_x, xh == 0)), "seg_x")
+    lo = tmap(lambda a, b: jnp.where(xh == 0, a, b), quarter, got)
+    hi = tmap(lambda a, b, c: jnp.where(xh == 0, b, a + c), quarter, got, got_x)
+    half = joined(lo, hi)
+    got = swap(add(half, keep(own_c, core == 0)), "frm")
+    lo = tmap(lambda a, b: jnp.where(core == 0, a, b), half, got)
+    hi = tmap(lambda a, b, c: jnp.where(core == 0, b, a + c), half, got, got_c)
+    return joined(lo, hi)
 
 
 def block_terms(phi_q, phi_k, values, span):

time: 84.9 us -> 82.1 us (0.967)
  starting transfers between devices: 36.3 us -> 39.9 us
  waiting for transfers between devices: 20.8 us -> 17.6 us
  other arithmetic: 4.37 us -> 2.41 us
    ppermute x17 -> x13, starting transfers between devices: 36.3 us -> 39.9 us  [send(): return tmap(lambda t: lax.ppermute(t, axis, perm=pairs), tree)]
    ppermute x17 -> x13, waiting for transfers between devices: 20.8 us -> 17.6 us  [send(): return tmap(lambda t: lax.ppermute(t, axis, perm=pairs), tree)]
    add x7 -> x8, other arithmetic: 1.86 us -> 0.14 us  [tmap(): return jax.tree.map(f, *trees)]
    select_n x3 -> x2, other arithmetic: 1.05 us -> 0.05 us  [the longest x1 0.03 us: entering(): hi = tmap(lambda a, b, c: jnp.where(core == 0, b, a + c), half, got, got_c)]
  transfers between devices with their start and end apart: 17 -> 13, of which waited for: 10 -> 10; matrix products, arithmetic and copies ran while one was open for 5% -> 5% of each run, Pallas kernels for 0% -> 0%
where the time goes in v4:
time: 82.1 us; the launch traced here: 81.7 us
  starting transfers between devices  39.9 us (49%)
  matrix products  17.9 us (22%)
  waiting for transfers between devices  17.6 us (21%)
  local copies, waits for them, and re-layouts  3.46 us (4%)
  other arithmetic  2.41 us (3%)
    ppermute x13, starting transfers between devices, send(): return tmap(lambda t: lax.ppermute(t, axis, perm=pairs), tree)  39.9 us
    ppermute x13, waiting for transfers between devices, send(): return tmap(lambda t: lax.ppermute(t, axis, perm=pairs), tree)  17.6 us
    dot_general x1, matrix products, shards(): jnp.einsum('rtd,de->rte', frames_in, w_qkv, preferred_element_type=jnp.fl...  6.06 us
    dot_general x1, matrix products, block_terms(): jnp.einsum('rnihd,rnjhd->rnhij', pq, pk, preferred_element_type=jnp.float32)  3.65 us
    convert_element_type x1, local copies, waits for them, and re-layouts, shards(): jnp.einsum('rtd,de->rte', frames_in, w_qkv, preferred_element_type=jnp.fl...  2.57 us
    dot_general x1, matrix products, finish(): jnp.einsum('rnihd,rnhde->rnihe', pq32, before_kv, precision=lax.Precision...  1.98 us
  transfers between devices with their start and end apart: 13, of which 10 were waited for; matrix products, arithmetic and copies ran while one was open for 5% of the time, Pallas kernels for 0%

profile of v4, /device:TPU:1, one launch (start us, length us, event | category | flops | bytes accessed | tf_op | source)
XLA Modules:
  0.0 81.7 jit_solution(10068671724463981724)
XLA Ops:
  0.0 0.0 copy-start
  0.0 6.1 %convolution_convert_fusion = bf16[256,3072]{1,0:T(8,128)(2,1)} fusion(bf16[1024,3072]{1,0:T(8,128)(2,1)} %param.4, bf16[1,256,1024]{2,1,0:T(8,128)(2,1)} %param.3), kind=kOutput, calls=%fused_computation.3 | convolution fusion | flops 1611399168 | bytes 8388608 | tf_op jit(solution)/shard_map/rtd,de->rte/dot_general | solution.py:152
  6.1 2.6 %copy.10 = bf16[256,3072]{0,1:T(8,128)(2,1)} copy(bf16[256,3072]{1,0:T(8,128)(2,1)} %convolution_convert_fusion) | data formatting | bytes 3145728 | tf_op jit(solution)/shard_map/convert_element_type | solution.py:152
  8.6 1.4 %convert_reduce_fusion = f32[16,64]{1,0:T(8,128)S(1)} fusion(bf16[1,256,3,16,64]{1,4,3,2,0:T(8,128)(2,1)} %bitcast.61), kind=kLoop, calls=%fused_computation.23 | loop fusion | flops 2096128 | bytes 528384 | tf_op jit(solution)/shard_map/reduce_sum | solution.py:124
  10.0 1.6 %fusion.13 = f32[16,64,64]{2,1,0:T(8,128)S(1)} fusion(bf16[1,256,3,16,64]{1,4,3,2,0:T(8,128)(2,1)} %bitcast.62), kind=kOutput, calls=%fused_computation.27 | convolution fusion | flops 35127296 | bytes 1310720 | tf_op jit(solution)/shard_map/rnjhd,rnjhe->rnhde/dot_general | solution.py:123
  11.6 0.1 reshape_squeeze.4
  11.8 3.3 %collective-permute-start = (f32[8,33,128]{2,1,0:T(8,128)S(1)}, f32[8,33,128]{2,1,0:T(8,128)S(1)}, u32[]{:S(2)}, u32[]{:S(2)}) collective-permute-start(f32[8,33,128]{2,1,0:T(8,128)S(1)} %fusion.22), channel_id=1, source_target_pairs={{0,2},{2,0},{1,3},{3,1},{4,6},{6,4},{5,7},{7,5},{8,10},{10,8},{9,1... | collective-permute-start | bytes 405512 | tf_op jit(solution)/shard_map/ppermute | solution.py:22
  15.1 1.0 %collective-permute-done = f32[8,33,128]{2,1,0:T(8,128)S(1)} collective-permute-done((f32[8,33,128]{2,1,0:T(8,128)S(1)}, f32[8,33,128]{2,1,0:T(8,128)S(1)}, u32[]{:S(2)}, u32[]{:S(2)}) %collective-permute-start) | collective-permute-done | bytes 135200 | tf_op jit(solution)/shard_map/ppermute | solution.py:22
  16.2 1.1 %collective-permute-start.1 = (f32[4,33,128]{2,1,0:T(8,128)S(1)}, f32[4,33,128]{2,1,0:T(8,128)S(1)}, u32[]{:S(2)}, u32[]{:S(2)}) collective-permute-start(f32[4,33,128]{2,1,0:T(8,128)S(1)} %constant_dynamic-slice_fusion.3), channel_id=1, source_target_pairs={{0,4},{4,0},{1,5},{5,1},{2,6},{6,2},{3,7},{7,3},{8,12},{12,8},{9,1... | collective-permute-start | bytes 202760 | tf_op jit(solution)/shard_map/ppermute | solution.py:22
  17.3 4.1 %collective-permute-done.1 = f32[4,33,128]{2,1,0:T(8,128)S(1)} collective-permute-done((f32[4,33,128]{2,1,0:T(8,128)S(1)}, f32[4,33,128]{2,1,0:T(8,128)S(1)}, u32[]{:S(2)}, u32[]{:S(2)}) %collective-permute-start.1) | collective-permute-done | bytes 67616 | tf_op jit(solution)/shard_map/ppermute | solution.py:22
  21.4 0.1 collective-permute-start.2
  21.5 2.7 %collective-permute-start.4 = (f32[1,33,128]{2,1,0:T(8,128)S(1)}, f32[1,33,128]{2,1,0:T(8,128)S(1)}, u32[]{:S(2)}, u32[]{:S(2)}) collective-permute-start(f32[1,33,128]{2,1,0:T(8,128)S(1)} %get-tuple-element.15), channel_id=1, source_target_pairs={{0,24},{8,0},{16,8},{24,16},{1,25},{9,1},{17,9},{25,17},{2,26},{10... | collective-permute-start | bytes 50696 | tf_op jit(solution)/shard_map/ppermute | solution.py:22
  24.2 0.0 collective-permute-start.3
  24.2 1.2 %collective-permute-done.2 = f32[1,33,128]{2,1,0:T(8,128)S(1)} collective-permute-done((f32[1,33,128]{2,1,0:T(8,128)S(1)}, f32[1,33,128]{2,1,0:T(8,128)S(1)}, u32[]{:S(2)}, u32[]{:S(2)}) %collective-permute-start.2) | collective-permute-done | bytes 16928 | tf_op jit(solution)/shard_map/ppermute | solution.py:22
  25.3 0.0 collective-permute-done.4
  25.3 3.0 %collective-permute-done.3 = f32[1,33,128]{2,1,0:T(8,128)S(1)} collective-permute-done((f32[1,33,128]{2,1,0:T(8,128)S(1)}, f32[1,33,128]{2,1,0:T(8,128)S(1)}, u32[]{:S(2)}, u32[]{:S(2)}) %collective-permute-start.3) | collective-permute-done | bytes 16928 | tf_op jit(solution)/shard_map/ppermute | solution.py:22
  28.3 2.0 %collective-permute-start.5 = (f32[1,33,128]{2,1,0:T(8,128)S(1)}, f32[1,33,128]{2,1,0:T(8,128)S(1)}, u32[]{:S(2)}, u32[]{:S(2)}) collective-permute-start(f32[1,33,128]{2,1,0:T(8,128)S(1)} %add_add_fusion), channel_id=1, source_target_pairs={{0,32},{32,64},{64,96},{96,128},{128,160},{160,192},{192,224},{1,3... | collective-permute-start | bytes 50696 | tf_op jit(solution)/shard_map/ppermute | solution.py:22
  30.3 0.9 %collective-permute-done.5 = f32[1,33,128]{2,1,0:T(8,128)S(1)} collective-permute-done((f32[1,33,128]{2,1,0:T(8,128)S(1)}, f32[1,33,128]{2,1,0:T(8,128)S(1)}, u32[]{:S(2)}, u32[]{:S(2)}) %collective-permute-start.5) | collective-permute-done | bytes 16928 | tf_op jit(solution)/shard_map/ppermute | solution.py:22
  31.2 5.0 %collective-permute-start.6 = (f32[1,33,128]{2,1,0:T(8,128)S(1)}, f32[1,33,128]{2,1,0:T(8,128)S(1)}, u32[]{:S(2)}, u32[]{:S(2)}) collective-permute-start(f32[1,33,128]{2,1,0:T(8,128)S(1)} %add.268), channel_id=1, source_target_pairs={{0,64},{32,96},{64,128},{96,160},{128,192},{160,224},{1,65},{33,97... | collective-permute-start | bytes 50696 | tf_op jit(solution)/shard_map/ppermute | solution.py:22
  36.2 0.9 %collective-permute-done.6 = f32[1,33,128]{2,1,0:T(8,128)S(1)} collective-permute-done((f32[1,33,128]{2,1,0:T(8,128)S(1)}, f32[1,33,128]{2,1,0:T(8,128)S(1)}, u32[]{:S(2)}, u32[]{:S(2)}) %collective-permute-start.6) | collective-permute-done | bytes 16928 | tf_op jit(solution)/shard_map/ppermute | solution.py:22
  37.1 10.9 %collective-permute-start.7 = (f32[1,33,128]{2,1,0:T(8,128)S(1)}, f32[1,33,128]{2,1,0:T(8,128)S(1)}, u32[]{:S(2)}, u32[]{:S(2)}) collective-permute-start(f32[1,33,128]{2,1,0:T(8,128)S(1)} %add.269), channel_id=1, source_target_pairs={{0,128},{32,160},{64,192},{96,224},{1,129},{33,161},{65,193},{97,2... | collective-permute-start | bytes 50696 | tf_op jit(solution)/shard_map/ppermute | solution.py:22
  48.1 0.8 collective-permute-done.7
  48.9 0.1 collective-permute-start.8
  49.0 2.7 %collective-permute-start.10 = (f32[1,33,128]{2,1,0:T(8,128)S(1)}, f32[1,33,128]{2,1,0:T(8,128)S(1)}, u32[]{:S(2)}, u32[]{:S(2)}) collective-permute-start(f32[1,33,128]{2,1,0:T(8,128)S(1)} %get-tuple-element.12), channel_id=1, source_target_pairs={{0,24},{8,0},{16,8},{24,16},{1,25},{9,1},{17,9},{25,17},{2,26},{10... | collective-permute-start | bytes 50696 | tf_op jit(solution)/shard_map/ppermute | solution.py:22
  51.7 0.3 collective-permute-start.9
  52.0 0.8 %collective-permute-done.8 = f32[1,33,128]{2,1,0:T(8,128)S(1)} collective-permute-done((f32[1,33,128]{2,1,0:T(8,128)S(1)}, f32[1,33,128]{2,1,0:T(8,128)S(1)}, u32[]{:S(2)}, u32[]{:S(2)}) %collective-permute-start.8) | collective-permute-done | bytes 16928 | tf_op jit(solution)/shard_map/ppermute | solution.py:22
  52.8 0.0 collective-permute-done.10
  52.8 3.0 %collective-permute-done.9 = f32[1,33,128]{2,1,0:T(8,128)S(1)} collective-permute-done((f32[1,33,128]{2,1,0:T(8,128)S(1)}, f32[1,33,128]{2,1,0:T(8,128)S(1)}, u32[]{:S(2)}, u32[]{:S(2)}) %collective-permute-start.9) | collective-permute-done | bytes 16928 | tf_op jit(solution)/shard_map/ppermute | solution.py:22
  55.8 0.6 gather_fusion
  56.4 2.8 %collective-permute-start.11 = (f32[4,33,128]{2,1,0:T(8,128)S(1)}, f32[4,33,128]{2,1,0:T(8,128)S(1)}, u32[]{:S(2)}, u32[]{:S(2)}) collective-permute-start(f32[4,33,128]{2,1,0:T(8,128)S(1)} %select_add_fusion.2), channel_id=1, source_target_pairs={{0,4},{4,0},{1,5},{5,1},{2,6},{6,2},{3,7},{7,3},{8,12},{12,8},{9,1... | collective-permute-start | bytes 202760 | tf_op jit(solution)/shard_map/ppermute | solution.py:22
  59.3 0.0 copy-start.2
  59.3 2.0 %collective-permute-done.11 = f32[4,33,128]{2,1,0:T(8,128)S(1)} collective-permute-done((f32[4,33,128]{2,1,0:T(8,128)S(1)}, f32[4,33,128]{2,1,0:T(8,128)S(1)}, u32[]{:S(2)}, u32[]{:S(2)}) %collective-permute-start.11) | collective-permute-done | bytes 67616 | tf_op jit(solution)/shard_map/ppermute | solution.py:22
  61.4 9.0 %collective-permute-start.12 = (f32[8,33,128]{2,1,0:T(8,128)S(1)}, f32[8,33,128]{2,1,0:T(8,128)S(1)}, u32[]{:S(2)}, u32[]{:S(2)}) collective-permute-start(f32[8,33,128]{2,1,0:T(8,128)S(1)} %select_add_fusion), channel_id=1, source_target_pairs={{0,2},{2,0},{1,3},{3,1},{4,6},{6,4},{5,7},{7,5},{8,10},{10,8},{9,1... | collective-permute-start | bytes 405512 | tf_op jit(solution)/shard_map/ppermute | solution.py:22
  70.4 3.7 %select_reduce_fusion = (f32[16,256]{1,0:T(8,128)S(1)}, bf16[16,256,256]{1,2,0:T(8,128)(2,1)}) fusion(pred[256,256]{0,1:T(8,128)(4,1)S(1)} %iota_compare_fusion, bf16[1,256,3,16,64]{1,4,3,2,0:T(8,128)(2,1)} %bitcast.63), kind=kOutput, calls=%fused_computation.1 | convolution fusion | flops 140505088 | bytes 3227648 | tf_op jit(solution)/shard_map/rnihd,rnjhd->rnhij/dot_general | solution.py:117
  74.0 0.0 copy-done.2
  74.1 0.0 collective-permute-done.12
  74.1 0.7 fusion.21
  74.8 1.6 %fusion.31 = f32[16,1,256]{2,1,0:T(1,128)S(1)} fusion(f32[16,64,1]{1,2,0:T(1,128)S(1)} %bitcast.75, bf16[1,256,3,16,64]{1,4,3,2,0:T(8,128)(2,1)} %bitcast.64), kind=kOutput, calls=%fused_computation.77 | convolution fusion | flops 4718592 | bytes 544768 | tf_op jit(solution)/shard_map/rnihd,rnhd->rnih/dot_general | solution.py:136
  76.5 0.0 copy-done.1
  76.5 0.0 copy-start.3
  76.5 0.2 broadcast_in_dim_broadcast_in_dim_reshape.3
  76.6 0.0 copy-start.4
  76.6 2.0 %fusion.18 = f32[16,64,256]{2,1,0:T(8,128)S(1)} fusion(f32[16,64,64]{2,1,0:T(8,128)S(1)} %broadcast_in_dim_broadcast_in_dim_reshape.3, f32[16,64,64]{2,1,0:T(8,128)S(1)} %fusion.13, bf16[1,256,3,16,64]{1,4,3,2,0:T(8,128)(2,1)} %bitcast.65), kind=kOutput, calls=%fused_computation.32 | convolution fusion | flops 203030528 | bytes 2097152 | tf_op jit(solution)/shard_map/rnihd,rnhde->rnihe/dot_general | solution.py:133
  78.6 0.0 copy-done.3
  78.6 0.0 copy-done.4
  78.7 1.5 %divide_convert_fusion = bf16[1,1,256,16,64]{2,4,3,1,0:T(8,128)(2,1)S(1)} fusion(f32[16,64,256]{2,1,0:T(8,128)S(1)} %fusion.18, bf16[16,256,256]{1,2,0:T(8,128)(2,1)S(1)} %copy-done.4, pred[256,256]{0,1:T(8,128)(4,1)S(1)} %copy-done.3, f32[256,16]{0,1:T(8,128)S(1)} %fusion.25, bf16[1,256,3,16,64]{1,4,3,2,0:T(8,128)(2,1)} %bitcast.66), kind=kOutput, calls=%fused_computation.24 | convolution fusion | flops 136052736 | bytes 4276224 | tf_op jit(solution)/shard_map/rnhij,rnjhd->rnihd/dot_general | solution.py:122
  80.2 0.0 copy-done
  80.2 1.5 %fusion.5 = bf16[1,256,1024]{2,1,0:T(8,128)(2,1)} fusion(bf16[256,1024]{0,1:T(8,128)(2,1)S(1)} %bitcast.67, bf16[1024,1024]{1,0:T(8,128)(2,1)S(1)} %copy-done), kind=kOutput, calls=%fused_computation.16 | convolution fusion | flops 537133056 | bytes 3145728 | tf_op jit(solution)/shard_map/rtd,de->rte/dot_general | solution.py:170
  (23 shorter events, 0.3 us)
Async XLA Ops:
  0.0 80.2 %copy-start = (bf16[1024,1024]{1,0:T(8,128)(2,1)S(1)}, bf16[1024,1024]{1,0:T(8,128)(2,1)}, u32[]{:S(2)}) copy-start(bf16[1024,1024]{1,0:T(8,128)(2,1)} %param.5) | copy-start | bytes 6291460
  11.8 4.3 %collective-permute-start = (f32[8,33,128]{2,1,0:T(8,128)S(1)}, f32[8,33,128]{2,1,0:T(8,128)S(1)}, u32[]{:S(2)}, u32[]{:S(2)}) collective-permute-start(f32[8,33,128]{2,1,0:T(8,128)S(1)} %fusion.22), channel_id=1, source_target_pairs={{0,2},{2,0},{1,3},{3,1},{4,6},{6,4},{5,7},{7,5},{8,10},{10,8},{9,1... | collective-permute-start | bytes 405512 | tf_op jit(solution)/shard_map/ppermute | solution.py:22
  16.2 5.2 %collective-permute-start.1 = (f32[4,33,128]{2,1,0:T(8,128)S(1)}, f32[4,33,128]{2,1,0:T(8,128)S(1)}, u32[]{:S(2)}, u32[]{:S(2)}) collective-permute-start(f32[4,33,128]{2,1,0:T(8,128)S(1)} %constant_dynamic-slice_fusion.3), channel_id=1, source_target_pairs={{0,4},{4,0},{1,5},{5,1},{2,6},{6,2},{3,7},{7,3},{8,12},{12,8},{9,1... | collective-permute-start | bytes 202760 | tf_op jit(solution)/shard_map/ppermute | solution.py:22
  21.4 3.9 %collective-permute-start.2 = (f32[1,33,128]{2,1,0:T(8,128)S(1)}, f32[1,33,128]{2,1,0:T(8,128)S(1)}, u32[]{:S(2)}, u32[]{:S(2)}) collective-permute-start(f32[1,33,128]{2,1,0:T(8,128)S(1)} %get-tuple-element.14), channel_id=1, source_target_pairs={{0,8},{8,16},{16,24},{24,0},{1,9},{9,17},{17,25},{25,1},{2,10},{10... | collective-permute-start | bytes 50696 | tf_op jit(solution)/shard_map/ppermute | solution.py:22
  21.5 3.8 %collective-permute-start.4 = (f32[1,33,128]{2,1,0:T(8,128)S(1)}, f32[1,33,128]{2,1,0:T(8,128)S(1)}, u32[]{:S(2)}, u32[]{:S(2)}) collective-permute-start(f32[1,33,128]{2,1,0:T(8,128)S(1)} %get-tuple-element.15), channel_id=1, source_target_pairs={{0,24},{8,0},{16,8},{24,16},{1,25},{9,1},{17,9},{25,17},{2,26},{10... | collective-permute-start | bytes 50696 | tf_op jit(solution)/shard_map/ppermute | solution.py:22
  24.2 4.1 %collective-permute-start.3 = (f32[1,33,128]{2,1,0:T(8,128)S(1)}, f32[1,33,128]{2,1,0:T(8,128)S(1)}, u32[]{:S(2)}, u32[]{:S(2)}) collective-permute-start(f32[1,33,128]{2,1,0:T(8,128)S(1)} %get-tuple-element.16), channel_id=1, source_target_pairs={{0,16},{8,24},{16,0},{24,8},{1,17},{9,25},{17,1},{25,9},{2,18},{10... | collective-permute-start | bytes 50696 | tf_op jit(solution)/shard_map/ppermute | solution.py:22
  28.3 2.9 %collective-permute-start.5 = (f32[1,33,128]{2,1,0:T(8,128)S(1)}, f32[1,33,128]{2,1,0:T(8,128)S(1)}, u32[]{:S(2)}, u32[]{:S(2)}) collective-permute-start(f32[1,33,128]{2,1,0:T(8,128)S(1)} %add_add_fusion), channel_id=1, source_target_pairs={{0,32},{32,64},{64,96},{96,128},{128,160},{160,192},{192,224},{1,3... | collective-permute-start | bytes 50696 | tf_op jit(solution)/shard_map/ppermute | solution.py:22
  31.2 5.9 %collective-permute-start.6 = (f32[1,33,128]{2,1,0:T(8,128)S(1)}, f32[1,33,128]{2,1,0:T(8,128)S(1)}, u32[]{:S(2)}, u32[]{:S(2)}) collective-permute-start(f32[1,33,128]{2,1,0:T(8,128)S(1)} %add.268), channel_id=1, source_target_pairs={{0,64},{32,96},{64,128},{96,160},{128,192},{160,224},{1,65},{33,97... | collective-permute-start | bytes 50696 | tf_op jit(solution)/shard_map/ppermute | solution.py:22
  37.1 11.8 %collective-permute-start.7 = (f32[1,33,128]{2,1,0:T(8,128)S(1)}, f32[1,33,128]{2,1,0:T(8,128)S(1)}, u32[]{:S(2)}, u32[]{:S(2)}) collective-permute-start(f32[1,33,128]{2,1,0:T(8,128)S(1)} %add.269), channel_id=1, source_target_pairs={{0,128},{32,160},{64,192},{96,224},{1,129},{33,161},{65,193},{97,2... | collective-permute-start | bytes 50696 | tf_op jit(solution)/shard_map/ppermute | solution.py:22
  48.9 3.9 %collective-permute-start.8 = (f32[1,33,128]{2,1,0:T(8,128)S(1)}, f32[1,33,128]{2,1,0:T(8,128)S(1)}, u32[]{:S(2)}, u32[]{:S(2)}) collective-permute-start(f32[1,33,128]{2,1,0:T(8,128)S(1)} %get-tuple-element.11), channel_id=1, source_target_pairs={{0,8},{8,16},{16,24},{24,0},{1,9},{9,17},{17,25},{25,1},{2,10},{10... | collective-permute-start | bytes 50696 | tf_op jit(solution)/shard_map/ppermute | solution.py:22
  49.0 3.8 %collective-permute-start.10 = (f32[1,33,128]{2,1,0:T(8,128)S(1)}, f32[1,33,128]{2,1,0:T(8,128)S(1)}, u32[]{:S(2)}, u32[]{:S(2)}) collective-permute-start(f32[1,33,128]{2,1,0:T(8,128)S(1)} %get-tuple-element.12), channel_id=1, source_target_pairs={{0,24},{8,0},{16,8},{24,16},{1,25},{9,1},{17,9},{25,17},{2,26},{10... | collective-permute-start | bytes 50696 | tf_op jit(solution)/shard_map/ppermute | solution.py:22
  51.7 4.1 %collective-permute-start.9 = (f32[1,33,128]{2,1,0:T(8,128)S(1)}, f32[1,33,128]{2,1,0:T(8,128)S(1)}, u32[]{:S(2)}, u32[]{:S(2)}) collective-permute-start(f32[1,33,128]{2,1,0:T(8,128)S(1)} %get-tuple-element.13), channel_id=1, source_target_pairs={{0,16},{8,24},{16,0},{24,8},{1,17},{9,25},{17,1},{25,9},{2,18},{10... | collective-permute-start | bytes 50696 | tf_op jit(solution)/shard_map/ppermute | solution.py:22
  56.4 4.9 %collective-permute-start.11 = (f32[4,33,128]{2,1,0:T(8,128)S(1)}, f32[4,33,128]{2,1,0:T(8,128)S(1)}, u32[]{:S(2)}, u32[]{:S(2)}) collective-permute-start(f32[4,33,128]{2,1,0:T(8,128)S(1)} %select_add_fusion.2), channel_id=1, source_target_pairs={{0,4},{4,0},{1,5},{5,1},{2,6},{6,2},{3,7},{7,3},{8,12},{12,8},{9,1... | collective-permute-start | bytes 202760 | tf_op jit(solution)/shard_map/ppermute | solution.py:22
  59.3 14.8 %copy-start.2 = (pred[256,256]{0,1:T(8,128)(4,1)}, pred[256,256]{0,1:T(8,128)(4,1)S(1)}, u32[]{:S(2)}) copy-start(pred[256,256]{0,1:T(8,128)(4,1)S(1)} %iota_compare_fusion) | copy-start | bytes 196612
  61.4 12.7 %collective-permute-start.12 = (f32[8,33,128]{2,1,0:T(8,128)S(1)}, f32[8,33,128]{2,1,0:T(8,128)S(1)}, u32[]{:S(2)}, u32[]{:S(2)}) collective-permute-start(f32[8,33,128]{2,1,0:T(8,128)S(1)} %select_add_fusion), channel_id=1, source_target_pairs={{0,2},{2,0},{1,3},{3,1},{4,6},{6,4},{5,7},{7,5},{8,10},{10,8},{9,1... | collective-permute-start | bytes 405512 | tf_op jit(solution)/shard_map/ppermute | solution.py:22
  74.8 1.6 %copy-start.1 = (f32[16,32,128]{2,1,0:T(8,128)S(1)}, f32[16,32,128]{2,1,0:T(8,128)}, u32[]{:S(2)}) copy-start(f32[16,32,128]{2,1,0:T(8,128)} %fusion.21) | copy-start | bytes 786436
  76.5 2.2 %copy-start.3 = (pred[256,256]{0,1:T(8,128)(4,1)S(1)}, pred[256,256]{0,1:T(8,128)(4,1)}, u32[]{:S(2)}) copy-start(pred[256,256]{0,1:T(8,128)(4,1)} %copy-done.2) | copy-start | bytes 196612
  76.6 2.0 %copy-start.4 = (bf16[16,256,256]{1,2,0:T(8,128)(2,1)S(1)}, bf16[16,256,256]{1,2,0:T(8,128)(2,1)}, u32[]{:S(2)}) copy-start(bf16[16,256,256]{1,2,0:T(8,128)(2,1)} %get-tuple-element.18) | copy-start | bytes 6291460

commit v5 on v4

--- a/solution.py
+++ b/solution.py
@@ -60,6 +60,7 @@
     core = lax.axis_index("frm")
     xh = lax.axis_index("seg_x")
     y = lax.axis_index("seg_y")
+    z = lax.axis_index("seg_z")
     n_y = lax.axis_size("seg_y")
     n_z = lax.axis_size("seg_z")
     add = lambda a, b: tmap(jnp.add, a, b)
@@ -67,22 +68,20 @@
     got_c = swap(part(total, 1 - core, 2), "frm")
     lo, hi = ordered(own_c, got_c, core == 0)
     chip = add(lo, hi)
-    own_x = part(chip, xh, 2)
-    got_x = swap(part(chip, 1 - xh, 2), "seg_x")
-    lo, hi = ordered(own_x, got_x, xh == 0)
-    row = add(lo, hi)
-    came = [part(row, y, n_y)] + [
-        send(part(row, (y + s) % n_y, n_y), "seg_y", cyclic(n_y, s)) for s in range(1, n_y)
+    came = [part(chip, y, n_y)] + [
+        send(part(chip, (y + s) % n_y, n_y), "seg_y", cyclic(n_y, s)) for s in range(1, n_y)
     ]
-    plane = came[0]
+    column = came[0]
     for c in came[1:]:
-        plane = add(plane, c)
-    upto = plane
-    s = 1
-    while s < n_z:
-        upto = add(upto, send(upto, "seg_z", forward(n_z, s)))
-        s *= 2
-    before_z = tmap(jnp.subtract, upto, plane)
+        column = add(column, c)
+    before_z = tmap(jnp.zeros_like, column)
+    left = right = column
+    for r in range(1, n_z // 2 + 1):
+        left = send(left, "seg_z", cyclic(n_z, 1))
+        before_z = add(before_z, keep(left, z >= r))
+        if r < n_z - r:
+            right = send(right, "seg_z", cyclic(n_z, -1))
+            before_z = add(before_z, keep(right, z + r >= n_z))
 
     def for_row(t):
         out = before_z
@@ -94,14 +93,11 @@
         send(for_row((y + s) % n_y), "seg_y", cyclic(n_y, s)) for s in range(1, n_y)
     ]
     order = (y - jnp.arange(n_y)) % n_y
-    quarter = tmap(
+    mine = tmap(
         lambda *p: jnp.stack(p)[order].reshape((-1,) + p[0].shape[1:]),
         *pieces,
     )
-    got = swap(add(quarter, keep(own_x, xh == 0)), "seg_x")
-    lo = tmap(lambda a, b: jnp.where(xh == 0, a, b), quarter, got)
-    hi = tmap(lambda a, b, c: jnp.where(xh == 0, b, a + c), quarter, got, got_x)
-    half = joined(lo, hi)
+    half = add(mine, swap(add(mine, keep(chip, xh == 0)), "seg_x"))
     got = swap(add(half, keep(own_c, core == 0)), "frm")
     lo = tmap(lambda a, b: jnp.where(core == 0, a, b), half, got)
     hi = tmap(lambda a, b, c: jnp.where(core == 0, b, a + c), half, got, got_c)

time: 82.1 us -> 75.8 us (0.923)
  starting transfers between devices: 39.9 us -> 30.4 us
  other arithmetic: 2.41 us -> 4.3 us
  waiting for transfers between devices: 17.6 us -> 19 us
    ppermute x13 -> x16, starting transfers between devices: 39.9 us -> 30.4 us  [send(): return tmap(lambda t: lax.ppermute(t, axis, perm=pairs), tree)]
    ppermute x13 -> x16, waiting for transfers between devices: 17.6 us -> 19 us  [send(): return tmap(lambda t: lax.ppermute(t, axis, perm=pairs), tree)]
    gather x1, other arithmetic: 0.01 us -> 1.28 us  [entering(): jnp.stack(p)[order].reshape((-1,) + p[0].shape[1:])]
  transfers between devices with their start and end apart: 13 -> 16, of which waited for: 10 -> 9; matrix products, arithmetic and copies ran while one was open for 5% -> 7% of each run, Pallas kernels for 0% -> 0%
where the time goes in v5:
time: 75.8 us; the launch traced here: 75.4 us
  starting transfers between devices  30.4 us (40%)
  waiting for transfers between devices  19 us (25%)
  matrix products  17.9 us (24%)
  other arithmetic  4.3 us (6%)
  local copies, waits for them, and re-layouts  3.58 us (5%)
    ppermute x16, starting transfers between devices, send(): return tmap(lambda t: lax.ppermute(t, axis, perm=pairs), tree)  30.4 us
    ppermute x16, waiting for transfers between devices, send(): return tmap(lambda t: lax.ppermute(t, axis, perm=pairs), tree)  19 us
    dot_general x1, matrix products, shards(): jnp.einsum('rtd,de->rte', frames_in, w_qkv, preferred_element_type=jnp.fl...  6.07 us
    dot_general x1, matrix products, block_terms(): jnp.einsum('rnihd,rnjhd->rnhij', pq, pk, preferred_element_type=jnp.float32)  3.66 us
    convert_element_type x1, local copies, waits for them, and re-layouts, shards(): jnp.einsum('rtd,de->rte', frames_in, w_qkv, preferred_element_type=jnp.fl...  2.57 us
    dot_general x1, matrix products, finish(): jnp.einsum('rnihd,rnhde->rnihe', pq32, before_kv, precision=lax.Precision...  1.98 us
    dot_general x1, matrix products, finish(): jnp.einsum('rnihd,rnhd->rnih', pq32, before_k, precision=lax.Precision.HI...  1.6 us
    dot_general x1, matrix products, block_terms(): jnp.einsum('rnjhd,rnjhe->rnhde', pk, vv, preferred_element_type=jnp.float32)  1.58 us
  transfers between devices with their start and end apart: 16, of which 9 were waited for; matrix products, arithmetic and copies ran while one was open for 7% of the time, Pallas kernels for 0%

profile of v5, /device:TPU:1, one launch (start us, length us, event | category | flops | bytes accessed | tf_op | source)
XLA Modules:
  0.0 75.4 jit_solution(4383246811852402079)
XLA Ops:
  0.0 6.1 %convolution_convert_fusion = bf16[256,3072]{1,0:T(8,128)(2,1)} fusion(bf16[1024,3072]{1,0:T(8,128)(2,1)} %param.4, bf16[1,256,1024]{2,1,0:T(8,128)(2,1)} %param.3), kind=kOutput, calls=%fused_computation.3 | convolution fusion | flops 1611399168 | bytes 8388608 | tf_op jit(solution)/shard_map/rtd,de->rte/dot_general | solution.py:148
  6.1 2.6 %copy.10 = bf16[256,3072]{0,1:T(8,128)(2,1)} copy(bf16[256,3072]{1,0:T(8,128)(2,1)} %convolution_convert_fusion) | data formatting | bytes 3145728 | tf_op jit(solution)/shard_map/convert_element_type | solution.py:148
  8.6 1.4 %convert_reduce_fusion = f32[16,64]{1,0:T(8,128)S(1)} fusion(bf16[1,256,3,16,64]{1,4,3,2,0:T(8,128)(2,1)} %bitcast.68), kind=kLoop, calls=%fused_computation.23 | loop fusion | flops 2096128 | bytes 528384 | tf_op jit(solution)/shard_map/reduce_sum | solution.py:120
  10.0 1.6 %fusion.13 = f32[16,64,64]{2,1,0:T(8,128)S(1)} fusion(bf16[1,256,3,16,64]{1,4,3,2,0:T(8,128)(2,1)} %bitcast.69), kind=kOutput, calls=%fused_computation.27 | convolution fusion | flops 35127296 | bytes 1310720 | tf_op jit(solution)/shard_map/rnjhd,rnjhe->rnhde/dot_general | solution.py:119
  11.6 0.1 reshape_squeeze.4
  11.8 3.3 %collective-permute-start = (f32[8,33,128]{2,1,0:T(8,128)S(1)}, f32[8,33,128]{2,1,0:T(8,128)S(1)}, u32[]{:S(2)}, u32[]{:S(2)}) collective-permute-start(f32[8,33,128]{2,1,0:T(8,128)S(1)} %fusion.22), channel_id=1, source_target_pairs={{0,2},{2,0},{1,3},{3,1},{4,6},{6,4},{5,7},{7,5},{8,10},{10,8},{9,1... | collective-permute-start | bytes 405512 | tf_op jit(solution)/shard_map/ppermute | solution.py:22
  15.1 1.0 %collective-permute-done = f32[8,33,128]{2,1,0:T(8,128)S(1)} collective-permute-done((f32[8,33,128]{2,1,0:T(8,128)S(1)}, f32[8,33,128]{2,1,0:T(8,128)S(1)}, u32[]{:S(2)}, u32[]{:S(2)}) %collective-permute-start) | collective-permute-done | bytes 135200 | tf_op jit(solution)/shard_map/ppermute | solution.py:22
  16.2 0.1 collective-permute-start.1
  16.3 2.7 %collective-permute-start.3 = (f32[2,33,128]{2,1,0:T(8,128)S(1)}, f32[2,33,128]{2,1,0:T(8,128)S(1)}, u32[]{:S(2)}, u32[]{:S(2)}) collective-permute-start(f32[2,33,128]{2,1,0:T(8,128)S(1)} %get-tuple-element.13), channel_id=1, source_target_pairs={{0,24},{8,0},{16,8},{24,16},{1,25},{9,1},{17,9},{25,17},{2,26},{10... | collective-permute-start | bytes 101384 | tf_op jit(solution)/shard_map/ppermute | solution.py:22
  18.9 0.0 collective-permute-start.2
  18.9 1.4 %collective-permute-done.1 = f32[2,33,128]{2,1,0:T(8,128)S(1)} collective-permute-done((f32[2,33,128]{2,1,0:T(8,128)S(1)}, f32[2,33,128]{2,1,0:T(8,128)S(1)}, u32[]{:S(2)}, u32[]{:S(2)}) %collective-permute-start.1) | collective-permute-done | bytes 33824 | tf_op jit(solution)/shard_map/ppermute | solution.py:22
  20.3 0.0 collective-permute-done.3
  20.3 3.0 %collective-permute-done.2 = f32[2,33,128]{2,1,0:T(8,128)S(1)} collective-permute-done((f32[2,33,128]{2,1,0:T(8,128)S(1)}, f32[2,33,128]{2,1,0:T(8,128)S(1)}, u32[]{:S(2)}, u32[]{:S(2)}) %collective-permute-start.2) | collective-permute-done | bytes 33824 | tf_op jit(solution)/shard_map/ppermute | solution.py:22
  23.3 0.2 collective-permute-start.4
  23.5 4.0 %collective-permute-start.5 = (f32[2,33,128]{2,1,0:T(8,128)S(1)}, f32[2,33,128]{2,1,0:T(8,128)S(1)}, u32[]{:S(2)}, u32[]{:S(2)}) collective-permute-start(f32[2,33,128]{2,1,0:T(8,128)S(1)} %add_add_fusion), channel_id=1, source_target_pairs={{0,224},{32,0},{64,32},{96,64},{128,96},{160,128},{192,160},{224,1... | collective-permute-start | bytes 101384 | tf_op jit(solution)/shard_map/ppermute | solution.py:22
  27.5 1.3 %collective-permute-done.4 = f32[2,33,128]{2,1,0:T(8,128)S(1)} collective-permute-done((f32[2,33,128]{2,1,0:T(8,128)S(1)}, f32[2,33,128]{2,1,0:T(8,128)S(1)}, u32[]{:S(2)}, u32[]{:S(2)}) %collective-permute-start.4) | collective-permute-done | bytes 33824 | tf_op jit(solution)/shard_map/ppermute | solution.py:22
  28.8 0.0 collective-permute-start.6
  28.8 0.0 collective-permute-done.5
  28.8 2.8 %collective-permute-start.7 = (f32[2,33,128]{2,1,0:T(8,128)S(1)}, f32[2,33,128]{2,1,0:T(8,128)S(1)}, u32[]{:S(2)}, u32[]{:S(2)}) collective-permute-start(f32[2,33,128]{2,1,0:T(8,128)S(1)} %collective-permute-done.5), channel_id=1, source_target_pairs={{0,224},{32,0},{64,32},{96,64},{128,96},{160,128},{192,160},{224,1... | collective-permute-start | bytes 101384 | tf_op jit(solution)/shard_map/ppermute | solution.py:22
  31.5 1.3 %collective-permute-done.6 = f32[2,33,128]{2,1,0:T(8,128)S(1)} collective-permute-done((f32[2,33,128]{2,1,0:T(8,128)S(1)}, f32[2,33,128]{2,1,0:T(8,128)S(1)}, u32[]{:S(2)}, u32[]{:S(2)}) %collective-permute-start.6) | collective-permute-done | bytes 33824 | tf_op jit(solution)/shard_map/ppermute | solution.py:22
  32.8 0.0 collective-permute-start.8
  32.8 0.0 collective-permute-done.7
  32.9 2.8 %collective-permute-start.9 = (f32[2,33,128]{2,1,0:T(8,128)S(1)}, f32[2,33,128]{2,1,0:T(8,128)}, u32[]{:S(2)}, u32[]{:S(2)}) collective-permute-start(f32[2,33,128]{2,1,0:T(8,128)S(1)} %collective-permute-done.7), channel_id=1, source_target_pairs={{0,224},{32,0},{64,32},{96,64},{128,96},{160,128},{192,160},{224,1... | collective-permute-start | bytes 101384 | tf_op jit(solution)/shard_map/ppermute | solution.py:22
  35.6 1.3 %collective-permute-done.8 = f32[2,33,128]{2,1,0:T(8,128)S(1)} collective-permute-done((f32[2,33,128]{2,1,0:T(8,128)S(1)}, f32[2,33,128]{2,1,0:T(8,128)S(1)}, u32[]{:S(2)}, u32[]{:S(2)}) %collective-permute-start.8) | collective-permute-done | bytes 33824 | tf_op jit(solution)/shard_map/ppermute | solution.py:22
  36.9 0.0 collective-permute-start.10
  36.9 0.6 fusion.26
  37.5 0.0 collective-permute-done.9
  37.5 0.0 copy-done.2
  37.5 3.8 %collective-permute-done.10 = f32[2,33,128]{2,1,0:T(8,128)} collective-permute-done((f32[2,33,128]{2,1,0:T(8,128)S(1)}, f32[2,33,128]{2,1,0:T(8,128)}, u32[]{:S(2)}, u32[]{:S(2)}) %collective-permute-start.10) | collective-permute-done | bytes 33824 | tf_op jit(solution)/shard_map/ppermute | solution.py:22
  41.5 0.4 collective-permute-start.11
  41.9 2.3 %collective-permute-start.13 = (f32[2,33,128]{2,1,0:T(8,128)S(1)}, f32[2,33,128]{2,1,0:T(8,128)S(1)}, u32[]{:S(2)}, u32[]{:S(2)}) collective-permute-start(f32[2,33,128]{2,1,0:T(8,128)S(1)} %get-tuple-element.10), channel_id=1, source_target_pairs={{0,24},{8,0},{16,8},{24,16},{1,25},{9,1},{17,9},{25,17},{2,26},{10... | collective-permute-start | bytes 101384 | tf_op jit(solution)/shard_map/ppermute | solution.py:22
  44.2 0.1 collective-permute-start.12
  44.3 1.3 %pad_clamp_fusion = s32[1024]{0:T(1024)} fusion(s32[4]{0:T(128)} %fusion.26), kind=kLoop, calls=%fused_computation.62 | loop fusion | flops 1024 | bytes 4112 | tf_op jit(solution)/shard_map/gather | solution.py:97
  45.6 0.0 collective-permute-done.11
  45.6 0.0 collective-permute-done.13
  45.6 3.0 %collective-permute-done.12 = f32[2,33,128]{2,1,0:T(8,128)S(1)} collective-permute-done((f32[2,33,128]{2,1,0:T(8,128)S(1)}, f32[2,33,128]{2,1,0:T(8,128)S(1)}, u32[]{:S(2)}, u32[]{:S(2)}) %collective-permute-start.12) | collective-permute-done | bytes 33824 | tf_op jit(solution)/shard_map/ppermute | solution.py:22
  48.6 0.7 gather_fusion
  49.3 2.8 %collective-permute-start.14 = (f32[8,33,128]{2,1,0:T(8,128)S(1)}, f32[8,33,128]{2,1,0:T(8,128)S(1)}, u32[]{:S(2)}, u32[]{:S(2)}) collective-permute-start(f32[8,33,128]{2,1,0:T(8,128)S(1)} %bitcast_add_fusion.1), channel_id=1, source_target_pairs={{0,4},{4,0},{1,5},{5,1},{2,6},{6,2},{3,7},{7,3},{8,12},{12,8},{9,1... | collective-permute-start | bytes 405512 | tf_op jit(solution)/shard_map/ppermute | solution.py:22
  52.2 2.9 %collective-permute-done.14 = f32[8,33,128]{2,1,0:T(8,128)S(1)} collective-permute-done((f32[8,33,128]{2,1,0:T(8,128)S(1)}, f32[8,33,128]{2,1,0:T(8,128)S(1)}, u32[]{:S(2)}, u32[]{:S(2)}) %collective-permute-start.14) | collective-permute-done | bytes 135200 | tf_op jit(solution)/shard_map/ppermute | solution.py:22
  55.1 9.0 %collective-permute-start.15 = (f32[8,33,128]{2,1,0:T(8,128)S(1)}, f32[8,33,128]{2,1,0:T(8,128)S(1)}, u32[]{:S(2)}, u32[]{:S(2)}) collective-permute-start(f32[8,33,128]{2,1,0:T(8,128)S(1)} %select_add_fusion), channel_id=1, source_target_pairs={{0,2},{2,0},{1,3},{3,1},{4,6},{6,4},{5,7},{7,5},{8,10},{10,8},{9,1... | collective-permute-start | bytes 405512 | tf_op jit(solution)/shard_map/ppermute | solution.py:22
  64.1 3.7 %select_reduce_fusion = (f32[16,256]{1,0:T(8,128)S(1)}, bf16[16,256,256]{1,2,0:T(8,128)(2,1)}) fusion(pred[256,256]{0,1:T(8,128)(4,1)S(1)} %iota_compare_fusion, bf16[1,256,3,16,64]{1,4,3,2,0:T(8,128)(2,1)} %bitcast.70), kind=kOutput, calls=%fused_computation.1 | convolution fusion | flops 140505088 | bytes 3227648 | tf_op jit(solution)/shard_map/rnihd,rnjhd->rnhij/dot_general | solution.py:113
  67.8 0.0 collective-permute-done.15
  67.8 0.7 fusion.21
  68.6 1.6 %fusion.30 = f32[16,1,256]{2,1,0:T(1,128)S(1)} fusion(f32[16,64,1]{1,2,0:T(1,128)S(1)} %bitcast.82, bf16[1,256,3,16,64]{1,4,3,2,0:T(8,128)(2,1)} %bitcast.71), kind=kOutput, calls=%fused_computation.73 | convolution fusion | flops 4718592 | bytes 544768 | tf_op jit(solution)/shard_map/rnihd,rnhd->rnih/dot_general | solution.py:132
  70.2 0.2 broadcast_in_dim_broadcast_in_dim_reshape.3
  70.4 2.0 %fusion.18 = f32[16,64,256]{2,1,0:T(8,128)S(1)} fusion(f32[16,64,64]{2,1,0:T(8,128)S(1)} %broadcast_in_dim_broadcast_in_dim_reshape.3, f32[16,64,64]{2,1,0:T(8,128)S(1)} %fusion.13, bf16[1,256,3,16,64]{1,4,3,2,0:T(8,128)(2,1)} %bitcast.72), kind=kOutput, calls=%fused_computation.32 | convolution fusion | flops 203030528 | bytes 2097152 | tf_op jit(solution)/shard_map/rnihd,rnhde->rnihe/dot_general | solution.py:129
  72.4 1.5 %divide_convert_fusion = bf16[1,1,256,16,64]{2,4,3,1,0:T(8,128)(2,1)S(1)} fusion(f32[16,64,256]{2,1,0:T(8,128)S(1)} %fusion.18, bf16[16,256,256]{1,2,0:T(8,128)(2,1)S(1)} %copy-done.3, pred[256,256]{0,1:T(8,128)(4,1)S(1)} %iota_compare_fusion, f32[256,16]{0,1:T(8,128)S(1)} %fusion.24, bf16[1,256,3,16,64]{1,4,3,2,0:T(8,128)(2,1)} %bitcast.73), kind=kOutput, calls=%fused_computation.24 | convolution fusion | flops 136052736 | bytes 4276224 | tf_op jit(solution)/shard_map/rnhij,rnjhd->rnihd/dot_general | solution.py:118
  73.9 1.5 %fusion.5 = bf16[1,256,1024]{2,1,0:T(8,128)(2,1)} fusion(bf16[256,1024]{0,1:T(8,128)(2,1)S(1)} %bitcast.74, bf16[1024,1024]{1,0:T(8,128)(2,1)S(1)} %copy-done), kind=kOutput, calls=%fused_computation.16 | convolution fusion | flops 537133056 | bytes 3145728 | tf_op jit(solution)/shard_map/rtd,de->rte/dot_general | solution.py:166
  (22 shorter events, 0.3 us)
Async XLA Ops:
  0.0 73.9 %copy-start = (bf16[1024,1024]{1,0:T(8,128)(2,1)S(1)}, bf16[1024,1024]{1,0:T(8,128)(2,1)}, u32[]{:S(2)}) copy-start(bf16[1024,1024]{1,0:T(8,128)(2,1)} %param.5) | copy-start | bytes 6291460
  11.8 4.3 %collective-permute-start = (f32[8,33,128]{2,1,0:T(8,128)S(1)}, f32[8,33,128]{2,1,0:T(8,128)S(1)}, u32[]{:S(2)}, u32[]{:S(2)}) collective-permute-start(f32[8,33,128]{2,1,0:T(8,128)S(1)} %fusion.22), channel_id=1, source_target_pairs={{0,2},{2,0},{1,3},{3,1},{4,6},{6,4},{5,7},{7,5},{8,10},{10,8},{9,1... | collective-permute-start | bytes 405512 | tf_op jit(solution)/shard_map/ppermute | solution.py:22
  16.2 4.1 %collective-permute-start.1 = (f32[2,33,128]{2,1,0:T(8,128)S(1)}, f32[2,33,128]{2,1,0:T(8,128)S(1)}, u32[]{:S(2)}, u32[]{:S(2)}) collective-permute-start(f32[2,33,128]{2,1,0:T(8,128)S(1)} %get-tuple-element.12), channel_id=1, source_target_pairs={{0,8},{8,16},{16,24},{24,0},{1,9},{9,17},{17,25},{25,1},{2,10},{10... | collective-permute-start | bytes 101384 | tf_op jit(solution)/shard_map/ppermute | solution.py:22
  16.3 4.1 %collective-permute-start.3 = (f32[2,33,128]{2,1,0:T(8,128)S(1)}, f32[2,33,128]{2,1,0:T(8,128)S(1)}, u32[]{:S(2)}, u32[]{:S(2)}) collective-permute-start(f32[2,33,128]{2,1,0:T(8,128)S(1)} %get-tuple-element.13), channel_id=1, source_target_pairs={{0,24},{8,0},{16,8},{24,16},{1,25},{9,1},{17,9},{25,17},{2,26},{10... | collective-permute-start | bytes 101384 | tf_op jit(solution)/shard_map/ppermute | solution.py:22
  18.9 4.4 %collective-permute-start.2 = (f32[2,33,128]{2,1,0:T(8,128)S(1)}, f32[2,33,128]{2,1,0:T(8,128)S(1)}, u32[]{:S(2)}, u32[]{:S(2)}) collective-permute-start(f32[2,33,128]{2,1,0:T(8,128)S(1)} %get-tuple-element.14), channel_id=1, source_target_pairs={{0,16},{8,24},{16,0},{24,8},{1,17},{9,25},{17,1},{25,9},{2,18},{10... | collective-permute-start | bytes 101384 | tf_op jit(solution)/shard_map/ppermute | solution.py:22
  23.3 5.5 %collective-permute-start.4 = (f32[2,33,128]{2,1,0:T(8,128)S(1)}, f32[2,33,128]{2,1,0:T(8,128)S(1)}, u32[]{:S(2)}, u32[]{:S(2)}) collective-permute-start(f32[2,33,128]{2,1,0:T(8,128)S(1)} %add_add_fusion), channel_id=1, source_target_pairs={{0,32},{32,64},{64,96},{96,128},{128,160},{160,192},{192,224},{224... | collective-permute-start | bytes 101384 | tf_op jit(solution)/shard_map/ppermute | solution.py:22
  23.5 5.3 %collective-permute-start.5 = (f32[2,33,128]{2,1,0:T(8,128)S(1)}, f32[2,33,128]{2,1,0:T(8,128)S(1)}, u32[]{:S(2)}, u32[]{:S(2)}) collective-permute-start(f32[2,33,128]{2,1,0:T(8,128)S(1)} %add_add_fusion), channel_id=1, source_target_pairs={{0,224},{32,0},{64,32},{96,64},{128,96},{160,128},{192,160},{224,1... | collective-permute-start | bytes 101384 | tf_op jit(solution)/shard_map/ppermute | solution.py:22
  28.8 4.1 %collective-permute-start.6 = (f32[2,33,128]{2,1,0:T(8,128)S(1)}, f32[2,33,128]{2,1,0:T(8,128)S(1)}, u32[]{:S(2)}, u32[]{:S(2)}) collective-permute-start(f32[2,33,128]{2,1,0:T(8,128)S(1)} %collective-permute-done.4), channel_id=1, source_target_pairs={{0,32},{32,64},{64,96},{96,128},{128,160},{160,192},{192,224},{224... | collective-permute-start | bytes 101384 | tf_op jit(solution)/shard_map/ppermute | solution.py:22
  28.8 4.1 %collective-permute-start.7 = (f32[2,33,128]{2,1,0:T(8,128)S(1)}, f32[2,33,128]{2,1,0:T(8,128)S(1)}, u32[]{:S(2)}, u32[]{:S(2)}) collective-permute-start(f32[2,33,128]{2,1,0:T(8,128)S(1)} %collective-permute-done.5), channel_id=1, source_target_pairs={{0,224},{32,0},{64,32},{96,64},{128,96},{160,128},{192,160},{224,1... | collective-permute-start | bytes 101384 | tf_op jit(solution)/shard_map/ppermute | solution.py:22
  32.8 4.1 %collective-permute-start.8 = (f32[2,33,128]{2,1,0:T(8,128)S(1)}, f32[2,33,128]{2,1,0:T(8,128)S(1)}, u32[]{:S(2)}, u32[]{:S(2)}) collective-permute-start(f32[2,33,128]{2,1,0:T(8,128)S(1)} %collective-permute-done.6), channel_id=1, source_target_pairs={{0,32},{32,64},{64,96},{96,128},{128,160},{160,192},{192,224},{224... | collective-permute-start | bytes 101384 | tf_op jit(solution)/shard_map/ppermute | solution.py:22
  32.9 4.7 %collective-permute-start.9 = (f32[2,33,128]{2,1,0:T(8,128)S(1)}, f32[2,33,128]{2,1,0:T(8,128)}, u32[]{:S(2)}, u32[]{:S(2)}) collective-permute-start(f32[2,33,128]{2,1,0:T(8,128)S(1)} %collective-permute-done.7), channel_id=1, source_target_pairs={{0,224},{32,0},{64,32},{96,64},{128,96},{160,128},{192,160},{224,1... | collective-permute-start | bytes 101384 | tf_op jit(solution)/shard_map/ppermute | solution.py:22
  36.9 0.6 copy-start.2
  36.9 4.5 %collective-permute-start.10 = (f32[2,33,128]{2,1,0:T(8,128)S(1)}, f32[2,33,128]{2,1,0:T(8,128)}, u32[]{:S(2)}, u32[]{:S(2)}) collective-permute-start(f32[2,33,128]{2,1,0:T(8,128)S(1)} %collective-permute-done.8), channel_id=1, source_target_pairs={{0,32},{32,64},{64,96},{96,128},{128,160},{160,192},{192,224},{224... | collective-permute-start | bytes 101384 | tf_op jit(solution)/shard_map/ppermute | solution.py:22
  41.5 4.1 %collective-permute-start.11 = (f32[2,33,128]{2,1,0:T(8,128)S(1)}, f32[2,33,128]{2,1,0:T(8,128)S(1)}, u32[]{:S(2)}, u32[]{:S(2)}) collective-permute-start(f32[2,33,128]{2,1,0:T(8,128)S(1)} %get-tuple-element.9), channel_id=1, source_target_pairs={{0,8},{8,16},{16,24},{24,0},{1,9},{9,17},{17,25},{25,1},{2,10},{10... | collective-permute-start | bytes 101384 | tf_op jit(solution)/shard_map/ppermute | solution.py:22
  41.9 3.7 %collective-permute-start.13 = (f32[2,33,128]{2,1,0:T(8,128)S(1)}, f32[2,33,128]{2,1,0:T(8,128)S(1)}, u32[]{:S(2)}, u32[]{:S(2)}) collective-permute-start(f32[2,33,128]{2,1,0:T(8,128)S(1)} %get-tuple-element.10), channel_id=1, source_target_pairs={{0,24},{8,0},{16,8},{24,16},{1,25},{9,1},{17,9},{25,17},{2,26},{10... | collective-permute-start | bytes 101384 | tf_op jit(solution)/shard_map/ppermute | solution.py:22
  44.2 4.4 %collective-permute-start.12 = (f32[2,33,128]{2,1,0:T(8,128)S(1)}, f32[2,33,128]{2,1,0:T(8,128)S(1)}, u32[]{:S(2)}, u32[]{:S(2)}) collective-permute-start(f32[2,33,128]{2,1,0:T(8,128)S(1)} %get-tuple-element.11), channel_id=1, source_target_pairs={{0,16},{8,24},{16,0},{24,8},{1,17},{9,25},{17,1},{25,9},{2,18},{10... | collective-permute-start | bytes 101384 | tf_op jit(solution)/shard_map/ppermute | solution.py:22
  49.3 5.8 %collective-permute-start.14 = (f32[8,33,128]{2,1,0:T(8,128)S(1)}, f32[8,33,128]{2,1,0:T(8,128)S(1)}, u32[]{:S(2)}, u32[]{:S(2)}) collective-permute-start(f32[8,33,128]{2,1,0:T(8,128)S(1)} %bitcast_add_fusion.1), channel_id=1, source_target_pairs={{0,4},{4,0},{1,5},{5,1},{2,6},{6,2},{3,7},{7,3},{8,12},{12,8},{9,1... | collective-permute-start | bytes 405512 | tf_op jit(solution)/shard_map/ppermute | solution.py:22
  55.1 12.7 %collective-permute-start.15 = (f32[8,33,128]{2,1,0:T(8,128)S(1)}, f32[8,33,128]{2,1,0:T(8,128)S(1)}, u32[]{:S(2)}, u32[]{:S(2)}) collective-permute-start(f32[8,33,128]{2,1,0:T(8,128)S(1)} %select_add_fusion), channel_id=1, source_target_pairs={{0,2},{2,0},{1,3},{3,1},{4,6},{6,4},{5,7},{7,5},{8,10},{10,8},{9,1... | collective-permute-start | bytes 405512 | tf_op jit(solution)/shard_map/ppermute | solution.py:22
  68.6 1.6 %copy-start.1 = (f32[16,32,128]{2,1,0:T(8,128)S(1)}, f32[16,32,128]{2,1,0:T(8,128)}, u32[]{:S(2)}) copy-start(f32[16,32,128]{2,1,0:T(8,128)} %fusion.21) | copy-start | bytes 786436
  70.3 2.0 %copy-start.3 = (bf16[16,256,256]{1,2,0:T(8,128)(2,1)S(1)}, bf16[16,256,256]{1,2,0:T(8,128)(2,1)}, u32[]{:S(2)}) copy-start(bf16[16,256,256]{1,2,0:T(8,128)(2,1)} %get-tuple-element.16) | copy-start | bytes 6291460

commit v6 on v5

--- a/solution.py
+++ b/solution.py
@@ -68,35 +68,13 @@
     got_c = swap(part(total, 1 - core, 2), "frm")
     lo, hi = ordered(own_c, got_c, core == 0)
     chip = add(lo, hi)
-    came = [part(chip, y, n_y)] + [
-        send(part(chip, (y + s) % n_y, n_y), "seg_y", cyclic(n_y, s)) for s in range(1, n_y)
-    ]
-    column = came[0]
-    for c in came[1:]:
-        column = add(column, c)
-    before_z = tmap(jnp.zeros_like, column)
-    left = right = column
-    for r in range(1, n_z // 2 + 1):
-        left = send(left, "seg_z", cyclic(n_z, 1))
-        before_z = add(before_z, keep(left, z >= r))
-        if r < n_z - r:
-            right = send(right, "seg_z", cyclic(n_z, -1))
-            before_z = add(before_z, keep(right, z + r >= n_z))
-
-    def for_row(t):
-        out = before_z
-        for s, c in enumerate(came):
-            out = add(out, keep(c, (y - s) % n_y < t))
-        return out
-
-    pieces = [for_row(y)] + [
-        send(for_row((y + s) % n_y), "seg_y", cyclic(n_y, s)) for s in range(1, n_y)
-    ]
-    order = (y - jnp.arange(n_y)) % n_y
-    mine = tmap(
-        lambda *p: jnp.stack(p)[order].reshape((-1,) + p[0].shape[1:]),
-        *pieces,
-    )
+    came = lax.all_to_all(chip.reshape((n_y, -1) + chip.shape[1:]), "seg_y", 0, 0)
+    column = jnp.sum(came, axis=0)
+    later = lax.broadcasted_iota(jnp.int32, (n_z,) + column.shape, 0) > z
+    before_z = lax.psum_scatter(jnp.where(later, column[None], 0.0), "seg_z", scatter_dimension=0)
+    rows_before = jnp.cumsum(came, axis=0) - came
+    mine = lax.all_to_all(before_z[None] + rows_before, "seg_y", 0, 0)
+    mine = mine.reshape((-1,) + mine.shape[2:])
     half = add(mine, swap(add(mine, keep(chip, xh == 0)), "seg_x"))
     got = swap(add(half, keep(own_c, core == 0)), "frm")
     lo = tmap(lambda a, b: jnp.where(core == 0, a, b), half, got)

time: 75.8 us -> 145 us (1.91)
  waiting for transfers between devices: 19 us -> 82 us
  between operations: 0.2 us -> 13.6 us
  starting transfers between devices: 30.4 us -> 21.9 us
  local copies, waits for them, and re-layouts: 3.58 us -> 5.98 us
    unnamed x0 -> x2, waiting for transfers between devices: none -> 68.8 us
    ppermute x16 -> x3, starting transfers between devices: 30.4 us -> 14.5 us  [send(): return tmap(lambda t: lax.ppermute(t, axis, perm=pairs), tree)]
    ppermute x16 -> x3, waiting for transfers between devices: 19 us -> 3.63 us  [send(): return tmap(lambda t: lax.ppermute(t, axis, perm=pairs), tree)]
    all_to_all x0 -> x2, waiting for transfers between devices: none -> 9.62 us  [the longest x1 4.85 us: entering(): mine = lax.all_to_all(before_z[None] + rows_before, 'seg_y', 0, 0)]
    all_to_all x0 -> x2, starting transfers between devices: none -> 7.33 us  [the longest x1 4 us: entering(): mine = lax.all_to_all(before_z[None] + rows_before, 'seg_y', 0, 0)]
    add x0 -> x1, local copies, waits for them, and re-layouts: none -> 1.45 us  [entering(): mine = lax.all_to_all(before_z[None] + rows_before, 'seg_y', 0, 0)]
  transfers between devices with their start and end apart: 16 -> 6, of which waited for: 9 -> 5; matrix products, arithmetic and copies ran while one was open for 7% -> 3% of each run, Pallas kernels for 0% -> 0%
where the time goes in v6:
time: 145 us
  waiting for transfers between devices  82 us (57%)
  starting transfers between devices  21.9 us (15%)
  matrix products  17.9 us (12%)
  between operations  13.6 us (9%)
  local copies, waits for them, and re-layouts  5.98 us (4%)
  other arithmetic  3.19 us (2%)
    unnamed x2, waiting for transfers between devices  68.8 us
    ppermute x3, starting transfers between devices, send(): return tmap(lambda t: lax.ppermute(t, axis, perm=pairs), tree)  14.5 us
    dot_general x1, matrix products, shards(): jnp.einsum('rtd,de->rte', frames_in, w_qkv, preferred_element_type=jnp.fl...  6.05 us
    all_to_all x1, waiting for transfers between devices, entering(): mine = lax.all_to_all(before_z[None] + rows_before, 'seg_y', 0, 0)  4.85 us
    all_to_all x1, waiting for transfers between devices, entering(): lax.all_to_all(chip.reshape((n_y, -1) + chip.shape[1:]), 'seg_y', 0, 0)  4.77 us
    all_to_all x1, starting transfers between devices, entering(): mine = lax.all_to_all(before_z[None] + rows_before, 'seg_y', 0, 0)  4 us
    dot_general x1, matrix products, block_terms(): jnp.einsum('rnihd,rnjhd->rnhij', pq, pk, preferred_element_type=jnp.float32)  3.66 us
    ppermute x3, waiting for transfers between devices, send(): return tmap(lambda t: lax.ppermute(t, axis, perm=pairs), tree)  3.63 us
  transfers between devices with their start and end apart: 6, of which 5 were waited for; matrix products, arithmetic and copies ran while one was open for 3% of the time, Pallas kernels for 0%

profile of v6, /device:TPU:1, one launch (start us, length us, event | category | flops | bytes accessed | tf_op | source)
XLA Modules:
  0.0 144.5 jit_solution(12564480689782379402)
XLA Ops:
  6.5 0.0 copy-start
  6.5 6.0 %convolution_convert_fusion = bf16[256,3072]{1,0:T(8,128)(2,1)} fusion(bf16[1024,3072]{1,0:T(8,128)(2,1)} %param.4, bf16[1,256,1024]{2,1,0:T(8,128)(2,1)} %param.3), kind=kOutput, calls=%fused_computation.2 | convolution fusion | flops 1611399168 | bytes 8388608 | tf_op jit(solution)/shard_map/rtd,de->rte/dot_general | solution.py:126
  12.6 2.6 %copy.25 = bf16[256,3072]{0,1:T(8,128)(2,1)} copy(bf16[256,3072]{1,0:T(8,128)(2,1)} %convolution_convert_fusion) | data formatting | bytes 3145728 | tf_op jit(solution)/shard_map/convert_element_type | solution.py:126
  15.2 1.4 convert_reduce_fusion
  16.5 1.6 %fusion.14 = f32[16,64,64]{2,1,0:T(8,128)S(1)} fusion(bf16[1,256,3,16,64]{1,4,3,2,0:T(8,128)(2,1)} %bitcast.61), kind=kOutput, calls=%fused_computation.28 | convolution fusion | flops 35127296 | bytes 1310720 | tf_op jit(solution)/shard_map/rnjhd,rnjhe->rnhde/dot_general | solution.py:97
  18.1 0.0 copy-start.1
  18.2 0.1 reshape_squeeze.4
  18.3 0.2 copy.27
  18.5 3.3 %collective-permute-start = (f32[8,33,128]{2,0,1:T(8,128)S(1)}, f32[8,33,128]{2,0,1:T(8,128)S(1)}, u32[]{:S(2)}, u32[]{:S(2)}) collective-permute-start(f32[8,33,128]{2,0,1:T(8,128)S(1)} %fusion.23), channel_id=1, source_target_pairs={{0,2},{2,0},{1,3},{3,1},{4,6},{6,4},{5,7},{7,5},{8,10},{10,8},{9,1... | collective-permute-start | bytes 405512 | tf_op jit(solution)/shard_map/ppermute | solution.py:22
  21.8 1.0 collective-permute-done
  22.8 0.7 copy.28
  23.5 3.3 %all-to-all-start = ((f32[4,2,33,128]{3,1,2,0:T(2,128)}), f32[4,2,33,128]{3,1,2,0:T(2,128)S(1)}, u32[]{:S(2)}, u32[]{:S(2)}) async-start(f32[4,2,33,128]{3,1,2,0:T(2,128)} %copy.28), calls=%async_computation | async-start | bytes 270336 | tf_op jit(solution)/shard_map/all_to_all | solution.py:71
  26.8 0.0 all-reduce.4.cloned.1.call-start
  26.9 4.8 %all-to-all-done = f32[4,2,33,128]{3,1,2,0:T(2,128)S(1)} async-done(((f32[4,2,33,128]{3,1,2,0:T(2,128)}), f32[4,2,33,128]{3,1,2,0:T(2,128)S(1)}, u32[]{:S(2)}, u32[]{:S(2)}) %all-to-all-start) | async-done | bytes 135200 | tf_op jit(solution)/shard_map/all_to_all | solution.py:71
  31.7 0.1 reduce_sum.28
  31.7 0.9 broadcast_select_fusion
  32.6 0.0 all-reduce.4.cloned.1.call-update
  32.6 0.0 copy-done.1
  32.6 0.7 dynamic-slice
  33.3 68.8 %all-reduce.4.cloned.1.call-done = f32[8,2,33,128]{3,1,2,0:T(2,128)} async-done(((f32[8,2,33,128]{3,1,2,0:T(2,128)}), f32[8,2,33,128]{3,1,2,0:T(2,128)}) %all-reduce.4.cloned.1.call-update) | async-done | bytes 270352
  102.0 1.4 %dynamic-slice_bitcast_fusion = f32[2,33,128]{2,0,1:T(2,128)S(1)} fusion(f32[8,2,33,128]{3,1,2,0:T(2,128)} %all-reduce.4.cloned.1.call-done, u32[]{:T(128)} %bitcast.20), kind=kLoop, calls=%fused_computation.52 | loop fusion | bytes 67588 | tf_op jit(solution)/shard_map/add | solution.py:76
  103.5 0.7 fusion.6
  104.2 4.0 %all-to-all-start.1 = ((f32[4,2,33,128]{3,1,2,0:T(2,128)}), f32[4,2,33,128]{3,1,2,0:T(2,128)S(1)}, u32[]{:S(2)}, u32[]{:S(2)}) async-start(f32[4,2,33,128]{3,1,2,0:T(2,128)} %fusion.6), calls=%async_computation.1 | async-start | bytes 270336 | tf_op jit(solution)/shard_map/all_to_all | solution.py:76
  108.2 4.8 %all-to-all-done.1 = f32[4,2,33,128]{3,1,2,0:T(2,128)S(1)} async-done(((f32[4,2,33,128]{3,1,2,0:T(2,128)}), f32[4,2,33,128]{3,1,2,0:T(2,128)S(1)}, u32[]{:S(2)}, u32[]{:S(2)}) %all-to-all-start.1) | async-done | bytes 135200 | tf_op jit(solution)/shard_map/all_to_all | solution.py:76
  113.1 2.8 %collective-permute-start.1 = (f32[8,33,128]{2,0,1:T(8,128)S(1)}, f32[8,33,128]{2,0,1:T(8,128)S(1)}, u32[]{:S(2)}, u32[]{:S(2)}) collective-permute-start(f32[8,33,128]{2,0,1:T(8,128)S(1)} %select_add_fusion.1), channel_id=1, source_target_pairs={{0,4},{4,0},{1,5},{5,1},{2,6},{6,2},{3,7},{7,3},{8,12},{12,8},{9,1... | collective-permute-start | bytes 405512 | tf_op jit(solution)/shard_map/ppermute | solution.py:22
  116.0 2.6 %collective-permute-done.1 = f32[8,33,128]{2,0,1:T(8,128)S(1)} collective-permute-done((f32[8,33,128]{2,0,1:T(8,128)S(1)}, f32[8,33,128]{2,0,1:T(8,128)S(1)}, u32[]{:S(2)}, u32[]{:S(2)}) %collective-permute-start.1) | collective-permute-done | bytes 135200 | tf_op jit(solution)/shard_map/ppermute | solution.py:22
  118.6 8.4 %collective-permute-start.2 = (f32[8,33,128]{2,0,1:T(8,128)S(1)}, f32[8,33,128]{2,0,1:T(8,128)S(1)}, u32[]{:S(2)}, u32[]{:S(2)}) collective-permute-start(f32[8,33,128]{2,0,1:T(8,128)S(1)} %get-tuple-element.5), channel_id=1, source_target_pairs={{0,2},{2,0},{1,3},{3,1},{4,6},{6,4},{5,7},{7,5},{8,10},{10,8},{9,1... | collective-permute-start | bytes 405512 | tf_op jit(solution)/shard_map/ppermute | solution.py:22
  127.1 3.7 %select_reduce_fusion = (f32[16,256]{1,0:T(8,128)S(1)}, bf16[16,256,256]{1,2,0:T(8,128)(2,1)}) fusion(pred[256,256]{0,1:T(8,128)(4,1)S(1)} %iota_compare_fusion, bf16[1,256,3,16,64]{1,4,3,2,0:T(8,128)(2,1)} %bitcast.62), kind=kOutput, calls=%fused_computation | convolution fusion | flops 140505088 | bytes 3227648 | tf_op jit(solution)/shard_map/rnihd,rnjhd->rnhij/dot_general | solution.py:91
  130.7 0.0 collective-permute-done.2
  130.8 0.1 copy.30
  130.9 1.6 %fusion.31 = f32[16,1,256]{2,1,0:T(1,128)S(1)} fusion(f32[16,64,1]{1,2,0:T(1,128)S(1)} %bitcast.70, bf16[1,256,3,16,64]{1,4,3,2,0:T(8,128)(2,1)} %bitcast.63), kind=kOutput, calls=%fused_computation.61 | convolution fusion | flops 4718592 | bytes 544768 | tf_op jit(solution)/shard_map/rnihd,rnhd->rnih/dot_general | solution.py:110
  132.5 0.2 broadcast_in_dim_broadcast_in_dim_reshape.3
  132.6 0.0 copy-start.2
  132.6 2.0 %fusion.19 = f32[16,64,256]{2,1,0:T(8,128)S(1)} fusion(f32[16,64,64]{2,1,0:T(8,128)S(1)} %broadcast_in_dim_broadcast_in_dim_reshape.3, f32[16,64,64]{2,1,0:T(8,128)S(1)} %fusion.14, bf16[1,256,3,16,64]{1,4,3,2,0:T(8,128)(2,1)} %bitcast.64), kind=kOutput, calls=%fused_computation.33 | convolution fusion | flops 203030528 | bytes 2097152 | tf_op jit(solution)/shard_map/rnihd,rnhde->rnihe/dot_general | solution.py:107
  134.6 0.0 copy-done.2
  134.6 1.5 %divide_convert_fusion = bf16[1,1,256,16,64]{2,4,3,1,0:T(8,128)(2,1)S(1)} fusion(f32[16,64,256]{2,1,0:T(8,128)S(1)} %fusion.19, bf16[16,256,256]{1,2,0:T(8,128)(2,1)S(1)} %copy-done.2, pred[256,256]{0,1:T(8,128)(4,1)S(1)} %iota_compare_fusion, f32[256,16]{0,1:T(8,128)S(1)} %fusion.25, bf16[1,256,3,16,64]{1,4,3,2,0:T(8,128)(2,1)} %bitcast.65), kind=kOutput, calls=%fused_computation.25 | convolution fusion | flops 136052736 | bytes 4276224 | tf_op jit(solution)/shard_map/rnhij,rnjhd->rnihd/dot_general | solution.py:96
  136.2 0.0 copy-done
  136.2 1.5 %fusion.5 = bf16[1,256,1024]{2,1,0:T(8,128)(2,1)} fusion(bf16[256,1024]{0,1:T(8,128)(2,1)S(1)} %bitcast.69, bf16[1024,1024]{1,0:T(8,128)(2,1)S(1)} %copy-done), kind=kOutput, calls=%fused_computation.15 | convolution fusion | flops 537133056 | bytes 3145728 | tf_op jit(solution)/shard_map/rtd,de->rte/dot_general | solution.py:144
  (12 shorter events, 0.2 us)
Async XLA Ops:
  6.5 129.6 %copy-start = (bf16[1024,1024]{1,0:T(8,128)(2,1)S(1)}, bf16[1024,1024]{1,0:T(8,128)(2,1)}, u32[]{:S(2)}) copy-start(bf16[1024,1024]{1,0:T(8,128)(2,1)} %param.5) | copy-start | bytes 6291460
  18.1 14.5 %copy-start.1 = (u32[256]{0:T(256)S(1)}, u32[256]{0:T(256)}, u32[]{:S(2)}) copy-start(u32[256]{0:T(256)} %constant.43) | copy-start | bytes 3076
  18.5 4.3 %collective-permute-start = (f32[8,33,128]{2,0,1:T(8,128)S(1)}, f32[8,33,128]{2,0,1:T(8,128)S(1)}, u32[]{:S(2)}, u32[]{:S(2)}) collective-permute-start(f32[8,33,128]{2,0,1:T(8,128)S(1)} %fusion.23), channel_id=1, source_target_pairs={{0,2},{2,0},{1,3},{3,1},{4,6},{6,4},{5,7},{7,5},{8,10},{10,8},{9,1... | collective-permute-start | bytes 405512 | tf_op jit(solution)/shard_map/ppermute | solution.py:22
  23.5 8.2 %all-to-all-start = ((f32[4,2,33,128]{3,1,2,0:T(2,128)}), f32[4,2,33,128]{3,1,2,0:T(2,128)S(1)}, u32[]{:S(2)}, u32[]{:S(2)}) async-start(f32[4,2,33,128]{3,1,2,0:T(2,128)} %copy.28), calls=%async_computation | async-start | bytes 270336 | tf_op jit(solution)/shard_map/all_to_all | solution.py:71
  26.8 75.2 %all-reduce.4.cloned.1.call-start = ((), (), s32[]{:S(2)}) async-start(), calls=%async_computation.2 | async-start | bytes 540672
  104.2 8.9 %all-to-all-start.1 = ((f32[4,2,33,128]{3,1,2,0:T(2,128)}), f32[4,2,33,128]{3,1,2,0:T(2,128)S(1)}, u32[]{:S(2)}, u32[]{:S(2)}) async-start(f32[4,2,33,128]{3,1,2,0:T(2,128)} %fusion.6), calls=%async_computation.1 | async-start | bytes 270336 | tf_op jit(solution)/shard_map/all_to_all | solution.py:76
  113.1 5.5 %collective-permute-start.1 = (f32[8,33,128]{2,0,1:T(8,128)S(1)}, f32[8,33,128]{2,0,1:T(8,128)S(1)}, u32[]{:S(2)}, u32[]{:S(2)}) collective-permute-start(f32[8,33,128]{2,0,1:T(8,128)S(1)} %select_add_fusion.1), channel_id=1, source_target_pairs={{0,4},{4,0},{1,5},{5,1},{2,6},{6,2},{3,7},{7,3},{8,12},{12,8},{9,1... | collective-permute-start | bytes 405512 | tf_op jit(solution)/shard_map/ppermute | solution.py:22
  118.6 12.1 %collective-permute-start.2 = (f32[8,33,128]{2,0,1:T(8,128)S(1)}, f32[8,33,128]{2,0,1:T(8,128)S(1)}, u32[]{:S(2)}, u32[]{:S(2)}) collective-permute-start(f32[8,33,128]{2,0,1:T(8,128)S(1)} %get-tuple-element.5), channel_id=1, source_target_pairs={{0,2},{2,0},{1,3},{3,1},{4,6},{6,4},{5,7},{7,5},{8,10},{10,8},{9,1... | collective-permute-start | bytes 405512 | tf_op jit(solution)/shard_map/ppermute | solution.py:22
  132.6 2.0 %copy-start.2 = (bf16[16,256,256]{1,2,0:T(8,128)(2,1)S(1)}, bf16[16,256,256]{1,2,0:T(8,128)(2,1)}, u32[]{:S(2)}) copy-start(bf16[16,256,256]{1,2,0:T(8,128)(2,1)} %get-tuple-element.10) | copy-start | bytes 6291460
Sparse Core Ops, SparseCore 0:
  32.7 69.2 all-reduce.3

commit v7 on v5

--- a/solution.py
+++ b/solution.py
@@ -56,7 +56,7 @@
     return [(i, (i + s) % n) for i in range(n)]
 
 
-def entering(total):
+def entering(total, carry):
     core = lax.axis_index("frm")
     xh = lax.axis_index("seg_x")
     y = lax.axis_index("seg_y")
@@ -82,6 +82,7 @@
         if r < n_z - r:
             right = send(right, "seg_z", cyclic(n_z, -1))
             before_z = add(before_z, keep(right, z + r >= n_z))
+    before_z, carry = lax.optimization_barrier((before_z, carry))
 
     def for_row(t):
         out = before_z
@@ -101,7 +102,7 @@
     got = swap(add(half, keep(own_c, core == 0)), "frm")
     lo = tmap(lambda a, b: jnp.where(core == 0, a, b), half, got)
     hi = tmap(lambda a, b, c: jnp.where(core == 0, b, a + c), half, got, got_c)
-    return joined(lo, hi)
+    return joined(lo, hi), carry
 
 
 def block_terms(phi_q, phi_k, values, span):
@@ -157,7 +158,9 @@
     dense = total_kv.reshape(HEADS, -1, lanes)
     rows_kv = dense.shape[1]
     norm = jnp.pad(total_k, ((0, 0), (0, lanes - total_k.shape[1])))[:, None]
-    prior = entering(jnp.concatenate([dense, norm], axis=1))
+    prior, (num_local, den_local) = entering(
+        jnp.concatenate([dense, norm], axis=1), (num_local, den_local)
+    )
     prior_kv = prior[:, :rows_kv].reshape(total_kv.shape)
     prior_k = prior[:, rows_kv, : total_k.shape[1]]
     heads_out = finish(

time: 75.8 us -> 74 us (0.976)
  waiting for transfers between devices: 19 us -> 13.8 us
  starting transfers between devices: 30.4 us -> 32.1 us
  other arithmetic: 4.3 us -> 5.73 us
    ppermute x16, waiting for transfers between devices: 19 us -> 13.8 us  [send(): return tmap(lambda t: lax.ppermute(t, axis, perm=pairs), tree)]
    ppermute x16, starting transfers between devices: 30.4 us -> 32.1 us  [send(): return tmap(lambda t: lax.ppermute(t, axis, perm=pairs), tree)]
    another operation x2, other arithmetic: 0.06 us -> 1.47 us  [entering(): jnp.stack(p)[order].reshape((-1,) + p[0].shape[1:])]
    dot_general x1, matrix products: 1.52 us -> 2.5 us  [block_terms(): jnp.einsum('rnhij,rnjhd->rnihd', weights, vv, preferred_element_type=jnp....]
  transfers between devices with their start and end apart: 16 -> 16, of which waited for: 9 -> 11; matrix products, arithmetic and copies ran while one was open for 7% -> 11% of each run, Pallas kernels for 0% -> 0%
where the time goes in v7:
time: 74 us; the launch traced here: 73.5 us
  starting transfers between devices  32.1 us (43%)
  matrix products  18.1 us (24%)
  waiting for transfers between devices  13.8 us (19%)
  other arithmetic  5.73 us (8%)
  local copies, waits for them, and re-layouts  3.62 us (5%)
    ppermute x16, starting transfers between devices, send(): return tmap(lambda t: lax.ppermute(t, axis, perm=pairs), tree)  32.1 us
    ppermute x16, waiting for transfers between devices, send(): return tmap(lambda t: lax.ppermute(t, axis, perm=pairs), tree)  13.8 us
    dot_general x1, matrix products, shards(): jnp.einsum('rtd,de->rte', frames_in, w_qkv, preferred_element_type=jnp.fl...  6.02 us
    dot_general x1, matrix products, block_terms(): jnp.einsum('rnihd,rnjhd->rnhij', pq, pk, preferred_element_type=jnp.float32)  2.93 us
    convert_element_type x1, local copies, waits for them, and re-layouts, shards(): jnp.einsum('rtd,de->rte', frames_in, w_qkv, preferred_element_type=jnp.fl...  2.61 us
    dot_general x1, matrix products, block_terms(): jnp.einsum('rnhij,rnjhd->rnihd', weights, vv, preferred_element_type=jnp....  2.5 us
    dot_general x1, matrix products, finish(): jnp.einsum('rnihd,rnhde->rnihe', pq32, before_kv, precision=lax.Precision...  1.92 us
    dot_general x1, matrix products, finish(): jnp.einsum('rnihd,rnhd->rnih', pq32, before_k, precision=lax.Precision.HI...  1.6 us
  transfers between devices with their start and end apart: 16, of which 11 were waited for; matrix products, arithmetic and copies ran while one was open for 11% of the time, Pallas kernels for 0%

profile of v7, /device:TPU:1, one launch (start us, length us, event | category | flops | bytes accessed | tf_op | source)
XLA Modules:
  0.0 73.5 jit_solution(13375675149490585781)
XLA Ops:
  0.0 6.0 %convolution_convert_fusion = bf16[256,3072]{1,0:T(8,128)(2,1)} fusion(bf16[1024,3072]{1,0:T(8,128)(2,1)} %param.4, bf16[1,256,1024]{2,1,0:T(8,128)(2,1)} %param.3), kind=kOutput, calls=%fused_computation.3 | convolution fusion | flops 1611399168 | bytes 8388608 | tf_op jit(solution)/shard_map/rtd,de->rte/dot_general | solution.py:149
  6.0 2.6 %copy.10 = bf16[256,3072]{0,1:T(8,128)(2,1)} copy(bf16[256,3072]{1,0:T(8,128)(2,1)} %convolution_convert_fusion) | data formatting | bytes 3145728 | tf_op jit(solution)/shard_map/convert_element_type | solution.py:149
  8.6 1.6 %fusion.14 = f32[16,64,64]{2,1,0:T(8,128)S(1)} fusion(bf16[1,256,3,16,64]{1,4,3,2,0:T(8,128)(2,1)} %bitcast.71), kind=kOutput, calls=%fused_computation.29 | convolution fusion | flops 35127296 | bytes 1310720 | tf_op jit(solution)/shard_map/rnjhd,rnjhe->rnhde/dot_general | solution.py:120
  10.2 1.4 %convert_reduce_fusion = f32[16,64]{1,0:T(8,128)S(1)} fusion(bf16[1,256,3,16,64]{1,4,3,2,0:T(8,128)(2,1)} %bitcast.72), kind=kLoop, calls=%fused_computation.23 | loop fusion | flops 2096128 | bytes 528384 | tf_op jit(solution)/shard_map/reduce_sum | solution.py:121
  11.6 0.1 reshape_squeeze.4
  11.8 3.3 %collective-permute-start = (f32[8,33,128]{2,1,0:T(8,128)S(1)}, f32[8,33,128]{2,1,0:T(8,128)S(1)}, u32[]{:S(2)}, u32[]{:S(2)}) collective-permute-start(f32[8,33,128]{2,1,0:T(8,128)S(1)} %fusion.20), channel_id=1, source_target_pairs={{0,2},{2,0},{1,3},{3,1},{4,6},{6,4},{5,7},{7,5},{8,10},{10,8},{9,1... | collective-permute-start | bytes 405512 | tf_op jit(solution)/shard_map/ppermute | solution.py:22
  15.1 1.0 %collective-permute-done = f32[8,33,128]{2,1,0:T(8,128)S(1)} collective-permute-done((f32[8,33,128]{2,1,0:T(8,128)S(1)}, f32[8,33,128]{2,1,0:T(8,128)S(1)}, u32[]{:S(2)}, u32[]{:S(2)}) %collective-permute-start) | collective-permute-done | bytes 135200 | tf_op jit(solution)/shard_map/ppermute | solution.py:22
  16.2 0.1 collective-permute-start.1
  16.3 2.2 %collective-permute-start.2 = (f32[2,33,128]{2,1,0:T(8,128)S(1)}, f32[2,33,128]{2,1,0:T(8,128)S(1)}, u32[]{:S(2)}, u32[]{:S(2)}) collective-permute-start(f32[2,33,128]{2,1,0:T(8,128)S(1)} %get-tuple-element.18), channel_id=1, source_target_pairs={{0,16},{8,24},{16,0},{24,8},{1,17},{9,25},{17,1},{25,9},{2,18},{10... | collective-permute-start | bytes 101384 | tf_op jit(solution)/shard_map/ppermute | solution.py:22
  18.4 1.1 %collective-permute-start.3 = (f32[2,33,128]{2,1,0:T(8,128)S(1)}, f32[2,33,128]{2,1,0:T(8,128)S(1)}, u32[]{:S(2)}, u32[]{:S(2)}) collective-permute-start(f32[2,33,128]{2,1,0:T(8,128)S(1)} %get-tuple-element.17), channel_id=1, source_target_pairs={{0,24},{8,0},{16,8},{24,16},{1,25},{9,1},{17,9},{25,17},{2,26},{10... | collective-permute-start | bytes 101384 | tf_op jit(solution)/shard_map/ppermute | solution.py:22
  19.5 0.8 %collective-permute-done.1 = f32[2,33,128]{2,1,0:T(8,128)S(1)} collective-permute-done((f32[2,33,128]{2,1,0:T(8,128)S(1)}, f32[2,33,128]{2,1,0:T(8,128)S(1)}, u32[]{:S(2)}, u32[]{:S(2)}) %collective-permute-start.1) | collective-permute-done | bytes 33824 | tf_op jit(solution)/shard_map/ppermute | solution.py:22
  20.3 1.1 %collective-permute-done.2 = f32[2,33,128]{2,1,0:T(8,128)S(1)} collective-permute-done((f32[2,33,128]{2,1,0:T(8,128)S(1)}, f32[2,33,128]{2,1,0:T(8,128)S(1)}, u32[]{:S(2)}, u32[]{:S(2)}) %collective-permute-start.2) | collective-permute-done | bytes 33824 | tf_op jit(solution)/shard_map/ppermute | solution.py:22
  21.4 0.2 collective-permute-done.3
  21.6 1.7 %collective-permute-start.4 = (f32[2,33,128]{2,1,0:T(8,128)S(1)}, f32[2,33,128]{2,1,0:T(8,128)S(1)}, u32[]{:S(2)}, u32[]{:S(2)}) collective-permute-start(f32[2,33,128]{2,1,0:T(8,128)S(1)} %add_add_fusion), channel_id=1, source_target_pairs={{0,32},{32,64},{64,96},{96,128},{128,160},{160,192},{192,224},{224... | collective-permute-start | bytes 101384 | tf_op jit(solution)/shard_map/ppermute | solution.py:22
  23.3 4.0 %collective-permute-start.5 = (f32[2,33,128]{2,1,0:T(8,128)S(1)}, f32[2,33,128]{2,1,0:T(8,128)S(1)}, u32[]{:S(2)}, u32[]{:S(2)}) collective-permute-start(f32[2,33,128]{2,1,0:T(8,128)S(1)} %add_add_fusion), channel_id=1, source_target_pairs={{0,224},{32,0},{64,32},{96,64},{128,96},{160,128},{192,160},{224,1... | collective-permute-start | bytes 101384 | tf_op jit(solution)/shard_map/ppermute | solution.py:22
  27.4 1.3 %collective-permute-done.4 = f32[2,33,128]{2,1,0:T(8,128)S(1)} collective-permute-done((f32[2,33,128]{2,1,0:T(8,128)S(1)}, f32[2,33,128]{2,1,0:T(8,128)S(1)}, u32[]{:S(2)}, u32[]{:S(2)}) %collective-permute-start.4) | collective-permute-done | bytes 33824 | tf_op jit(solution)/shard_map/ppermute | solution.py:22
  28.6 0.0 collective-permute-start.6
  28.7 2.9 %select_reduce_fusion = (f32[16,256]{1,0:T(8,128)}, bf16[16,256,256]{1,2,0:T(8,128)(2,1)S(1)}) fusion(pred[256,256]{0,1:T(8,128)(4,1)S(1)} %iota_compare_fusion, bf16[1,256,3,16,64]{1,4,3,2,0:T(8,128)(2,1)} %bitcast.73), kind=kOutput, calls=%fused_computation.1 | convolution fusion | flops 140505088 | bytes 3227648 | tf_op jit(solution)/shard_map/rnihd,rnjhd->rnhij/dot_general | solution.py:114
  31.6 2.7 %collective-permute-start.7 = (f32[2,33,128]{2,1,0:T(8,128)S(1)}, f32[2,33,128]{2,1,0:T(8,128)S(1)}, u32[]{:S(2)}, u32[]{:S(2)}) collective-permute-start(f32[2,33,128]{2,1,0:T(8,128)S(1)} %collective-permute-done.5), channel_id=1, source_target_pairs={{0,224},{32,0},{64,32},{96,64},{128,96},{160,128},{192,160},{224,1... | collective-permute-start | bytes 101384 | tf_op jit(solution)/shard_map/ppermute | solution.py:22
  34.3 0.0 collective-permute-done.6
  34.3 2.5 %fusion.3 = f32[1,1,256,16,64]{2,4,3,1,0:T(8,128)} fusion(bf16[16,256,256]{1,2,0:T(8,128)(2,1)S(1)} %get-tuple-element.20, pred[256,256]{0,1:T(8,128)(4,1)S(1)} %iota_compare_fusion, bf16[1,256,3,16,64]{1,4,3,2,0:T(8,128)(2,1)} %bitcast.74), kind=kOutput, calls=%fused_computation.13 | convolution fusion | flops 135266304 | bytes 3735552 | tf_op jit(solution)/shard_map/rnhij,rnjhd->rnihd/dot_general | solution.py:119
  36.8 2.7 %collective-permute-start.9 = (f32[2,33,128]{2,1,0:T(8,128)S(1)}, f32[2,33,128]{2,1,0:T(8,128)S(1)}, u32[]{:S(2)}, u32[]{:S(2)}) collective-permute-start(f32[2,33,128]{2,1,0:T(8,128)S(1)} %collective-permute-done.7), channel_id=1, source_target_pairs={{0,224},{32,0},{64,32},{96,64},{128,96},{160,128},{192,160},{224,1... | collective-permute-start | bytes 101384 | tf_op jit(solution)/shard_map/ppermute | solution.py:22
  39.5 0.0 collective-permute-done.8
  39.5 0.0 collective-permute-start.10
  39.5 0.5 fusion.24
  40.0 0.6 collective-permute-done.9
  40.6 3.3 %collective-permute-done.10 = f32[2,33,128]{2,1,0:T(8,128)} collective-permute-done((f32[2,33,128]{2,1,0:T(8,128)}, f32[2,33,128]{2,1,0:T(8,128)}, u32[]{:S(2)}, u32[]{:S(2)}) %collective-permute-start.10) | collective-permute-done | bytes 33824 | tf_op jit(solution)/shard_map/ppermute | solution.py:22
  44.0 0.1 collective-permute-start.11
  44.1 0.7 add_bitcast_fusion
  44.7 3.2 %collective-permute-start.12 = (f32[2,33,128]{2,1,0:T(8,128)S(1)}, f32[2,33,128]{2,1,0:T(8,128)S(1)}, u32[]{:S(2)}, u32[]{:S(2)}) collective-permute-start(f32[2,33,128]{2,1,0:T(8,128)S(1)} %get-tuple-element.15), channel_id=1, source_target_pairs={{0,16},{8,24},{16,0},{24,8},{1,17},{9,25},{17,1},{25,9},{2,18},{10... | collective-permute-start | bytes 101384 | tf_op jit(solution)/shard_map/ppermute | solution.py:22
  47.9 0.1 collective-permute-start.13
  48.0 1.2 %pad_clamp_fusion = s32[1024]{0:T(1024)} fusion(s32[4]{0:T(128)} %fusion.24), kind=kLoop, calls=%fused_computation.61 | loop fusion | flops 1024 | bytes 4112 | tf_op jit(solution)/shard_map/gather | solution.py:98
  49.2 0.0 collective-permute-done.11
  49.2 0.1 collective-permute-done.12
  49.3 1.5 %collective-permute-done.13 = f32[2,33,128]{2,1,0:T(8,128)S(1)} collective-permute-done((f32[2,33,128]{2,1,0:T(8,128)S(1)}, f32[2,33,128]{2,1,0:T(8,128)S(1)}, u32[]{:S(2)}, u32[]{:S(2)}) %collective-permute-start.13) | collective-permute-done | bytes 33824 | tf_op jit(solution)/shard_map/ppermute | solution.py:22
  50.7 0.8 %pad_maximum_fusion = f32[4,2,33,128]{3,2,1,0:T(8,128)S(1)} fusion(f32[1,2,33,128]{3,2,1,0:T(8,128)S(1)} %bitcast.83, f32[1,2,33,128]{3,2,1,0:T(8,128)S(1)} %bitcast.82, f32[1,2,33,128]{3,2,1,0:T(8,128)} %bitcast.81, f32[1,2,33,128]{3,2,1,0:T(8,128)} %get-tuple-element.13), kind=kLoop, calls=%fused_computation.44 | loop fusion | flops 101376 | bytes 270336 | tf_op jit(solution)/shard_map/stack | solution.py:98
  51.5 0.7 gather_fusion
  52.3 2.8 %collective-permute-start.14 = (f32[8,33,128]{2,1,0:T(8,128)S(1)}, f32[8,33,128]{2,1,0:T(8,128)S(1)}, u32[]{:S(2)}, u32[]{:S(2)}) collective-permute-start(f32[8,33,128]{2,1,0:T(8,128)S(1)} %bitcast_add_fusion.1), channel_id=1, source_target_pairs={{0,4},{4,0},{1,5},{5,1},{2,6},{6,2},{3,7},{7,3},{8,12},{12,8},{9,1... | collective-permute-start | bytes 405512 | tf_op jit(solution)/shard_map/ppermute | solution.py:22
  55.1 2.9 %collective-permute-done.14 = f32[8,33,128]{2,1,0:T(8,128)S(1)} collective-permute-done((f32[8,33,128]{2,1,0:T(8,128)S(1)}, f32[8,33,128]{2,1,0:T(8,128)S(1)}, u32[]{:S(2)}, u32[]{:S(2)}) %collective-permute-start.14) | collective-permute-done | bytes 135200 | tf_op jit(solution)/shard_map/ppermute | solution.py:22
  58.0 8.2 %collective-permute-start.15 = (f32[8,33,128]{2,1,0:T(8,128)S(1)}, f32[8,33,128]{2,1,0:T(8,128)S(1)}, u32[]{:S(2)}, u32[]{:S(2)}) collective-permute-start(f32[8,33,128]{2,1,0:T(8,128)S(1)} %select_add_fusion), channel_id=1, source_target_pairs={{0,2},{2,0},{1,3},{3,1},{4,6},{6,4},{5,7},{7,5},{8,10},{10,8},{9,1... | collective-permute-start | bytes 405512 | tf_op jit(solution)/shard_map/ppermute | solution.py:22
  66.2 1.0 %collective-permute-done.15 = f32[8,33,128]{2,1,0:T(8,128)S(1)} collective-permute-done((f32[8,33,128]{2,1,0:T(8,128)S(1)}, f32[8,33,128]{2,1,0:T(8,128)S(1)}, u32[]{:S(2)}, u32[]{:S(2)}) %collective-permute-start.15) | collective-permute-done | bytes 135200 | tf_op jit(solution)/shard_map/ppermute | solution.py:22
  67.2 0.1 add_select_fusion
  67.3 0.7 fusion.19
  68.0 1.6 %fusion.28 = f32[16,1,256]{2,1,0:T(1,128)S(1)} fusion(f32[16,64,1]{1,2,0:T(1,128)S(1)} %bitcast.86, bf16[1,256,3,16,64]{1,4,3,2,0:T(8,128)(2,1)} %bitcast.75), kind=kOutput, calls=%fused_computation.72 | convolution fusion | flops 4718592 | bytes 544768 | tf_op jit(solution)/shard_map/rnihd,rnhd->rnih/dot_general | solution.py:133
  69.7 0.2 broadcast_in_dim_broadcast_in_dim_reshape.3
  69.8 1.9 %convolution_bitcast_fusion = f32[1,1,256,16,64]{2,4,3,1,0:T(8,128)S(1)} fusion(f32[16,64,64]{2,1,0:T(8,128)S(1)} %broadcast_in_dim_broadcast_in_dim_reshape.3, f32[16,64,64]{2,1,0:T(8,128)S(1)} %fusion.14, bf16[1,256,3,16,64]{1,4,3,2,0:T(8,128)(2,1)} %bitcast.76), kind=kOutput, calls=%fused_computation.14 | convolution fusion | flops 203030528 | bytes 2097152 | tf_op jit(solution)/shard_map/rnihd,rnhde->rnihe/dot_general | solution.py:130
  71.8 0.2 divide_convert_fusion
  72.0 1.5 %fusion.4 = bf16[1,256,1024]{2,1,0:T(8,128)(2,1)} fusion(bf16[256,1024]{0,1:T(8,128)(2,1)S(1)} %bitcast.77, bf16[1024,1024]{1,0:T(8,128)(2,1)S(1)} %copy-done), kind=kOutput, calls=%fused_computation.16 | convolution fusion | flops 537133056 | bytes 3145728 | tf_op jit(solution)/shard_map/rtd,de->rte/dot_general | solution.py:169
  (30 shorter events, 0.3 us)
Async XLA Ops:
  0.0 72.0 %copy-start = (bf16[1024,1024]{1,0:T(8,128)(2,1)S(1)}, bf16[1024,1024]{1,0:T(8,128)(2,1)}, u32[]{:S(2)}) copy-start(bf16[1024,1024]{1,0:T(8,128)(2,1)} %param.5) | copy-start | bytes 6291460
  11.8 4.3 %collective-permute-start = (f32[8,33,128]{2,1,0:T(8,128)S(1)}, f32[8,33,128]{2,1,0:T(8,128)S(1)}, u32[]{:S(2)}, u32[]{:S(2)}) collective-permute-start(f32[8,33,128]{2,1,0:T(8,128)S(1)} %fusion.20), channel_id=1, source_target_pairs={{0,2},{2,0},{1,3},{3,1},{4,6},{6,4},{5,7},{7,5},{8,10},{10,8},{9,1... | collective-permute-start | bytes 405512 | tf_op jit(solution)/shard_map/ppermute | solution.py:22
  16.2 4.2 %collective-permute-start.1 = (f32[2,33,128]{2,1,0:T(8,128)S(1)}, f32[2,33,128]{2,1,0:T(8,128)S(1)}, u32[]{:S(2)}, u32[]{:S(2)}) collective-permute-start(f32[2,33,128]{2,1,0:T(8,128)S(1)} %get-tuple-element.16), channel_id=1, source_target_pairs={{0,8},{8,16},{16,24},{24,0},{1,9},{9,17},{17,25},{25,1},{2,10},{10... | collective-permute-start | bytes 101384 | tf_op jit(solution)/shard_map/ppermute | solution.py:22
  16.3 5.2 %collective-permute-start.2 = (f32[2,33,128]{2,1,0:T(8,128)S(1)}, f32[2,33,128]{2,1,0:T(8,128)S(1)}, u32[]{:S(2)}, u32[]{:S(2)}) collective-permute-start(f32[2,33,128]{2,1,0:T(8,128)S(1)} %get-tuple-element.18), channel_id=1, source_target_pairs={{0,16},{8,24},{16,0},{24,8},{1,17},{9,25},{17,1},{25,9},{2,18},{10... | collective-permute-start | bytes 101384 | tf_op jit(solution)/shard_map/ppermute | solution.py:22
  18.4 3.2 %collective-permute-start.3 = (f32[2,33,128]{2,1,0:T(8,128)S(1)}, f32[2,33,128]{2,1,0:T(8,128)S(1)}, u32[]{:S(2)}, u32[]{:S(2)}) collective-permute-start(f32[2,33,128]{2,1,0:T(8,128)S(1)} %get-tuple-element.17), channel_id=1, source_target_pairs={{0,24},{8,0},{16,8},{24,16},{1,25},{9,1},{17,9},{25,17},{2,26},{10... | collective-permute-start | bytes 101384 | tf_op jit(solution)/shard_map/ppermute | solution.py:22
  21.6 7.0 %collective-permute-start.4 = (f32[2,33,128]{2,1,0:T(8,128)S(1)}, f32[2,33,128]{2,1,0:T(8,128)S(1)}, u32[]{:S(2)}, u32[]{:S(2)}) collective-permute-start(f32[2,33,128]{2,1,0:T(8,128)S(1)} %add_add_fusion), channel_id=1, source_target_pairs={{0,32},{32,64},{64,96},{96,128},{128,160},{160,192},{192,224},{224... | collective-permute-start | bytes 101384 | tf_op jit(solution)/shard_map/ppermute | solution.py:22
  23.3 8.2 %collective-permute-start.5 = (f32[2,33,128]{2,1,0:T(8,128)S(1)}, f32[2,33,128]{2,1,0:T(8,128)S(1)}, u32[]{:S(2)}, u32[]{:S(2)}) collective-permute-start(f32[2,33,128]{2,1,0:T(8,128)S(1)} %add_add_fusion), channel_id=1, source_target_pairs={{0,224},{32,0},{64,32},{96,64},{128,96},{160,128},{192,160},{224,1... | collective-permute-start | bytes 101384 | tf_op jit(solution)/shard_map/ppermute | solution.py:22
  28.6 5.6 %collective-permute-start.6 = (f32[2,33,128]{2,1,0:T(8,128)S(1)}, f32[2,33,128]{2,1,0:T(8,128)S(1)}, u32[]{:S(2)}, u32[]{:S(2)}) collective-permute-start(f32[2,33,128]{2,1,0:T(8,128)S(1)} %collective-permute-done.4), channel_id=1, source_target_pairs={{0,32},{32,64},{64,96},{96,128},{128,160},{160,192},{192,224},{224... | collective-permute-start | bytes 101384 | tf_op jit(solution)/shard_map/ppermute | solution.py:22
  31.6 5.2 %collective-permute-start.7 = (f32[2,33,128]{2,1,0:T(8,128)S(1)}, f32[2,33,128]{2,1,0:T(8,128)S(1)}, u32[]{:S(2)}, u32[]{:S(2)}) collective-permute-start(f32[2,33,128]{2,1,0:T(8,128)S(1)} %collective-permute-done.5), channel_id=1, source_target_pairs={{0,224},{32,0},{64,32},{96,64},{128,96},{160,128},{192,160},{224,1... | collective-permute-start | bytes 101384 | tf_op jit(solution)/shard_map/ppermute | solution.py:22
  34.3 2.5 %copy-start.4 = (f32[2,33,128]{2,1,0:T(8,128)}, f32[2,33,128]{2,1,0:T(8,128)S(1)}, u32[]{:S(2)}) copy-start(f32[2,33,128]{2,1,0:T(8,128)S(1)} %collective-permute-done.6) | copy-start | bytes 101380
  34.3 5.2 %collective-permute-start.8 = (f32[2,33,128]{2,1,0:T(8,128)S(1)}, f32[2,33,128]{2,1,0:T(8,128)}, u32[]{:S(2)}, u32[]{:S(2)}) collective-permute-start(f32[2,33,128]{2,1,0:T(8,128)S(1)} %collective-permute-done.6), channel_id=1, source_target_pairs={{0,32},{32,64},{64,96},{96,128},{128,160},{160,192},{192,224},{224... | collective-permute-start | bytes 101384 | tf_op jit(solution)/shard_map/ppermute | solution.py:22
  36.8 3.8 %copy-start.5 = (f32[2,33,128]{2,1,0:T(8,128)}, f32[2,33,128]{2,1,0:T(8,128)S(1)}, u32[]{:S(2)}) copy-start(f32[2,33,128]{2,1,0:T(8,128)S(1)} %collective-permute-done.7) | copy-start | bytes 101380
  36.8 3.8 %collective-permute-start.9 = (f32[2,33,128]{2,1,0:T(8,128)S(1)}, f32[2,33,128]{2,1,0:T(8,128)S(1)}, u32[]{:S(2)}, u32[]{:S(2)}) collective-permute-start(f32[2,33,128]{2,1,0:T(8,128)S(1)} %collective-permute-done.7), channel_id=1, source_target_pairs={{0,224},{32,0},{64,32},{96,64},{128,96},{160,128},{192,160},{224,1... | collective-permute-start | bytes 101384 | tf_op jit(solution)/shard_map/ppermute | solution.py:22
  39.5 4.4 %collective-permute-start.10 = (f32[2,33,128]{2,1,0:T(8,128)}, f32[2,33,128]{2,1,0:T(8,128)}, u32[]{:S(2)}, u32[]{:S(2)}) collective-permute-start(f32[2,33,128]{2,1,0:T(8,128)} %collective-permute-done.8), channel_id=1, source_target_pairs={{0,32},{32,64},{64,96},{96,128},{128,160},{160,192},{192,224},{224... | collective-permute-start | bytes 101384 | tf_op jit(solution)/shard_map/ppermute | solution.py:22
  44.0 5.2 %collective-permute-start.11 = (f32[2,33,128]{2,1,0:T(8,128)S(1)}, f32[2,33,128]{2,1,0:T(8,128)S(1)}, u32[]{:S(2)}, u32[]{:S(2)}) collective-permute-start(f32[2,33,128]{2,1,0:T(8,128)S(1)} %select_add_fusion.4), channel_id=1, source_target_pairs={{0,8},{8,16},{16,24},{24,0},{1,9},{9,17},{17,25},{25,1},{2,10},{10... | collective-permute-start | bytes 101384 | tf_op jit(solution)/shard_map/ppermute | solution.py:22
  44.7 4.5 %collective-permute-start.12 = (f32[2,33,128]{2,1,0:T(8,128)S(1)}, f32[2,33,128]{2,1,0:T(8,128)S(1)}, u32[]{:S(2)}, u32[]{:S(2)}) collective-permute-start(f32[2,33,128]{2,1,0:T(8,128)S(1)} %get-tuple-element.15), channel_id=1, source_target_pairs={{0,16},{8,24},{16,0},{24,8},{1,17},{9,25},{17,1},{25,9},{2,18},{10... | collective-permute-start | bytes 101384 | tf_op jit(solution)/shard_map/ppermute | solution.py:22
  47.9 2.9 %collective-permute-start.13 = (f32[2,33,128]{2,1,0:T(8,128)S(1)}, f32[2,33,128]{2,1,0:T(8,128)S(1)}, u32[]{:S(2)}, u32[]{:S(2)}) collective-permute-start(f32[2,33,128]{2,1,0:T(8,128)S(1)} %get-tuple-element.14), channel_id=1, source_target_pairs={{0,24},{8,0},{16,8},{24,16},{1,25},{9,1},{17,9},{25,17},{2,26},{10... | collective-permute-start | bytes 101384 | tf_op jit(solution)/shard_map/ppermute | solution.py:22
  49.2 1.6 %copy-start.3 = (f32[2,33,128]{2,1,0:T(8,128)}, f32[2,33,128]{2,1,0:T(8,128)S(1)}, u32[]{:S(2)}) copy-start(f32[2,33,128]{2,1,0:T(8,128)S(1)} %collective-permute-done.11) | copy-start | bytes 101380
  52.3 5.8 %collective-permute-start.14 = (f32[8,33,128]{2,1,0:T(8,128)S(1)}, f32[8,33,128]{2,1,0:T(8,128)S(1)}, u32[]{:S(2)}, u32[]{:S(2)}) collective-permute-start(f32[8,33,128]{2,1,0:T(8,128)S(1)} %bitcast_add_fusion.1), channel_id=1, source_target_pairs={{0,4},{4,0},{1,5},{5,1},{2,6},{6,2},{3,7},{7,3},{8,12},{12,8},{9,1... | collective-permute-start | bytes 405512 | tf_op jit(solution)/shard_map/ppermute | solution.py:22
  58.0 9.2 %collective-permute-start.15 = (f32[8,33,128]{2,1,0:T(8,128)S(1)}, f32[8,33,128]{2,1,0:T(8,128)S(1)}, u32[]{:S(2)}, u32[]{:S(2)}) collective-permute-start(f32[8,33,128]{2,1,0:T(8,128)S(1)} %select_add_fusion), channel_id=1, source_target_pairs={{0,2},{2,0},{1,3},{3,1},{4,6},{6,4},{5,7},{7,5},{8,10},{10,8},{9,1... | collective-permute-start | bytes 405512 | tf_op jit(solution)/shard_map/ppermute | solution.py:22
  68.0 1.6 %copy-start.1 = (f32[16,32,128]{2,1,0:T(8,128)S(1)}, f32[16,32,128]{2,1,0:T(8,128)}, u32[]{:S(2)}) copy-start(f32[16,32,128]{2,1,0:T(8,128)} %fusion.19) | copy-start | bytes 786436
  69.7 2.1 %copy-start.6 = (f32[16,256]{1,0:T(8,128)S(1)}, f32[16,256]{1,0:T(8,128)}, u32[]{:S(2)}) copy-start(f32[16,256]{1,0:T(8,128)} %get-tuple-element.19) | copy-start | bytes 49156
  69.8 2.0 %copy-start.2 = (f32[1,1,256,16,64]{2,4,3,1,0:T(8,128)S(1)}, f32[1,1,256,16,64]{2,4,3,1,0:T(8,128)}, u32[]{:S(2)}) copy-start(f32[1,1,256,16,64]{2,4,3,1,0:T(8,128)} %fusion.3) | copy-start | bytes 3145732

commit v8 on v7

--- a/solution.py
+++ b/solution.py
@@ -146,10 +146,10 @@
 def shards(frames_in, w_qkv, w_out):
     rows, tok_local, width = frames_in.shape
     head_dim = width // HEADS
-    qkv = jnp.einsum("rtd,de->rte", frames_in, w_qkv, preferred_element_type=jnp.float32).astype(
+    qkv = jnp.einsum("rtd,de->ret", frames_in, w_qkv, preferred_element_type=jnp.float32).astype(
         jnp.bfloat16
     )
-    parts = qkv.reshape(rows, tok_local, 3, HEADS, head_dim)
+    parts = jnp.transpose(qkv.reshape(rows, 3, HEADS, head_dim, tok_local), (0, 4, 1, 2, 3))
     phi_q, phi_k, values = split_qkv(parts)
     pq, num_local, den_local, kv_blocks, k_blocks = block_terms(phi_q, phi_k, values, SPAN)
     total_kv = jnp.sum(kv_blocks, axis=1)[0]

time: 74 us -> 68.7 us (0.928)
  matrix products: 18.1 us -> 15.7 us
  other arithmetic: 5.73 us -> 3.64 us
  local copies, waits for them, and re-layouts: 3.62 us -> 1.79 us
  waiting for transfers between devices: 13.8 us -> 14.7 us
    convert_element_type x1 -> x0, local copies, waits for them, and re-layouts: 2.61 us -> none  [shards(): jnp.einsum('rtd,de->rte', frames_in, w_qkv, preferred_element_type=jnp.fl...]
    dot_general x1, matrix products: 1.57 us -> 0.38 us  [block_terms(): jnp.einsum('rnjhd,rnjhe->rnhde', pk, vv, preferred_element_type=jnp.float32)]
    dot_general x1, matrix products: 6.02 us -> 4.9 us  [shards(): jnp.einsum('rtd,de->ret', frames_in, w_qkv, preferred_element_type=jnp.fl...]
    reduce_sum x1, other arithmetic: 1.39 us -> 0.34 us  [block_terms(): k_blocks = jnp.sum(pk, axis=2, dtype=jnp.float32)]
    ppermute x16, waiting for transfers between devices: 13.8 us -> 14.7 us  [send(): return tmap(lambda t: lax.ppermute(t, axis, perm=pairs), tree)]
    unnamed x14, local copies, waits for them, and re-layouts: 0.03 us -> 0.8 us
  transfers between devices with their start and end apart: 16 -> 16, of which waited for: 11 -> 11; matrix products, arithmetic and copies ran while one was open for 11% -> 10% of each run, Pallas kernels for 0% -> 0%
where the time goes in v8:
time: 68.7 us; the launch traced here: 68.4 us
  starting transfers between devices  32.1 us (47%)
  matrix products  15.7 us (23%)
  waiting for transfers between devices  14.7 us (21%)
  other arithmetic  3.64 us (5%)
  local copies, waits for them, and re-layouts  1.79 us (3%)
    ppermute x16, starting transfers between devices, send(): return tmap(lambda t: lax.ppermute(t, axis, perm=pairs), tree)  32.1 us
    ppermute x16, waiting for transfers between devices, send(): return tmap(lambda t: lax.ppermute(t, axis, perm=pairs), tree)  14.7 us
    dot_general x1, matrix products, shards(): jnp.einsum('rtd,de->ret', frames_in, w_qkv, preferred_element_type=jnp.fl...  4.9 us
    dot_general x1, matrix products, block_terms(): jnp.einsum('rnihd,rnjhd->rnhij', pq, pk, preferred_element_type=jnp.float32)  2.92 us
    dot_general x1, matrix products, block_terms(): jnp.einsum('rnhij,rnjhd->rnihd', weights, vv, preferred_element_type=jnp....  2.49 us
    dot_general x1, matrix products, finish(): jnp.einsum('rnihd,rnhde->rnihe', pq32, before_kv, precision=lax.Precision...  1.92 us
    dot_general x1, matrix products, finish(): jnp.einsum('rnihd,rnhd->rnih', pq32, before_k, precision=lax.Precision.HI...  1.6 us
    dot_general x1, matrix products, shards(): jnp.einsum('rtd,de->rte', heads_out, w_out, preferred_element_type=jnp.fl...  1.52 us
  transfers between devices with their start and end apart: 16, of which 11 were waited for; matrix products, arithmetic and copies ran while one was open for 10% of the time, Pallas kernels for 0%

profile of v8, /device:TPU:1, one launch (start us, length us, event | category | flops | bytes accessed | tf_op | source)
XLA Modules:
  0.0 68.4 jit_solution(9422364156194307092)
XLA Ops:
  0.0 4.9 %convolution_convert_fusion = bf16[3072,256]{1,0:T(8,128)(2,1)S(1)} fusion(bf16[1024,3072]{1,0:T(8,128)(2,1)} %param.4, bf16[1,256,1024]{2,1,0:T(8,128)(2,1)} %param.3), kind=kOutput, calls=%fused_computation.3 | convolution fusion | flops 1611399168 | bytes 8388608 | tf_op jit(solution)/shard_map/rtd,de->ret/dot_general | solution.py:149
  4.9 0.4 fusion.14
  5.3 0.8 %copy-done.3 = bf16[3072,256]{1,0:T(8,128)(2,1)} copy-done((bf16[3072,256]{1,0:T(8,128)(2,1)}, bf16[3072,256]{1,0:T(8,128)(2,1)S(1)}, u32[]{:S(2)}) %copy-start.3) | copy-done | bytes 1572888
  6.1 0.3 convert_reduce_fusion
  6.4 0.1 reshape_squeeze.4
  6.6 3.3 %collective-permute-start = (f32[8,33,128]{2,1,0:T(8,128)S(1)}, f32[8,33,128]{2,1,0:T(8,128)S(1)}, u32[]{:S(2)}, u32[]{:S(2)}) collective-permute-start(f32[8,33,128]{2,1,0:T(8,128)S(1)} %fusion.20), channel_id=1, source_target_pairs={{0,2},{2,0},{1,3},{3,1},{4,6},{6,4},{5,7},{7,5},{8,10},{10,8},{9,1... | collective-permute-start | bytes 405512 | tf_op jit(solution)/shard_map/ppermute | solution.py:22
  9.9 1.0 %collective-permute-done = f32[8,33,128]{2,1,0:T(8,128)S(1)} collective-permute-done((f32[8,33,128]{2,1,0:T(8,128)S(1)}, f32[8,33,128]{2,1,0:T(8,128)S(1)}, u32[]{:S(2)}, u32[]{:S(2)}) %collective-permute-start) | collective-permute-done | bytes 135200 | tf_op jit(solution)/shard_map/ppermute | solution.py:22
  11.0 0.1 collective-permute-start.1
  11.1 2.2 %collective-permute-start.2 = (f32[2,33,128]{2,1,0:T(8,128)S(1)}, f32[2,33,128]{2,1,0:T(8,128)S(1)}, u32[]{:S(2)}, u32[]{:S(2)}) collective-permute-start(f32[2,33,128]{2,1,0:T(8,128)S(1)} %get-tuple-element.18), channel_id=1, source_target_pairs={{0,16},{8,24},{16,0},{24,8},{1,17},{9,25},{17,1},{25,9},{2,18},{10... | collective-permute-start | bytes 101384 | tf_op jit(solution)/shard_map/ppermute | solution.py:22
  13.3 1.1 %collective-permute-start.3 = (f32[2,33,128]{2,1,0:T(8,128)S(1)}, f32[2,33,128]{2,1,0:T(8,128)S(1)}, u32[]{:S(2)}, u32[]{:S(2)}) collective-permute-start(f32[2,33,128]{2,1,0:T(8,128)S(1)} %get-tuple-element.17), channel_id=1, source_target_pairs={{0,24},{8,0},{16,8},{24,16},{1,25},{9,1},{17,9},{25,17},{2,26},{10... | collective-permute-start | bytes 101384 | tf_op jit(solution)/shard_map/ppermute | solution.py:22
  14.3 0.8 %collective-permute-done.1 = f32[2,33,128]{2,1,0:T(8,128)S(1)} collective-permute-done((f32[2,33,128]{2,1,0:T(8,128)S(1)}, f32[2,33,128]{2,1,0:T(8,128)S(1)}, u32[]{:S(2)}, u32[]{:S(2)}) %collective-permute-start.1) | collective-permute-done | bytes 33824 | tf_op jit(solution)/shard_map/ppermute | solution.py:22
  15.2 1.1 %collective-permute-done.2 = f32[2,33,128]{2,1,0:T(8,128)S(1)} collective-permute-done((f32[2,33,128]{2,1,0:T(8,128)S(1)}, f32[2,33,128]{2,1,0:T(8,128)S(1)}, u32[]{:S(2)}, u32[]{:S(2)}) %collective-permute-start.2) | collective-permute-done | bytes 33824 | tf_op jit(solution)/shard_map/ppermute | solution.py:22
  16.2 0.2 collective-permute-done.3
  16.5 1.7 %collective-permute-start.4 = (f32[2,33,128]{2,1,0:T(8,128)S(1)}, f32[2,33,128]{2,1,0:T(8,128)S(1)}, u32[]{:S(2)}, u32[]{:S(2)}) collective-permute-start(f32[2,33,128]{2,1,0:T(8,128)S(1)} %add_add_fusion), channel_id=1, source_target_pairs={{0,32},{32,64},{64,96},{96,128},{128,160},{160,192},{192,224},{224... | collective-permute-start | bytes 101384 | tf_op jit(solution)/shard_map/ppermute | solution.py:22
  18.2 4.0 %collective-permute-start.5 = (f32[2,33,128]{2,1,0:T(8,128)S(1)}, f32[2,33,128]{2,1,0:T(8,128)S(1)}, u32[]{:S(2)}, u32[]{:S(2)}) collective-permute-start(f32[2,33,128]{2,1,0:T(8,128)S(1)} %add_add_fusion), channel_id=1, source_target_pairs={{0,224},{32,0},{64,32},{96,64},{128,96},{160,128},{192,160},{224,1... | collective-permute-start | bytes 101384 | tf_op jit(solution)/shard_map/ppermute | solution.py:22
  22.2 1.3 %collective-permute-done.4 = f32[2,33,128]{2,1,0:T(8,128)S(1)} collective-permute-done((f32[2,33,128]{2,1,0:T(8,128)S(1)}, f32[2,33,128]{2,1,0:T(8,128)S(1)}, u32[]{:S(2)}, u32[]{:S(2)}) %collective-permute-start.4) | collective-permute-done | bytes 33824 | tf_op jit(solution)/shard_map/ppermute | solution.py:22
  23.5 0.0 collective-permute-start.6
  23.5 2.9 %select_reduce_fusion = (f32[16,256]{1,0:T(8,128)}, bf16[16,256,256]{1,2,0:T(8,128)(2,1)S(1)}) fusion(pred[256,256]{0,1:T(8,128)(4,1)S(1)} %iota_compare_fusion, bf16[1,256,3,16,64]{1,4,3,2,0:T(8,128)(2,1)} %bitcast.76), kind=kOutput, calls=%fused_computation.1 | convolution fusion | flops 140505088 | bytes 3227648 | tf_op jit(solution)/shard_map/rnihd,rnjhd->rnhij/dot_general | solution.py:114
  26.4 0.0 collective-permute-done.5
  26.4 2.7 %collective-permute-start.7 = (f32[2,33,128]{2,1,0:T(8,128)S(1)}, f32[2,33,128]{2,1,0:T(8,128)S(1)}, u32[]{:S(2)}, u32[]{:S(2)}) collective-permute-start(f32[2,33,128]{2,1,0:T(8,128)S(1)} %collective-permute-done.5), channel_id=1, source_target_pairs={{0,224},{32,0},{64,32},{96,64},{128,96},{160,128},{192,160},{224,1... | collective-permute-start | bytes 101384 | tf_op jit(solution)/shard_map/ppermute | solution.py:22
  29.1 0.0 collective-permute-done.6
  29.1 2.5 %fusion.3 = f32[1,1,256,16,64]{2,4,3,1,0:T(8,128)} fusion(bf16[16,256,256]{1,2,0:T(8,128)(2,1)S(1)} %get-tuple-element.20, pred[256,256]{0,1:T(8,128)(4,1)S(1)} %iota_compare_fusion, bf16[1,256,3,16,64]{1,4,3,2,0:T(8,128)(2,1)} %bitcast.77), kind=kOutput, calls=%fused_computation.13 | convolution fusion | flops 135266304 | bytes 3735552 | tf_op jit(solution)/shard_map/rnhij,rnjhd->rnihd/dot_general | solution.py:119
  31.6 0.0 collective-permute-done.7
  31.6 2.7 %collective-permute-start.9 = (f32[2,33,128]{2,1,0:T(8,128)S(1)}, f32[2,33,128]{2,1,0:T(8,128)S(1)}, u32[]{:S(2)}, u32[]{:S(2)}) collective-permute-start(f32[2,33,128]{2,1,0:T(8,128)S(1)} %collective-permute-done.7), channel_id=1, source_target_pairs={{0,224},{32,0},{64,32},{96,64},{128,96},{160,128},{192,160},{224,1... | collective-permute-start | bytes 101384 | tf_op jit(solution)/shard_map/ppermute | solution.py:22
  34.3 0.0 collective-permute-done.8
  34.3 0.0 collective-permute-start.10
  34.5 1.0 %collective-permute-done.9 = f32[2,33,128]{2,1,0:T(8,128)S(1)} collective-permute-done((f32[2,33,128]{2,1,0:T(8,128)S(1)}, f32[2,33,128]{2,1,0:T(8,128)S(1)}, u32[]{:S(2)}, u32[]{:S(2)}) %collective-permute-start.9) | collective-permute-done | bytes 33824 | tf_op jit(solution)/shard_map/ppermute | solution.py:22
  35.4 3.3 %collective-permute-done.10 = f32[2,33,128]{2,1,0:T(8,128)} collective-permute-done((f32[2,33,128]{2,1,0:T(8,128)}, f32[2,33,128]{2,1,0:T(8,128)}, u32[]{:S(2)}, u32[]{:S(2)}) %collective-permute-start.10) | collective-permute-done | bytes 33824 | tf_op jit(solution)/shard_map/ppermute | solution.py:22
  38.8 0.1 collective-permute-start.11
  38.9 0.7 add_bitcast_fusion
  39.5 3.1 %collective-permute-start.12 = (f32[2,33,128]{2,1,0:T(8,128)S(1)}, f32[2,33,128]{2,1,0:T(8,128)S(1)}, u32[]{:S(2)}, u32[]{:S(2)}) collective-permute-start(f32[2,33,128]{2,1,0:T(8,128)S(1)} %get-tuple-element.15), channel_id=1, source_target_pairs={{0,16},{8,24},{16,0},{24,8},{1,17},{9,25},{17,1},{25,9},{2,18},{10... | collective-permute-start | bytes 101384 | tf_op jit(solution)/shard_map/ppermute | solution.py:22
  42.7 0.1 collective-permute-start.13
  42.8 0.6 pad_clamp_fusion
  43.4 0.7 collective-permute-done.12
  44.1 1.5 %collective-permute-done.13 = f32[2,33,128]{2,1,0:T(8,128)S(1)} collective-permute-done((f32[2,33,128]{2,1,0:T(8,128)S(1)}, f32[2,33,128]{2,1,0:T(8,128)S(1)}, u32[]{:S(2)}, u32[]{:S(2)}) %collective-permute-start.13) | collective-permute-done | bytes 33824 | tf_op jit(solution)/shard_map/ppermute | solution.py:22
  45.5 0.8 %pad_maximum_fusion = f32[4,2,33,128]{3,2,1,0:T(8,128)S(1)} fusion(f32[1,2,33,128]{3,2,1,0:T(8,128)S(1)} %bitcast.84, f32[1,2,33,128]{3,2,1,0:T(8,128)S(1)} %bitcast.83, f32[1,2,33,128]{3,2,1,0:T(8,128)} %bitcast.13, f32[1,2,33,128]{3,2,1,0:T(8,128)} %get-tuple-element.13), kind=kLoop, calls=%fused_computation.44 | loop fusion | flops 101376 | bytes 270336 | tf_op jit(solution)/shard_map/stack | solution.py:98
  46.3 0.7 gather_fusion
  47.1 2.8 %collective-permute-start.14 = (f32[8,33,128]{2,1,0:T(8,128)S(1)}, f32[8,33,128]{2,1,0:T(8,128)S(1)}, u32[]{:S(2)}, u32[]{:S(2)}) collective-permute-start(f32[8,33,128]{2,1,0:T(8,128)S(1)} %bitcast_add_fusion.1), channel_id=1, source_target_pairs={{0,4},{4,0},{1,5},{5,1},{2,6},{6,2},{3,7},{7,3},{8,12},{12,8},{9,1... | collective-permute-start | bytes 405512 | tf_op jit(solution)/shard_map/ppermute | solution.py:22
  49.9 2.9 %collective-permute-done.14 = f32[8,33,128]{2,1,0:T(8,128)S(1)} collective-permute-done((f32[8,33,128]{2,1,0:T(8,128)S(1)}, f32[8,33,128]{2,1,0:T(8,128)S(1)}, u32[]{:S(2)}, u32[]{:S(2)}) %collective-permute-start.14) | collective-permute-done | bytes 135200 | tf_op jit(solution)/shard_map/ppermute | solution.py:22
  52.9 8.2 %collective-permute-start.15 = (f32[8,33,128]{2,1,0:T(8,128)S(1)}, f32[8,33,128]{2,1,0:T(8,128)S(1)}, u32[]{:S(2)}, u32[]{:S(2)}) collective-permute-start(f32[8,33,128]{2,1,0:T(8,128)S(1)} %select_add_fusion), channel_id=1, source_target_pairs={{0,2},{2,0},{1,3},{3,1},{4,6},{6,4},{5,7},{7,5},{8,10},{10,8},{9,1... | collective-permute-start | bytes 405512 | tf_op jit(solution)/shard_map/ppermute | solution.py:22
  61.0 1.0 %collective-permute-done.15 = f32[8,33,128]{2,1,0:T(8,128)S(1)} collective-permute-done((f32[8,33,128]{2,1,0:T(8,128)S(1)}, f32[8,33,128]{2,1,0:T(8,128)S(1)}, u32[]{:S(2)}, u32[]{:S(2)}) %collective-permute-start.15) | collective-permute-done | bytes 135200 | tf_op jit(solution)/shard_map/ppermute | solution.py:22
  62.0 0.1 add_select_fusion
  62.1 0.7 %fusion.19 = f32[16,32,128]{2,1,0:T(8,128)} fusion(f32[8,33,128]{2,1,0:T(8,128)S(1)} %get-tuple-element.12, f32[8,33,128]{2,1,0:T(8,128)S(1)} %get-tuple-element.11), kind=kLoop, calls=%fused_computation.40 | loop fusion | flops 65536 | bytes 532480 | tf_op jit(solution)/shard_map/concatenate | solution.py:52
  62.9 1.6 %fusion.28 = f32[16,1,256]{2,1,0:T(1,128)S(1)} fusion(f32[16,64,1]{1,2,0:T(1,128)S(1)} %bitcast.87, bf16[1,256,3,16,64]{1,4,3,2,0:T(8,128)(2,1)} %bitcast.78), kind=kOutput, calls=%fused_computation.72 | convolution fusion | flops 4718592 | bytes 544768 | tf_op jit(solution)/shard_map/rnihd,rnhd->rnih/dot_general | solution.py:133
  64.5 0.2 broadcast_in_dim_broadcast_in_dim_reshape.3
  64.6 1.9 %convolution_bitcast_fusion = f32[1,1,256,16,64]{2,4,3,1,0:T(8,128)S(1)} fusion(f32[16,64,64]{2,1,0:T(8,128)S(1)} %broadcast_in_dim_broadcast_in_dim_reshape.3, f32[16,64,64]{2,1,0:T(8,128)S(1)} %fusion.14, bf16[1,256,3,16,64]{1,4,3,2,0:T(8,128)(2,1)} %bitcast.79), kind=kOutput, calls=%fused_computation.14 | convolution fusion | flops 203030528 | bytes 2097152 | tf_op jit(solution)/shard_map/rnihd,rnhde->rnihe/dot_general | solution.py:130
  66.6 0.2 divide_convert_fusion
  66.8 1.5 %fusion.4 = bf16[1,256,1024]{2,1,0:T(8,128)(2,1)} fusion(bf16[256,1024]{0,1:T(8,128)(2,1)S(1)} %bitcast.73, bf16[1024,1024]{1,0:T(8,128)(2,1)S(1)} %copy-done), kind=kOutput, calls=%fused_computation.16 | convolution fusion | flops 537133056 | bytes 3145728 | tf_op jit(solution)/shard_map/rtd,de->rte/dot_general | solution.py:169
  (29 shorter events, 0.3 us)
Async XLA Ops:
  0.0 66.8 %copy-start = (bf16[1024,1024]{1,0:T(8,128)(2,1)S(1)}, bf16[1024,1024]{1,0:T(8,128)(2,1)}, u32[]{:S(2)}) copy-start(bf16[1024,1024]{1,0:T(8,128)(2,1)} %param.5) | copy-start | bytes 6291460
  4.9 1.2 %copy-start.3 = (bf16[3072,256]{1,0:T(8,128)(2,1)}, bf16[3072,256]{1,0:T(8,128)(2,1)S(1)}, u32[]{:S(2)}) copy-start(bf16[3072,256]{1,0:T(8,128)(2,1)S(1)} %convolution_convert_fusion) | copy-start | bytes 4718596
  6.6 4.3 %collective-permute-start = (f32[8,33,128]{2,1,0:T(8,128)S(1)}, f32[8,33,128]{2,1,0:T(8,128)S(1)}, u32[]{:S(2)}, u32[]{:S(2)}) collective-permute-start(f32[8,33,128]{2,1,0:T(8,128)S(1)} %fusion.20), channel_id=1, source_target_pairs={{0,2},{2,0},{1,3},{3,1},{4,6},{6,4},{5,7},{7,5},{8,10},{10,8},{9,1... | collective-permute-start | bytes 405512 | tf_op jit(solution)/shard_map/ppermute | solution.py:22
  11.0 4.2 %collective-permute-start.1 = (f32[2,33,128]{2,1,0:T(8,128)S(1)}, f32[2,33,128]{2,1,0:T(8,128)S(1)}, u32[]{:S(2)}, u32[]{:S(2)}) collective-permute-start(f32[2,33,128]{2,1,0:T(8,128)S(1)} %get-tuple-element.16), channel_id=1, source_target_pairs={{0,8},{8,16},{16,24},{24,0},{1,9},{9,17},{17,25},{25,1},{2,10},{10... | collective-permute-start | bytes 101384 | tf_op jit(solution)/shard_map/ppermute | solution.py:22
  11.1 5.2 %collective-permute-start.2 = (f32[2,33,128]{2,1,0:T(8,128)S(1)}, f32[2,33,128]{2,1,0:T(8,128)S(1)}, u32[]{:S(2)}, u32[]{:S(2)}) collective-permute-start(f32[2,33,128]{2,1,0:T(8,128)S(1)} %get-tuple-element.18), channel_id=1, source_target_pairs={{0,16},{8,24},{16,0},{24,8},{1,17},{9,25},{17,1},{25,9},{2,18},{10... | collective-permute-start | bytes 101384 | tf_op jit(solution)/shard_map/ppermute | solution.py:22
  13.3 3.2 %collective-permute-start.3 = (f32[2,33,128]{2,1,0:T(8,128)S(1)}, f32[2,33,128]{2,1,0:T(8,128)S(1)}, u32[]{:S(2)}, u32[]{:S(2)}) collective-permute-start(f32[2,33,128]{2,1,0:T(8,128)S(1)} %get-tuple-element.17), channel_id=1, source_target_pairs={{0,24},{8,0},{16,8},{24,16},{1,25},{9,1},{17,9},{25,17},{2,26},{10... | collective-permute-start | bytes 101384 | tf_op jit(solution)/shard_map/ppermute | solution.py:22
  16.5 7.0 %collective-permute-start.4 = (f32[2,33,128]{2,1,0:T(8,128)S(1)}, f32[2,33,128]{2,1,0:T(8,128)S(1)}, u32[]{:S(2)}, u32[]{:S(2)}) collective-permute-start(f32[2,33,128]{2,1,0:T(8,128)S(1)} %add_add_fusion), channel_id=1, source_target_pairs={{0,32},{32,64},{64,96},{96,128},{128,160},{160,192},{192,224},{224... | collective-permute-start | bytes 101384 | tf_op jit(solution)/shard_map/ppermute | solution.py:22
  18.2 8.2 %collective-permute-start.5 = (f32[2,33,128]{2,1,0:T(8,128)S(1)}, f32[2,33,128]{2,1,0:T(8,128)S(1)}, u32[]{:S(2)}, u32[]{:S(2)}) collective-permute-start(f32[2,33,128]{2,1,0:T(8,128)S(1)} %add_add_fusion), channel_id=1, source_target_pairs={{0,224},{32,0},{64,32},{96,64},{128,96},{160,128},{192,160},{224,1... | collective-permute-start | bytes 101384 | tf_op jit(solution)/shard_map/ppermute | solution.py:22
  23.5 5.6 %collective-permute-start.6 = (f32[2,33,128]{2,1,0:T(8,128)S(1)}, f32[2,33,128]{2,1,0:T(8,128)S(1)}, u32[]{:S(2)}, u32[]{:S(2)}) collective-permute-start(f32[2,33,128]{2,1,0:T(8,128)S(1)} %collective-permute-done.4), channel_id=1, source_target_pairs={{0,32},{32,64},{64,96},{96,128},{128,160},{160,192},{192,224},{224... | collective-permute-start | bytes 101384 | tf_op jit(solution)/shard_map/ppermute | solution.py:22
  26.4 5.2 %collective-permute-start.7 = (f32[2,33,128]{2,1,0:T(8,128)S(1)}, f32[2,33,128]{2,1,0:T(8,128)S(1)}, u32[]{:S(2)}, u32[]{:S(2)}) collective-permute-start(f32[2,33,128]{2,1,0:T(8,128)S(1)} %collective-permute-done.5), channel_id=1, source_target_pairs={{0,224},{32,0},{64,32},{96,64},{128,96},{160,128},{192,160},{224,1... | collective-permute-start | bytes 101384 | tf_op jit(solution)/shard_map/ppermute | solution.py:22
  29.1 2.5 %copy-start.4 = (f32[2,33,128]{2,1,0:T(8,128)}, f32[2,33,128]{2,1,0:T(8,128)S(1)}, u32[]{:S(2)}) copy-start(f32[2,33,128]{2,1,0:T(8,128)S(1)} %collective-permute-done.6) | copy-start | bytes 101380
  29.1 5.2 %collective-permute-start.8 = (f32[2,33,128]{2,1,0:T(8,128)S(1)}, f32[2,33,128]{2,1,0:T(8,128)}, u32[]{:S(2)}, u32[]{:S(2)}) collective-permute-start(f32[2,33,128]{2,1,0:T(8,128)S(1)} %collective-permute-done.6), channel_id=1, source_target_pairs={{0,32},{32,64},{64,96},{96,128},{128,160},{160,192},{192,224},{224... | collective-permute-start | bytes 101384 | tf_op jit(solution)/shard_map/ppermute | solution.py:22
  31.6 3.8 %copy-start.5 = (f32[2,33,128]{2,1,0:T(8,128)}, f32[2,33,128]{2,1,0:T(8,128)S(1)}, u32[]{:S(2)}) copy-start(f32[2,33,128]{2,1,0:T(8,128)S(1)} %collective-permute-done.7) | copy-start | bytes 101380
  31.6 3.8 %collective-permute-start.9 = (f32[2,33,128]{2,1,0:T(8,128)S(1)}, f32[2,33,128]{2,1,0:T(8,128)S(1)}, u32[]{:S(2)}, u32[]{:S(2)}) collective-permute-start(f32[2,33,128]{2,1,0:T(8,128)S(1)} %collective-permute-done.7), channel_id=1, source_target_pairs={{0,224},{32,0},{64,32},{96,64},{128,96},{160,128},{192,160},{224,1... | collective-permute-start | bytes 101384 | tf_op jit(solution)/shard_map/ppermute | solution.py:22
  34.3 4.4 %collective-permute-start.10 = (f32[2,33,128]{2,1,0:T(8,128)}, f32[2,33,128]{2,1,0:T(8,128)}, u32[]{:S(2)}, u32[]{:S(2)}) collective-permute-start(f32[2,33,128]{2,1,0:T(8,128)} %collective-permute-done.8), channel_id=1, source_target_pairs={{0,32},{32,64},{64,96},{96,128},{128,160},{160,192},{192,224},{224... | collective-permute-start | bytes 101384 | tf_op jit(solution)/shard_map/ppermute | solution.py:22
  38.8 4.6 %collective-permute-start.11 = (f32[2,33,128]{2,1,0:T(8,128)S(1)}, f32[2,33,128]{2,1,0:T(8,128)}, u32[]{:S(2)}, u32[]{:S(2)}) collective-permute-start(f32[2,33,128]{2,1,0:T(8,128)S(1)} %select_add_fusion.4), channel_id=1, source_target_pairs={{0,8},{8,16},{16,24},{24,0},{1,9},{9,17},{17,25},{25,1},{2,10},{10... | collective-permute-start | bytes 101384 | tf_op jit(solution)/shard_map/ppermute | solution.py:22
  39.5 4.5 %collective-permute-start.12 = (f32[2,33,128]{2,1,0:T(8,128)S(1)}, f32[2,33,128]{2,1,0:T(8,128)S(1)}, u32[]{:S(2)}, u32[]{:S(2)}) collective-permute-start(f32[2,33,128]{2,1,0:T(8,128)S(1)} %get-tuple-element.15), channel_id=1, source_target_pairs={{0,16},{8,24},{16,0},{24,8},{1,17},{9,25},{17,1},{25,9},{2,18},{10... | collective-permute-start | bytes 101384 | tf_op jit(solution)/shard_map/ppermute | solution.py:22
  42.7 2.9 %collective-permute-start.13 = (f32[2,33,128]{2,1,0:T(8,128)S(1)}, f32[2,33,128]{2,1,0:T(8,128)S(1)}, u32[]{:S(2)}, u32[]{:S(2)}) collective-permute-start(f32[2,33,128]{2,1,0:T(8,128)S(1)} %get-tuple-element.14), channel_id=1, source_target_pairs={{0,24},{8,0},{16,8},{24,16},{1,25},{9,1},{17,9},{25,17},{2,26},{10... | collective-permute-start | bytes 101384 | tf_op jit(solution)/shard_map/ppermute | solution.py:22
  47.1 5.8 %collective-permute-start.14 = (f32[8,33,128]{2,1,0:T(8,128)S(1)}, f32[8,33,128]{2,1,0:T(8,128)S(1)}, u32[]{:S(2)}, u32[]{:S(2)}) collective-permute-start(f32[8,33,128]{2,1,0:T(8,128)S(1)} %bitcast_add_fusion.1), channel_id=1, source_target_pairs={{0,4},{4,0},{1,5},{5,1},{2,6},{6,2},{3,7},{7,3},{8,12},{12,8},{9,1... | collective-permute-start | bytes 405512 | tf_op jit(solution)/shard_map/ppermute | solution.py:22
  52.9 9.2 %collective-permute-start.15 = (f32[8,33,128]{2,1,0:T(8,128)S(1)}, f32[8,33,128]{2,1,0:T(8,128)S(1)}, u32[]{:S(2)}, u32[]{:S(2)}) collective-permute-start(f32[8,33,128]{2,1,0:T(8,128)S(1)} %select_add_fusion), channel_id=1, source_target_pairs={{0,2},{2,0},{1,3},{3,1},{4,6},{6,4},{5,7},{7,5},{8,10},{10,8},{9,1... | collective-permute-start | bytes 405512 | tf_op jit(solution)/shard_map/ppermute | solution.py:22
  62.8 1.6 %copy-start.1 = (f32[16,32,128]{2,1,0:T(8,128)S(1)}, f32[16,32,128]{2,1,0:T(8,128)}, u32[]{:S(2)}) copy-start(f32[16,32,128]{2,1,0:T(8,128)} %fusion.19) | copy-start | bytes 786436
  64.5 2.1 %copy-start.6 = (f32[16,256]{1,0:T(8,128)S(1)}, f32[16,256]{1,0:T(8,128)}, u32[]{:S(2)}) copy-start(f32[16,256]{1,0:T(8,128)} %get-tuple-element.19) | copy-start | bytes 49156
  64.6 2.0 %copy-start.2 = (f32[1,1,256,16,64]{2,4,3,1,0:T(8,128)S(1)}, f32[1,1,256,16,64]{2,4,3,1,0:T(8,128)}, u32[]{:S(2)}) copy-start(f32[1,1,256,16,64]{2,4,3,1,0:T(8,128)} %fusion.3) | copy-start | bytes 3145732

commit v9 on v8

--- a/solution.py
+++ b/solution.py
@@ -74,14 +74,17 @@
     column = came[0]
     for c in came[1:]:
         column = add(column, c)
-    before_z = tmap(jnp.zeros_like, column)
-    left = right = column
+    lo, hi = ordered(column, swap(column, "frm"), core == 0)
+    both = joined(lo, hi)
+    ring = [(z_ * 2, ((z_ + 1) % n_z) * 2) for z_ in range(n_z)]
+    ring += [(z_ * 2 + 1, ((z_ - 1) % n_z) * 2 + 1) for z_ in range(n_z)]
+    stream = tmap(jnp.zeros_like, both)
+    piece = both
     for r in range(1, n_z // 2 + 1):
-        left = send(left, "seg_z", cyclic(n_z, 1))
-        before_z = add(before_z, keep(left, z >= r))
-        if r < n_z - r:
-            right = send(right, "seg_z", cyclic(n_z, -1))
-            before_z = add(before_z, keep(right, z + r >= n_z))
+        piece = send(piece, ("seg_z", "frm"), ring)
+        early = jnp.where(core == 0, z >= r, (z + r >= n_z) & (r < n_z - r))
+        stream = add(stream, keep(piece, early))
+    before_z = add(part(stream, core, 2), swap(part(stream, 1 - core, 2), "frm"))
     before_z, carry = lax.optimization_barrier((before_z, carry))
 
     def for_row(t):

time: 68.7 us -> 71.8 us (1.045)
  starting transfers between devices: 32.1 us -> 36.1 us
  waiting for transfers between devices: 14.7 us -> 12.9 us
  other arithmetic: 3.64 us -> 4.72 us
    ppermute x16 -> x15, starting transfers between devices: 32.1 us -> 36.1 us  [send(): return tmap(lambda t: lax.ppermute(t, axis, perm=pairs), tree)]
    ppermute x16 -> x15, waiting for transfers between devices: 14.7 us -> 12.9 us  [send(): return tmap(lambda t: lax.ppermute(t, axis, perm=pairs), tree)]
  transfers between devices with their start and end apart: 16 -> 15, of which waited for: 11 -> 12; matrix products, arithmetic and copies ran while one was open for 10% -> 11% of each run, Pallas kernels for 0% -> 0%
where the time goes in v9:
time: 71.8 us; the launch traced here: 71.5 us
  starting transfers between devices  36.1 us (50%)
  matrix products  15.7 us (22%)
  waiting for transfers between devices  12.9 us (18%)
  other arithmetic  4.72 us (7%)
  local copies, waits for them, and re-layouts  1.8 us (3%)
    ppermute x15, starting transfers between devices, send(): return tmap(lambda t: lax.ppermute(t, axis, perm=pairs), tree)  36.1 us
    ppermute x15, waiting for transfers between devices, send(): return tmap(lambda t: lax.ppermute(t, axis, perm=pairs), tree)  12.9 us
    dot_general x1, matrix products, shards(): jnp.einsum('rtd,de->ret', frames_in, w_qkv, preferred_element_type=jnp.fl...  4.9 us
    dot_general x1, matrix products, block_terms(): jnp.einsum('rnihd,rnjhd->rnhij', pq, pk, preferred_element_type=jnp.float32)  2.92 us
    dot_general x1, matrix products, block_terms(): jnp.einsum('rnhij,rnjhd->rnihd', weights, vv, preferred_element_type=jnp....  2.48 us
    dot_general x1, matrix products, finish(): jnp.einsum('rnihd,rnhde->rnihe', pq32, before_kv, precision=lax.Precision...  1.92 us
    dot_general x1, matrix products, finish(): jnp.einsum('rnihd,rnhd->rnih', pq32, before_k, precision=lax.Precision.HI...  1.6 us
    dot_general x1, matrix products, shards(): jnp.einsum('rtd,de->rte', heads_out, w_out, preferred_element_type=jnp.fl...  1.52 us
  transfers between devices with their start and end apart: 15, of which 12 were waited for; matrix products, arithmetic and copies ran while one was open for 11% of the time, Pallas kernels for 0%

profile of v9, /device:TPU:1, one launch (start us, length us, event | category | flops | bytes accessed | tf_op | source)
XLA Modules:
  0.0 71.5 jit_solution(12349208132901676780)
XLA Ops:
  0.0 4.9 %convolution_convert_fusion = bf16[3072,256]{1,0:T(8,128)(2,1)S(1)} fusion(bf16[1024,3072]{1,0:T(8,128)(2,1)} %param.4, bf16[1,256,1024]{2,1,0:T(8,128)(2,1)} %param.3), kind=kOutput, calls=%fused_computation.3 | convolution fusion | flops 1611399168 | bytes 8388608 | tf_op jit(solution)/shard_map/rtd,de->ret/dot_general | solution.py:152
  4.9 0.4 fusion.14
  5.3 0.8 %copy-done.3 = bf16[3072,256]{1,0:T(8,128)(2,1)} copy-done((bf16[3072,256]{1,0:T(8,128)(2,1)}, bf16[3072,256]{1,0:T(8,128)(2,1)S(1)}, u32[]{:S(2)}) %copy-start.3) | copy-done | bytes 1572888
  6.1 0.3 convert_reduce_fusion
  6.4 0.1 reshape_squeeze.4
  6.6 3.3 %collective-permute-start = (f32[8,33,128]{2,1,0:T(8,128)S(1)}, f32[8,33,128]{2,1,0:T(8,128)S(1)}, u32[]{:S(2)}, u32[]{:S(2)}) collective-permute-start(f32[8,33,128]{2,1,0:T(8,128)S(1)} %fusion.20), channel_id=1, source_target_pairs={{0,2},{2,0},{1,3},{3,1},{4,6},{6,4},{5,7},{7,5},{8,10},{10,8},{9,1... | collective-permute-start | bytes 405512 | tf_op jit(solution)/shard_map/ppermute | solution.py:22
  9.9 1.0 %collective-permute-done = f32[8,33,128]{2,1,0:T(8,128)S(1)} collective-permute-done((f32[8,33,128]{2,1,0:T(8,128)S(1)}, f32[8,33,128]{2,1,0:T(8,128)S(1)}, u32[]{:S(2)}, u32[]{:S(2)}) %collective-permute-start) | collective-permute-done | bytes 135200 | tf_op jit(solution)/shard_map/ppermute | solution.py:22
  11.0 0.1 collective-permute-start.1
  11.1 2.2 %collective-permute-start.2 = (f32[2,33,128]{2,1,0:T(8,128)S(1)}, f32[2,33,128]{2,1,0:T(8,128)S(1)}, u32[]{:S(2)}, u32[]{:S(2)}) collective-permute-start(f32[2,33,128]{2,1,0:T(8,128)S(1)} %get-tuple-element.18), channel_id=1, source_target_pairs={{0,16},{8,24},{16,0},{24,8},{1,17},{9,25},{17,1},{25,9},{2,18},{10... | collective-permute-start | bytes 101384 | tf_op jit(solution)/shard_map/ppermute | solution.py:22
  13.3 1.1 %collective-permute-start.3 = (f32[2,33,128]{2,1,0:T(8,128)S(1)}, f32[2,33,128]{2,1,0:T(8,128)S(1)}, u32[]{:S(2)}, u32[]{:S(2)}) collective-permute-start(f32[2,33,128]{2,1,0:T(8,128)S(1)} %get-tuple-element.17), channel_id=1, source_target_pairs={{0,24},{8,0},{16,8},{24,16},{1,25},{9,1},{17,9},{25,17},{2,26},{10... | collective-permute-start | bytes 101384 | tf_op jit(solution)/shard_map/ppermute | solution.py:22
  14.3 0.8 %collective-permute-done.1 = f32[2,33,128]{2,1,0:T(8,128)S(1)} collective-permute-done((f32[2,33,128]{2,1,0:T(8,128)S(1)}, f32[2,33,128]{2,1,0:T(8,128)S(1)}, u32[]{:S(2)}, u32[]{:S(2)}) %collective-permute-start.1) | collective-permute-done | bytes 33824 | tf_op jit(solution)/shard_map/ppermute | solution.py:22
  15.2 1.1 %collective-permute-done.2 = f32[2,33,128]{2,1,0:T(8,128)S(1)} collective-permute-done((f32[2,33,128]{2,1,0:T(8,128)S(1)}, f32[2,33,128]{2,1,0:T(8,128)S(1)}, u32[]{:S(2)}, u32[]{:S(2)}) %collective-permute-start.2) | collective-permute-done | bytes 33824 | tf_op jit(solution)/shard_map/ppermute | solution.py:22
  16.2 0.2 collective-permute-done.3
  16.5 1.9 %collective-permute-start.4 = (f32[2,33,128]{2,1,0:T(8,128)S(1)}, f32[2,33,128]{2,1,0:T(8,128)S(1)}, u32[]{:S(2)}, u32[]{:S(2)}) collective-permute-start(f32[2,33,128]{2,1,0:T(8,128)S(1)} %add_add_fusion), channel_id=1, source_target_pairs={{0,2},{2,0},{1,3},{3,1},{4,6},{6,4},{5,7},{7,5},{8,10},{10,8},{9,1... | collective-permute-start | bytes 101384 | tf_op jit(solution)/shard_map/ppermute | solution.py:22
  18.3 0.9 %collective-permute-done.4 = f32[2,33,128]{2,1,0:T(8,128)S(1)} collective-permute-done((f32[2,33,128]{2,1,0:T(8,128)S(1)}, f32[2,33,128]{2,1,0:T(8,128)S(1)}, u32[]{:S(2)}, u32[]{:S(2)}) %collective-permute-start.4) | collective-permute-done | bytes 33824 | tf_op jit(solution)/shard_map/ppermute | solution.py:22
  19.2 5.6 %collective-permute-start.5 = (f32[4,33,128]{2,1,0:T(8,128)S(1)}, f32[4,33,128]{2,1,0:T(8,128)S(1)}, u32[]{:S(2)}, u32[]{:S(2)}) collective-permute-start(f32[4,33,128]{2,1,0:T(8,128)S(1)} %pad_maximum_fusion.1), channel_id=1, source_target_pairs={{0,32},{32,64},{64,96},{96,128},{128,160},{160,192},{192,224},{224... | collective-permute-start | bytes 202760 | tf_op jit(solution)/shard_map/ppermute | solution.py:22
  24.8 1.5 %collective-permute-done.5 = f32[4,33,128]{2,1,0:T(8,128)S(1)} collective-permute-done((f32[4,33,128]{2,1,0:T(8,128)S(1)}, f32[4,33,128]{2,1,0:T(8,128)S(1)}, u32[]{:S(2)}, u32[]{:S(2)}) %collective-permute-start.5) | collective-permute-done | bytes 67616 | tf_op jit(solution)/shard_map/ppermute | solution.py:22
  26.3 3.0 %collective-permute-start.6 = (f32[4,33,128]{2,1,0:T(8,128)S(1)}, f32[4,33,128]{2,1,0:T(8,128)S(1)}, u32[]{:S(2)}, u32[]{:S(2)}) collective-permute-start(f32[4,33,128]{2,1,0:T(8,128)S(1)} %collective-permute-done.5), channel_id=1, source_target_pairs={{0,32},{32,64},{64,96},{96,128},{128,160},{160,192},{192,224},{224... | collective-permute-start | bytes 202760 | tf_op jit(solution)/shard_map/ppermute | solution.py:22
  29.4 1.5 %collective-permute-done.6 = f32[4,33,128]{2,1,0:T(8,128)S(1)} collective-permute-done((f32[4,33,128]{2,1,0:T(8,128)S(1)}, f32[4,33,128]{2,1,0:T(8,128)S(1)}, u32[]{:S(2)}, u32[]{:S(2)}) %collective-permute-start.6) | collective-permute-done | bytes 67616 | tf_op jit(solution)/shard_map/ppermute | solution.py:22
  30.8 3.0 %collective-permute-start.7 = (f32[4,33,128]{2,1,0:T(8,128)S(1)}, f32[4,33,128]{2,1,0:T(8,128)}, u32[]{:S(2)}, u32[]{:S(2)}) collective-permute-start(f32[4,33,128]{2,1,0:T(8,128)S(1)} %collective-permute-done.6), channel_id=1, source_target_pairs={{0,32},{32,64},{64,96},{96,128},{128,160},{160,192},{192,224},{224... | collective-permute-start | bytes 202760 | tf_op jit(solution)/shard_map/ppermute | solution.py:22
  33.9 2.9 %select_reduce_fusion = (f32[16,256]{1,0:T(8,128)}, bf16[16,256,256]{1,2,0:T(8,128)(2,1)S(1)}) fusion(pred[256,256]{0,1:T(8,128)(4,1)S(1)} %iota_compare_fusion, bf16[1,256,3,16,64]{1,4,3,2,0:T(8,128)(2,1)} %bitcast.76), kind=kOutput, calls=%fused_computation.1 | convolution fusion | flops 140505088 | bytes 3227648 | tf_op jit(solution)/shard_map/rnihd,rnjhd->rnhij/dot_general | solution.py:117
  36.8 0.0 collective-permute-done.7
  36.8 1.7 %collective-permute-start.8 = (f32[4,33,128]{2,1,0:T(8,128)}, f32[4,33,128]{2,1,0:T(8,128)}, u32[]{:S(2)}, u32[]{:S(2)}) collective-permute-start(f32[4,33,128]{2,1,0:T(8,128)} %collective-permute-done.7), channel_id=1, source_target_pairs={{0,32},{32,64},{64,96},{96,128},{128,160},{160,192},{192,224},{224... | collective-permute-start | bytes 202760 | tf_op jit(solution)/shard_map/ppermute | solution.py:22
  38.5 2.5 %fusion.3 = f32[1,1,256,16,64]{2,4,3,1,0:T(8,128)} fusion(bf16[16,256,256]{1,2,0:T(8,128)(2,1)S(1)} %get-tuple-element.22, pred[256,256]{0,1:T(8,128)(4,1)S(1)} %iota_compare_fusion, bf16[1,256,3,16,64]{1,4,3,2,0:T(8,128)(2,1)} %bitcast.77), kind=kOutput, calls=%fused_computation.13 | convolution fusion | flops 135266304 | bytes 3735552 | tf_op jit(solution)/shard_map/rnhij,rnjhd->rnihd/dot_general | solution.py:122
  40.9 0.0 collective-permute-done.8
  41.0 4.4 %collective-permute-start.9 = (f32[2,33,128]{2,1,0:T(8,128)S(1)}, f32[2,33,128]{2,1,0:T(8,128)S(1)}, u32[]{:S(2)}, u32[]{:S(2)}) collective-permute-start(f32[2,33,128]{2,1,0:T(8,128)S(1)} %constant_dynamic-slice_fusion), channel_id=1, source_target_pairs={{0,2},{2,0},{1,3},{3,1},{4,6},{6,4},{5,7},{7,5},{8,10},{10,8},{9,1... | collective-permute-start | bytes 101384 | tf_op jit(solution)/shard_map/ppermute | solution.py:22
  45.4 0.5 fusion.24
  45.9 0.4 collective-permute-done.9
  46.3 0.3 collective-permute-start.10
  46.6 0.7 add_bitcast_fusion
  47.3 3.4 %collective-permute-start.11 = (f32[2,33,128]{2,1,0:T(8,128)S(1)}, f32[2,33,128]{2,1,0:T(8,128)S(1)}, u32[]{:S(2)}, u32[]{:S(2)}) collective-permute-start(f32[2,33,128]{2,1,0:T(8,128)S(1)} %get-tuple-element.15), channel_id=1, source_target_pairs={{0,16},{8,24},{16,0},{24,8},{1,17},{9,25},{17,1},{25,9},{2,18},{10... | collective-permute-start | bytes 101384 | tf_op jit(solution)/shard_map/ppermute | solution.py:22
  50.7 1.2 %pad_clamp_fusion = s32[1024]{0:T(1024)} fusion(s32[4]{0:T(128)} %fusion.24), kind=kLoop, calls=%fused_computation.65 | loop fusion | flops 1024 | bytes 4112 | tf_op jit(solution)/shard_map/gather | solution.py:101
  51.9 0.0 collective-permute-done.10
  51.9 0.5 collective-permute-done.11
  52.4 1.2 %collective-permute-done.12 = f32[2,33,128]{2,1,0:T(8,128)S(1)} collective-permute-done((f32[2,33,128]{2,1,0:T(8,128)S(1)}, f32[2,33,128]{2,1,0:T(8,128)S(1)}, u32[]{:S(2)}, u32[]{:S(2)}) %collective-permute-start.12) | collective-permute-done | bytes 33824 | tf_op jit(solution)/shard_map/ppermute | solution.py:22
  53.6 0.8 %pad_maximum_fusion = f32[4,2,33,128]{3,2,1,0:T(8,128)S(1)} fusion(f32[1,2,33,128]{3,2,1,0:T(8,128)S(1)} %bitcast.85, f32[1,2,33,128]{3,2,1,0:T(8,128)S(1)} %bitcast.84, f32[1,2,33,128]{3,2,1,0:T(8,128)} %bitcast.83, f32[1,2,33,128]{3,2,1,0:T(8,128)} %get-tuple-element.13), kind=kLoop, calls=%fused_computation.44 | loop fusion | flops 101376 | bytes 270336 | tf_op jit(solution)/shard_map/stack | solution.py:101
  54.4 0.7 gather_fusion
  55.1 2.8 %collective-permute-start.13 = (f32[8,33,128]{2,1,0:T(8,128)S(1)}, f32[8,33,128]{2,1,0:T(8,128)S(1)}, u32[]{:S(2)}, u32[]{:S(2)}) collective-permute-start(f32[8,33,128]{2,1,0:T(8,128)S(1)} %bitcast_add_fusion.1), channel_id=1, source_target_pairs={{0,4},{4,0},{1,5},{5,1},{2,6},{6,2},{3,7},{7,3},{8,12},{12,8},{9,1... | collective-permute-start | bytes 405512 | tf_op jit(solution)/shard_map/ppermute | solution.py:22
  57.9 2.9 %collective-permute-done.13 = f32[8,33,128]{2,1,0:T(8,128)S(1)} collective-permute-done((f32[8,33,128]{2,1,0:T(8,128)S(1)}, f32[8,33,128]{2,1,0:T(8,128)S(1)}, u32[]{:S(2)}, u32[]{:S(2)}) %collective-permute-start.13) | collective-permute-done | bytes 135200 | tf_op jit(solution)/shard_map/ppermute | solution.py:22
  60.9 3.3 %collective-permute-start.14 = (f32[8,33,128]{2,1,0:T(8,128)S(1)}, f32[8,33,128]{2,1,0:T(8,128)S(1)}, u32[]{:S(2)}, u32[]{:S(2)}) collective-permute-start(f32[8,33,128]{2,1,0:T(8,128)S(1)} %select_add_fusion), channel_id=1, source_target_pairs={{0,2},{2,0},{1,3},{3,1},{4,6},{6,4},{5,7},{7,5},{8,10},{10,8},{9,1... | collective-permute-start | bytes 405512 | tf_op jit(solution)/shard_map/ppermute | solution.py:22
  64.2 1.0 %collective-permute-done.14 = f32[8,33,128]{2,1,0:T(8,128)S(1)} collective-permute-done((f32[8,33,128]{2,1,0:T(8,128)S(1)}, f32[8,33,128]{2,1,0:T(8,128)S(1)}, u32[]{:S(2)}, u32[]{:S(2)}) %collective-permute-start.14) | collective-permute-done | bytes 135200 | tf_op jit(solution)/shard_map/ppermute | solution.py:22
  65.2 0.1 add_select_fusion
  65.3 0.7 %fusion.19 = f32[16,32,128]{2,1,0:T(8,128)} fusion(f32[8,33,128]{2,1,0:T(8,128)S(1)} %get-tuple-element.12, f32[8,33,128]{2,1,0:T(8,128)S(1)} %get-tuple-element.11), kind=kLoop, calls=%fused_computation.40 | loop fusion | flops 65536 | bytes 532480 | tf_op jit(solution)/shard_map/concatenate | solution.py:52
  66.0 1.6 %fusion.28 = f32[16,1,256]{2,1,0:T(1,128)S(1)} fusion(f32[16,64,1]{1,2,0:T(1,128)S(1)} %bitcast.88, bf16[1,256,3,16,64]{1,4,3,2,0:T(8,128)(2,1)} %bitcast.78), kind=kOutput, calls=%fused_computation.77 | convolution fusion | flops 4718592 | bytes 544768 | tf_op jit(solution)/shard_map/rnihd,rnhd->rnih/dot_general | solution.py:136
  67.6 0.2 broadcast_in_dim_broadcast_in_dim_reshape.3
  67.8 1.9 %convolution_bitcast_fusion = f32[1,1,256,16,64]{2,4,3,1,0:T(8,128)S(1)} fusion(f32[16,64,64]{2,1,0:T(8,128)S(1)} %broadcast_in_dim_broadcast_in_dim_reshape.3, f32[16,64,64]{2,1,0:T(8,128)S(1)} %fusion.14, bf16[1,256,3,16,64]{1,4,3,2,0:T(8,128)(2,1)} %bitcast.79), kind=kOutput, calls=%fused_computation.14 | convolution fusion | flops 203030528 | bytes 2097152 | tf_op jit(solution)/shard_map/rnihd,rnhde->rnihe/dot_general | solution.py:133
  69.8 0.2 divide_convert_fusion
  70.0 1.5 %fusion.4 = bf16[1,256,1024]{2,1,0:T(8,128)(2,1)} fusion(bf16[256,1024]{0,1:T(8,128)(2,1)S(1)} %bitcast.73, bf16[1024,1024]{1,0:T(8,128)(2,1)S(1)} %copy-done), kind=kOutput, calls=%fused_computation.16 | convolution fusion | flops 537133056 | bytes 3145728 | tf_op jit(solution)/shard_map/rtd,de->rte/dot_general | solution.py:172
  (31 shorter events, 0.3 us)
Async XLA Ops:
  0.0 70.0 %copy-start = (bf16[1024,1024]{1,0:T(8,128)(2,1)S(1)}, bf16[1024,1024]{1,0:T(8,128)(2,1)}, u32[]{:S(2)}) copy-start(bf16[1024,1024]{1,0:T(8,128)(2,1)} %param.5) | copy-start | bytes 6291460
  4.9 1.2 %copy-start.3 = (bf16[3072,256]{1,0:T(8,128)(2,1)}, bf16[3072,256]{1,0:T(8,128)(2,1)S(1)}, u32[]{:S(2)}) copy-start(bf16[3072,256]{1,0:T(8,128)(2,1)S(1)} %convolution_convert_fusion) | copy-start | bytes 4718596
  6.6 4.3 %collective-permute-start = (f32[8,33,128]{2,1,0:T(8,128)S(1)}, f32[8,33,128]{2,1,0:T(8,128)S(1)}, u32[]{:S(2)}, u32[]{:S(2)}) collective-permute-start(f32[8,33,128]{2,1,0:T(8,128)S(1)} %fusion.20), channel_id=1, source_target_pairs={{0,2},{2,0},{1,3},{3,1},{4,6},{6,4},{5,7},{7,5},{8,10},{10,8},{9,1... | collective-permute-start | bytes 405512 | tf_op jit(solution)/shard_map/ppermute | solution.py:22
  11.0 4.2 %collective-permute-start.1 = (f32[2,33,128]{2,1,0:T(8,128)S(1)}, f32[2,33,128]{2,1,0:T(8,128)S(1)}, u32[]{:S(2)}, u32[]{:S(2)}) collective-permute-start(f32[2,33,128]{2,1,0:T(8,128)S(1)} %get-tuple-element.16), channel_id=1, source_target_pairs={{0,8},{8,16},{16,24},{24,0},{1,9},{9,17},{17,25},{25,1},{2,10},{10... | collective-permute-start | bytes 101384 | tf_op jit(solution)/shard_map/ppermute | solution.py:22
  11.1 5.2 %collective-permute-start.2 = (f32[2,33,128]{2,1,0:T(8,128)S(1)}, f32[2,33,128]{2,1,0:T(8,128)S(1)}, u32[]{:S(2)}, u32[]{:S(2)}) collective-permute-start(f32[2,33,128]{2,1,0:T(8,128)S(1)} %get-tuple-element.18), channel_id=1, source_target_pairs={{0,16},{8,24},{16,0},{24,8},{1,17},{9,25},{17,1},{25,9},{2,18},{10... | collective-permute-start | bytes 101384 | tf_op jit(solution)/shard_map/ppermute | solution.py:22
  13.3 3.2 %collective-permute-start.3 = (f32[2,33,128]{2,1,0:T(8,128)S(1)}, f32[2,33,128]{2,1,0:T(8,128)S(1)}, u32[]{:S(2)}, u32[]{:S(2)}) collective-permute-start(f32[2,33,128]{2,1,0:T(8,128)S(1)} %get-tuple-element.17), channel_id=1, source_target_pairs={{0,24},{8,0},{16,8},{24,16},{1,25},{9,1},{17,9},{25,17},{2,26},{10... | collective-permute-start | bytes 101384 | tf_op jit(solution)/shard_map/ppermute | solution.py:22
  16.5 2.7 %collective-permute-start.4 = (f32[2,33,128]{2,1,0:T(8,128)S(1)}, f32[2,33,128]{2,1,0:T(8,128)S(1)}, u32[]{:S(2)}, u32[]{:S(2)}) collective-permute-start(f32[2,33,128]{2,1,0:T(8,128)S(1)} %add_add_fusion), channel_id=1, source_target_pairs={{0,2},{2,0},{1,3},{3,1},{4,6},{6,4},{5,7},{7,5},{8,10},{10,8},{9,1... | collective-permute-start | bytes 101384 | tf_op jit(solution)/shard_map/ppermute | solution.py:22
  19.2 7.1 %collective-permute-start.5 = (f32[4,33,128]{2,1,0:T(8,128)S(1)}, f32[4,33,128]{2,1,0:T(8,128)S(1)}, u32[]{:S(2)}, u32[]{:S(2)}) collective-permute-start(f32[4,33,128]{2,1,0:T(8,128)S(1)} %pad_maximum_fusion.1), channel_id=1, source_target_pairs={{0,32},{32,64},{64,96},{96,128},{128,160},{160,192},{192,224},{224... | collective-permute-start | bytes 202760 | tf_op jit(solution)/shard_map/ppermute | solution.py:22
  26.3 4.5 %collective-permute-start.6 = (f32[4,33,128]{2,1,0:T(8,128)S(1)}, f32[4,33,128]{2,1,0:T(8,128)S(1)}, u32[]{:S(2)}, u32[]{:S(2)}) collective-permute-start(f32[4,33,128]{2,1,0:T(8,128)S(1)} %collective-permute-done.5), channel_id=1, source_target_pairs={{0,32},{32,64},{64,96},{96,128},{128,160},{160,192},{192,224},{224... | collective-permute-start | bytes 202760 | tf_op jit(solution)/shard_map/ppermute | solution.py:22
  30.8 10.1 %copy-start.4 = (f32[4,33,128]{2,1,0:T(8,128)}, f32[4,33,128]{2,1,0:T(8,128)S(1)}, u32[]{:S(2)}) copy-start(f32[4,33,128]{2,1,0:T(8,128)S(1)} %collective-permute-done.6) | copy-start | bytes 202756
  30.8 5.9 %collective-permute-start.7 = (f32[4,33,128]{2,1,0:T(8,128)S(1)}, f32[4,33,128]{2,1,0:T(8,128)}, u32[]{:S(2)}, u32[]{:S(2)}) collective-permute-start(f32[4,33,128]{2,1,0:T(8,128)S(1)} %collective-permute-done.6), channel_id=1, source_target_pairs={{0,32},{32,64},{64,96},{96,128},{128,160},{160,192},{192,224},{224... | collective-permute-start | bytes 202760 | tf_op jit(solution)/shard_map/ppermute | solution.py:22
  36.8 4.2 %collective-permute-start.8 = (f32[4,33,128]{2,1,0:T(8,128)}, f32[4,33,128]{2,1,0:T(8,128)}, u32[]{:S(2)}, u32[]{:S(2)}) collective-permute-start(f32[4,33,128]{2,1,0:T(8,128)} %collective-permute-done.7), channel_id=1, source_target_pairs={{0,32},{32,64},{64,96},{96,128},{128,160},{160,192},{192,224},{224... | collective-permute-start | bytes 202760 | tf_op jit(solution)/shard_map/ppermute | solution.py:22
  41.0 5.3 %collective-permute-start.9 = (f32[2,33,128]{2,1,0:T(8,128)S(1)}, f32[2,33,128]{2,1,0:T(8,128)S(1)}, u32[]{:S(2)}, u32[]{:S(2)}) collective-permute-start(f32[2,33,128]{2,1,0:T(8,128)S(1)} %constant_dynamic-slice_fusion), channel_id=1, source_target_pairs={{0,2},{2,0},{1,3},{3,1},{4,6},{6,4},{5,7},{7,5},{8,10},{10,8},{9,1... | collective-permute-start | bytes 101384 | tf_op jit(solution)/shard_map/ppermute | solution.py:22
  46.3 5.6 %collective-permute-start.10 = (f32[2,33,128]{2,1,0:T(8,128)S(1)}, f32[2,33,128]{2,1,0:T(8,128)S(1)}, u32[]{:S(2)}, u32[]{:S(2)}) collective-permute-start(f32[2,33,128]{2,1,0:T(8,128)S(1)} %select_add_fusion.5), channel_id=1, source_target_pairs={{0,8},{8,16},{16,24},{24,0},{1,9},{9,17},{17,25},{25,1},{2,10},{10... | collective-permute-start | bytes 101384 | tf_op jit(solution)/shard_map/ppermute | solution.py:22
  47.3 5.1 %collective-permute-start.11 = (f32[2,33,128]{2,1,0:T(8,128)S(1)}, f32[2,33,128]{2,1,0:T(8,128)S(1)}, u32[]{:S(2)}, u32[]{:S(2)}) collective-permute-start(f32[2,33,128]{2,1,0:T(8,128)S(1)} %get-tuple-element.15), channel_id=1, source_target_pairs={{0,16},{8,24},{16,0},{24,8},{1,17},{9,25},{17,1},{25,9},{2,18},{10... | collective-permute-start | bytes 101384 | tf_op jit(solution)/shard_map/ppermute | solution.py:22
  50.7 2.9 %collective-permute-start.12 = (f32[2,33,128]{2,1,0:T(8,128)S(1)}, f32[2,33,128]{2,1,0:T(8,128)S(1)}, u32[]{:S(2)}, u32[]{:S(2)}) collective-permute-start(f32[2,33,128]{2,1,0:T(8,128)S(1)} %get-tuple-element.14), channel_id=1, source_target_pairs={{0,24},{8,0},{16,8},{24,16},{1,25},{9,1},{17,9},{25,17},{2,26},{10... | collective-permute-start | bytes 101384 | tf_op jit(solution)/shard_map/ppermute | solution.py:22
  51.9 1.7 %copy-start.5 = (f32[2,33,128]{2,1,0:T(8,128)}, f32[2,33,128]{2,1,0:T(8,128)S(1)}, u32[]{:S(2)}) copy-start(f32[2,33,128]{2,1,0:T(8,128)S(1)} %collective-permute-done.10) | copy-start | bytes 101380
  55.1 5.8 %collective-permute-start.13 = (f32[8,33,128]{2,1,0:T(8,128)S(1)}, f32[8,33,128]{2,1,0:T(8,128)S(1)}, u32[]{:S(2)}, u32[]{:S(2)}) collective-permute-start(f32[8,33,128]{2,1,0:T(8,128)S(1)} %bitcast_add_fusion.1), channel_id=1, source_target_pairs={{0,4},{4,0},{1,5},{5,1},{2,6},{6,2},{3,7},{7,3},{8,12},{12,8},{9,1... | collective-permute-start | bytes 405512 | tf_op jit(solution)/shard_map/ppermute | solution.py:22
  60.9 4.3 %collective-permute-start.14 = (f32[8,33,128]{2,1,0:T(8,128)S(1)}, f32[8,33,128]{2,1,0:T(8,128)S(1)}, u32[]{:S(2)}, u32[]{:S(2)}) collective-permute-start(f32[8,33,128]{2,1,0:T(8,128)S(1)} %select_add_fusion), channel_id=1, source_target_pairs={{0,2},{2,0},{1,3},{3,1},{4,6},{6,4},{5,7},{7,5},{8,10},{10,8},{9,1... | collective-permute-start | bytes 405512 | tf_op jit(solution)/shard_map/ppermute | solution.py:22
  66.0 1.6 %copy-start.1 = (f32[16,32,128]{2,1,0:T(8,128)S(1)}, f32[16,32,128]{2,1,0:T(8,128)}, u32[]{:S(2)}) copy-start(f32[16,32,128]{2,1,0:T(8,128)} %fusion.19) | copy-start | bytes 786436
  67.6 2.1 %copy-start.6 = (f32[16,256]{1,0:T(8,128)S(1)}, f32[16,256]{1,0:T(8,128)}, u32[]{:S(2)}) copy-start(f32[16,256]{1,0:T(8,128)} %get-tuple-element.21) | copy-start | bytes 49156
  67.8 2.0 %copy-start.2 = (f32[1,1,256,16,64]{2,4,3,1,0:T(8,128)S(1)}, f32[1,1,256,16,64]{2,4,3,1,0:T(8,128)}, u32[]{:S(2)}) copy-start(f32[1,1,256,16,64]{2,4,3,1,0:T(8,128)} %fusion.3) | copy-start | bytes 3145732

commit v10 on v8

--- a/solution.py
+++ b/solution.py
@@ -146,11 +146,16 @@
 def shards(frames_in, w_qkv, w_out):
     rows, tok_local, width = frames_in.shape
     head_dim = width // HEADS
-    qkv = jnp.einsum("rtd,de->ret", frames_in, w_qkv, preferred_element_type=jnp.float32).astype(
-        jnp.bfloat16
-    )
-    parts = jnp.transpose(qkv.reshape(rows, 3, HEADS, head_dim, tok_local), (0, 4, 1, 2, 3))
-    phi_q, phi_k, values = split_qkv(parts)
+    def project(w, count):
+        out = jnp.einsum("rtd,de->ret", frames_in, w, preferred_element_type=jnp.float32)
+        out = out.astype(jnp.bfloat16).reshape(rows, count, HEADS, head_dim, tok_local)
+        return jnp.transpose(out, (0, 4, 1, 2, 3))
+
+    keys_values = project(w_qkv[:, width:], 2)
+    queries = project(w_qkv[:, :width], 1)
+    phi_q = features(queries[:, :, 0].astype(jnp.float32)).astype(jnp.bfloat16)
+    phi_k = features(keys_values[:, :, 0].astype(jnp.float32)).astype(jnp.bfloat16)
+    values = keys_values[:, :, 1]
     pq, num_local, den_local, kv_blocks, k_blocks = block_terms(phi_q, phi_k, values, SPAN)
     total_kv = jnp.sum(kv_blocks, axis=1)[0]
     total_k = jnp.sum(k_blocks, axis=1)[0]

time: 68.7 us -> 67.7 us (0.985)
  waiting for transfers between devices: 14.7 us -> 12.2 us
  local copies, waits for them, and re-layouts: 1.79 us -> 3.93 us
  matrix products: 15.7 us -> 14.3 us
    ppermute x16, waiting for transfers between devices: 14.7 us -> 12.2 us  [send(): return tmap(lambda t: lax.ppermute(t, axis, perm=pairs), tree)]
    add x6, other arithmetic: 0.15 us -> 1.63 us  [tmap(): return jax.tree.map(f, *trees)]
    dot_general x1 -> x2, matrix products: 4.9 us -> 6.24 us  [project(): jnp.einsum('rtd,de->ret', frames_in, w, preferred_element_type=jnp.float32)]
    dot_general x1, matrix products: 1.6 us -> 0.32 us  [finish(): jnp.einsum('rnihd,rnhd->rnih', pq32, before_k, precision=lax.Precision.HI...]
    dot_general x1, matrix products: 2.49 us -> 1.45 us  [block_terms(): jnp.einsum('rnhij,rnjhd->rnihd', weights, vv, preferred_element_type=jnp....]
    another operation x1, local copies, waits for them, and re-layouts: 0.15 us -> 1.1 us  [finish(): before_kv = jnp.cumsum(kv_blocks, axis=1) - kv_blocks + prior_kv[:, None]]
    another operation x2, other arithmetic: 1.47 us -> 0.69 us  [entering(): jnp.stack(p)[order].reshape((-1,) + p[0].shape[1:])]
    dynamic_slice x1, local copies, waits for them, and re-layouts: 0.02 us -> 0.73 us  [one(): return lax.dynamic_slice_in_dim(t, index * size, size, axis=0)]
  transfers between devices with their start and end apart: 16 -> 16, of which waited for: 11 -> 8; matrix products, arithmetic and copies ran while one was open for 10% -> 12% of each run, Pallas kernels for 0% -> 0%
where the time goes in v10:
time: 67.7 us; the launch traced here: 67.4 us
  starting transfers between devices  32.3 us (48%)
  matrix products  14.3 us (21%)
  waiting for transfers between devices  12.2 us (18%)
  other arithmetic  4.31 us (6%)
  local copies, waits for them, and re-layouts  3.93 us (6%)
    ppermute x16, starting transfers between devices, send(): return tmap(lambda t: lax.ppermute(t, axis, perm=pairs), tree)  32.3 us
    ppermute x16, waiting for transfers between devices, send(): return tmap(lambda t: lax.ppermute(t, axis, perm=pairs), tree)  12.2 us
    dot_general x2, matrix products, project(): jnp.einsum('rtd,de->ret', frames_in, w, preferred_element_type=jnp.float32)  6.24 us
    dot_general x1, matrix products, block_terms(): jnp.einsum('rnihd,rnjhd->rnhij', pq, pk, preferred_element_type=jnp.float32)  2.67 us
    dot_general x1, matrix products, finish(): jnp.einsum('rnihd,rnhde->rnihe', pq32, before_kv, precision=lax.Precision...  1.76 us
    add x6, other arithmetic, tmap(): return jax.tree.map(f, *trees)  1.63 us
    dot_general x1, matrix products, shards(): jnp.einsum('rtd,de->rte', heads_out, w_out, preferred_element_type=jnp.fl...  1.52 us
    dot_general x1, matrix products, block_terms(): jnp.einsum('rnhij,rnjhd->rnihd', weights, vv, preferred_element_type=jnp....  1.45 us
  transfers between devices with their start and end apart: 16, of which 8 were waited for; matrix products, arithmetic and copies ran while one was open for 12% of the time, Pallas kernels for 0%

profile of v10, /device:TPU:1, one launch (start us, length us, event | category | flops | bytes accessed | tf_op | source)
XLA Modules:
  0.0 67.4 jit_solution(13984296701649083986)
XLA Ops:
  0.0 3.8 %fusion.2 = bf16[2048,256]{1,0:T(8,128)(2,1)S(1)} fusion(bf16[1024,3072]{1,0:T(8,128)(2,1)} %param.4, bf16[1,256,1024]{2,1,0:T(8,128)(2,1)} %param.3), kind=kOutput, calls=%fused_computation.5 | convolution fusion | flops 1074266112 | bytes 5767168 | tf_op jit(solution)/shard_map/rtd,de->ret/dot_general | solution.py:150
  3.8 0.4 fusion.25
  4.2 0.6 copy-done.8
  4.8 0.3 convert_reduce_fusion
  5.1 0.1 reshape_squeeze.4
  5.3 3.3 %collective-permute-start = (f32[8,33,128]{2,1,0:T(8,128)S(1)}, f32[8,33,128]{2,1,0:T(8,128)S(1)}, u32[]{:S(2)}, u32[]{:S(2)}) collective-permute-start(f32[8,33,128]{2,1,0:T(8,128)S(1)} %fusion.32), channel_id=1, source_target_pairs={{0,2},{2,0},{1,3},{3,1},{4,6},{6,4},{5,7},{7,5},{8,10},{10,8},{9,1... | collective-permute-start | bytes 405512 | tf_op jit(solution)/shard_map/ppermute | solution.py:22
  8.6 1.0 %collective-permute-done = f32[8,33,128]{2,1,0:T(8,128)S(1)} collective-permute-done((f32[8,33,128]{2,1,0:T(8,128)S(1)}, f32[8,33,128]{2,1,0:T(8,128)S(1)}, u32[]{:S(2)}, u32[]{:S(2)}) %collective-permute-start) | collective-permute-done | bytes 135200 | tf_op jit(solution)/shard_map/ppermute | solution.py:22
  9.7 0.7 %constant_dynamic-slice_fusion.2 = (f32[2,33,128]{2,1,0:T(8,128)}, f32[2,33,128]{2,1,0:T(8,128)}, f32[2,33,128]{2,1,0:T(8,128)}) fusion(f32[8,33,128]{2,1,0:T(8,128)S(1)} %select_add_fusion.1, s32[]{:T(128)S(6)} %select_n.323, s32[]{:T(128)S(6)} %select_n.327, s32[]{:T(128)S(6)} %select_n.325), kind=kLoop, calls=%fused_computation.72 | loop fusion | bytes 202764 | tf_op jit(solution)/shard_map/dynamic_slice | solution.py:36
  10.4 0.0 collective-permute-start.1
  10.4 2.2 %collective-permute-start.2 = (f32[2,33,128]{2,1,0:T(8,128)}, f32[2,33,128]{2,1,0:T(8,128)S(1)}, u32[]{:S(2)}, u32[]{:S(2)}) collective-permute-start(f32[2,33,128]{2,1,0:T(8,128)} %get-tuple-element.18), channel_id=1, source_target_pairs={{0,16},{8,24},{16,0},{24,8},{1,17},{9,25},{17,1},{25,9},{2,18},{10... | collective-permute-start | bytes 101384 | tf_op jit(solution)/shard_map/ppermute | solution.py:22
  12.6 1.1 %collective-permute-start.3 = (f32[2,33,128]{2,1,0:T(8,128)}, f32[2,33,128]{2,1,0:T(8,128)S(1)}, u32[]{:S(2)}, u32[]{:S(2)}) collective-permute-start(f32[2,33,128]{2,1,0:T(8,128)} %get-tuple-element.17), channel_id=1, source_target_pairs={{0,24},{8,0},{16,8},{24,16},{1,25},{9,1},{17,9},{25,17},{2,26},{10... | collective-permute-start | bytes 101384 | tf_op jit(solution)/shard_map/ppermute | solution.py:22
  13.7 2.5 %fusion.19 = bf16[1024,256]{1,0:T(8,128)(2,1)S(1)} fusion(bf16[1024,3072]{1,0:T(8,128)(2,1)} %param.4, bf16[1,256,1024]{2,1,0:T(8,128)(2,1)} %param.3), kind=kOutput, calls=%fused_computation.26 | convolution fusion | flops 538705920 | bytes 3145728 | tf_op jit(solution)/shard_map/rtd,de->ret/dot_general | solution.py:150
  16.2 0.0 copy-start.1
  16.2 0.0 collective-permute-done.1
  16.2 0.0 collective-permute-done.2
  16.2 0.9 %add_add_fusion = f32[2,33,128]{2,1,0:T(8,128)S(1)} fusion(f32[2,33,128]{2,1,0:T(8,128)S(1)} %collective-permute-done.3, f32[2,33,128]{2,1,0:T(8,128)S(1)} %collective-permute-done.2, f32[2,33,128]{2,1,0:T(8,128)S(1)} %collective-permute-done.1, f32[8,33,128]{2,1,0:T(8,128)} %copy-done.3, s32[]{:T(128)S(6)} %select_n.321), kind=kLoop, calls=%fused_computation.61 | loop fusion | flops 25344 | bytes 168964 | tf_op jit(solution)/shard_map/add | solution.py:18
  17.1 1.7 %collective-permute-start.4 = (f32[2,33,128]{2,1,0:T(8,128)S(1)}, f32[2,33,128]{2,1,0:T(8,128)S(1)}, u32[]{:S(2)}, u32[]{:S(2)}) collective-permute-start(f32[2,33,128]{2,1,0:T(8,128)S(1)} %add_add_fusion), channel_id=1, source_target_pairs={{0,32},{32,64},{64,96},{96,128},{128,160},{160,192},{192,224},{224... | collective-permute-start | bytes 101384 | tf_op jit(solution)/shard_map/ppermute | solution.py:22
  18.8 4.0 %collective-permute-start.5 = (f32[2,33,128]{2,1,0:T(8,128)S(1)}, f32[2,33,128]{2,1,0:T(8,128)S(1)}, u32[]{:S(2)}, u32[]{:S(2)}) collective-permute-start(f32[2,33,128]{2,1,0:T(8,128)S(1)} %add_add_fusion), channel_id=1, source_target_pairs={{0,224},{32,0},{64,32},{96,64},{128,96},{160,128},{192,160},{224,1... | collective-permute-start | bytes 101384 | tf_op jit(solution)/shard_map/ppermute | solution.py:22
  22.8 1.3 %collective-permute-done.4 = f32[2,33,128]{2,1,0:T(8,128)S(1)} collective-permute-done((f32[2,33,128]{2,1,0:T(8,128)S(1)}, f32[2,33,128]{2,1,0:T(8,128)S(1)}, u32[]{:S(2)}, u32[]{:S(2)}) %collective-permute-start.4) | collective-permute-done | bytes 33824 | tf_op jit(solution)/shard_map/ppermute | solution.py:22
  24.1 0.0 collective-permute-start.6
  24.1 2.7 %select_reduce_fusion = (f32[16,256]{1,0:T(8,128)}, bf16[16,256,256]{1,2,0:T(8,128)(2,1)S(1)}) fusion(pred[256,256]{0,1:T(8,128)(4,1)S(1)} %iota_compare_fusion, bf16[256,16,64]{0,2,1:T(8,128)(2,1)S(1)} %bitcast.75, bf16[1,256,2,16,64]{1,4,3,2,0:T(8,128)(2,1)} %bitcast.81), kind=kOutput, calls=%fused_computation.3 | convolution fusion | flops 138932224 | bytes 3227648 | tf_op jit(solution)/shard_map/rnihd,rnjhd->rnhij/dot_general | solution.py:114
  26.8 2.8 %collective-permute-start.7 = (f32[2,33,128]{2,1,0:T(8,128)S(1)}, f32[2,33,128]{2,1,0:T(8,128)S(1)}, u32[]{:S(2)}, u32[]{:S(2)}) collective-permute-start(f32[2,33,128]{2,1,0:T(8,128)S(1)} %collective-permute-done.5), channel_id=1, source_target_pairs={{0,224},{32,0},{64,32},{96,64},{128,96},{160,128},{192,160},{224,1... | collective-permute-start | bytes 101384 | tf_op jit(solution)/shard_map/ppermute | solution.py:22
  29.6 1.5 %fusion.10 = f32[1,1,256,16,64]{2,4,3,1,0:T(8,128)} fusion(bf16[16,256,256]{1,2,0:T(8,128)(2,1)S(1)} %get-tuple-element.20, pred[256,256]{0,1:T(8,128)(4,1)S(1)} %iota_compare_fusion, bf16[1,256,2,16,64]{1,4,3,2,0:T(8,128)(2,1)S(1)} %bitcast.82), kind=kOutput, calls=%fused_computation.17 | convolution fusion | flops 135266304 | bytes 3735552 | tf_op jit(solution)/shard_map/rnhij,rnjhd->rnihd/dot_general | solution.py:119
  31.1 2.7 %collective-permute-start.9 = (f32[2,33,128]{2,1,0:T(8,128)S(1)}, f32[2,33,128]{2,1,0:T(8,128)S(1)}, u32[]{:S(2)}, u32[]{:S(2)}) collective-permute-start(f32[2,33,128]{2,1,0:T(8,128)S(1)} %collective-permute-done.7), channel_id=1, source_target_pairs={{0,224},{32,0},{64,32},{96,64},{128,96},{160,128},{192,160},{224,1... | collective-permute-start | bytes 101384 | tf_op jit(solution)/shard_map/ppermute | solution.py:22
  33.8 0.0 collective-permute-start.10
  33.9 1.0 %collective-permute-done.9 = f32[2,33,128]{2,1,0:T(8,128)S(1)} collective-permute-done((f32[2,33,128]{2,1,0:T(8,128)S(1)}, f32[2,33,128]{2,1,0:T(8,128)S(1)}, u32[]{:S(2)}, u32[]{:S(2)}) %collective-permute-start.9) | collective-permute-done | bytes 33824 | tf_op jit(solution)/shard_map/ppermute | solution.py:22
  34.9 0.6 copy-done.14
  35.5 2.5 %collective-permute-done.10 = f32[2,33,128]{2,1,0:T(8,128)} collective-permute-done((f32[2,33,128]{2,1,0:T(8,128)S(1)}, f32[2,33,128]{2,1,0:T(8,128)}, u32[]{:S(2)}, u32[]{:S(2)}) %collective-permute-start.10) | collective-permute-done | bytes 33824 | tf_op jit(solution)/shard_map/ppermute | solution.py:22
  38.0 0.6 select_add_fusion.4
  38.7 0.4 collective-permute-start.11
  39.1 0.7 %add_bitcast_fusion = (f32[1,2,33,128]{3,2,1,0:T(8,128)S(1)}, f32[2,33,128]{2,1,0:T(8,128)}, f32[2,33,128]{2,1,0:T(8,128)}) fusion(f32[2,33,128]{2,1,0:T(8,128)S(1)} %collective-permute-done.3, f32[2,33,128]{2,1,0:T(8,128)S(1)} %collective-permute-done.2, f32[2,33,128]{2,1,0:T(8,128)S(1)} %collective-permute-done.1, f32[2,33,128]{2,1,0:T(8,128)S(1)} %select_add_fusion.5, ...), kind=kLoop, calls=%fused_computation.59 | loop fusion | flops 202752 | bytes 270352 | tf_op jit(solution)/shard_map/stack | solution.py:98
  39.7 2.7 %collective-permute-start.12 = (f32[2,33,128]{2,1,0:T(8,128)}, f32[2,33,128]{2,1,0:T(8,128)S(1)}, u32[]{:S(2)}, u32[]{:S(2)}) collective-permute-start(f32[2,33,128]{2,1,0:T(8,128)} %get-tuple-element.15), channel_id=1, source_target_pairs={{0,16},{8,24},{16,0},{24,8},{1,17},{9,25},{17,1},{25,9},{2,18},{10... | collective-permute-start | bytes 101384 | tf_op jit(solution)/shard_map/ppermute | solution.py:22
  42.4 0.6 pad_clamp_fusion
  43.0 1.3 %collective-permute-done.12 = f32[2,33,128]{2,1,0:T(8,128)S(1)} collective-permute-done((f32[2,33,128]{2,1,0:T(8,128)}, f32[2,33,128]{2,1,0:T(8,128)S(1)}, u32[]{:S(2)}, u32[]{:S(2)}) %collective-permute-start.12) | collective-permute-done | bytes 33824 | tf_op jit(solution)/shard_map/ppermute | solution.py:22
  44.3 1.2 %collective-permute-done.13 = f32[2,33,128]{2,1,0:T(8,128)S(1)} collective-permute-done((f32[2,33,128]{2,1,0:T(8,128)}, f32[2,33,128]{2,1,0:T(8,128)S(1)}, u32[]{:S(2)}, u32[]{:S(2)}) %collective-permute-start.13) | collective-permute-done | bytes 33824 | tf_op jit(solution)/shard_map/ppermute | solution.py:22
  45.5 0.7 %gather_fusion = f32[4,2,33,128]{3,2,1,0:T(8,128)S(1)} fusion(f32[4,2,33,128]{3,2,1,0:T(8,128)S(1)} %pad_maximum_fusion, s32[1024]{0:T(1024)} %pad_clamp_fusion), kind=kCustom, calls=%fused_computation | custom fusion | bytes 270352 | tf_op jit(solution)/shard_map/gather | solution.py:98
  46.2 0.0 copy-start.2
  46.2 2.8 %collective-permute-start.14 = (f32[8,33,128]{2,1,0:T(8,128)S(1)}, f32[8,33,128]{2,1,0:T(8,128)S(1)}, u32[]{:S(2)}, u32[]{:S(2)}) collective-permute-start(f32[8,33,128]{2,1,0:T(8,128)S(1)} %bitcast_add_fusion.1), channel_id=1, source_target_pairs={{0,4},{4,0},{1,5},{5,1},{2,6},{6,2},{3,7},{7,3},{8,12},{12,8},{9,1... | collective-permute-start | bytes 405512 | tf_op jit(solution)/shard_map/ppermute | solution.py:22
  49.0 2.9 %collective-permute-done.14 = f32[8,33,128]{2,1,0:T(8,128)S(1)} collective-permute-done((f32[8,33,128]{2,1,0:T(8,128)S(1)}, f32[8,33,128]{2,1,0:T(8,128)S(1)}, u32[]{:S(2)}, u32[]{:S(2)}) %collective-permute-start.14) | collective-permute-done | bytes 135200 | tf_op jit(solution)/shard_map/ppermute | solution.py:22
  52.0 8.6 %collective-permute-start.15 = (f32[8,33,128]{2,1,0:T(8,128)S(1)}, f32[8,33,128]{2,1,0:T(8,128)S(1)}, u32[]{:S(2)}, u32[]{:S(2)}) collective-permute-start(f32[8,33,128]{2,1,0:T(8,128)S(1)} %select_add_fusion), channel_id=1, source_target_pairs={{0,2},{2,0},{1,3},{3,1},{4,6},{6,4},{5,7},{7,5},{8,10},{10,8},{9,1... | collective-permute-start | bytes 405512 | tf_op jit(solution)/shard_map/ppermute | solution.py:22
  60.6 1.0 %collective-permute-done.15 = f32[8,33,128]{2,1,0:T(8,128)S(1)} collective-permute-done((f32[8,33,128]{2,1,0:T(8,128)S(1)}, f32[8,33,128]{2,1,0:T(8,128)S(1)}, u32[]{:S(2)}, u32[]{:S(2)}) %collective-permute-start.15) | collective-permute-done | bytes 135200 | tf_op jit(solution)/shard_map/ppermute | solution.py:22
  61.6 0.1 add_select_fusion
  61.7 0.7 %fusion.31 = f32[16,32,128]{2,1,0:T(8,128)} fusion(f32[8,33,128]{2,1,0:T(8,128)S(1)} %get-tuple-element.12, f32[8,33,128]{2,1,0:T(8,128)S(1)} %get-tuple-element.11), kind=kLoop, calls=%fused_computation.45 | loop fusion | flops 65536 | bytes 532480 | tf_op jit(solution)/shard_map/concatenate | solution.py:52
  62.4 0.3 fusion.40
  62.7 1.1 %broadcast_in_dim_broadcast_in_dim_reshape.3 = f32[16,64,64]{2,1,0:T(8,128)S(1)} reshape(f32[16,32,128]{2,1,0:T(8,128)} %fusion.31) | data formatting | bytes 524288 | tf_op jit(solution)/shard_map/broadcast_in_dim;broadcast_in_dim;reshape | solution.py:127
  63.9 1.8 %convolution_bitcast_fusion = f32[1,1,256,16,64]{2,4,3,1,0:T(8,128)S(1)} fusion(bf16[256,16,64]{0,2,1:T(8,128)(2,1)} %bitcast.76, f32[16,64,64]{2,1,0:T(8,128)S(1)} %broadcast_in_dim_broadcast_in_dim_reshape.3, f32[16,64,64]{2,1,0:T(8,128)S(1)} %fusion.25), kind=kOutput, calls=%fused_computation.18 | convolution fusion | flops 201457664 | bytes 2097152 | tf_op jit(solution)/shard_map/rnihd,rnhde->rnihe/dot_general | solution.py:130
  65.7 0.2 divide_convert_fusion
  65.9 1.5 %fusion.14 = bf16[1,256,1024]{2,1,0:T(8,128)(2,1)} fusion(bf16[256,1024]{0,1:T(8,128)(2,1)S(1)} %bitcast.78, bf16[1024,1024]{1,0:T(8,128)(2,1)S(1)} %copy-done), kind=kOutput, calls=%fused_computation.21 | convolution fusion | flops 537133056 | bytes 3145728 | tf_op jit(solution)/shard_map/rtd,de->rte/dot_general | solution.py:174
  (48 shorter events, 0.3 us)
Async XLA Ops:
  0.0 65.9 %copy-start = (bf16[1024,1024]{1,0:T(8,128)(2,1)S(1)}, bf16[1024,1024]{1,0:T(8,128)(2,1)}, u32[]{:S(2)}) copy-start(bf16[1024,1024]{1,0:T(8,128)(2,1)} %param.5) | copy-start | bytes 6291460
  3.8 1.0 %copy-start.8 = (bf16[2048,256]{1,0:T(8,128)(2,1)}, bf16[2048,256]{1,0:T(8,128)(2,1)S(1)}, u32[]{:S(2)}) copy-start(bf16[2048,256]{1,0:T(8,128)(2,1)S(1)} %fusion.2) | copy-start | bytes 3145732
  5.3 4.3 %collective-permute-start = (f32[8,33,128]{2,1,0:T(8,128)S(1)}, f32[8,33,128]{2,1,0:T(8,128)S(1)}, u32[]{:S(2)}, u32[]{:S(2)}) collective-permute-start(f32[8,33,128]{2,1,0:T(8,128)S(1)} %fusion.32), channel_id=1, source_target_pairs={{0,2},{2,0},{1,3},{3,1},{4,6},{6,4},{5,7},{7,5},{8,10},{10,8},{9,1... | collective-permute-start | bytes 405512 | tf_op jit(solution)/shard_map/ppermute | solution.py:22
  9.6 3.0 %copy-start.6 = (f32[8,33,128]{2,1,0:T(8,128)}, f32[8,33,128]{2,1,0:T(8,128)S(1)}, u32[]{:S(2)}) copy-start(f32[8,33,128]{2,1,0:T(8,128)S(1)} %collective-permute-done) | copy-start | bytes 405508
  9.7 3.0 %copy-start.3 = (f32[8,33,128]{2,1,0:T(8,128)}, f32[8,33,128]{2,1,0:T(8,128)S(1)}, u32[]{:S(2)}) copy-start(f32[8,33,128]{2,1,0:T(8,128)S(1)} %select_add_fusion.1) | copy-start | bytes 405508
  10.4 5.8 %collective-permute-start.1 = (f32[2,33,128]{2,1,0:T(8,128)}, f32[2,33,128]{2,1,0:T(8,128)S(1)}, u32[]{:S(2)}, u32[]{:S(2)}) collective-permute-start(f32[2,33,128]{2,1,0:T(8,128)} %get-tuple-element.16), channel_id=1, source_target_pairs={{0,8},{8,16},{16,24},{24,0},{1,9},{9,17},{17,25},{25,1},{2,10},{10... | collective-permute-start | bytes 101384 | tf_op jit(solution)/shard_map/ppermute | solution.py:22
  10.4 5.8 %collective-permute-start.2 = (f32[2,33,128]{2,1,0:T(8,128)}, f32[2,33,128]{2,1,0:T(8,128)S(1)}, u32[]{:S(2)}, u32[]{:S(2)}) collective-permute-start(f32[2,33,128]{2,1,0:T(8,128)} %get-tuple-element.18), channel_id=1, source_target_pairs={{0,16},{8,24},{16,0},{24,8},{1,17},{9,25},{17,1},{25,9},{2,18},{10... | collective-permute-start | bytes 101384 | tf_op jit(solution)/shard_map/ppermute | solution.py:22
  12.6 3.6 %collective-permute-start.3 = (f32[2,33,128]{2,1,0:T(8,128)}, f32[2,33,128]{2,1,0:T(8,128)S(1)}, u32[]{:S(2)}, u32[]{:S(2)}) collective-permute-start(f32[2,33,128]{2,1,0:T(8,128)} %get-tuple-element.17), channel_id=1, source_target_pairs={{0,24},{8,0},{16,8},{24,16},{1,25},{9,1},{17,9},{25,17},{2,26},{10... | collective-permute-start | bytes 101384 | tf_op jit(solution)/shard_map/ppermute | solution.py:22
  16.2 10.6 %copy-start.1 = (bf16[1024,256]{1,0:T(8,128)(2,1)}, bf16[1024,256]{1,0:T(8,128)(2,1)S(1)}, u32[]{:S(2)}) copy-start(bf16[1024,256]{1,0:T(8,128)(2,1)S(1)} %fusion.19) | copy-start | bytes 1572868
  17.1 7.0 %collective-permute-start.4 = (f32[2,33,128]{2,1,0:T(8,128)S(1)}, f32[2,33,128]{2,1,0:T(8,128)S(1)}, u32[]{:S(2)}, u32[]{:S(2)}) collective-permute-start(f32[2,33,128]{2,1,0:T(8,128)S(1)} %add_add_fusion), channel_id=1, source_target_pairs={{0,32},{32,64},{64,96},{96,128},{128,160},{160,192},{192,224},{224... | collective-permute-start | bytes 101384 | tf_op jit(solution)/shard_map/ppermute | solution.py:22
  18.8 8.0 %collective-permute-start.5 = (f32[2,33,128]{2,1,0:T(8,128)S(1)}, f32[2,33,128]{2,1,0:T(8,128)S(1)}, u32[]{:S(2)}, u32[]{:S(2)}) collective-permute-start(f32[2,33,128]{2,1,0:T(8,128)S(1)} %add_add_fusion), channel_id=1, source_target_pairs={{0,224},{32,0},{64,32},{96,64},{128,96},{160,128},{192,160},{224,1... | collective-permute-start | bytes 101384 | tf_op jit(solution)/shard_map/ppermute | solution.py:22
  24.1 2.7 %copy-start.10 = (f32[2,33,128]{2,1,0:T(8,128)}, f32[2,33,128]{2,1,0:T(8,128)S(1)}, u32[]{:S(2)}) copy-start(f32[2,33,128]{2,1,0:T(8,128)S(1)} %collective-permute-done.4) | copy-start | bytes 101380
  24.1 5.4 %collective-permute-start.6 = (f32[2,33,128]{2,1,0:T(8,128)S(1)}, f32[2,33,128]{2,1,0:T(8,128)S(1)}, u32[]{:S(2)}, u32[]{:S(2)}) collective-permute-start(f32[2,33,128]{2,1,0:T(8,128)S(1)} %collective-permute-done.4), channel_id=1, source_target_pairs={{0,32},{32,64},{64,96},{96,128},{128,160},{160,192},{192,224},{224... | collective-permute-start | bytes 101384 | tf_op jit(solution)/shard_map/ppermute | solution.py:22
  24.1 5.5 %copy-start.9 = (bf16[2048,256]{1,0:T(8,128)(2,1)S(1)}, bf16[2048,256]{1,0:T(8,128)(2,1)}, u32[]{:S(2)}) copy-start(bf16[2048,256]{1,0:T(8,128)(2,1)} %copy-done.8) | copy-start | bytes 3145732
  26.8 4.3 %copy-start.12 = (f32[2,33,128]{2,1,0:T(8,128)}, f32[2,33,128]{2,1,0:T(8,128)S(1)}, u32[]{:S(2)}) copy-start(f32[2,33,128]{2,1,0:T(8,128)S(1)} %collective-permute-done.5) | copy-start | bytes 101380
  26.8 4.3 %collective-permute-start.7 = (f32[2,33,128]{2,1,0:T(8,128)S(1)}, f32[2,33,128]{2,1,0:T(8,128)S(1)}, u32[]{:S(2)}, u32[]{:S(2)}) collective-permute-start(f32[2,33,128]{2,1,0:T(8,128)S(1)} %collective-permute-done.5), channel_id=1, source_target_pairs={{0,224},{32,0},{64,32},{96,64},{128,96},{160,128},{192,160},{224,1... | collective-permute-start | bytes 101384 | tf_op jit(solution)/shard_map/ppermute | solution.py:22
  29.6 1.5 %copy-start.13 = (f32[2,33,128]{2,1,0:T(8,128)}, f32[2,33,128]{2,1,0:T(8,128)S(1)}, u32[]{:S(2)}) copy-start(f32[2,33,128]{2,1,0:T(8,128)S(1)} %collective-permute-done.6) | copy-start | bytes 101380
  29.6 4.2 %collective-permute-start.8 = (f32[2,33,128]{2,1,0:T(8,128)S(1)}, f32[2,33,128]{2,1,0:T(8,128)S(1)}, u32[]{:S(2)}, u32[]{:S(2)}) collective-permute-start(f32[2,33,128]{2,1,0:T(8,128)S(1)} %collective-permute-done.6), channel_id=1, source_target_pairs={{0,32},{32,64},{64,96},{96,128},{128,160},{160,192},{192,224},{224... | collective-permute-start | bytes 101384 | tf_op jit(solution)/shard_map/ppermute | solution.py:22
  29.6 8.4 %copy-start.11 = (f32[2,33,128]{2,1,0:T(8,128)S(1)}, f32[2,33,128]{2,1,0:T(8,128)}, u32[]{:S(2)}) copy-start(f32[2,33,128]{2,1,0:T(8,128)} %copy-done.10) | copy-start | bytes 101380
  29.6 8.4 %copy-start.4 = (f32[8,33,128]{2,1,0:T(8,128)S(1)}, f32[8,33,128]{2,1,0:T(8,128)}, u32[]{:S(2)}) copy-start(f32[8,33,128]{2,1,0:T(8,128)} %copy-done.3) | copy-start | bytes 405508
  31.1 30.6 %copy-start.7 = (f32[8,33,128]{2,1,0:T(8,128)S(1)}, f32[8,33,128]{2,1,0:T(8,128)}, u32[]{:S(2)}) copy-start(f32[8,33,128]{2,1,0:T(8,128)} %copy-done.6) | copy-start | bytes 405508
  31.1 3.8 %collective-permute-start.9 = (f32[2,33,128]{2,1,0:T(8,128)S(1)}, f32[2,33,128]{2,1,0:T(8,128)S(1)}, u32[]{:S(2)}, u32[]{:S(2)}) collective-permute-start(f32[2,33,128]{2,1,0:T(8,128)S(1)} %collective-permute-done.7), channel_id=1, source_target_pairs={{0,224},{32,0},{64,32},{96,64},{128,96},{160,128},{192,160},{224,1... | collective-permute-start | bytes 101384 | tf_op jit(solution)/shard_map/ppermute | solution.py:22
  33.8 4.2 %collective-permute-start.10 = (f32[2,33,128]{2,1,0:T(8,128)S(1)}, f32[2,33,128]{2,1,0:T(8,128)}, u32[]{:S(2)}, u32[]{:S(2)}) collective-permute-start(f32[2,33,128]{2,1,0:T(8,128)S(1)} %collective-permute-done.8), channel_id=1, source_target_pairs={{0,32},{32,64},{64,96},{96,128},{128,160},{160,192},{192,224},{224... | collective-permute-start | bytes 101384 | tf_op jit(solution)/shard_map/ppermute | solution.py:22
  34.9 0.6 copy-start.14
  38.7 4.3 %collective-permute-start.11 = (f32[2,33,128]{2,1,0:T(8,128)}, f32[2,33,128]{2,1,0:T(8,128)S(1)}, u32[]{:S(2)}, u32[]{:S(2)}) collective-permute-start(f32[2,33,128]{2,1,0:T(8,128)} %select_add_fusion.4), channel_id=1, source_target_pairs={{0,8},{8,16},{16,24},{24,0},{1,9},{9,17},{17,25},{25,1},{2,10},{10... | collective-permute-start | bytes 101384 | tf_op jit(solution)/shard_map/ppermute | solution.py:22
  39.7 4.6 %collective-permute-start.12 = (f32[2,33,128]{2,1,0:T(8,128)}, f32[2,33,128]{2,1,0:T(8,128)S(1)}, u32[]{:S(2)}, u32[]{:S(2)}) collective-permute-start(f32[2,33,128]{2,1,0:T(8,128)} %get-tuple-element.15), channel_id=1, source_target_pairs={{0,16},{8,24},{16,0},{24,8},{1,17},{9,25},{17,1},{25,9},{2,18},{10... | collective-permute-start | bytes 101384 | tf_op jit(solution)/shard_map/ppermute | solution.py:22
  42.4 3.1 %collective-permute-start.13 = (f32[2,33,128]{2,1,0:T(8,128)}, f32[2,33,128]{2,1,0:T(8,128)S(1)}, u32[]{:S(2)}, u32[]{:S(2)}) collective-permute-start(f32[2,33,128]{2,1,0:T(8,128)} %get-tuple-element.14), channel_id=1, source_target_pairs={{0,24},{8,0},{16,8},{24,16},{1,25},{9,1},{17,9},{25,17},{2,26},{10... | collective-permute-start | bytes 101384 | tf_op jit(solution)/shard_map/ppermute | solution.py:22
  46.2 16.3 %copy-start.2 = (bf16[1024,256]{1,0:T(8,128)(2,1)S(1)}, bf16[1024,256]{1,0:T(8,128)(2,1)}, u32[]{:S(2)}) copy-start(bf16[1024,256]{1,0:T(8,128)(2,1)} %copy-done.1) | copy-start | bytes 1572868
  46.2 5.8 %collective-permute-start.14 = (f32[8,33,128]{2,1,0:T(8,128)S(1)}, f32[8,33,128]{2,1,0:T(8,128)S(1)}, u32[]{:S(2)}, u32[]{:S(2)}) collective-permute-start(f32[8,33,128]{2,1,0:T(8,128)S(1)} %bitcast_add_fusion.1), channel_id=1, source_target_pairs={{0,4},{4,0},{1,5},{5,1},{2,6},{6,2},{3,7},{7,3},{8,12},{12,8},{9,1... | collective-permute-start | bytes 405512 | tf_op jit(solution)/shard_map/ppermute | solution.py:22
  52.0 9.6 %collective-permute-start.15 = (f32[8,33,128]{2,1,0:T(8,128)S(1)}, f32[8,33,128]{2,1,0:T(8,128)S(1)}, u32[]{:S(2)}, u32[]{:S(2)}) collective-permute-start(f32[8,33,128]{2,1,0:T(8,128)S(1)} %select_add_fusion), channel_id=1, source_target_pairs={{0,2},{2,0},{1,3},{3,1},{4,6},{6,4},{5,7},{7,5},{8,10},{10,8},{9,1... | collective-permute-start | bytes 405512 | tf_op jit(solution)/shard_map/ppermute | solution.py:22
  62.4 3.2 %copy-start.15 = (f32[16,256]{1,0:T(8,128)S(1)}, f32[16,256]{1,0:T(8,128)}, u32[]{:S(2)}) copy-start(f32[16,256]{1,0:T(8,128)} %get-tuple-element.19) | copy-start | bytes 49156
  63.8 1.8 %copy-start.5 = (f32[1,1,256,16,64]{2,4,3,1,0:T(8,128)S(1)}, f32[1,1,256,16,64]{2,4,3,1,0:T(8,128)}, u32[]{:S(2)}) copy-start(f32[1,1,256,16,64]{2,4,3,1,0:T(8,128)} %fusion.10) | copy-start | bytes 3145732

commit v11 on v10

--- a/solution.py
+++ b/solution.py
@@ -100,9 +100,8 @@
     )
     half = add(mine, swap(add(mine, keep(chip, xh == 0)), "seg_x"))
     got = swap(add(half, keep(own_c, core == 0)), "frm")
-    lo = tmap(lambda a, b: jnp.where(core == 0, a, b), half, got)
-    hi = tmap(lambda a, b, c: jnp.where(core == 0, b, a + c), half, got, got_c)
-    return joined(lo, hi), carry
+    own = tmap(lambda a, c: jnp.where(core == 0, a, a + c), half, got_c)
+    return (own, got), carry
 
 
 def block_terms(phi_q, phi_k, values, span):
@@ -163,17 +162,26 @@
     dense = total_kv.reshape(HEADS, -1, lanes)
     rows_kv = dense.shape[1]
     norm = jnp.pad(total_k, ((0, 0), (0, lanes - total_k.shape[1])))[:, None]
-    prior, (num_local, den_local) = entering(
+    (own, other), (num_local, den_local) = entering(
         jnp.concatenate([dense, norm], axis=1), (num_local, den_local)
     )
-    prior_kv = prior[:, :rows_kv].reshape(total_kv.shape)
-    prior_k = prior[:, rows_kv, : total_k.shape[1]]
-    heads_out = finish(
-        pq, num_local, den_local, kv_blocks, k_blocks, prior_kv[None], prior_k[None]
-    )
-    return jnp.einsum("rtd,de->rte", heads_out, w_out, preferred_element_type=jnp.float32).astype(
-        jnp.bfloat16
-    )
+    core = lax.axis_index("frm")
+    half_heads = HEADS // 2
+
+    def heads_of(prior, which):
+        first = which * half_heads
+        pick = lambda t, axis: lax.dynamic_slice_in_dim(t, first, half_heads, axis=axis)
+        prior_kv = prior[:, :rows_kv].reshape((half_heads,) + total_kv.shape[1:])
+        prior_k = prior[:, rows_kv, : total_k.shape[1]]
+        heads_out = finish(
+            pick(pq, 3), pick(num_local, 3), pick(den_local, 2),
+            pick(kv_blocks, 2), pick(k_blocks, 2), prior_kv[None], prior_k[None],
+        )
+        rows_w = lax.dynamic_slice_in_dim(w_out, first * head_dim, half_heads * head_dim, axis=0)
+        return jnp.einsum("rtd,de->rte", heads_out, rows_w, preferred_element_type=jnp.float32)
+
+    out = heads_of(own, core) + heads_of(other, 1 - core)
+    return out.astype(jnp.bfloat16)
 
 
 def solution(mesh):

time: 67.7 us -> 67.1 us (level)
  matrix products: 14.3 us -> 18.1 us
  other arithmetic: 4.31 us -> 0.88 us
    dot_general x1 -> x2, matrix products: 0.32 us -> 2.32 us  [finish(): jnp.einsum('rnihd,rnhd->rnih', pq32, before_k, precision=lax.Precision.HI...]
    add x6, other arithmetic: 1.63 us -> 0.27 us  [tmap(): return jax.tree.map(f, *trees)]
    dot_general x1 -> x2, matrix products: 1.76 us -> 2.96 us  [finish(): jnp.einsum('rnihd,rnhde->rnihe', pq32, before_kv, precision=lax.Precision...]
    another operation x1 -> x2, local copies, waits for them, and re-layouts: 1.1 us -> 0.2 us  [finish(): before_kv = jnp.cumsum(kv_blocks, axis=1) - kv_blocks + prior_kv[:, None]]
    slice x0 -> x4, local copies, waits for them, and re-layouts: none -> 0.9 us  [the longest x1 0.85 us: heads_of(): prior_k = prior[:, rows_kv, :total_k.shape[1]]]
    dot_general x2, matrix products: 6.24 us -> 7.03 us  [project(): jnp.einsum('rtd,de->ret', frames_in, w, preferred_element_type=jnp.float32)]
    concatenate x2 -> x0, other arithmetic: 0.73 us -> none  [joined(): return tmap(lambda a, b: jnp.concatenate([a, b], axis=0), lo, hi)]
    dynamic_slice x1, local copies, waits for them, and re-layouts: 0.73 us -> 0.04 us  [one(): return lax.dynamic_slice_in_dim(t, index * size, size, axis=0)]
  transfers between devices with their start and end apart: 16 -> 16, of which waited for: 8 -> 9; matrix products, arithmetic and copies ran while one was open for 12% -> 11% of each run, Pallas kernels for 0% -> 0%
where the time goes in v11:
time: 67.1 us; the launch traced here: 66.8 us
  starting transfers between devices  32.2 us (48%)
  matrix products  18.1 us (27%)
  waiting for transfers between devices  11.8 us (18%)
  local copies, waits for them, and re-layouts  3.48 us (5%)
  other arithmetic  0.88 us (1%)
    ppermute x16, starting transfers between devices, send(): return tmap(lambda t: lax.ppermute(t, axis, perm=pairs), tree)  32.2 us
    ppermute x16, waiting for transfers between devices, send(): return tmap(lambda t: lax.ppermute(t, axis, perm=pairs), tree)  11.8 us
    dot_general x2, matrix products, project(): jnp.einsum('rtd,de->ret', frames_in, w, preferred_element_type=jnp.float32)  7.03 us
    dot_general x2, matrix products, finish(): jnp.einsum('rnihd,rnhde->rnihe', pq32, before_kv, precision=lax.Precision...  2.96 us
    dot_general x2, matrix products, finish(): jnp.einsum('rnihd,rnhd->rnih', pq32, before_k, precision=lax.Precision.HI...  2.32 us
    dot_general x1, matrix products, block_terms(): jnp.einsum('rnihd,rnjhd->rnhij', pq, pk, preferred_element_type=jnp.float32)  2.23 us
    dot_general x2, matrix products, heads_of(): jnp.einsum('rtd,de->rte', heads_out, rows_w, preferred_element_type=jnp.f...  1.74 us
    dot_general x1, matrix products, block_terms(): jnp.einsum('rnhij,rnjhd->rnihd', weights, vv, preferred_element_type=jnp....  1.45 us
  transfers between devices with their start and end apart: 16, of which 9 were waited for; matrix products, arithmetic and copies ran while one was open for 11% of the time, Pallas kernels for 0%

profile of v11, /device:TPU:1, one launch (start us, length us, event | category | flops | bytes accessed | tf_op | source)
XLA Modules:
  0.0 66.8 jit_solution(4821611988617996298)
XLA Ops:
  0.0 3.8 %fusion.2 = bf16[2048,256]{1,0:T(8,128)(2,1)S(1)} fusion(bf16[1024,3072]{1,0:T(8,128)(2,1)} %param.4, bf16[1,256,1024]{2,1,0:T(8,128)(2,1)} %param.3), kind=kOutput, calls=%fused_computation.5 | convolution fusion | flops 1074266112 | bytes 5767168 | tf_op jit(solution)/shard_map/rtd,de->ret/dot_general | solution.py:149
  3.8 0.4 fusion.35
  4.2 0.6 copy-done.1
  4.8 0.3 convert_reduce_fusion
  5.1 0.1 reshape_squeeze.4
  5.3 0.2 copy.4
  5.5 3.3 %collective-permute-start = (f32[8,33,128]{2,0,1:T(8,128)S(1)}, f32[8,33,128]{2,0,1:T(8,128)S(1)}, u32[]{:S(2)}, u32[]{:S(2)}) collective-permute-start(f32[8,33,128]{2,0,1:T(8,128)S(1)} %fusion.55), channel_id=1, source_target_pairs={{0,2},{2,0},{1,3},{3,1},{4,6},{6,4},{5,7},{7,5},{8,10},{10,8},{9,1... | collective-permute-start | bytes 405512 | tf_op jit(solution)/shard_map/ppermute | solution.py:22
  8.8 1.0 %collective-permute-done = f32[8,33,128]{2,0,1:T(8,128)S(1)} collective-permute-done((f32[8,33,128]{2,0,1:T(8,128)S(1)}, f32[8,33,128]{2,0,1:T(8,128)S(1)}, u32[]{:S(2)}, u32[]{:S(2)}) %collective-permute-start) | collective-permute-done | bytes 135200 | tf_op jit(solution)/shard_map/ppermute | solution.py:22
  9.8 0.1 collective-permute-start.1
  9.9 2.2 %collective-permute-start.2 = (f32[2,33,128]{2,0,1:T(2,128)S(1)}, f32[2,33,128]{2,0,1:T(2,128)S(1)}, u32[]{:S(2)}, u32[]{:S(2)}) collective-permute-start(f32[2,33,128]{2,0,1:T(2,128)S(1)} %get-tuple-element.18), channel_id=1, source_target_pairs={{0,16},{8,24},{16,0},{24,8},{1,17},{9,25},{17,1},{25,9},{2,18},{10... | collective-permute-start | bytes 101384 | tf_op jit(solution)/shard_map/ppermute | solution.py:22
  12.1 1.1 %collective-permute-start.3 = (f32[2,33,128]{2,0,1:T(2,128)S(1)}, f32[2,33,128]{2,0,1:T(2,128)S(1)}, u32[]{:S(2)}, u32[]{:S(2)}) collective-permute-start(f32[2,33,128]{2,0,1:T(2,128)S(1)} %get-tuple-element.17), channel_id=1, source_target_pairs={{0,24},{8,0},{16,8},{24,16},{1,25},{9,1},{17,9},{25,17},{2,26},{10... | collective-permute-start | bytes 101384 | tf_op jit(solution)/shard_map/ppermute | solution.py:22
  13.2 3.3 %fusion.26 = bf16[1024,256]{1,0:T(8,128)(2,1)} fusion(bf16[1024,3072]{1,0:T(8,128)(2,1)} %param.4, bf16[1,256,1024]{2,1,0:T(8,128)(2,1)} %param.3), kind=kOutput, calls=%fused_computation.34 | convolution fusion | flops 538705920 | bytes 3145728 | tf_op jit(solution)/shard_map/rtd,de->ret/dot_general | solution.py:149
  16.5 0.0 collective-permute-done.3
  16.5 1.7 %collective-permute-start.4 = (f32[2,33,128]{2,0,1:T(2,128)S(1)}, f32[2,33,128]{2,0,1:T(2,128)S(1)}, u32[]{:S(2)}, u32[]{:S(2)}) collective-permute-start(f32[2,33,128]{2,0,1:T(2,128)S(1)} %add_add_fusion), channel_id=1, source_target_pairs={{0,32},{32,64},{64,96},{96,128},{128,160},{160,192},{192,224},{224... | collective-permute-start | bytes 101384 | tf_op jit(solution)/shard_map/ppermute | solution.py:22
  18.2 4.0 %collective-permute-start.5 = (f32[2,33,128]{2,0,1:T(2,128)S(1)}, f32[2,33,128]{2,0,1:T(2,128)S(1)}, u32[]{:S(2)}, u32[]{:S(2)}) collective-permute-start(f32[2,33,128]{2,0,1:T(2,128)S(1)} %add_add_fusion), channel_id=1, source_target_pairs={{0,224},{32,0},{64,32},{96,64},{128,96},{160,128},{192,160},{224,1... | collective-permute-start | bytes 101384 | tf_op jit(solution)/shard_map/ppermute | solution.py:22
  22.3 1.2 %collective-permute-done.4 = f32[2,33,128]{2,0,1:T(2,128)S(1)} collective-permute-done((f32[2,33,128]{2,0,1:T(2,128)S(1)}, f32[2,33,128]{2,0,1:T(2,128)S(1)}, u32[]{:S(2)}, u32[]{:S(2)}) %collective-permute-start.4) | collective-permute-done | bytes 33824 | tf_op jit(solution)/shard_map/ppermute | solution.py:22
  23.5 2.2 %select_reduce_fusion = (f32[16,256]{1,0:T(8,128)S(1)}, bf16[16,256,256]{1,2,0:T(8,128)(2,1)S(1)}) fusion(pred[256,256]{0,1:T(8,128)(4,1)S(1)} %iota_compare_fusion, bf16[256,16,64]{0,2,1:T(8,128)(2,1)} %bitcast.115, bf16[1,256,2,16,64]{1,4,3,2,0:T(8,128)(2,1)} %bitcast.124), kind=kOutput, calls=%fused_computation.3 | convolution fusion | flops 138932224 | bytes 3227648 | tf_op jit(solution)/shard_map/rnihd,rnjhd->rnhij/dot_general | solution.py:113
  25.7 2.7 %collective-permute-start.7 = (f32[2,33,128]{2,0,1:T(2,128)S(1)}, f32[2,33,128]{2,0,1:T(2,128)S(1)}, u32[]{:S(2)}, u32[]{:S(2)}) collective-permute-start(f32[2,33,128]{2,0,1:T(2,128)S(1)} %collective-permute-done.5), channel_id=1, source_target_pairs={{0,224},{32,0},{64,32},{96,64},{128,96},{160,128},{192,160},{224,1... | collective-permute-start | bytes 101384 | tf_op jit(solution)/shard_map/ppermute | solution.py:22
  28.5 1.5 %fusion.10 = f32[1,1,256,16,64]{2,4,3,1,0:T(8,128)} fusion(bf16[16,256,256]{1,2,0:T(8,128)(2,1)S(1)} %get-tuple-element.24, pred[256,256]{0,1:T(8,128)(4,1)S(1)} %iota_compare_fusion, bf16[1,256,2,16,64]{1,4,3,2,0:T(8,128)(2,1)S(1)} %bitcast.125), kind=kOutput, calls=%fused_computation.17 | convolution fusion | flops 135266304 | bytes 3735552 | tf_op jit(solution)/shard_map/rnhij,rnjhd->rnihd/dot_general | solution.py:118
  29.9 2.7 %collective-permute-start.9 = (f32[2,33,128]{2,0,1:T(2,128)S(1)}, f32[2,33,128]{2,0,1:T(2,128)S(1)}, u32[]{:S(2)}, u32[]{:S(2)}) collective-permute-start(f32[2,33,128]{2,0,1:T(2,128)S(1)} %collective-permute-done.7), channel_id=1, source_target_pairs={{0,224},{32,0},{64,32},{96,64},{128,96},{160,128},{192,160},{224,1... | collective-permute-start | bytes 101384 | tf_op jit(solution)/shard_map/ppermute | solution.py:22
  32.6 0.0 collective-permute-start.10
  32.7 0.9 %collective-permute-done.9 = f32[2,33,128]{2,0,1:T(2,128)S(1)} collective-permute-done((f32[2,33,128]{2,0,1:T(2,128)S(1)}, f32[2,33,128]{2,0,1:T(2,128)S(1)}, u32[]{:S(2)}, u32[]{:S(2)}) %collective-permute-start.9) | collective-permute-done | bytes 33824 | tf_op jit(solution)/shard_map/ppermute | solution.py:22
  33.6 3.1 %collective-permute-done.10 = f32[2,33,128]{2,0,1:T(2,128)} collective-permute-done((f32[2,33,128]{2,0,1:T(2,128)S(1)}, f32[2,33,128]{2,0,1:T(2,128)}, u32[]{:S(2)}, u32[]{:S(2)}) %collective-permute-start.10) | collective-permute-done | bytes 33824 | tf_op jit(solution)/shard_map/ppermute | solution.py:22
  36.7 0.1 select_add_fusion.6
  36.8 0.1 select_add_fusion.5
  36.8 0.5 collective-permute-start.11
  37.3 0.1 add_bitcast_fusion
  37.5 1.8 %collective-permute-start.12 = (f32[2,33,128]{2,0,1:T(2,128)S(1)}, f32[2,33,128]{2,0,1:T(2,128)S(1)}, u32[]{:S(2)}, u32[]{:S(2)}) collective-permute-start(f32[2,33,128]{2,0,1:T(2,128)S(1)} %get-tuple-element.15), channel_id=1, source_target_pairs={{0,16},{8,24},{16,0},{24,8},{1,17},{9,25},{17,1},{25,9},{2,18},{10... | collective-permute-start | bytes 101384 | tf_op jit(solution)/shard_map/ppermute | solution.py:22
  39.2 0.7 %collective-permute-start.13 = (f32[2,33,128]{2,0,1:T(2,128)S(1)}, f32[2,33,128]{2,0,1:T(2,128)S(1)}, u32[]{:S(2)}, u32[]{:S(2)}) collective-permute-start(f32[2,33,128]{2,0,1:T(2,128)S(1)} %get-tuple-element.14), channel_id=1, source_target_pairs={{0,24},{8,0},{16,8},{24,16},{1,25},{9,1},{17,9},{25,17},{2,26},{10... | collective-permute-start | bytes 101384 | tf_op jit(solution)/shard_map/ppermute | solution.py:22
  40.0 1.1 %collective-permute-done.11 = f32[2,33,128]{2,0,1:T(2,128)S(1)} collective-permute-done((f32[2,33,128]{2,0,1:T(2,128)S(1)}, f32[2,33,128]{2,0,1:T(2,128)S(1)}, u32[]{:S(2)}, u32[]{:S(2)}) %collective-permute-start.11) | collective-permute-done | bytes 33824 | tf_op jit(solution)/shard_map/ppermute | solution.py:22
  41.1 0.7 %collective-permute-done.12 = f32[2,33,128]{2,0,1:T(2,128)S(1)} collective-permute-done((f32[2,33,128]{2,0,1:T(2,128)S(1)}, f32[2,33,128]{2,0,1:T(2,128)S(1)}, u32[]{:S(2)}, u32[]{:S(2)}) %collective-permute-start.12) | collective-permute-done | bytes 33824 | tf_op jit(solution)/shard_map/ppermute | solution.py:22
  41.8 0.2 collective-permute-done.13
  42.1 0.1 pad_maximum_fusion
  42.1 0.7 %gather_fusion = f32[4,2,33,128]{3,1,2,0:T(2,128)S(1)} fusion(f32[4,2,33,128]{3,1,2,0:T(2,128)S(1)} %pad_maximum_fusion, s32[1024]{0:T(1024)S(1)} %pad_clamp_fusion), kind=kCustom, calls=%fused_computation | custom fusion | bytes 270352 | tf_op jit(solution)/shard_map/gather | solution.py:98
  42.9 2.8 %collective-permute-start.14 = (f32[8,33,128]{2,0,1:T(8,128)S(1)}, f32[8,33,128]{2,0,1:T(8,128)S(1)}, u32[]{:S(2)}, u32[]{:S(2)}) collective-permute-start(f32[8,33,128]{2,0,1:T(8,128)S(1)} %select_add_fusion.1), channel_id=1, source_target_pairs={{0,4},{4,0},{1,5},{5,1},{2,6},{6,2},{3,7},{7,3},{8,12},{12,8},{9,1... | collective-permute-start | bytes 405512 | tf_op jit(solution)/shard_map/ppermute | solution.py:22
  45.8 2.6 %collective-permute-done.14 = f32[8,33,128]{2,0,1:T(8,128)S(1)} collective-permute-done((f32[8,33,128]{2,0,1:T(8,128)S(1)}, f32[8,33,128]{2,0,1:T(8,128)S(1)}, u32[]{:S(2)}, u32[]{:S(2)}) %collective-permute-start.14) | collective-permute-done | bytes 135200 | tf_op jit(solution)/shard_map/ppermute | solution.py:22
  48.4 8.5 %collective-permute-start.15 = (f32[8,33,128]{2,1,0:T(8,128)S(1)}, f32[8,33,128]{2,1,0:T(8,128)S(1)}, u32[]{:S(2)}, u32[]{:S(2)}) collective-permute-start(f32[8,33,128]{2,1,0:T(8,128)S(1)} %copy.9), channel_id=1, source_target_pairs={{0,2},{2,0},{1,3},{3,1},{4,6},{6,4},{5,7},{7,5},{8,10},{10,8},{9,1... | collective-permute-start | bytes 405512 | tf_op jit(solution)/shard_map/ppermute | solution.py:22
  57.0 0.1 broadcast_in_dim_broadcast_in_dim_reshape.6
  57.1 0.9 %collective-permute-done.15 = f32[8,33,128]{2,1,0:T(8,128)S(1)} collective-permute-done((f32[8,33,128]{2,1,0:T(8,128)S(1)}, f32[8,33,128]{2,1,0:T(8,128)S(1)}, u32[]{:S(2)}, u32[]{:S(2)}) %collective-permute-start.15) | collective-permute-done | bytes 135200 | tf_op jit(solution)/shard_map/ppermute | solution.py:22
  58.0 0.7 copy-done.3
  58.7 0.1 broadcast_in_dim_broadcast_in_dim_reshape.7
  58.8 0.8 %slice.39 = f32[8,1,64]{2,1,0:T(1,128)S(1)} slice(f32[8,33,128]{2,1,0:T(8,128)} %copy-done.3), slice={[0:8], [32:33], [0:64]} | slice | bytes 4096 | tf_op jit(solution)/shard_map/slice | solution.py:175
  59.7 1.2 %fusion.42 = f32[8,1,256]{2,1,0:T(1,128)S(1)} fusion(f32[8,64,1]{1,2,0:T(1,128)S(1)} %bitcast.130, bf16[1,1,16,64,256]{4,3,2,1,0:T(8,128)(2,1)} %bitcast.116, s32[]{:T(128)S(6)} %select_n.334), kind=kOutput, calls=%fused_computation.52 | convolution fusion | flops 1572864 | bytes 272388 | tf_op jit(solution)/shard_map/rnihd,rnhd->rnih/dot_general | solution.py:132
  60.8 1.2 %fusion.39 = f32[8,1,256]{2,1,0:T(1,128)S(1)} fusion(f32[8,64,1]{1,2,0:T(1,128)S(1)} %bitcast.129, bf16[1,1,16,64,256]{4,3,2,1,0:T(8,128)(2,1)} %bitcast.117, s32[]{:T(128)S(6)} %select_n.335), kind=kOutput, calls=%fused_computation.49 | convolution fusion | flops 1572864 | bytes 272388 | tf_op jit(solution)/shard_map/rnihd,rnhd->rnih/dot_general | solution.py:132
  62.0 1.6 %fusion.20 = bf16[1,1,256,8,64]{2,4,3,1,0:T(8,128)(2,1)S(1)} fusion(f32[1,1,256,16,64]{2,4,3,1,0:T(8,128)} %fusion.10, s32[]{:T(128)S(6)} %select_n.335, f32[256,8]{0,1:T(8,128)S(1)} %get-tuple-element.19, f32[8,64,64]{2,1,0:T(8,128)S(1)} %broadcast_in_dim_broadcast_in_dim_reshape.7, f32[16,64,64]{2,1,0:T(8,128)S(1)} %fusion.35, ...), kind=kOutput, calls=%fused_computation.28 | convolution fusion | flops 101122048 | bytes 1582592 | tf_op jit(solution)/shard_map/rnihd,rnhde->rnihe/dot_general | solution.py:129
  63.6 1.4 %fusion.21 = bf16[1,1,256,8,64]{2,4,3,1,0:T(8,128)(2,1)S(1)} fusion(f32[1,1,256,16,64]{2,4,3,1,0:T(8,128)S(1)} %copy-done.4, s32[]{:T(128)S(6)} %select_n.334, f32[256,8]{0,1:T(8,128)S(1)} %get-tuple-element.20, f32[8,64,64]{2,1,0:T(8,128)S(1)} %broadcast_in_dim_broadcast_in_dim_reshape.6, f32[16,64,64]{2,1,0:T(8,128)S(1)} %fusion.35, ...), kind=kOutput, calls=%fused_computation.29 | convolution fusion | flops 101122048 | bytes 1582592 | tf_op jit(solution)/shard_map/rnihd,rnhde->rnihe/dot_general | solution.py:129
  65.0 0.5 fusion.29
  65.5 1.3 %fusion.15 = bf16[1,256,1024]{2,1,0:T(8,128)(2,1)} fusion(f32[256,1024]{1,0:T(8,128)S(1)} %fusion.29, bf16[256,512]{0,1:T(8,128)(2,1)S(1)} %bitcast.120, bf16[1024,1024]{1,0:T(8,128)(2,1)S(1)} %copy-done, s32[]{:T(128)S(6)} %select_n.404), kind=kOutput, calls=%fused_computation.21 | convolution fusion | flops 268959744 | bytes 2883588 | tf_op jit(solution)/shard_map/rtd,de->rte/dot_general | solution.py:181
  (33 shorter events, 0.4 us)
Async XLA Ops:
  0.0 65.0 %copy-start = (bf16[1024,1024]{1,0:T(8,128)(2,1)S(1)}, bf16[1024,1024]{1,0:T(8,128)(2,1)}, u32[]{:S(2)}) copy-start(bf16[1024,1024]{1,0:T(8,128)(2,1)} %param.5) | copy-start | bytes 6291460
  3.8 1.0 %copy-start.1 = (bf16[2048,256]{1,0:T(8,128)(2,1)}, bf16[2048,256]{1,0:T(8,128)(2,1)S(1)}, u32[]{:S(2)}) copy-start(bf16[2048,256]{1,0:T(8,128)(2,1)S(1)} %fusion.2) | copy-start | bytes 3145732
  5.5 4.3 %collective-permute-start = (f32[8,33,128]{2,0,1:T(8,128)S(1)}, f32[8,33,128]{2,0,1:T(8,128)S(1)}, u32[]{:S(2)}, u32[]{:S(2)}) collective-permute-start(f32[8,33,128]{2,0,1:T(8,128)S(1)} %fusion.55), channel_id=1, source_target_pairs={{0,2},{2,0},{1,3},{3,1},{4,6},{6,4},{5,7},{7,5},{8,10},{10,8},{9,1... | collective-permute-start | bytes 405512 | tf_op jit(solution)/shard_map/ppermute | solution.py:22
  9.8 6.6 %collective-permute-start.1 = (f32[2,33,128]{2,0,1:T(2,128)S(1)}, f32[2,33,128]{2,0,1:T(2,128)S(1)}, u32[]{:S(2)}, u32[]{:S(2)}) collective-permute-start(f32[2,33,128]{2,0,1:T(2,128)S(1)} %get-tuple-element.16), channel_id=1, source_target_pairs={{0,8},{8,16},{16,24},{24,0},{1,9},{9,17},{17,25},{25,1},{2,10},{10... | collective-permute-start | bytes 101384 | tf_op jit(solution)/shard_map/ppermute | solution.py:22
  9.9 6.5 %collective-permute-start.2 = (f32[2,33,128]{2,0,1:T(2,128)S(1)}, f32[2,33,128]{2,0,1:T(2,128)S(1)}, u32[]{:S(2)}, u32[]{:S(2)}) collective-permute-start(f32[2,33,128]{2,0,1:T(2,128)S(1)} %get-tuple-element.18), channel_id=1, source_target_pairs={{0,16},{8,24},{16,0},{24,8},{1,17},{9,25},{17,1},{25,9},{2,18},{10... | collective-permute-start | bytes 101384 | tf_op jit(solution)/shard_map/ppermute | solution.py:22
  12.1 4.3 %collective-permute-start.3 = (f32[2,33,128]{2,0,1:T(2,128)S(1)}, f32[2,33,128]{2,0,1:T(2,128)S(1)}, u32[]{:S(2)}, u32[]{:S(2)}) collective-permute-start(f32[2,33,128]{2,0,1:T(2,128)S(1)} %get-tuple-element.17), channel_id=1, source_target_pairs={{0,24},{8,0},{16,8},{24,16},{1,25},{9,1},{17,9},{25,17},{2,26},{10... | collective-permute-start | bytes 101384 | tf_op jit(solution)/shard_map/ppermute | solution.py:22
  16.5 7.0 %collective-permute-start.4 = (f32[2,33,128]{2,0,1:T(2,128)S(1)}, f32[2,33,128]{2,0,1:T(2,128)S(1)}, u32[]{:S(2)}, u32[]{:S(2)}) collective-permute-start(f32[2,33,128]{2,0,1:T(2,128)S(1)} %add_add_fusion), channel_id=1, source_target_pairs={{0,32},{32,64},{64,96},{96,128},{128,160},{160,192},{192,224},{224... | collective-permute-start | bytes 101384 | tf_op jit(solution)/shard_map/ppermute | solution.py:22
  18.2 7.5 %collective-permute-start.5 = (f32[2,33,128]{2,0,1:T(2,128)S(1)}, f32[2,33,128]{2,0,1:T(2,128)S(1)}, u32[]{:S(2)}, u32[]{:S(2)}) collective-permute-start(f32[2,33,128]{2,0,1:T(2,128)S(1)} %add_add_fusion), channel_id=1, source_target_pairs={{0,224},{32,0},{64,32},{96,64},{128,96},{160,128},{192,160},{224,1... | collective-permute-start | bytes 101384 | tf_op jit(solution)/shard_map/ppermute | solution.py:22
  23.5 5.0 %collective-permute-start.6 = (f32[2,33,128]{2,0,1:T(2,128)S(1)}, f32[2,33,128]{2,0,1:T(2,128)S(1)}, u32[]{:S(2)}, u32[]{:S(2)}) collective-permute-start(f32[2,33,128]{2,0,1:T(2,128)S(1)} %collective-permute-done.4), channel_id=1, source_target_pairs={{0,32},{32,64},{64,96},{96,128},{128,160},{160,192},{192,224},{224... | collective-permute-start | bytes 101384 | tf_op jit(solution)/shard_map/ppermute | solution.py:22
  23.5 5.0 %copy-start.2 = (bf16[2048,256]{1,0:T(8,128)(2,1)S(1)}, bf16[2048,256]{1,0:T(8,128)(2,1)}, u32[]{:S(2)}) copy-start(bf16[2048,256]{1,0:T(8,128)(2,1)} %copy-done.1) | copy-start | bytes 3145732
  25.7 4.2 %collective-permute-start.7 = (f32[2,33,128]{2,0,1:T(2,128)S(1)}, f32[2,33,128]{2,0,1:T(2,128)S(1)}, u32[]{:S(2)}, u32[]{:S(2)}) collective-permute-start(f32[2,33,128]{2,0,1:T(2,128)S(1)} %collective-permute-done.5), channel_id=1, source_target_pairs={{0,224},{32,0},{64,32},{96,64},{128,96},{160,128},{192,160},{224,1... | collective-permute-start | bytes 101384 | tf_op jit(solution)/shard_map/ppermute | solution.py:22
  28.5 4.1 %collective-permute-start.8 = (f32[2,33,128]{2,0,1:T(2,128)S(1)}, f32[2,33,128]{2,0,1:T(2,128)S(1)}, u32[]{:S(2)}, u32[]{:S(2)}) collective-permute-start(f32[2,33,128]{2,0,1:T(2,128)S(1)} %collective-permute-done.6), channel_id=1, source_target_pairs={{0,32},{32,64},{64,96},{96,128},{128,160},{160,192},{192,224},{224... | collective-permute-start | bytes 101384 | tf_op jit(solution)/shard_map/ppermute | solution.py:22
  29.9 3.7 %collective-permute-start.9 = (f32[2,33,128]{2,0,1:T(2,128)S(1)}, f32[2,33,128]{2,0,1:T(2,128)S(1)}, u32[]{:S(2)}, u32[]{:S(2)}) collective-permute-start(f32[2,33,128]{2,0,1:T(2,128)S(1)} %collective-permute-done.7), channel_id=1, source_target_pairs={{0,224},{32,0},{64,32},{96,64},{128,96},{160,128},{192,160},{224,1... | collective-permute-start | bytes 101384 | tf_op jit(solution)/shard_map/ppermute | solution.py:22
  32.6 4.1 %collective-permute-start.10 = (f32[2,33,128]{2,0,1:T(2,128)S(1)}, f32[2,33,128]{2,0,1:T(2,128)}, u32[]{:S(2)}, u32[]{:S(2)}) collective-permute-start(f32[2,33,128]{2,0,1:T(2,128)S(1)} %collective-permute-done.8), channel_id=1, source_target_pairs={{0,32},{32,64},{64,96},{96,128},{128,160},{160,192},{192,224},{224... | collective-permute-start | bytes 101384 | tf_op jit(solution)/shard_map/ppermute | solution.py:22
  36.8 4.2 %collective-permute-start.11 = (f32[2,33,128]{2,0,1:T(2,128)S(1)}, f32[2,33,128]{2,0,1:T(2,128)S(1)}, u32[]{:S(2)}, u32[]{:S(2)}) collective-permute-start(f32[2,33,128]{2,0,1:T(2,128)S(1)} %select_add_fusion.5), channel_id=1, source_target_pairs={{0,8},{8,16},{16,24},{24,0},{1,9},{9,17},{17,25},{25,1},{2,10},{10... | collective-permute-start | bytes 101384 | tf_op jit(solution)/shard_map/ppermute | solution.py:22
  37.5 4.4 %collective-permute-start.12 = (f32[2,33,128]{2,0,1:T(2,128)S(1)}, f32[2,33,128]{2,0,1:T(2,128)S(1)}, u32[]{:S(2)}, u32[]{:S(2)}) collective-permute-start(f32[2,33,128]{2,0,1:T(2,128)S(1)} %get-tuple-element.15), channel_id=1, source_target_pairs={{0,16},{8,24},{16,0},{24,8},{1,17},{9,25},{17,1},{25,9},{2,18},{10... | collective-permute-start | bytes 101384 | tf_op jit(solution)/shard_map/ppermute | solution.py:22
  39.2 2.8 %collective-permute-start.13 = (f32[2,33,128]{2,0,1:T(2,128)S(1)}, f32[2,33,128]{2,0,1:T(2,128)S(1)}, u32[]{:S(2)}, u32[]{:S(2)}) collective-permute-start(f32[2,33,128]{2,0,1:T(2,128)S(1)} %get-tuple-element.14), channel_id=1, source_target_pairs={{0,24},{8,0},{16,8},{24,16},{1,25},{9,1},{17,9},{25,17},{2,26},{10... | collective-permute-start | bytes 101384 | tf_op jit(solution)/shard_map/ppermute | solution.py:22
  42.9 5.5 %collective-permute-start.14 = (f32[8,33,128]{2,0,1:T(8,128)S(1)}, f32[8,33,128]{2,0,1:T(8,128)S(1)}, u32[]{:S(2)}, u32[]{:S(2)}) collective-permute-start(f32[8,33,128]{2,0,1:T(8,128)S(1)} %select_add_fusion.1), channel_id=1, source_target_pairs={{0,4},{4,0},{1,5},{5,1},{2,6},{6,2},{3,7},{7,3},{8,12},{12,8},{9,1... | collective-permute-start | bytes 405512 | tf_op jit(solution)/shard_map/ppermute | solution.py:22
  48.4 9.6 %collective-permute-start.15 = (f32[8,33,128]{2,1,0:T(8,128)S(1)}, f32[8,33,128]{2,1,0:T(8,128)S(1)}, u32[]{:S(2)}, u32[]{:S(2)}) collective-permute-start(f32[8,33,128]{2,1,0:T(8,128)S(1)} %copy.9), channel_id=1, source_target_pairs={{0,2},{2,0},{1,3},{3,1},{4,6},{6,4},{5,7},{7,5},{8,10},{10,8},{9,1... | collective-permute-start | bytes 405512 | tf_op jit(solution)/shard_map/ppermute | solution.py:22
  58.0 0.7 %copy-start.3 = (f32[8,33,128]{2,1,0:T(8,128)}, f32[8,33,128]{2,1,0:T(8,128)S(1)}, u32[]{:S(2)}) copy-start(f32[8,33,128]{2,1,0:T(8,128)S(1)} %collective-permute-done.15) | copy-start | bytes 405508
  58.8 4.8 %copy-start.4 = (f32[1,1,256,16,64]{2,4,3,1,0:T(8,128)S(1)}, f32[1,1,256,16,64]{2,4,3,1,0:T(8,128)}, u32[]{:S(2)}) copy-start(f32[1,1,256,16,64]{2,4,3,1,0:T(8,128)} %fusion.10) | copy-start | bytes 3145732

commit v12 on v11

--- a/solution.py
+++ b/solution.py
@@ -125,13 +125,13 @@
     rows, count, span, heads, dim = pq.shape
     before_kv = jnp.cumsum(kv_blocks, axis=1) - kv_blocks + prior_kv[:, None]
     before_k = jnp.cumsum(k_blocks, axis=1) - k_blocks + prior_k[:, None]
+    high = before_kv.astype(jnp.bfloat16)
+    low = (before_kv - high.astype(jnp.float32)).astype(jnp.bfloat16)
+    carried = jnp.einsum("rnihd,rnhde->rnihe", pq, high, preferred_element_type=jnp.float32)
+    carried = carried + jnp.einsum("rnihd,rnhde->rnihe", pq, low, preferred_element_type=jnp.float32)
+    num = num_local + carried
     pq32 = pq.astype(jnp.float32)
-    num = num_local + jnp.einsum(
-        "rnihd,rnhde->rnihe", pq32, before_kv, precision=lax.Precision.HIGHEST
-    )
-    den = jnp.transpose(den_local, (0, 1, 3, 2)) + jnp.einsum(
-        "rnihd,rnhd->rnih", pq32, before_k, precision=lax.Precision.HIGHEST
-    )
+    den = jnp.transpose(den_local, (0, 1, 3, 2)) + jnp.sum(pq32 * before_k[:, :, None], axis=-1)
     result = (num / den[..., None]).astype(jnp.bfloat16)
     return result.reshape(rows, count * span, heads * dim)
 

time: 67.1 us -> 81.4 us (1.21)
  other arithmetic: 0.88 us -> 9.1 us
  local copies, waits for them, and re-layouts: 3.48 us -> 11.5 us
  matrix products: 18.1 us -> 16.6 us
  waiting for transfers between devices: 11.8 us -> 10.4 us
    add x6, other arithmetic: 0.27 us -> 3.41 us  [tmap(): return jax.tree.map(f, *trees)]
    another operation x2, other arithmetic: 0.19 us -> 3.06 us  [entering(): jnp.stack(p)[order].reshape((-1,) + p[0].shape[1:])]
    another operation x2, local copies, waits for them, and re-layouts: 0.2 us -> 2.7 us  [finish(): before_kv = jnp.cumsum(kv_blocks, axis=1) - kv_blocks + prior_kv[:, None]]
    gather x2, local copies, waits for them, and re-layouts: 0.74 us -> 3.2 us  [entering(): jnp.stack(p)[order].reshape((-1,) + p[0].shape[1:])]
    slice x3, local copies, waits for them, and re-layouts: 0.05 us -> 2.25 us  [heads_of(): prior_kv = prior[:, :rows_kv].reshape((half_heads,) + total_kv.shape[1:])]
    ppermute x16, waiting for transfers between devices: 11.8 us -> 10.4 us  [send(): return tmap(lambda t: lax.ppermute(t, axis, perm=pairs), tree)]
    dot_general x4, matrix products: 5.28 us -> 4.12 us  [the longest x2 2.48 us: finish(): jnp.einsum('rnihd,rnhde->rnihe', pq, high, preferred_element_type=jnp.flo...]
  transfers between devices with their start and end apart: 16 -> 16, of which waited for: 9 -> 7; matrix products, arithmetic and copies ran while one was open for 11% -> 15% of each run, Pallas kernels for 0% -> 0%
where the time goes in v12:
time: 81.4 us; the launch traced here: 80.6 us
  starting transfers between devices  32.9 us (40%)
  matrix products  16.6 us (20%)
  local copies, waits for them, and re-layouts  11.5 us (14%)
  waiting for transfers between devices  10.4 us (13%)
  other arithmetic  9.1 us (11%)
    ppermute x16, starting transfers between devices, send(): return tmap(lambda t: lax.ppermute(t, axis, perm=pairs), tree)  32.9 us
    ppermute x16, waiting for transfers between devices, send(): return tmap(lambda t: lax.ppermute(t, axis, perm=pairs), tree)  10.4 us
    dot_general x2, matrix products, project(): jnp.einsum('rtd,de->ret', frames_in, w, preferred_element_type=jnp.float32)  6.23 us
    add x6, other arithmetic, tmap(): return jax.tree.map(f, *trees)  3.41 us
    gather x2, local copies, waits for them, and re-layouts, entering(): jnp.stack(p)[order].reshape((-1,) + p[0].shape[1:])  3.2 us
    another operation x2, other arithmetic, entering(): jnp.stack(p)[order].reshape((-1,) + p[0].shape[1:])  3.06 us
    another operation x2, local copies, waits for them, and re-layouts, finish(): before_kv = jnp.cumsum(kv_blocks, axis=1) - kv_blocks + prior_kv[:, None]  2.7 us
    dot_general x1, matrix products, block_terms(): jnp.einsum('rnihd,rnjhd->rnhij', pq, pk, preferred_element_type=jnp.float32)  2.67 us
  transfers between devices with their start and end apart: 16, of which 7 were waited for; matrix products, arithmetic and copies ran while one was open for 15% of the time, Pallas kernels for 0%

profile of v12, /device:TPU:1, one launch (start us, length us, event | category | flops | bytes accessed | tf_op | source)
XLA Modules:
  0.0 80.6 jit_solution(7800369116406281609)
XLA Ops:
  0.0 3.8 %fusion.2 = bf16[2048,256]{1,0:T(8,128)(2,1)S(1)} fusion(bf16[1024,3072]{1,0:T(8,128)(2,1)} %param.4, bf16[1,256,1024]{2,1,0:T(8,128)(2,1)} %param.3), kind=kOutput, calls=%fused_computation.5 | convolution fusion | flops 1074266112 | bytes 5767168 | tf_op jit(solution)/shard_map/rtd,de->ret/dot_general | solution.py:149
  3.8 0.4 fusion.39
  4.2 0.6 copy-done.4
  4.8 0.3 convert_reduce_fusion
  5.7 3.3 %collective-permute-start = (f32[8,33,128]{2,0,1:T(8,128)S(1)}, f32[8,33,128]{2,0,1:T(8,128)S(1)}, u32[]{:S(2)}, u32[]{:S(2)}) collective-permute-start(f32[8,33,128]{2,0,1:T(8,128)S(1)} %fusion.53), channel_id=1, source_target_pairs={{0,2},{2,0},{1,3},{3,1},{4,6},{6,4},{5,7},{7,5},{8,10},{10,8},{9,1... | collective-permute-start | bytes 405512 | tf_op jit(solution)/shard_map/ppermute | solution.py:22
  9.0 1.0 %collective-permute-done = f32[8,33,128]{2,0,1:T(8,128)S(1)} collective-permute-done((f32[8,33,128]{2,0,1:T(8,128)S(1)}, f32[8,33,128]{2,0,1:T(8,128)S(1)}, u32[]{:S(2)}, u32[]{:S(2)}) %collective-permute-start) | collective-permute-done | bytes 135200 | tf_op jit(solution)/shard_map/ppermute | solution.py:22
  10.1 0.7 constant_dynamic-slice_fusion.4
  10.7 2.2 %collective-permute-start.2 = (f32[2,33,128]{2,0,1:T(2,128)}, f32[2,33,128]{2,0,1:T(2,128)}, u32[]{:S(2)}, u32[]{:S(2)}) collective-permute-start(f32[2,33,128]{2,0,1:T(2,128)} %get-tuple-element.20), channel_id=1, source_target_pairs={{0,16},{8,24},{16,0},{24,8},{1,17},{9,25},{17,1},{25,9},{2,18},{10... | collective-permute-start | bytes 101384 | tf_op jit(solution)/shard_map/ppermute | solution.py:22
  12.9 1.1 %collective-permute-start.3 = (f32[2,33,128]{2,0,1:T(2,128)}, f32[2,33,128]{2,0,1:T(2,128)}, u32[]{:S(2)}, u32[]{:S(2)}) collective-permute-start(f32[2,33,128]{2,0,1:T(2,128)} %get-tuple-element.19), channel_id=1, source_target_pairs={{0,24},{8,0},{16,8},{24,16},{1,25},{9,1},{17,9},{25,17},{2,26},{10... | collective-permute-start | bytes 101384 | tf_op jit(solution)/shard_map/ppermute | solution.py:22
  14.0 2.5 %fusion.28 = bf16[1024,256]{1,0:T(8,128)(2,1)S(1)} fusion(bf16[1024,3072]{1,0:T(8,128)(2,1)} %param.4, bf16[1,256,1024]{2,1,0:T(8,128)(2,1)} %param.3), kind=kOutput, calls=%fused_computation.36 | convolution fusion | flops 538705920 | bytes 3145728 | tf_op jit(solution)/shard_map/rtd,de->ret/dot_general | solution.py:149
  16.5 0.8 %add_add_fusion = f32[2,33,128]{2,0,1:T(2,128)S(1)} fusion(f32[2,33,128]{2,0,1:T(2,128)} %collective-permute-done.3, f32[2,33,128]{2,0,1:T(2,128)} %collective-permute-done.2, f32[2,33,128]{2,0,1:T(2,128)} %collective-permute-done.1, f32[8,33,128]{2,0,1:T(8,128)S(1)} %select_add_fusion.2, s32[]{:T(128)S(6)} %select_n.338), kind=kLoop, calls=%fused_computation.86 | loop fusion | flops 25344 | bytes 168964 | tf_op jit(solution)/shard_map/add | solution.py:18
  17.4 1.7 %collective-permute-start.4 = (f32[2,33,128]{2,0,1:T(2,128)S(1)}, f32[2,33,128]{2,0,1:T(2,128)S(1)}, u32[]{:S(2)}, u32[]{:S(2)}) collective-permute-start(f32[2,33,128]{2,0,1:T(2,128)S(1)} %add_add_fusion), channel_id=1, source_target_pairs={{0,32},{32,64},{64,96},{96,128},{128,160},{160,192},{192,224},{224... | collective-permute-start | bytes 101384 | tf_op jit(solution)/shard_map/ppermute | solution.py:22
  19.1 4.0 %collective-permute-start.5 = (f32[2,33,128]{2,0,1:T(2,128)S(1)}, f32[2,33,128]{2,0,1:T(2,128)S(1)}, u32[]{:S(2)}, u32[]{:S(2)}) collective-permute-start(f32[2,33,128]{2,0,1:T(2,128)S(1)} %add_add_fusion), channel_id=1, source_target_pairs={{0,224},{32,0},{64,32},{96,64},{128,96},{160,128},{192,160},{224,1... | collective-permute-start | bytes 101384 | tf_op jit(solution)/shard_map/ppermute | solution.py:22
  23.1 1.2 %collective-permute-done.4 = f32[2,33,128]{2,0,1:T(2,128)S(1)} collective-permute-done((f32[2,33,128]{2,0,1:T(2,128)S(1)}, f32[2,33,128]{2,0,1:T(2,128)S(1)}, u32[]{:S(2)}, u32[]{:S(2)}) %collective-permute-start.4) | collective-permute-done | bytes 33824 | tf_op jit(solution)/shard_map/ppermute | solution.py:22
  24.3 2.7 %select_reduce_fusion = (f32[16,256]{1,0:T(8,128)}, bf16[16,256,256]{1,2,0:T(8,128)(2,1)S(1)}) fusion(pred[256,256]{0,1:T(8,128)(4,1)S(1)} %iota_compare_fusion, bf16[256,16,64]{0,2,1:T(8,128)(2,1)S(1)} %bitcast.109, bf16[1,256,2,16,64]{1,4,3,2,0:T(8,128)(2,1)} %bitcast.121), kind=kOutput, calls=%fused_computation.3 | convolution fusion | flops 138932224 | bytes 3227648 | tf_op jit(solution)/shard_map/rnihd,rnjhd->rnhij/dot_general | solution.py:113
  27.0 2.7 %collective-permute-start.7 = (f32[2,33,128]{2,0,1:T(2,128)S(1)}, f32[2,33,128]{2,0,1:T(2,128)}, u32[]{:S(2)}, u32[]{:S(2)}) collective-permute-start(f32[2,33,128]{2,0,1:T(2,128)S(1)} %collective-permute-done.5), channel_id=1, source_target_pairs={{0,224},{32,0},{64,32},{96,64},{128,96},{160,128},{192,160},{224,1... | collective-permute-start | bytes 101384 | tf_op jit(solution)/shard_map/ppermute | solution.py:22
  29.7 1.5 %fusion.10 = f32[1,1,256,16,64]{2,4,3,1,0:T(8,128)} fusion(bf16[16,256,256]{1,2,0:T(8,128)(2,1)S(1)} %get-tuple-element.26, pred[256,256]{0,1:T(8,128)(4,1)S(1)} %iota_compare_fusion, bf16[1,256,2,16,64]{1,4,3,2,0:T(8,128)(2,1)S(1)} %bitcast.122), kind=kOutput, calls=%fused_computation.17 | convolution fusion | flops 135266304 | bytes 3735552 | tf_op jit(solution)/shard_map/rnhij,rnjhd->rnihd/dot_general | solution.py:118
  31.2 2.7 %collective-permute-start.9 = (f32[2,33,128]{2,0,1:T(2,128)}, f32[2,33,128]{2,0,1:T(2,128)}, u32[]{:S(2)}, u32[]{:S(2)}) collective-permute-start(f32[2,33,128]{2,0,1:T(2,128)} %collective-permute-done.7), channel_id=1, source_target_pairs={{0,224},{32,0},{64,32},{96,64},{128,96},{160,128},{192,160},{224,1... | collective-permute-start | bytes 101384 | tf_op jit(solution)/shard_map/ppermute | solution.py:22
  33.9 0.6 fusion.74
  34.5 0.7 collective-permute-done.9
  35.3 3.0 %collective-permute-done.10 = f32[2,33,128]{2,0,1:T(2,128)} collective-permute-done((f32[2,33,128]{2,0,1:T(2,128)}, f32[2,33,128]{2,0,1:T(2,128)}, u32[]{:S(2)}, u32[]{:S(2)}) %collective-permute-start.10) | collective-permute-done | bytes 33824 | tf_op jit(solution)/shard_map/ppermute | solution.py:22
  38.3 0.7 select_add_fusion.5
  39.0 1.2 %collective-permute-start.11 = (f32[2,33,128]{2,0,1:T(2,128)}, f32[2,33,128]{2,0,1:T(2,128)}, u32[]{:S(2)}, u32[]{:S(2)}) collective-permute-start(f32[2,33,128]{2,0,1:T(2,128)} %select_add_fusion.5), channel_id=1, source_target_pairs={{0,8},{8,16},{16,24},{24,0},{1,9},{9,17},{17,25},{25,1},{2,10},{10... | collective-permute-start | bytes 101384 | tf_op jit(solution)/shard_map/ppermute | solution.py:22
  40.2 1.5 %add_bitcast_fusion = (f32[1,2,33,128]{3,1,2,0:T(2,128)}, f32[2,33,128]{2,0,1:T(2,128)}, f32[2,33,128]{2,0,1:T(2,128)}) fusion(f32[2,33,128]{2,0,1:T(2,128)} %collective-permute-done.3, f32[2,33,128]{2,0,1:T(2,128)} %collective-permute-done.2, f32[2,33,128]{2,0,1:T(2,128)} %collective-permute-done.1, f32[2,33,128]{2,0,1:T(2,128)S(1)} %select_add_fusion.6, ...), kind=kLoop, calls=%fused_computation.84 | loop fusion | flops 202752 | bytes 270352 | tf_op jit(solution)/shard_map/stack | solution.py:98
  41.7 1.8 %collective-permute-start.12 = (f32[2,33,128]{2,0,1:T(2,128)}, f32[2,33,128]{2,0,1:T(2,128)}, u32[]{:S(2)}, u32[]{:S(2)}) collective-permute-start(f32[2,33,128]{2,0,1:T(2,128)} %get-tuple-element.17), channel_id=1, source_target_pairs={{0,16},{8,24},{16,0},{24,8},{1,17},{9,25},{17,1},{25,9},{2,18},{10... | collective-permute-start | bytes 101384 | tf_op jit(solution)/shard_map/ppermute | solution.py:22
  43.5 0.9 %collective-permute-start.13 = (f32[2,33,128]{2,0,1:T(2,128)}, f32[2,33,128]{2,0,1:T(2,128)}, u32[]{:S(2)}, u32[]{:S(2)}) collective-permute-start(f32[2,33,128]{2,0,1:T(2,128)} %get-tuple-element.16), channel_id=1, source_target_pairs={{0,24},{8,0},{16,8},{24,16},{1,25},{9,1},{17,9},{25,17},{2,26},{10... | collective-permute-start | bytes 101384 | tf_op jit(solution)/shard_map/ppermute | solution.py:22
  44.4 0.7 pad_clamp_fusion
  45.1 1.2 %collective-permute-done.12 = f32[2,33,128]{2,0,1:T(2,128)} collective-permute-done((f32[2,33,128]{2,0,1:T(2,128)}, f32[2,33,128]{2,0,1:T(2,128)}, u32[]{:S(2)}, u32[]{:S(2)}) %collective-permute-start.12) | collective-permute-done | bytes 33824 | tf_op jit(solution)/shard_map/ppermute | solution.py:22
  46.6 1.5 %pad_maximum_fusion = f32[4,2,33,128]{3,1,2,0:T(2,128)} fusion(f32[1,2,33,128]{3,1,2,0:T(2,128)} %bitcast.16, f32[1,2,33,128]{3,1,2,0:T(2,128)} %bitcast.15, f32[1,2,33,128]{3,1,2,0:T(2,128)} %bitcast.14, f32[1,2,33,128]{3,1,2,0:T(2,128)} %get-tuple-element.15), kind=kLoop, calls=%fused_computation.75 | loop fusion | flops 101376 | bytes 270336 | tf_op jit(solution)/shard_map/stack | solution.py:98
  48.1 2.2 %gather_fusion = f32[4,2,33,128]{3,1,2,0:T(2,128)} fusion(f32[4,2,33,128]{3,1,2,0:T(2,128)} %pad_maximum_fusion, s32[1024]{0:T(1024)S(1)} %pad_clamp_fusion), kind=kCustom, calls=%fused_computation | custom fusion | bytes 270352 | tf_op jit(solution)/shard_map/gather | solution.py:98
  50.4 1.0 %copy.6 = f32[4,2,33,128]{3,1,0,2:T(2,128)S(1)} copy(f32[4,2,33,128]{3,1,2,0:T(2,128)} %gather_fusion) | data formatting | bytes 270336 | tf_op jit(solution)/shard_map/gather | solution.py:98
  51.4 0.7 select_add_fusion.1
  52.1 2.7 %collective-permute-start.14 = (f32[8,33,128]{2,0,1:T(8,128)}, f32[8,33,128]{2,0,1:T(8,128)}, u32[]{:S(2)}, u32[]{:S(2)}) collective-permute-start(f32[8,33,128]{2,0,1:T(8,128)} %select_add_fusion.1), channel_id=1, source_target_pairs={{0,4},{4,0},{1,5},{5,1},{2,6},{6,2},{3,7},{7,3},{8,12},{12,8},{9,1... | collective-permute-start | bytes 405512 | tf_op jit(solution)/shard_map/ppermute | solution.py:22
  54.8 2.9 %collective-permute-done.14 = f32[8,33,128]{2,0,1:T(8,128)} collective-permute-done((f32[8,33,128]{2,0,1:T(8,128)}, f32[8,33,128]{2,0,1:T(8,128)}, u32[]{:S(2)}, u32[]{:S(2)}) %collective-permute-start.14) | collective-permute-done | bytes 135200 | tf_op jit(solution)/shard_map/ppermute | solution.py:22
  57.7 1.1 %select_add_fusion = (f32[8,33,128]{2,0,1:T(8,128)S(1)}, f32[8,33,128]{2,0,1:T(8,128)S(1)}) fusion(pred[]{:T(512)S(6)} %eq.33, f32[8,33,128]{2,0,1:T(8,128)} %bitcast.116, f32[8,33,128]{2,0,1:T(8,128)} %collective-permute-done.14, s32[]{:T(128)S(6)} %select_n.334, f32[16,1,128]{2,0,1:T(8,128)S(1)} %pad_bitcast_fusion, f32[16,32,128]{2,0,1:T(8,128)S(1)} %copy.4, ...), kind=kLoop, calls=%fused_computation.76 | loop fusion | flops 202752 | bytes 946181 | tf_op jit(solution)/shard_map/add | solution.py:18
  58.8 0.7 copy.10
  59.5 8.5 %collective-permute-start.15 = (f32[8,33,128]{2,1,0:T(8,128)}, f32[8,33,128]{2,1,0:T(8,128)}, u32[]{:S(2)}, u32[]{:S(2)}) collective-permute-start(f32[8,33,128]{2,1,0:T(8,128)} %copy.10), channel_id=1, source_target_pairs={{0,2},{2,0},{1,3},{3,1},{4,6},{6,4},{5,7},{7,5},{8,10},{10,8},{9,1... | collective-permute-start | bytes 405512 | tf_op jit(solution)/shard_map/ppermute | solution.py:22
  68.0 0.7 copy.7
  68.7 1.0 %broadcast_in_dim_broadcast_in_dim_reshape.6 = f32[8,64,64]{2,1,0:T(8,128)S(1)} reshape(f32[8,32,128]{2,1,0:T(8,128)} %copy.7) | data formatting | bytes 262144 | tf_op jit(solution)/shard_map/broadcast_in_dim;broadcast_in_dim;reshape | solution.py:126
  69.7 1.1 %fusion.47 = f32[8,64,256]{2,1,0:T(8,128)} fusion(bf16[1,1,16,64,256]{4,3,2,1,0:T(8,128)(2,1)S(1)} %bitcast.110, s32[]{:T(128)S(6)} %select_n.334, f32[8,64,64]{2,1,0:T(8,128)S(1)} %broadcast_in_dim_broadcast_in_dim_reshape.6, f32[16,64,64]{2,1,0:T(8,128)S(1)} %fusion.39), kind=kOutput, calls=%fused_computation.59 | convolution fusion | flops 16875520 | bytes 1311744 | tf_op jit(solution)/shard_map/rnihd,rnhde->rnihe/dot_general | solution.py:130
  70.8 1.6 %slice.38 = f32[8,32,128]{2,1,0:T(8,128)} slice(f32[8,33,128]{2,1,0:T(8,128)} %collective-permute-done.15), slice={[0:8], [0:32], [0:128]} | slice | bytes 262144 | tf_op jit(solution)/shard_map/slice | solution.py:174
  72.4 1.7 %broadcast_in_dim_broadcast_in_dim_reshape.7 = f32[8,64,64]{2,1,0:T(8,128)} reshape(f32[8,32,128]{2,1,0:T(8,128)} %slice.38) | data formatting | bytes 262144 | tf_op jit(solution)/shard_map/broadcast_in_dim;broadcast_in_dim;reshape | solution.py:126
  74.1 1.3 %fusion.43 = f32[8,64,256]{2,1,0:T(8,128)S(1)} fusion(bf16[1,1,16,64,256]{4,3,2,1,0:T(8,128)(2,1)S(1)} %bitcast.111, s32[]{:T(128)S(6)} %select_n.335, f32[8,64,64]{2,1,0:T(8,128)} %broadcast_in_dim_broadcast_in_dim_reshape.7, f32[16,64,64]{2,1,0:T(8,128)S(1)} %fusion.39), kind=kOutput, calls=%fused_computation.55 | convolution fusion | flops 16973824 | bytes 1180672 | tf_op jit(solution)/shard_map/rnihd,rnhde->rnihe/dot_general | solution.py:131
  75.4 0.8 slice.39
  76.4 0.7 fusion.61
  77.2 1.4 %fusion.22 = bf16[1,1,256,8,64]{2,4,3,1,0:T(8,128)(2,1)S(1)} fusion(f32[8,64,256]{2,1,0:T(8,128)S(1)} %fusion.43, f32[1,1,256,16,64]{2,4,3,1,0:T(8,128)} %fusion.10, s32[]{:T(128)S(6)} %select_n.335, f32[256,8]{0,1:T(8,128)S(1)} %get-tuple-element.21, bf16[1,1,16,64,256]{4,3,2,1,0:T(8,128)(2,1)S(1)} %bitcast.113, ...), kind=kOutput, calls=%fused_computation.30 | convolution fusion | flops 17399808 | bytes 1975808 | tf_op jit(solution)/shard_map/rnihd,rnhde->rnihe/dot_general | solution.py:130
  78.9 0.5 fusion.31
  79.4 1.3 %fusion.15 = bf16[1,256,1024]{2,1,0:T(8,128)(2,1)} fusion(f32[256,1024]{1,0:T(8,128)S(1)} %fusion.31, bf16[256,512]{0,1:T(8,128)(2,1)S(1)} %bitcast.117, bf16[1024,1024]{1,0:T(8,128)(2,1)S(1)} %copy-done, s32[]{:T(128)S(6)} %select_n.404), kind=kOutput, calls=%fused_computation.21 | convolution fusion | flops 268959744 | bytes 2883588 | tf_op jit(solution)/shard_map/rtd,de->rte/dot_general | solution.py:181
  (48 shorter events, 1.6 us)
Async XLA Ops:
  0.0 78.9 %copy-start = (bf16[1024,1024]{1,0:T(8,128)(2,1)S(1)}, bf16[1024,1024]{1,0:T(8,128)(2,1)}, u32[]{:S(2)}) copy-start(bf16[1024,1024]{1,0:T(8,128)(2,1)} %param.5) | copy-start | bytes 6291460
  3.8 1.0 %copy-start.4 = (bf16[2048,256]{1,0:T(8,128)(2,1)}, bf16[2048,256]{1,0:T(8,128)(2,1)S(1)}, u32[]{:S(2)}) copy-start(bf16[2048,256]{1,0:T(8,128)(2,1)S(1)} %fusion.2) | copy-start | bytes 3145732
  5.1 0.6 copy-start.6
  5.7 4.3 %collective-permute-start = (f32[8,33,128]{2,0,1:T(8,128)S(1)}, f32[8,33,128]{2,0,1:T(8,128)S(1)}, u32[]{:S(2)}, u32[]{:S(2)}) collective-permute-start(f32[8,33,128]{2,0,1:T(8,128)S(1)} %fusion.53), channel_id=1, source_target_pairs={{0,2},{2,0},{1,3},{3,1},{4,6},{6,4},{5,7},{7,5},{8,10},{10,8},{9,1... | collective-permute-start | bytes 405512 | tf_op jit(solution)/shard_map/ppermute | solution.py:22
  10.0 2.9 %copy-start.2 = (f32[8,33,128]{2,0,1:T(8,128)}, f32[8,33,128]{2,0,1:T(8,128)S(1)}, u32[]{:S(2)}) copy-start(f32[8,33,128]{2,0,1:T(8,128)S(1)} %collective-permute-done) | copy-start | bytes 405508
  10.7 5.8 %collective-permute-start.1 = (f32[2,33,128]{2,0,1:T(2,128)}, f32[2,33,128]{2,0,1:T(2,128)}, u32[]{:S(2)}, u32[]{:S(2)}) collective-permute-start(f32[2,33,128]{2,0,1:T(2,128)} %get-tuple-element.18), channel_id=1, source_target_pairs={{0,8},{8,16},{16,24},{24,0},{1,9},{9,17},{17,25},{25,1},{2,10},{10... | collective-permute-start | bytes 101384 | tf_op jit(solution)/shard_map/ppermute | solution.py:22
  10.7 5.8 %collective-permute-start.2 = (f32[2,33,128]{2,0,1:T(2,128)}, f32[2,33,128]{2,0,1:T(2,128)}, u32[]{:S(2)}, u32[]{:S(2)}) collective-permute-start(f32[2,33,128]{2,0,1:T(2,128)} %get-tuple-element.20), channel_id=1, source_target_pairs={{0,16},{8,24},{16,0},{24,8},{1,17},{9,25},{17,1},{25,9},{2,18},{10... | collective-permute-start | bytes 101384 | tf_op jit(solution)/shard_map/ppermute | solution.py:22
  12.9 3.6 %collective-permute-start.3 = (f32[2,33,128]{2,0,1:T(2,128)}, f32[2,33,128]{2,0,1:T(2,128)}, u32[]{:S(2)}, u32[]{:S(2)}) collective-permute-start(f32[2,33,128]{2,0,1:T(2,128)} %get-tuple-element.19), channel_id=1, source_target_pairs={{0,24},{8,0},{16,8},{24,16},{1,25},{9,1},{17,9},{25,17},{2,26},{10... | collective-permute-start | bytes 101384 | tf_op jit(solution)/shard_map/ppermute | solution.py:22
  17.4 7.0 %collective-permute-start.4 = (f32[2,33,128]{2,0,1:T(2,128)S(1)}, f32[2,33,128]{2,0,1:T(2,128)S(1)}, u32[]{:S(2)}, u32[]{:S(2)}) collective-permute-start(f32[2,33,128]{2,0,1:T(2,128)S(1)} %add_add_fusion), channel_id=1, source_target_pairs={{0,32},{32,64},{64,96},{96,128},{128,160},{160,192},{192,224},{224... | collective-permute-start | bytes 101384 | tf_op jit(solution)/shard_map/ppermute | solution.py:22
  19.1 7.9 %collective-permute-start.5 = (f32[2,33,128]{2,0,1:T(2,128)S(1)}, f32[2,33,128]{2,0,1:T(2,128)S(1)}, u32[]{:S(2)}, u32[]{:S(2)}) collective-permute-start(f32[2,33,128]{2,0,1:T(2,128)S(1)} %add_add_fusion), channel_id=1, source_target_pairs={{0,224},{32,0},{64,32},{96,64},{128,96},{160,128},{192,160},{224,1... | collective-permute-start | bytes 101384 | tf_op jit(solution)/shard_map/ppermute | solution.py:22
  24.3 2.7 %copy-start.8 = (f32[2,33,128]{2,0,1:T(2,128)}, f32[2,33,128]{2,0,1:T(2,128)S(1)}, u32[]{:S(2)}) copy-start(f32[2,33,128]{2,0,1:T(2,128)S(1)} %collective-permute-done.4) | copy-start | bytes 101380
  24.3 5.4 %collective-permute-start.6 = (f32[2,33,128]{2,0,1:T(2,128)S(1)}, f32[2,33,128]{2,0,1:T(2,128)S(1)}, u32[]{:S(2)}, u32[]{:S(2)}) collective-permute-start(f32[2,33,128]{2,0,1:T(2,128)S(1)} %collective-permute-done.4), channel_id=1, source_target_pairs={{0,32},{32,64},{64,96},{96,128},{128,160},{160,192},{192,224},{224... | collective-permute-start | bytes 101384 | tf_op jit(solution)/shard_map/ppermute | solution.py:22
  24.3 5.4 %copy-start.5 = (bf16[2048,256]{1,0:T(8,128)(2,1)S(1)}, bf16[2048,256]{1,0:T(8,128)(2,1)}, u32[]{:S(2)}) copy-start(bf16[2048,256]{1,0:T(8,128)(2,1)} %copy-done.4) | copy-start | bytes 3145732
  27.0 4.2 %copy-start.9 = (f32[2,33,128]{2,0,1:T(2,128)}, f32[2,33,128]{2,0,1:T(2,128)S(1)}, u32[]{:S(2)}) copy-start(f32[2,33,128]{2,0,1:T(2,128)S(1)} %collective-permute-done.5) | copy-start | bytes 101380
  27.0 4.2 %collective-permute-start.7 = (f32[2,33,128]{2,0,1:T(2,128)S(1)}, f32[2,33,128]{2,0,1:T(2,128)}, u32[]{:S(2)}, u32[]{:S(2)}) collective-permute-start(f32[2,33,128]{2,0,1:T(2,128)S(1)} %collective-permute-done.5), channel_id=1, source_target_pairs={{0,224},{32,0},{64,32},{96,64},{128,96},{160,128},{192,160},{224,1... | collective-permute-start | bytes 101384 | tf_op jit(solution)/shard_map/ppermute | solution.py:22
  29.7 1.5 %copy-start.10 = (f32[2,33,128]{2,0,1:T(2,128)}, f32[2,33,128]{2,0,1:T(2,128)S(1)}, u32[]{:S(2)}) copy-start(f32[2,33,128]{2,0,1:T(2,128)S(1)} %collective-permute-done.6) | copy-start | bytes 101380
  29.7 4.2 %collective-permute-start.8 = (f32[2,33,128]{2,0,1:T(2,128)S(1)}, f32[2,33,128]{2,0,1:T(2,128)}, u32[]{:S(2)}, u32[]{:S(2)}) collective-permute-start(f32[2,33,128]{2,0,1:T(2,128)S(1)} %collective-permute-done.6), channel_id=1, source_target_pairs={{0,32},{32,64},{64,96},{96,128},{128,160},{160,192},{192,224},{224... | collective-permute-start | bytes 101384 | tf_op jit(solution)/shard_map/ppermute | solution.py:22
  31.2 4.1 %collective-permute-start.9 = (f32[2,33,128]{2,0,1:T(2,128)}, f32[2,33,128]{2,0,1:T(2,128)}, u32[]{:S(2)}, u32[]{:S(2)}) collective-permute-start(f32[2,33,128]{2,0,1:T(2,128)} %collective-permute-done.7), channel_id=1, source_target_pairs={{0,224},{32,0},{64,32},{96,64},{128,96},{160,128},{192,160},{224,1... | collective-permute-start | bytes 101384 | tf_op jit(solution)/shard_map/ppermute | solution.py:22
  33.9 4.3 %collective-permute-start.10 = (f32[2,33,128]{2,0,1:T(2,128)}, f32[2,33,128]{2,0,1:T(2,128)}, u32[]{:S(2)}, u32[]{:S(2)}) collective-permute-start(f32[2,33,128]{2,0,1:T(2,128)} %collective-permute-done.8), channel_id=1, source_target_pairs={{0,32},{32,64},{64,96},{96,128},{128,160},{160,192},{192,224},{224... | collective-permute-start | bytes 101384 | tf_op jit(solution)/shard_map/ppermute | solution.py:22
  39.0 6.1 %collective-permute-start.11 = (f32[2,33,128]{2,0,1:T(2,128)}, f32[2,33,128]{2,0,1:T(2,128)}, u32[]{:S(2)}, u32[]{:S(2)}) collective-permute-start(f32[2,33,128]{2,0,1:T(2,128)} %select_add_fusion.5), channel_id=1, source_target_pairs={{0,8},{8,16},{16,24},{24,0},{1,9},{9,17},{17,25},{25,1},{2,10},{10... | collective-permute-start | bytes 101384 | tf_op jit(solution)/shard_map/ppermute | solution.py:22
  41.7 4.6 %collective-permute-start.12 = (f32[2,33,128]{2,0,1:T(2,128)}, f32[2,33,128]{2,0,1:T(2,128)}, u32[]{:S(2)}, u32[]{:S(2)}) collective-permute-start(f32[2,33,128]{2,0,1:T(2,128)} %get-tuple-element.17), channel_id=1, source_target_pairs={{0,16},{8,24},{16,0},{24,8},{1,17},{9,25},{17,1},{25,9},{2,18},{10... | collective-permute-start | bytes 101384 | tf_op jit(solution)/shard_map/ppermute | solution.py:22
  43.5 3.1 %collective-permute-start.13 = (f32[2,33,128]{2,0,1:T(2,128)}, f32[2,33,128]{2,0,1:T(2,128)}, u32[]{:S(2)}, u32[]{:S(2)}) collective-permute-start(f32[2,33,128]{2,0,1:T(2,128)} %get-tuple-element.16), channel_id=1, source_target_pairs={{0,24},{8,0},{16,8},{24,16},{1,25},{9,1},{17,9},{25,17},{2,26},{10... | collective-permute-start | bytes 101384 | tf_op jit(solution)/shard_map/ppermute | solution.py:22
  51.4 0.7 copy-start.1
  52.1 5.7 %collective-permute-start.14 = (f32[8,33,128]{2,0,1:T(8,128)}, f32[8,33,128]{2,0,1:T(8,128)}, u32[]{:S(2)}, u32[]{:S(2)}) collective-permute-start(f32[8,33,128]{2,0,1:T(8,128)} %select_add_fusion.1), channel_id=1, source_target_pairs={{0,4},{4,0},{1,5},{5,1},{2,6},{6,2},{3,7},{7,3},{8,12},{12,8},{9,1... | collective-permute-start | bytes 405512 | tf_op jit(solution)/shard_map/ppermute | solution.py:22
  59.5 11.3 %collective-permute-start.15 = (f32[8,33,128]{2,1,0:T(8,128)}, f32[8,33,128]{2,1,0:T(8,128)}, u32[]{:S(2)}, u32[]{:S(2)}) collective-permute-start(f32[8,33,128]{2,1,0:T(8,128)} %copy.10), channel_id=1, source_target_pairs={{0,2},{2,0},{1,3},{3,1},{4,6},{6,4},{5,7},{7,5},{8,10},{10,8},{9,1... | collective-permute-start | bytes 405512 | tf_op jit(solution)/shard_map/ppermute | solution.py:22
  68.0 8.2 %copy-start.7 = (f32[16,64]{1,0:T(8,128)S(1)}, f32[16,64]{1,0:T(8,128)}, u32[]{:S(2)}) copy-start(f32[16,64]{1,0:T(8,128)} %copy-done.6) | copy-start | bytes 12292
  74.1 4.5 %copy-start.3 = (f32[8,64,256]{2,1,0:T(8,128)S(1)}, f32[8,64,256]{2,1,0:T(8,128)}, u32[]{:S(2)}) copy-start(f32[8,64,256]{2,1,0:T(8,128)} %fusion.47) | copy-start | bytes 1572868
  74.1 4.5 %copy-start.11 = (f32[1,1,256,16,64]{2,4,3,1,0:T(8,128)S(1)}, f32[1,1,256,16,64]{2,4,3,1,0:T(8,128)}, u32[]{:S(2)}) copy-start(f32[1,1,256,16,64]{2,4,3,1,0:T(8,128)} %fusion.10) | copy-start | bytes 3145732

commit v13 on v11

--- a/solution.py
+++ b/solution.py
@@ -129,9 +129,7 @@
     num = num_local + jnp.einsum(
         "rnihd,rnhde->rnihe", pq32, before_kv, precision=lax.Precision.HIGHEST
     )
-    den = jnp.transpose(den_local, (0, 1, 3, 2)) + jnp.einsum(
-        "rnihd,rnhd->rnih", pq32, before_k, precision=lax.Precision.HIGHEST
-    )
+    den = jnp.transpose(den_local, (0, 1, 3, 2)) + jnp.sum(pq32 * before_k[:, :, None], axis=-1)
     result = (num / den[..., None]).astype(jnp.bfloat16)
     return result.reshape(rows, count * span, heads * dim)
 

time: 67.1 us -> 66 us (0.984)
  matrix products: 18.1 us -> 15.8 us
  other arithmetic: 0.88 us -> 2.14 us
    dot_general x2 -> x0, matrix products: 2.32 us -> none  [finish(): jnp.einsum('rnihd,rnhd->rnih', pq32, before_k, precision=lax.Precision.HI...]
    reduce_sum x0 -> x1, other arithmetic: none -> 1.26 us  [finish(): jnp.sum(pq32 * before_k[:, :, None], axis=-1)]
where the time goes in v13:
time: 66 us; the launch traced here: 65.7 us
  starting transfers between devices  32.2 us (49%)
  matrix products  15.8 us (24%)
  waiting for transfers between devices  11.8 us (18%)
  local copies, waits for them, and re-layouts  3.48 us (5%)
  other arithmetic  2.14 us (3%)
    ppermute x16, starting transfers between devices, send(): return tmap(lambda t: lax.ppermute(t, axis, perm=pairs), tree)  32.2 us
    ppermute x16, waiting for transfers between devices, send(): return tmap(lambda t: lax.ppermute(t, axis, perm=pairs), tree)  11.8 us
    dot_general x2, matrix products, project(): jnp.einsum('rtd,de->ret', frames_in, w, preferred_element_type=jnp.float32)  7.02 us
    dot_general x2, matrix products, finish(): jnp.einsum('rnihd,rnhde->rnihe', pq32, before_kv, precision=lax.Precision...  2.96 us
    dot_general x1, matrix products, block_terms(): jnp.einsum('rnihd,rnjhd->rnhij', pq, pk, preferred_element_type=jnp.float32)  2.23 us
    dot_general x2, matrix products, heads_of(): jnp.einsum('rtd,de->rte', heads_out, rows_w, preferred_element_type=jnp.f...  1.74 us
    dot_general x1, matrix products, block_terms(): jnp.einsum('rnhij,rnjhd->rnihd', weights, vv, preferred_element_type=jnp....  1.44 us
  transfers between devices with their start and end apart: 16, of which 9 were waited for; matrix products, arithmetic and copies ran while one was open for 11% of the time, Pallas kernels for 0%

profile of v13, /device:TPU:1, one launch (start us, length us, event | category | flops | bytes accessed | tf_op | source)
XLA Modules:
  0.0 65.7 jit_solution(8623467669148597557)
XLA Ops:
  0.0 3.8 %fusion.2 = bf16[2048,256]{1,0:T(8,128)(2,1)S(1)} fusion(bf16[1024,3072]{1,0:T(8,128)(2,1)} %param.4, bf16[1,256,1024]{2,1,0:T(8,128)(2,1)} %param.3), kind=kOutput, calls=%fused_computation.5 | convolution fusion | flops 1074266112 | bytes 5767168 | tf_op jit(solution)/shard_map/rtd,de->ret/dot_general | solution.py:147
  3.8 0.4 fusion.37
  4.2 0.6 copy-done.1
  4.8 0.3 convert_reduce_fusion
  5.1 0.1 reshape_squeeze.4
  5.3 0.2 copy.4
  5.5 3.3 %collective-permute-start = (f32[8,33,128]{2,0,1:T(8,128)S(1)}, f32[8,33,128]{2,0,1:T(8,128)S(1)}, u32[]{:S(2)}, u32[]{:S(2)}) collective-permute-start(f32[8,33,128]{2,0,1:T(8,128)S(1)} %fusion.51), channel_id=1, source_target_pairs={{0,2},{2,0},{1,3},{3,1},{4,6},{6,4},{5,7},{7,5},{8,10},{10,8},{9,1... | collective-permute-start | bytes 405512 | tf_op jit(solution)/shard_map/ppermute | solution.py:22
  8.8 1.0 %collective-permute-done = f32[8,33,128]{2,0,1:T(8,128)S(1)} collective-permute-done((f32[8,33,128]{2,0,1:T(8,128)S(1)}, f32[8,33,128]{2,0,1:T(8,128)S(1)}, u32[]{:S(2)}, u32[]{:S(2)}) %collective-permute-start) | collective-permute-done | bytes 135200 | tf_op jit(solution)/shard_map/ppermute | solution.py:22
  9.8 0.1 collective-permute-start.1
  9.9 2.2 %collective-permute-start.2 = (f32[2,33,128]{2,0,1:T(2,128)S(1)}, f32[2,33,128]{2,0,1:T(2,128)S(1)}, u32[]{:S(2)}, u32[]{:S(2)}) collective-permute-start(f32[2,33,128]{2,0,1:T(2,128)S(1)} %get-tuple-element.20), channel_id=1, source_target_pairs={{0,16},{8,24},{16,0},{24,8},{1,17},{9,25},{17,1},{25,9},{2,18},{10... | collective-permute-start | bytes 101384 | tf_op jit(solution)/shard_map/ppermute | solution.py:22
  12.1 1.1 %collective-permute-start.3 = (f32[2,33,128]{2,0,1:T(2,128)S(1)}, f32[2,33,128]{2,0,1:T(2,128)S(1)}, u32[]{:S(2)}, u32[]{:S(2)}) collective-permute-start(f32[2,33,128]{2,0,1:T(2,128)S(1)} %get-tuple-element.19), channel_id=1, source_target_pairs={{0,24},{8,0},{16,8},{24,16},{1,25},{9,1},{17,9},{25,17},{2,26},{10... | collective-permute-start | bytes 101384 | tf_op jit(solution)/shard_map/ppermute | solution.py:22
  13.2 3.2 %fusion.26 = bf16[1024,256]{1,0:T(8,128)(2,1)} fusion(bf16[1024,3072]{1,0:T(8,128)(2,1)} %param.4, bf16[1,256,1024]{2,1,0:T(8,128)(2,1)} %param.3), kind=kOutput, calls=%fused_computation.34 | convolution fusion | flops 538705920 | bytes 3145728 | tf_op jit(solution)/shard_map/rtd,de->ret/dot_general | solution.py:147
  16.4 0.0 collective-permute-done.1
  16.4 0.0 collective-permute-done.2
  16.5 1.7 %collective-permute-start.4 = (f32[2,33,128]{2,0,1:T(2,128)S(1)}, f32[2,33,128]{2,0,1:T(2,128)S(1)}, u32[]{:S(2)}, u32[]{:S(2)}) collective-permute-start(f32[2,33,128]{2,0,1:T(2,128)S(1)} %add_add_fusion), channel_id=1, source_target_pairs={{0,32},{32,64},{64,96},{96,128},{128,160},{160,192},{192,224},{224... | collective-permute-start | bytes 101384 | tf_op jit(solution)/shard_map/ppermute | solution.py:22
  18.2 4.0 %collective-permute-start.5 = (f32[2,33,128]{2,0,1:T(2,128)S(1)}, f32[2,33,128]{2,0,1:T(2,128)S(1)}, u32[]{:S(2)}, u32[]{:S(2)}) collective-permute-start(f32[2,33,128]{2,0,1:T(2,128)S(1)} %add_add_fusion), channel_id=1, source_target_pairs={{0,224},{32,0},{64,32},{96,64},{128,96},{160,128},{192,160},{224,1... | collective-permute-start | bytes 101384 | tf_op jit(solution)/shard_map/ppermute | solution.py:22
  22.3 1.2 %collective-permute-done.4 = f32[2,33,128]{2,0,1:T(2,128)S(1)} collective-permute-done((f32[2,33,128]{2,0,1:T(2,128)S(1)}, f32[2,33,128]{2,0,1:T(2,128)S(1)}, u32[]{:S(2)}, u32[]{:S(2)}) %collective-permute-start.4) | collective-permute-done | bytes 33824 | tf_op jit(solution)/shard_map/ppermute | solution.py:22
  23.5 2.2 %select_reduce_fusion = (f32[16,256]{1,0:T(8,128)S(1)}, bf16[16,256,256]{1,2,0:T(8,128)(2,1)S(1)}) fusion(pred[256,256]{0,1:T(8,128)(4,1)S(1)} %iota_compare_fusion, bf16[256,16,64]{0,2,1:T(8,128)(2,1)} %bitcast.107, bf16[1,256,2,16,64]{1,4,3,2,0:T(8,128)(2,1)} %bitcast.115), kind=kOutput, calls=%fused_computation.3 | convolution fusion | flops 138932224 | bytes 3227648 | tf_op jit(solution)/shard_map/rnihd,rnjhd->rnhij/dot_general | solution.py:113
  25.7 2.7 %collective-permute-start.7 = (f32[2,33,128]{2,0,1:T(2,128)S(1)}, f32[2,33,128]{2,0,1:T(2,128)S(1)}, u32[]{:S(2)}, u32[]{:S(2)}) collective-permute-start(f32[2,33,128]{2,0,1:T(2,128)S(1)} %collective-permute-done.5), channel_id=1, source_target_pairs={{0,224},{32,0},{64,32},{96,64},{128,96},{160,128},{192,160},{224,1... | collective-permute-start | bytes 101384 | tf_op jit(solution)/shard_map/ppermute | solution.py:22
  28.5 1.4 %fusion.10 = f32[1,1,256,16,64]{2,4,3,1,0:T(8,128)} fusion(bf16[16,256,256]{1,2,0:T(8,128)(2,1)S(1)} %get-tuple-element.26, pred[256,256]{0,1:T(8,128)(4,1)S(1)} %iota_compare_fusion, bf16[1,256,2,16,64]{1,4,3,2,0:T(8,128)(2,1)S(1)} %bitcast.116), kind=kOutput, calls=%fused_computation.17 | convolution fusion | flops 135266304 | bytes 3735552 | tf_op jit(solution)/shard_map/rnhij,rnjhd->rnihd/dot_general | solution.py:118
  29.9 2.7 %collective-permute-start.9 = (f32[2,33,128]{2,0,1:T(2,128)S(1)}, f32[2,33,128]{2,0,1:T(2,128)S(1)}, u32[]{:S(2)}, u32[]{:S(2)}) collective-permute-start(f32[2,33,128]{2,0,1:T(2,128)S(1)} %collective-permute-done.7), channel_id=1, source_target_pairs={{0,224},{32,0},{64,32},{96,64},{128,96},{160,128},{192,160},{224,1... | collective-permute-start | bytes 101384 | tf_op jit(solution)/shard_map/ppermute | solution.py:22
  32.6 0.0 collective-permute-start.10
  32.7 0.9 %collective-permute-done.9 = f32[2,33,128]{2,0,1:T(2,128)S(1)} collective-permute-done((f32[2,33,128]{2,0,1:T(2,128)S(1)}, f32[2,33,128]{2,0,1:T(2,128)S(1)}, u32[]{:S(2)}, u32[]{:S(2)}) %collective-permute-start.9) | collective-permute-done | bytes 33824 | tf_op jit(solution)/shard_map/ppermute | solution.py:22
  33.6 3.1 %collective-permute-done.10 = f32[2,33,128]{2,0,1:T(2,128)} collective-permute-done((f32[2,33,128]{2,0,1:T(2,128)S(1)}, f32[2,33,128]{2,0,1:T(2,128)}, u32[]{:S(2)}, u32[]{:S(2)}) %collective-permute-start.10) | collective-permute-done | bytes 33824 | tf_op jit(solution)/shard_map/ppermute | solution.py:22
  36.7 0.1 select_add_fusion.6
  36.8 0.1 select_add_fusion.5
  36.8 0.5 collective-permute-start.11
  37.3 0.1 add_bitcast_fusion
  37.4 1.8 %collective-permute-start.12 = (f32[2,33,128]{2,0,1:T(2,128)S(1)}, f32[2,33,128]{2,0,1:T(2,128)S(1)}, u32[]{:S(2)}, u32[]{:S(2)}) collective-permute-start(f32[2,33,128]{2,0,1:T(2,128)S(1)} %get-tuple-element.17), channel_id=1, source_target_pairs={{0,16},{8,24},{16,0},{24,8},{1,17},{9,25},{17,1},{25,9},{2,18},{10... | collective-permute-start | bytes 101384 | tf_op jit(solution)/shard_map/ppermute | solution.py:22
  39.2 0.7 %collective-permute-start.13 = (f32[2,33,128]{2,0,1:T(2,128)S(1)}, f32[2,33,128]{2,0,1:T(2,128)S(1)}, u32[]{:S(2)}, u32[]{:S(2)}) collective-permute-start(f32[2,33,128]{2,0,1:T(2,128)S(1)} %get-tuple-element.16), channel_id=1, source_target_pairs={{0,24},{8,0},{16,8},{24,16},{1,25},{9,1},{17,9},{25,17},{2,26},{10... | collective-permute-start | bytes 101384 | tf_op jit(solution)/shard_map/ppermute | solution.py:22
  39.9 1.1 %collective-permute-done.11 = f32[2,33,128]{2,0,1:T(2,128)S(1)} collective-permute-done((f32[2,33,128]{2,0,1:T(2,128)S(1)}, f32[2,33,128]{2,0,1:T(2,128)S(1)}, u32[]{:S(2)}, u32[]{:S(2)}) %collective-permute-start.11) | collective-permute-done | bytes 33824 | tf_op jit(solution)/shard_map/ppermute | solution.py:22
  41.1 0.7 %collective-permute-done.12 = f32[2,33,128]{2,0,1:T(2,128)S(1)} collective-permute-done((f32[2,33,128]{2,0,1:T(2,128)S(1)}, f32[2,33,128]{2,0,1:T(2,128)S(1)}, u32[]{:S(2)}, u32[]{:S(2)}) %collective-permute-start.12) | collective-permute-done | bytes 33824 | tf_op jit(solution)/shard_map/ppermute | solution.py:22
  41.8 0.2 collective-permute-done.13
  42.1 0.1 pad_maximum_fusion
  42.1 0.7 %gather_fusion = f32[4,2,33,128]{3,1,2,0:T(2,128)S(1)} fusion(f32[4,2,33,128]{3,1,2,0:T(2,128)S(1)} %pad_maximum_fusion, s32[1024]{0:T(1024)S(1)} %pad_clamp_fusion), kind=kCustom, calls=%fused_computation | custom fusion | bytes 270352 | tf_op jit(solution)/shard_map/gather | solution.py:98
  42.9 2.8 %collective-permute-start.14 = (f32[8,33,128]{2,0,1:T(8,128)S(1)}, f32[8,33,128]{2,0,1:T(8,128)S(1)}, u32[]{:S(2)}, u32[]{:S(2)}) collective-permute-start(f32[8,33,128]{2,0,1:T(8,128)S(1)} %select_add_fusion.1), channel_id=1, source_target_pairs={{0,4},{4,0},{1,5},{5,1},{2,6},{6,2},{3,7},{7,3},{8,12},{12,8},{9,1... | collective-permute-start | bytes 405512 | tf_op jit(solution)/shard_map/ppermute | solution.py:22
  45.7 2.6 %collective-permute-done.14 = f32[8,33,128]{2,0,1:T(8,128)S(1)} collective-permute-done((f32[8,33,128]{2,0,1:T(8,128)S(1)}, f32[8,33,128]{2,0,1:T(8,128)S(1)}, u32[]{:S(2)}, u32[]{:S(2)}) %collective-permute-start.14) | collective-permute-done | bytes 135200 | tf_op jit(solution)/shard_map/ppermute | solution.py:22
  48.4 8.5 %collective-permute-start.15 = (f32[8,33,128]{2,1,0:T(8,128)S(1)}, f32[8,33,128]{2,1,0:T(8,128)S(1)}, u32[]{:S(2)}, u32[]{:S(2)}) collective-permute-start(f32[8,33,128]{2,1,0:T(8,128)S(1)} %copy.9), channel_id=1, source_target_pairs={{0,2},{2,0},{1,3},{3,1},{4,6},{6,4},{5,7},{7,5},{8,10},{10,8},{9,1... | collective-permute-start | bytes 405512 | tf_op jit(solution)/shard_map/ppermute | solution.py:22
  57.0 0.1 broadcast_in_dim_broadcast_in_dim_reshape.6
  57.1 0.9 %collective-permute-done.15 = f32[8,33,128]{2,1,0:T(8,128)S(1)} collective-permute-done((f32[8,33,128]{2,1,0:T(8,128)S(1)}, f32[8,33,128]{2,1,0:T(8,128)S(1)}, u32[]{:S(2)}, u32[]{:S(2)}) %collective-permute-start.15) | collective-permute-done | bytes 135200 | tf_op jit(solution)/shard_map/ppermute | solution.py:22
  58.0 0.7 %copy-done.3 = f32[8,33,128]{2,1,0:T(8,128)} copy-done((f32[8,33,128]{2,1,0:T(8,128)}, f32[8,33,128]{2,1,0:T(8,128)S(1)}, u32[]{:S(2)}) %copy-start.3) | copy-done | bytes 135192
  58.7 0.1 broadcast_in_dim_broadcast_in_dim_reshape.7
  58.8 0.8 %slice.39 = f32[8,1,64]{2,1,0:T(1,128)S(1)} slice(f32[8,33,128]{2,1,0:T(8,128)} %copy-done.3), slice={[0:8], [32:33], [0:64]} | slice | bytes 4096 | tf_op jit(solution)/shard_map/slice | solution.py:173
  59.7 1.3 %fusion.33 = (f32[256,8]{0,1:T(8,128)S(1)}, f32[256,8]{0,1:T(8,128)S(1)}) fusion(f32[8,64]{1,0:T(8,128)S(1)} %get-tuple-element.24, bf16[1,1,16,64,256]{4,3,2,1,0:T(8,128)(2,1)} %bitcast.108, s32[]{:T(128)S(6)} %select_n.335, f32[8,64]{1,0:T(8,128)S(1)} %get-tuple-element.23, s32[]{:T(128)S(6)} %select_n.334), kind=kLoop, calls=%fused_computation.42 | loop fusion | flops 782336 | bytes 544776 | tf_op jit(solution)/shard_map/reduce_sum | solution.py:132
  61.0 1.6 %fusion.20 = bf16[1,1,256,8,64]{2,4,3,1,0:T(8,128)(2,1)S(1)} fusion(f32[1,1,256,16,64]{2,4,3,1,0:T(8,128)} %fusion.10, s32[]{:T(128)S(6)} %select_n.335, f32[256,8]{0,1:T(8,128)S(1)} %get-tuple-element.21, f32[8,64,64]{2,1,0:T(8,128)S(1)} %broadcast_in_dim_broadcast_in_dim_reshape.7, f32[16,64,64]{2,1,0:T(8,128)S(1)} %fusion.37, ...), kind=kOutput, calls=%fused_computation.28 | convolution fusion | flops 101122048 | bytes 1582592 | tf_op jit(solution)/shard_map/rnihd,rnhde->rnihe/dot_general | solution.py:129
  62.5 1.4 %fusion.21 = bf16[1,1,256,8,64]{2,4,3,1,0:T(8,128)(2,1)S(1)} fusion(f32[1,1,256,16,64]{2,4,3,1,0:T(8,128)S(1)} %copy-done.4, s32[]{:T(128)S(6)} %select_n.334, f32[256,8]{0,1:T(8,128)S(1)} %get-tuple-element.22, f32[8,64,64]{2,1,0:T(8,128)S(1)} %broadcast_in_dim_broadcast_in_dim_reshape.6, f32[16,64,64]{2,1,0:T(8,128)S(1)} %fusion.37, ...), kind=kOutput, calls=%fused_computation.29 | convolution fusion | flops 101122048 | bytes 1582592 | tf_op jit(solution)/shard_map/rnihd,rnhde->rnihe/dot_general | solution.py:129
  64.0 0.5 fusion.29
  64.4 1.3 %fusion.15 = bf16[1,256,1024]{2,1,0:T(8,128)(2,1)} fusion(f32[256,1024]{1,0:T(8,128)S(1)} %fusion.29, bf16[256,512]{0,1:T(8,128)(2,1)S(1)} %bitcast.111, bf16[1024,1024]{1,0:T(8,128)(2,1)S(1)} %copy-done, s32[]{:T(128)S(6)} %select_n.404), kind=kOutput, calls=%fused_computation.21 | convolution fusion | flops 268959744 | bytes 2883588 | tf_op jit(solution)/shard_map/rtd,de->rte/dot_general | solution.py:179
  (32 shorter events, 0.4 us)
Async XLA Ops:
  0.0 64.0 %copy-start = (bf16[1024,1024]{1,0:T(8,128)(2,1)S(1)}, bf16[1024,1024]{1,0:T(8,128)(2,1)}, u32[]{:S(2)}) copy-start(bf16[1024,1024]{1,0:T(8,128)(2,1)} %param.5) | copy-start | bytes 6291460
  3.8 1.0 %copy-start.1 = (bf16[2048,256]{1,0:T(8,128)(2,1)}, bf16[2048,256]{1,0:T(8,128)(2,1)S(1)}, u32[]{:S(2)}) copy-start(bf16[2048,256]{1,0:T(8,128)(2,1)S(1)} %fusion.2) | copy-start | bytes 3145732
  5.5 4.3 %collective-permute-start = (f32[8,33,128]{2,0,1:T(8,128)S(1)}, f32[8,33,128]{2,0,1:T(8,128)S(1)}, u32[]{:S(2)}, u32[]{:S(2)}) collective-permute-start(f32[8,33,128]{2,0,1:T(8,128)S(1)} %fusion.51), channel_id=1, source_target_pairs={{0,2},{2,0},{1,3},{3,1},{4,6},{6,4},{5,7},{7,5},{8,10},{10,8},{9,1... | collective-permute-start | bytes 405512 | tf_op jit(solution)/shard_map/ppermute | solution.py:22
  9.8 6.6 %collective-permute-start.1 = (f32[2,33,128]{2,0,1:T(2,128)S(1)}, f32[2,33,128]{2,0,1:T(2,128)S(1)}, u32[]{:S(2)}, u32[]{:S(2)}) collective-permute-start(f32[2,33,128]{2,0,1:T(2,128)S(1)} %get-tuple-element.18), channel_id=1, source_target_pairs={{0,8},{8,16},{16,24},{24,0},{1,9},{9,17},{17,25},{25,1},{2,10},{10... | collective-permute-start | bytes 101384 | tf_op jit(solution)/shard_map/ppermute | solution.py:22
  9.9 6.5 %collective-permute-start.2 = (f32[2,33,128]{2,0,1:T(2,128)S(1)}, f32[2,33,128]{2,0,1:T(2,128)S(1)}, u32[]{:S(2)}, u32[]{:S(2)}) collective-permute-start(f32[2,33,128]{2,0,1:T(2,128)S(1)} %get-tuple-element.20), channel_id=1, source_target_pairs={{0,16},{8,24},{16,0},{24,8},{1,17},{9,25},{17,1},{25,9},{2,18},{10... | collective-permute-start | bytes 101384 | tf_op jit(solution)/shard_map/ppermute | solution.py:22
  12.1 4.3 %collective-permute-start.3 = (f32[2,33,128]{2,0,1:T(2,128)S(1)}, f32[2,33,128]{2,0,1:T(2,128)S(1)}, u32[]{:S(2)}, u32[]{:S(2)}) collective-permute-start(f32[2,33,128]{2,0,1:T(2,128)S(1)} %get-tuple-element.19), channel_id=1, source_target_pairs={{0,24},{8,0},{16,8},{24,16},{1,25},{9,1},{17,9},{25,17},{2,26},{10... | collective-permute-start | bytes 101384 | tf_op jit(solution)/shard_map/ppermute | solution.py:22
  16.5 7.0 %collective-permute-start.4 = (f32[2,33,128]{2,0,1:T(2,128)S(1)}, f32[2,33,128]{2,0,1:T(2,128)S(1)}, u32[]{:S(2)}, u32[]{:S(2)}) collective-permute-start(f32[2,33,128]{2,0,1:T(2,128)S(1)} %add_add_fusion), channel_id=1, source_target_pairs={{0,32},{32,64},{64,96},{96,128},{128,160},{160,192},{192,224},{224... | collective-permute-start | bytes 101384 | tf_op jit(solution)/shard_map/ppermute | solution.py:22
  18.2 7.5 %collective-permute-start.5 = (f32[2,33,128]{2,0,1:T(2,128)S(1)}, f32[2,33,128]{2,0,1:T(2,128)S(1)}, u32[]{:S(2)}, u32[]{:S(2)}) collective-permute-start(f32[2,33,128]{2,0,1:T(2,128)S(1)} %add_add_fusion), channel_id=1, source_target_pairs={{0,224},{32,0},{64,32},{96,64},{128,96},{160,128},{192,160},{224,1... | collective-permute-start | bytes 101384 | tf_op jit(solution)/shard_map/ppermute | solution.py:22
  23.5 5.0 %collective-permute-start.6 = (f32[2,33,128]{2,0,1:T(2,128)S(1)}, f32[2,33,128]{2,0,1:T(2,128)S(1)}, u32[]{:S(2)}, u32[]{:S(2)}) collective-permute-start(f32[2,33,128]{2,0,1:T(2,128)S(1)} %collective-permute-done.4), channel_id=1, source_target_pairs={{0,32},{32,64},{64,96},{96,128},{128,160},{160,192},{192,224},{224... | collective-permute-start | bytes 101384 | tf_op jit(solution)/shard_map/ppermute | solution.py:22
  23.5 5.0 %copy-start.2 = (bf16[2048,256]{1,0:T(8,128)(2,1)S(1)}, bf16[2048,256]{1,0:T(8,128)(2,1)}, u32[]{:S(2)}) copy-start(bf16[2048,256]{1,0:T(8,128)(2,1)} %copy-done.1) | copy-start | bytes 3145732
  25.7 4.2 %collective-permute-start.7 = (f32[2,33,128]{2,0,1:T(2,128)S(1)}, f32[2,33,128]{2,0,1:T(2,128)S(1)}, u32[]{:S(2)}, u32[]{:S(2)}) collective-permute-start(f32[2,33,128]{2,0,1:T(2,128)S(1)} %collective-permute-done.5), channel_id=1, source_target_pairs={{0,224},{32,0},{64,32},{96,64},{128,96},{160,128},{192,160},{224,1... | collective-permute-start | bytes 101384 | tf_op jit(solution)/shard_map/ppermute | solution.py:22
  28.5 4.1 %collective-permute-start.8 = (f32[2,33,128]{2,0,1:T(2,128)S(1)}, f32[2,33,128]{2,0,1:T(2,128)S(1)}, u32[]{:S(2)}, u32[]{:S(2)}) collective-permute-start(f32[2,33,128]{2,0,1:T(2,128)S(1)} %collective-permute-done.6), channel_id=1, source_target_pairs={{0,32},{32,64},{64,96},{96,128},{128,160},{160,192},{192,224},{224... | collective-permute-start | bytes 101384 | tf_op jit(solution)/shard_map/ppermute | solution.py:22
  29.9 3.7 %collective-permute-start.9 = (f32[2,33,128]{2,0,1:T(2,128)S(1)}, f32[2,33,128]{2,0,1:T(2,128)S(1)}, u32[]{:S(2)}, u32[]{:S(2)}) collective-permute-start(f32[2,33,128]{2,0,1:T(2,128)S(1)} %collective-permute-done.7), channel_id=1, source_target_pairs={{0,224},{32,0},{64,32},{96,64},{128,96},{160,128},{192,160},{224,1... | collective-permute-start | bytes 101384 | tf_op jit(solution)/shard_map/ppermute | solution.py:22
  32.6 4.1 %collective-permute-start.10 = (f32[2,33,128]{2,0,1:T(2,128)S(1)}, f32[2,33,128]{2,0,1:T(2,128)}, u32[]{:S(2)}, u32[]{:S(2)}) collective-permute-start(f32[2,33,128]{2,0,1:T(2,128)S(1)} %collective-permute-done.8), channel_id=1, source_target_pairs={{0,32},{32,64},{64,96},{96,128},{128,160},{160,192},{192,224},{224... | collective-permute-start | bytes 101384 | tf_op jit(solution)/shard_map/ppermute | solution.py:22
  36.8 4.2 %collective-permute-start.11 = (f32[2,33,128]{2,0,1:T(2,128)S(1)}, f32[2,33,128]{2,0,1:T(2,128)S(1)}, u32[]{:S(2)}, u32[]{:S(2)}) collective-permute-start(f32[2,33,128]{2,0,1:T(2,128)S(1)} %select_add_fusion.5), channel_id=1, source_target_pairs={{0,8},{8,16},{16,24},{24,0},{1,9},{9,17},{17,25},{25,1},{2,10},{10... | collective-permute-start | bytes 101384 | tf_op jit(solution)/shard_map/ppermute | solution.py:22
  37.4 4.4 %collective-permute-start.12 = (f32[2,33,128]{2,0,1:T(2,128)S(1)}, f32[2,33,128]{2,0,1:T(2,128)S(1)}, u32[]{:S(2)}, u32[]{:S(2)}) collective-permute-start(f32[2,33,128]{2,0,1:T(2,128)S(1)} %get-tuple-element.17), channel_id=1, source_target_pairs={{0,16},{8,24},{16,0},{24,8},{1,17},{9,25},{17,1},{25,9},{2,18},{10... | collective-permute-start | bytes 101384 | tf_op jit(solution)/shard_map/ppermute | solution.py:22
  39.2 2.8 %collective-permute-start.13 = (f32[2,33,128]{2,0,1:T(2,128)S(1)}, f32[2,33,128]{2,0,1:T(2,128)S(1)}, u32[]{:S(2)}, u32[]{:S(2)}) collective-permute-start(f32[2,33,128]{2,0,1:T(2,128)S(1)} %get-tuple-element.16), channel_id=1, source_target_pairs={{0,24},{8,0},{16,8},{24,16},{1,25},{9,1},{17,9},{25,17},{2,26},{10... | collective-permute-start | bytes 101384 | tf_op jit(solution)/shard_map/ppermute | solution.py:22
  42.9 5.5 %collective-permute-start.14 = (f32[8,33,128]{2,0,1:T(8,128)S(1)}, f32[8,33,128]{2,0,1:T(8,128)S(1)}, u32[]{:S(2)}, u32[]{:S(2)}) collective-permute-start(f32[8,33,128]{2,0,1:T(8,128)S(1)} %select_add_fusion.1), channel_id=1, source_target_pairs={{0,4},{4,0},{1,5},{5,1},{2,6},{6,2},{3,7},{7,3},{8,12},{12,8},{9,1... | collective-permute-start | bytes 405512 | tf_op jit(solution)/shard_map/ppermute | solution.py:22
  48.4 9.6 %collective-permute-start.15 = (f32[8,33,128]{2,1,0:T(8,128)S(1)}, f32[8,33,128]{2,1,0:T(8,128)S(1)}, u32[]{:S(2)}, u32[]{:S(2)}) collective-permute-start(f32[8,33,128]{2,1,0:T(8,128)S(1)} %copy.9), channel_id=1, source_target_pairs={{0,2},{2,0},{1,3},{3,1},{4,6},{6,4},{5,7},{7,5},{8,10},{10,8},{9,1... | collective-permute-start | bytes 405512 | tf_op jit(solution)/shard_map/ppermute | solution.py:22
  58.0 0.7 %copy-start.3 = (f32[8,33,128]{2,1,0:T(8,128)}, f32[8,33,128]{2,1,0:T(8,128)S(1)}, u32[]{:S(2)}) copy-start(f32[8,33,128]{2,1,0:T(8,128)S(1)} %collective-permute-done.15) | copy-start | bytes 405508
  58.8 3.7 %copy-start.4 = (f32[1,1,256,16,64]{2,4,3,1,0:T(8,128)S(1)}, f32[1,1,256,16,64]{2,4,3,1,0:T(8,128)}, u32[]{:S(2)}) copy-start(f32[1,1,256,16,64]{2,4,3,1,0:T(8,128)} %fusion.10) | copy-start | bytes 3145732

commit v14 on v13

--- a/solution.py
+++ b/solution.py
@@ -178,7 +178,9 @@
         rows_w = lax.dynamic_slice_in_dim(w_out, first * head_dim, half_heads * head_dim, axis=0)
         return jnp.einsum("rtd,de->rte", heads_out, rows_w, preferred_element_type=jnp.float32)
 
-    out = heads_of(own, core) + heads_of(other, 1 - core)
+    mine = heads_of(own, core)
+    other, mine = lax.optimization_barrier((other, mine))
+    out = mine + heads_of(other, 1 - core)
     return out.astype(jnp.bfloat16)
 
 

time: 66 us -> 68.9 us (1.044)
  other arithmetic: 2.14 us -> 7.12 us
  local copies, waits for them, and re-layouts: 3.48 us -> 1.97 us
  waiting for transfers between devices: 11.8 us -> 11.1 us
    div x1 -> x2, other arithmetic: 0.01 us -> 1.41 us  [finish(): result = (num / den[..., None]).astype(jnp.bfloat16)]
    convert_element_type x0 -> x1, other arithmetic: none -> 0.94 us  [shards(): return out.astype(jnp.bfloat16)]
    reduce_sum x1 -> x2, other arithmetic: 1.26 us -> 2.2 us  [finish(): jnp.sum(pq32 * before_k[:, :, None], axis=-1)]
    select_n x1, other arithmetic: 0.04 us -> 0.95 us  [entering(): own = tmap(lambda a, c: jnp.where(core == 0, a, a + c), half, got_c)]
    slice x1, local copies, waits for them, and re-layouts: 0.85 us -> 0.01 us  [heads_of(): prior_k = prior[:, rows_kv, :total_k.shape[1]]]
    dot_general x2, matrix products: 1.74 us -> 0.92 us  [heads_of(): jnp.einsum('rtd,de->rte', heads_out, rows_w, preferred_element_type=jnp.f...]
    another operation x2, other arithmetic: 0.19 us -> 0.95 us  [entering(): jnp.stack(p)[order].reshape((-1,) + p[0].shape[1:])]
  transfers between devices with their start and end apart: 16 -> 16, of which waited for: 9 -> 8; matrix products, arithmetic and copies ran while one was open for 11% -> 17% of each run, Pallas kernels for 0% -> 0%
where the time goes in v14:
time: 68.9 us; the launch traced here: 68.4 us
  starting transfers between devices  32.1 us (47%)
  matrix products  15.8 us (23%)
  waiting for transfers between devices  11.1 us (16%)
  other arithmetic  7.12 us (10%)
  local copies, waits for them, and re-layouts  1.97 us (3%)
    ppermute x16, starting transfers between devices, send(): return tmap(lambda t: lax.ppermute(t, axis, perm=pairs), tree)  32.1 us
    ppermute x16, waiting for transfers between devices, send(): return tmap(lambda t: lax.ppermute(t, axis, perm=pairs), tree)  11.1 us
    dot_general x2, matrix products, project(): jnp.einsum('rtd,de->ret', frames_in, w, preferred_element_type=jnp.float32)  7.03 us
    dot_general x2, matrix products, finish(): jnp.einsum('rnihd,rnhde->rnihe', pq32, before_kv, precision=lax.Precision...  3.18 us
    dot_general x1, matrix products, block_terms(): jnp.einsum('rnihd,rnjhd->rnhij', pq, pk, preferred_element_type=jnp.float32)  2.83 us
    reduce_sum x2, other arithmetic, finish(): jnp.sum(pq32 * before_k[:, :, None], axis=-1)  2.2 us
    dot_general x1, matrix products, block_terms(): jnp.einsum('rnhij,rnjhd->rnihd', weights, vv, preferred_element_type=jnp....  1.45 us
    div x2, other arithmetic, finish(): result = (num / den[..., None]).astype(jnp.bfloat16)  1.41 us
  transfers between devices with their start and end apart: 16, of which 8 were waited for; matrix products, arithmetic and copies ran while one was open for 17% of the time, Pallas kernels for 0%

profile of v14, /device:TPU:1, one launch (start us, length us, event | category | flops | bytes accessed | tf_op | source)
XLA Modules:
  0.0 68.4 jit_solution(15940295235415210024)
XLA Ops:
  0.0 3.8 %fusion.2 = bf16[2048,256]{1,0:T(8,128)(2,1)S(1)} fusion(bf16[1024,3072]{1,0:T(8,128)(2,1)} %param.4, bf16[1,256,1024]{2,1,0:T(8,128)(2,1)} %param.3), kind=kOutput, calls=%fused_computation.5 | convolution fusion | flops 1074266112 | bytes 5767168 | tf_op jit(solution)/shard_map/rtd,de->ret/dot_general | solution.py:147
  3.8 0.4 fusion.34
  4.2 0.6 copy-done.2
  4.8 0.3 convert_reduce_fusion
  5.1 0.1 reshape_squeeze.4
  5.3 0.2 copy.4
  5.5 3.3 %collective-permute-start = (f32[8,33,128]{2,0,1:T(8,128)S(1)}, f32[8,33,128]{2,0,1:T(8,128)S(1)}, u32[]{:S(2)}, u32[]{:S(2)}) collective-permute-start(f32[8,33,128]{2,0,1:T(8,128)S(1)} %fusion.48), channel_id=1, source_target_pairs={{0,2},{2,0},{1,3},{3,1},{4,6},{6,4},{5,7},{7,5},{8,10},{10,8},{9,1... | collective-permute-start | bytes 405512 | tf_op jit(solution)/shard_map/ppermute | solution.py:22
  8.8 1.0 %collective-permute-done = f32[8,33,128]{2,0,1:T(8,128)S(1)} collective-permute-done((f32[8,33,128]{2,0,1:T(8,128)S(1)}, f32[8,33,128]{2,0,1:T(8,128)S(1)}, u32[]{:S(2)}, u32[]{:S(2)}) %collective-permute-start) | collective-permute-done | bytes 135200 | tf_op jit(solution)/shard_map/ppermute | solution.py:22
  9.8 0.1 collective-permute-start.1
  9.9 2.2 %collective-permute-start.2 = (f32[2,33,128]{2,0,1:T(2,128)S(1)}, f32[2,33,128]{2,0,1:T(2,128)S(1)}, u32[]{:S(2)}, u32[]{:S(2)}) collective-permute-start(f32[2,33,128]{2,0,1:T(2,128)S(1)} %get-tuple-element.22), channel_id=1, source_target_pairs={{0,16},{8,24},{16,0},{24,8},{1,17},{9,25},{17,1},{25,9},{2,18},{10... | collective-permute-start | bytes 101384 | tf_op jit(solution)/shard_map/ppermute | solution.py:22
  12.1 1.1 %collective-permute-start.3 = (f32[2,33,128]{2,0,1:T(2,128)S(1)}, f32[2,33,128]{2,0,1:T(2,128)S(1)}, u32[]{:S(2)}, u32[]{:S(2)}) collective-permute-start(f32[2,33,128]{2,0,1:T(2,128)S(1)} %get-tuple-element.21), channel_id=1, source_target_pairs={{0,24},{8,0},{16,8},{24,16},{1,25},{9,1},{17,9},{25,17},{2,26},{10... | collective-permute-start | bytes 101384 | tf_op jit(solution)/shard_map/ppermute | solution.py:22
  13.2 3.3 %fusion.24 = bf16[1024,256]{1,0:T(8,128)(2,1)} fusion(bf16[1024,3072]{1,0:T(8,128)(2,1)} %param.4, bf16[1,256,1024]{2,1,0:T(8,128)(2,1)} %param.3), kind=kOutput, calls=%fused_computation.33 | convolution fusion | flops 538705920 | bytes 3145728 | tf_op jit(solution)/shard_map/rtd,de->ret/dot_general | solution.py:147
  16.5 1.7 %collective-permute-start.4 = (f32[2,33,128]{2,0,1:T(2,128)S(1)}, f32[2,33,128]{2,0,1:T(2,128)S(1)}, u32[]{:S(2)}, u32[]{:S(2)}) collective-permute-start(f32[2,33,128]{2,0,1:T(2,128)S(1)} %add_add_fusion), channel_id=1, source_target_pairs={{0,32},{32,64},{64,96},{96,128},{128,160},{160,192},{192,224},{224... | collective-permute-start | bytes 101384 | tf_op jit(solution)/shard_map/ppermute | solution.py:22
  18.2 4.0 %collective-permute-start.5 = (f32[2,33,128]{2,0,1:T(2,128)S(1)}, f32[2,33,128]{2,0,1:T(2,128)S(1)}, u32[]{:S(2)}, u32[]{:S(2)}) collective-permute-start(f32[2,33,128]{2,0,1:T(2,128)S(1)} %add_add_fusion), channel_id=1, source_target_pairs={{0,224},{32,0},{64,32},{96,64},{128,96},{160,128},{192,160},{224,1... | collective-permute-start | bytes 101384 | tf_op jit(solution)/shard_map/ppermute | solution.py:22
  22.3 1.2 %collective-permute-done.4 = f32[2,33,128]{2,0,1:T(2,128)S(1)} collective-permute-done((f32[2,33,128]{2,0,1:T(2,128)S(1)}, f32[2,33,128]{2,0,1:T(2,128)S(1)}, u32[]{:S(2)}, u32[]{:S(2)}) %collective-permute-start.4) | collective-permute-done | bytes 33824 | tf_op jit(solution)/shard_map/ppermute | solution.py:22
  23.5 2.8 %select_reduce_fusion = (f32[16,256]{1,0:T(8,128)}, bf16[16,256,256]{1,2,0:T(8,128)(2,1)S(1)}) fusion(pred[256,256]{0,1:T(8,128)(4,1)S(1)} %iota_compare_fusion, bf16[256,16,64]{0,2,1:T(8,128)(2,1)} %bitcast.109, bf16[1,256,2,16,64]{1,4,3,2,0:T(8,128)(2,1)} %bitcast.118), kind=kOutput, calls=%fused_computation.3 | convolution fusion | flops 138932224 | bytes 3227648 | tf_op jit(solution)/shard_map/rnihd,rnjhd->rnhij/dot_general | solution.py:113
  26.3 2.7 %collective-permute-start.7 = (f32[2,33,128]{2,0,1:T(2,128)S(1)}, f32[2,33,128]{2,0,1:T(2,128)S(1)}, u32[]{:S(2)}, u32[]{:S(2)}) collective-permute-start(f32[2,33,128]{2,0,1:T(2,128)S(1)} %collective-permute-done.5), channel_id=1, source_target_pairs={{0,224},{32,0},{64,32},{96,64},{128,96},{160,128},{192,160},{224,1... | collective-permute-start | bytes 101384 | tf_op jit(solution)/shard_map/ppermute | solution.py:22
  29.0 1.5 %fusion.10 = f32[1,1,256,16,64]{2,4,3,1,0:T(8,128)} fusion(bf16[16,256,256]{1,2,0:T(8,128)(2,1)S(1)} %get-tuple-element.24, pred[256,256]{0,1:T(8,128)(4,1)S(1)} %iota_compare_fusion, bf16[1,256,2,16,64]{1,4,3,2,0:T(8,128)(2,1)S(1)} %bitcast.119), kind=kOutput, calls=%fused_computation.17 | convolution fusion | flops 135266304 | bytes 3735552 | tf_op jit(solution)/shard_map/rnhij,rnjhd->rnihd/dot_general | solution.py:118
  30.4 2.7 %collective-permute-start.9 = (f32[2,33,128]{2,0,1:T(2,128)S(1)}, f32[2,33,128]{2,0,1:T(2,128)S(1)}, u32[]{:S(2)}, u32[]{:S(2)}) collective-permute-start(f32[2,33,128]{2,0,1:T(2,128)S(1)} %collective-permute-done.7), channel_id=1, source_target_pairs={{0,224},{32,0},{64,32},{96,64},{128,96},{160,128},{192,160},{224,1... | collective-permute-start | bytes 101384 | tf_op jit(solution)/shard_map/ppermute | solution.py:22
  33.1 0.0 collective-permute-start.10
  33.3 0.9 %collective-permute-done.9 = f32[2,33,128]{2,0,1:T(2,128)S(1)} collective-permute-done((f32[2,33,128]{2,0,1:T(2,128)S(1)}, f32[2,33,128]{2,0,1:T(2,128)S(1)}, u32[]{:S(2)}, u32[]{:S(2)}) %collective-permute-start.9) | collective-permute-done | bytes 33824 | tf_op jit(solution)/shard_map/ppermute | solution.py:22
  34.1 3.1 %collective-permute-done.10 = f32[2,33,128]{2,0,1:T(2,128)} collective-permute-done((f32[2,33,128]{2,0,1:T(2,128)S(1)}, f32[2,33,128]{2,0,1:T(2,128)}, u32[]{:S(2)}, u32[]{:S(2)}) %collective-permute-start.10) | collective-permute-done | bytes 33824 | tf_op jit(solution)/shard_map/ppermute | solution.py:22
  37.2 0.1 select_add_fusion.6
  37.3 0.1 select_add_fusion.5
  37.4 0.5 collective-permute-start.11
  37.8 0.1 add_bitcast_fusion
  38.0 1.8 %collective-permute-start.12 = (f32[2,33,128]{2,0,1:T(2,128)S(1)}, f32[2,33,128]{2,0,1:T(2,128)S(1)}, u32[]{:S(2)}, u32[]{:S(2)}) collective-permute-start(f32[2,33,128]{2,0,1:T(2,128)S(1)} %get-tuple-element.19), channel_id=1, source_target_pairs={{0,16},{8,24},{16,0},{24,8},{1,17},{9,25},{17,1},{25,9},{2,18},{10... | collective-permute-start | bytes 101384 | tf_op jit(solution)/shard_map/ppermute | solution.py:22
  39.7 0.7 %collective-permute-start.13 = (f32[2,33,128]{2,0,1:T(2,128)S(1)}, f32[2,33,128]{2,0,1:T(2,128)}, u32[]{:S(2)}, u32[]{:S(2)}) collective-permute-start(f32[2,33,128]{2,0,1:T(2,128)S(1)} %get-tuple-element.18), channel_id=1, source_target_pairs={{0,24},{8,0},{16,8},{24,16},{1,25},{9,1},{17,9},{25,17},{2,26},{10... | collective-permute-start | bytes 101384 | tf_op jit(solution)/shard_map/ppermute | solution.py:22
  40.5 1.1 %collective-permute-done.11 = f32[2,33,128]{2,0,1:T(2,128)S(1)} collective-permute-done((f32[2,33,128]{2,0,1:T(2,128)S(1)}, f32[2,33,128]{2,0,1:T(2,128)S(1)}, u32[]{:S(2)}, u32[]{:S(2)}) %collective-permute-start.11) | collective-permute-done | bytes 33824 | tf_op jit(solution)/shard_map/ppermute | solution.py:22
  41.6 0.7 %collective-permute-done.12 = f32[2,33,128]{2,0,1:T(2,128)S(1)} collective-permute-done((f32[2,33,128]{2,0,1:T(2,128)S(1)}, f32[2,33,128]{2,0,1:T(2,128)S(1)}, u32[]{:S(2)}, u32[]{:S(2)}) %collective-permute-start.12) | collective-permute-done | bytes 33824 | tf_op jit(solution)/shard_map/ppermute | solution.py:22
  42.3 0.4 collective-permute-done.13
  42.7 0.8 %pad_maximum_fusion = f32[4,2,33,128]{3,1,2,0:T(2,128)S(1)} fusion(f32[1,2,33,128]{3,1,2,0:T(2,128)} %bitcast.16, f32[1,2,33,128]{3,1,2,0:T(2,128)S(1)} %bitcast.121, f32[1,2,33,128]{3,1,2,0:T(2,128)S(1)} %bitcast.120, f32[1,2,33,128]{3,1,2,0:T(2,128)S(1)} %get-tuple-element.17), kind=kLoop, calls=%fused_computation.68 | loop fusion | flops 101376 | bytes 270336 | tf_op jit(solution)/shard_map/stack | solution.py:98
  43.5 0.7 %gather_fusion = f32[4,2,33,128]{3,1,2,0:T(2,128)S(1)} fusion(f32[4,2,33,128]{3,1,2,0:T(2,128)S(1)} %pad_maximum_fusion, s32[1024]{0:T(1024)S(1)} %pad_clamp_fusion), kind=kCustom, calls=%fused_computation | custom fusion | bytes 270352 | tf_op jit(solution)/shard_map/gather | solution.py:98
  44.3 2.8 %collective-permute-start.14 = (f32[8,33,128]{2,0,1:T(8,128)S(1)}, f32[8,33,128]{2,0,1:T(8,128)}, u32[]{:S(2)}, u32[]{:S(2)}) collective-permute-start(f32[8,33,128]{2,0,1:T(8,128)S(1)} %select_add_fusion.1), channel_id=1, source_target_pairs={{0,4},{4,0},{1,5},{5,1},{2,6},{6,2},{3,7},{7,3},{8,12},{12,8},{9,1... | collective-permute-start | bytes 405512 | tf_op jit(solution)/shard_map/ppermute | solution.py:22
  47.1 2.7 %collective-permute-done.14 = f32[8,33,128]{2,0,1:T(8,128)} collective-permute-done((f32[8,33,128]{2,0,1:T(8,128)S(1)}, f32[8,33,128]{2,0,1:T(8,128)}, u32[]{:S(2)}, u32[]{:S(2)}) %collective-permute-start.14) | collective-permute-done | bytes 135200 | tf_op jit(solution)/shard_map/ppermute | solution.py:22
  49.9 1.0 %add_select_fusion = (f32[8,33,128]{2,0,1:T(8,128)S(1)}, f32[8,33,128]{2,0,1:T(8,128)S(1)}) fusion(f32[8,33,128]{2,0,1:T(8,128)S(1)} %collective-permute-done, pred[]{:T(512)S(6)} %eq.33, f32[8,33,128]{2,0,1:T(8,128)S(1)} %bitcast.108, f32[8,33,128]{2,0,1:T(8,128)} %collective-permute-done.14, s32[]{:T(128)S(6)} %select_n.334, ...), kind=kLoop, calls=%fused_computation.65 | loop fusion | flops 202752 | bytes 946181 | tf_op jit(solution)/shard_map/jit(_where)/select_n | solution.py:103
  50.9 0.1 broadcast_in_dim_broadcast_in_dim_reshape.6
  51.0 8.5 %collective-permute-start.15 = (f32[8,33,128]{2,1,0:T(8,128)S(1)}, f32[8,33,128]{2,1,0:T(8,128)S(1)}, u32[]{:S(2)}, u32[]{:S(2)}) collective-permute-start(f32[8,33,128]{2,1,0:T(8,128)S(1)} %copy.7), channel_id=1, source_target_pairs={{0,2},{2,0},{1,3},{3,1},{4,6},{6,4},{5,7},{7,5},{8,10},{10,8},{9,1... | collective-permute-start | bytes 405512 | tf_op jit(solution)/shard_map/ppermute | solution.py:22
  59.5 1.1 %fusion.31 = f32[256,8]{0,1:T(8,128)S(1)} fusion(f32[8,64]{1,0:T(8,128)S(1)} %fusion.57, bf16[1,1,16,64,256]{4,3,2,1,0:T(8,128)(2,1)} %bitcast.110, s32[]{:T(128)S(6)} %select_n.334), kind=kLoop, calls=%fused_computation.43 | loop fusion | flops 391168 | bytes 272388 | tf_op jit(solution)/shard_map/reduce_sum | solution.py:132
  60.6 0.7 %fusion.51 = f32[256,8]{0,1:T(8,128)S(1)} fusion(f32[256,8]{0,1:T(8,128)S(1)} %fusion.31, f32[1,1,16,256]{3,2,1,0:T(8,128)} %bitcast.122, s32[]{:T(128)S(6)} %select_n.334), kind=kLoop, calls=%fused_computation.81 | loop fusion | flops 2048 | bytes 24580 | tf_op jit(solution)/shard_map/div | solution.py:133
  61.4 1.5 %fusion.19 = bf16[1,1,256,8,64]{2,4,3,1,0:T(8,128)(2,1)S(1)} fusion(f32[1,1,256,16,64]{2,4,3,1,0:T(8,128)} %fusion.10, s32[]{:T(128)S(6)} %select_n.334, f32[256,8]{0,1:T(8,128)S(1)} %fusion.51, f32[8,64,64]{2,1,0:T(8,128)S(1)} %broadcast_in_dim_broadcast_in_dim_reshape.6, f32[16,64,64]{2,1,0:T(8,128)S(1)} %fusion.34, bf16[1,1,16,64,256]{4,3,2,1,0:T(8,128)(2,1)} %bitcast.111), kind=kOutput, calls=%fused_computation.28 | convolution fusion | flops 101122048 | bytes 1582592 | tf_op jit(solution)/shard_map/rnihd,rnhde->rnihe/dot_general | solution.py:129
  62.9 0.5 convolution_bitcast_fusion.1
  63.4 0.1 broadcast_in_dim_broadcast_in_dim_reshape.7
  63.5 1.1 %fusion.30 = f32[256,8]{0,1:T(8,128)S(1)} fusion(f32[8,64]{1,0:T(8,128)S(1)} %fusion.59, bf16[1,1,16,64,256]{4,3,2,1,0:T(8,128)(2,1)} %bitcast.112, s32[]{:T(128)S(6)} %select_n.335), kind=kLoop, calls=%fused_computation.41 | loop fusion | flops 391168 | bytes 272388 | tf_op jit(solution)/shard_map/reduce_sum | solution.py:132
  64.7 0.7 %fusion.50 = f32[256,8]{0,1:T(8,128)S(1)} fusion(f32[256,8]{0,1:T(8,128)S(1)} %fusion.30, f32[1,1,16,256]{3,2,1,0:T(8,128)} %bitcast.123, s32[]{:T(128)S(6)} %select_n.335), kind=kLoop, calls=%fused_computation.79 | loop fusion | flops 2048 | bytes 24580 | tf_op jit(solution)/shard_map/div | solution.py:133
  65.4 1.6 %fusion.18 = bf16[1,1,256,8,64]{2,4,3,1,0:T(8,128)(2,1)S(1)} fusion(f32[1,1,256,16,64]{2,4,3,1,0:T(8,128)} %fusion.10, s32[]{:T(128)S(6)} %select_n.335, f32[256,8]{0,1:T(8,128)S(1)} %fusion.50, f32[8,64,64]{2,1,0:T(8,128)S(1)} %broadcast_in_dim_broadcast_in_dim_reshape.7, f32[16,64,64]{2,1,0:T(8,128)} %copy-done.1, bf16[1,1,16,64,256]{4,3,2,1,0:T(8,128)(2,1)} %bitcast.113), kind=kOutput, calls=%fused_computation.27 | convolution fusion | flops 101122048 | bytes 1451520 | tf_op jit(solution)/shard_map/rnihd,rnhde->rnihe/dot_general | solution.py:129
  67.0 0.5 convolution_bitcast_fusion
  67.5 0.9 %add_convert_fusion = bf16[1,256,1024]{2,1,0:T(8,128)(2,1)} fusion(f32[1,256,1024]{2,1,0:T(8,128)S(1)} %convolution_bitcast_fusion.1, f32[1,256,1024]{2,1,0:T(8,128)S(1)} %convolution_bitcast_fusion), kind=kLoop, calls=%fused_computation.36 | loop fusion | flops 524288 | bytes 2621440 | tf_op jit(solution)/shard_map/convert_element_type | solution.py:184
  (34 shorter events, 0.4 us)
Async XLA Ops:
  0.0 62.9 %copy-start = (bf16[1024,1024]{1,0:T(8,128)(2,1)S(1)}, bf16[1024,1024]{1,0:T(8,128)(2,1)}, u32[]{:S(2)}) copy-start(bf16[1024,1024]{1,0:T(8,128)(2,1)} %param.5) | copy-start | bytes 6291460
  3.8 1.0 %copy-start.2 = (bf16[2048,256]{1,0:T(8,128)(2,1)}, bf16[2048,256]{1,0:T(8,128)(2,1)S(1)}, u32[]{:S(2)}) copy-start(bf16[2048,256]{1,0:T(8,128)(2,1)S(1)} %fusion.2) | copy-start | bytes 3145732
  4.8 56.6 %copy-start.1 = (f32[16,64,64]{2,1,0:T(8,128)}, f32[16,64,64]{2,1,0:T(8,128)S(1)}, u32[]{:S(2)}) copy-start(f32[16,64,64]{2,1,0:T(8,128)S(1)} %fusion.34) | copy-start | bytes 786436
  5.5 4.3 %collective-permute-start = (f32[8,33,128]{2,0,1:T(8,128)S(1)}, f32[8,33,128]{2,0,1:T(8,128)S(1)}, u32[]{:S(2)}, u32[]{:S(2)}) collective-permute-start(f32[8,33,128]{2,0,1:T(8,128)S(1)} %fusion.48), channel_id=1, source_target_pairs={{0,2},{2,0},{1,3},{3,1},{4,6},{6,4},{5,7},{7,5},{8,10},{10,8},{9,1... | collective-permute-start | bytes 405512 | tf_op jit(solution)/shard_map/ppermute | solution.py:22
  9.8 6.6 %collective-permute-start.1 = (f32[2,33,128]{2,0,1:T(2,128)S(1)}, f32[2,33,128]{2,0,1:T(2,128)S(1)}, u32[]{:S(2)}, u32[]{:S(2)}) collective-permute-start(f32[2,33,128]{2,0,1:T(2,128)S(1)} %get-tuple-element.20), channel_id=1, source_target_pairs={{0,8},{8,16},{16,24},{24,0},{1,9},{9,17},{17,25},{25,1},{2,10},{10... | collective-permute-start | bytes 101384 | tf_op jit(solution)/shard_map/ppermute | solution.py:22
  9.9 6.5 %collective-permute-start.2 = (f32[2,33,128]{2,0,1:T(2,128)S(1)}, f32[2,33,128]{2,0,1:T(2,128)S(1)}, u32[]{:S(2)}, u32[]{:S(2)}) collective-permute-start(f32[2,33,128]{2,0,1:T(2,128)S(1)} %get-tuple-element.22), channel_id=1, source_target_pairs={{0,16},{8,24},{16,0},{24,8},{1,17},{9,25},{17,1},{25,9},{2,18},{10... | collective-permute-start | bytes 101384 | tf_op jit(solution)/shard_map/ppermute | solution.py:22
  12.1 4.3 %collective-permute-start.3 = (f32[2,33,128]{2,0,1:T(2,128)S(1)}, f32[2,33,128]{2,0,1:T(2,128)S(1)}, u32[]{:S(2)}, u32[]{:S(2)}) collective-permute-start(f32[2,33,128]{2,0,1:T(2,128)S(1)} %get-tuple-element.21), channel_id=1, source_target_pairs={{0,24},{8,0},{16,8},{24,16},{1,25},{9,1},{17,9},{25,17},{2,26},{10... | collective-permute-start | bytes 101384 | tf_op jit(solution)/shard_map/ppermute | solution.py:22
  16.5 7.0 %collective-permute-start.4 = (f32[2,33,128]{2,0,1:T(2,128)S(1)}, f32[2,33,128]{2,0,1:T(2,128)S(1)}, u32[]{:S(2)}, u32[]{:S(2)}) collective-permute-start(f32[2,33,128]{2,0,1:T(2,128)S(1)} %add_add_fusion), channel_id=1, source_target_pairs={{0,32},{32,64},{64,96},{96,128},{128,160},{160,192},{192,224},{224... | collective-permute-start | bytes 101384 | tf_op jit(solution)/shard_map/ppermute | solution.py:22
  18.2 8.1 %collective-permute-start.5 = (f32[2,33,128]{2,0,1:T(2,128)S(1)}, f32[2,33,128]{2,0,1:T(2,128)S(1)}, u32[]{:S(2)}, u32[]{:S(2)}) collective-permute-start(f32[2,33,128]{2,0,1:T(2,128)S(1)} %add_add_fusion), channel_id=1, source_target_pairs={{0,224},{32,0},{64,32},{96,64},{128,96},{160,128},{192,160},{224,1... | collective-permute-start | bytes 101384 | tf_op jit(solution)/shard_map/ppermute | solution.py:22
  23.5 5.5 %collective-permute-start.6 = (f32[2,33,128]{2,0,1:T(2,128)S(1)}, f32[2,33,128]{2,0,1:T(2,128)S(1)}, u32[]{:S(2)}, u32[]{:S(2)}) collective-permute-start(f32[2,33,128]{2,0,1:T(2,128)S(1)} %collective-permute-done.4), channel_id=1, source_target_pairs={{0,32},{32,64},{64,96},{96,128},{128,160},{160,192},{192,224},{224... | collective-permute-start | bytes 101384 | tf_op jit(solution)/shard_map/ppermute | solution.py:22
  23.5 5.5 %copy-start.3 = (bf16[2048,256]{1,0:T(8,128)(2,1)S(1)}, bf16[2048,256]{1,0:T(8,128)(2,1)}, u32[]{:S(2)}) copy-start(bf16[2048,256]{1,0:T(8,128)(2,1)} %copy-done.2) | copy-start | bytes 3145732
  26.3 4.1 %collective-permute-start.7 = (f32[2,33,128]{2,0,1:T(2,128)S(1)}, f32[2,33,128]{2,0,1:T(2,128)S(1)}, u32[]{:S(2)}, u32[]{:S(2)}) collective-permute-start(f32[2,33,128]{2,0,1:T(2,128)S(1)} %collective-permute-done.5), channel_id=1, source_target_pairs={{0,224},{32,0},{64,32},{96,64},{128,96},{160,128},{192,160},{224,1... | collective-permute-start | bytes 101384 | tf_op jit(solution)/shard_map/ppermute | solution.py:22
  29.0 4.1 %collective-permute-start.8 = (f32[2,33,128]{2,0,1:T(2,128)S(1)}, f32[2,33,128]{2,0,1:T(2,128)S(1)}, u32[]{:S(2)}, u32[]{:S(2)}) collective-permute-start(f32[2,33,128]{2,0,1:T(2,128)S(1)} %collective-permute-done.6), channel_id=1, source_target_pairs={{0,32},{32,64},{64,96},{96,128},{128,160},{160,192},{192,224},{224... | collective-permute-start | bytes 101384 | tf_op jit(solution)/shard_map/ppermute | solution.py:22
  30.4 3.7 %collective-permute-start.9 = (f32[2,33,128]{2,0,1:T(2,128)S(1)}, f32[2,33,128]{2,0,1:T(2,128)S(1)}, u32[]{:S(2)}, u32[]{:S(2)}) collective-permute-start(f32[2,33,128]{2,0,1:T(2,128)S(1)} %collective-permute-done.7), channel_id=1, source_target_pairs={{0,224},{32,0},{64,32},{96,64},{128,96},{160,128},{192,160},{224,1... | collective-permute-start | bytes 101384 | tf_op jit(solution)/shard_map/ppermute | solution.py:22
  33.1 4.1 %collective-permute-start.10 = (f32[2,33,128]{2,0,1:T(2,128)S(1)}, f32[2,33,128]{2,0,1:T(2,128)}, u32[]{:S(2)}, u32[]{:S(2)}) collective-permute-start(f32[2,33,128]{2,0,1:T(2,128)S(1)} %collective-permute-done.8), channel_id=1, source_target_pairs={{0,32},{32,64},{64,96},{96,128},{128,160},{160,192},{192,224},{224... | collective-permute-start | bytes 101384 | tf_op jit(solution)/shard_map/ppermute | solution.py:22
  37.4 4.2 %collective-permute-start.11 = (f32[2,33,128]{2,0,1:T(2,128)S(1)}, f32[2,33,128]{2,0,1:T(2,128)S(1)}, u32[]{:S(2)}, u32[]{:S(2)}) collective-permute-start(f32[2,33,128]{2,0,1:T(2,128)S(1)} %select_add_fusion.5), channel_id=1, source_target_pairs={{0,8},{8,16},{16,24},{24,0},{1,9},{9,17},{17,25},{25,1},{2,10},{10... | collective-permute-start | bytes 101384 | tf_op jit(solution)/shard_map/ppermute | solution.py:22
  38.0 4.4 %collective-permute-start.12 = (f32[2,33,128]{2,0,1:T(2,128)S(1)}, f32[2,33,128]{2,0,1:T(2,128)S(1)}, u32[]{:S(2)}, u32[]{:S(2)}) collective-permute-start(f32[2,33,128]{2,0,1:T(2,128)S(1)} %get-tuple-element.19), channel_id=1, source_target_pairs={{0,16},{8,24},{16,0},{24,8},{1,17},{9,25},{17,1},{25,9},{2,18},{10... | collective-permute-start | bytes 101384 | tf_op jit(solution)/shard_map/ppermute | solution.py:22
  39.7 2.9 %collective-permute-start.13 = (f32[2,33,128]{2,0,1:T(2,128)S(1)}, f32[2,33,128]{2,0,1:T(2,128)}, u32[]{:S(2)}, u32[]{:S(2)}) collective-permute-start(f32[2,33,128]{2,0,1:T(2,128)S(1)} %get-tuple-element.18), channel_id=1, source_target_pairs={{0,24},{8,0},{16,8},{24,16},{1,25},{9,1},{17,9},{25,17},{2,26},{10... | collective-permute-start | bytes 101384 | tf_op jit(solution)/shard_map/ppermute | solution.py:22
  44.3 5.6 %collective-permute-start.14 = (f32[8,33,128]{2,0,1:T(8,128)S(1)}, f32[8,33,128]{2,0,1:T(8,128)}, u32[]{:S(2)}, u32[]{:S(2)}) collective-permute-start(f32[8,33,128]{2,0,1:T(8,128)S(1)} %select_add_fusion.1), channel_id=1, source_target_pairs={{0,4},{4,0},{1,5},{5,1},{2,6},{6,2},{3,7},{7,3},{8,12},{12,8},{9,1... | collective-permute-start | bytes 405512 | tf_op jit(solution)/shard_map/ppermute | solution.py:22
  51.0 12.4 %collective-permute-start.15 = (f32[8,33,128]{2,1,0:T(8,128)S(1)}, f32[8,33,128]{2,1,0:T(8,128)S(1)}, u32[]{:S(2)}, u32[]{:S(2)}) collective-permute-start(f32[8,33,128]{2,1,0:T(8,128)S(1)} %copy.7), channel_id=1, source_target_pairs={{0,2},{2,0},{1,3},{3,1},{4,6},{6,4},{5,7},{7,5},{8,10},{10,8},{9,1... | collective-permute-start | bytes 405512 | tf_op jit(solution)/shard_map/ppermute | solution.py:22

commit v15 on v13

--- a/solution.py
+++ b/solution.py
@@ -74,6 +74,12 @@
     column = came[0]
     for c in came[1:]:
         column = add(column, c)
+    column = add(column, swap(column, "seg_x"))
+    stacked = jnp.stack(came)
+    column, stacked = lax.optimization_barrier((column, stacked))
+    theirs = swap(jnp.concatenate([stacked.reshape((-1,) + chip.shape[1:]), chip], axis=0), "seg_x")
+    their_came = theirs[: stacked.shape[0] * stacked.shape[1]].reshape(stacked.shape)
+    their_chip = theirs[stacked.shape[0] * stacked.shape[1]:]
     before_z = tmap(jnp.zeros_like, column)
     left = right = column
     for r in range(1, n_z // 2 + 1):
@@ -87,7 +93,7 @@
     def for_row(t):
         out = before_z
         for s, c in enumerate(came):
-            out = add(out, keep(c, (y - s) % n_y < t))
+            out = add(out, keep(c + their_came[s], (y - s) % n_y < t))
         return out
 
     pieces = [for_row(y)] + [
@@ -98,7 +104,7 @@
         lambda *p: jnp.stack(p)[order].reshape((-1,) + p[0].shape[1:]),
         *pieces,
     )
-    half = add(mine, swap(add(mine, keep(chip, xh == 0)), "seg_x"))
+    half = add(mine, keep(their_chip, xh == 1))
     got = swap(add(half, keep(own_c, core == 0)), "frm")
     own = tmap(lambda a, c: jnp.where(core == 0, a, a + c), half, got_c)
     return (own, got), carry

time: 66 us -> 72.5 us (1.098)
  other arithmetic: 2.14 us -> 6.72 us
  starting transfers between devices: 32.2 us -> 33.4 us
  local copies, waits for them, and re-layouts: 3.48 us -> 2.31 us
  waiting for transfers between devices: 11.8 us -> 12.9 us
    another operation x2, other arithmetic: 0.19 us -> 1.53 us  [entering(): jnp.stack(p)[order].reshape((-1,) + p[0].shape[1:])]
    ppermute x16 -> x17, starting transfers between devices: 32.2 us -> 33.4 us  [send(): return tmap(lambda t: lax.ppermute(t, axis, perm=pairs), tree)]
    ppermute x16 -> x17, waiting for transfers between devices: 11.8 us -> 12.9 us  [send(): return tmap(lambda t: lax.ppermute(t, axis, perm=pairs), tree)]
    select_n x1, other arithmetic: 0.04 us -> 0.96 us  [entering(): own = tmap(lambda a, c: jnp.where(core == 0, a, a + c), half, got_c)]
    slice x1 -> x0, local copies, waits for them, and re-layouts: 0.85 us -> none  [heads_of(): prior_k = prior[:, rows_kv, :total_k.shape[1]]]
    add x1, other arithmetic: 0.01 us -> 0.78 us  [finish(): before_k = jnp.cumsum(k_blocks, axis=1) - k_blocks + prior_k[:, None]]
  transfers between devices with their start and end apart: 16 -> 17, of which waited for: 9 -> 10; matrix products, arithmetic and copies ran while one was open for 11% -> 12% of each run, Pallas kernels for 0% -> 0%
where the time goes in v15:
time: 72.5 us; the launch traced here: 72.1 us
  starting transfers between devices  33.4 us (46%)
  matrix products  16.4 us (23%)
  waiting for transfers between devices  12.9 us (18%)
  other arithmetic  6.72 us (9%)
  local copies, waits for them, and re-layouts  2.31 us (3%)
    ppermute x17, starting transfers between devices, send(): return tmap(lambda t: lax.ppermute(t, axis, perm=pairs), tree)  33.4 us
    ppermute x17, waiting for transfers between devices, send(): return tmap(lambda t: lax.ppermute(t, axis, perm=pairs), tree)  12.9 us
    dot_general x2, matrix products, project(): jnp.einsum('rtd,de->ret', frames_in, w, preferred_element_type=jnp.float32)  7.03 us
    dot_general x2, matrix products, finish(): jnp.einsum('rnihd,rnhde->rnihe', pq32, before_kv, precision=lax.Precision...  2.94 us
    dot_general x1, matrix products, block_terms(): jnp.einsum('rnihd,rnjhd->rnhij', pq, pk, preferred_element_type=jnp.float32)  2.83 us
    dot_general x2, matrix products, heads_of(): jnp.einsum('rtd,de->rte', heads_out, rows_w, preferred_element_type=jnp.f...  1.73 us
    another operation x2, other arithmetic, entering(): jnp.stack(p)[order].reshape((-1,) + p[0].shape[1:])  1.53 us
    dot_general x1, matrix products, block_terms(): jnp.einsum('rnhij,rnjhd->rnihd', weights, vv, preferred_element_type=jnp....  1.46 us
  transfers between devices with their start and end apart: 17, of which 10 were waited for; matrix products, arithmetic and copies ran while one was open for 12% of the time, Pallas kernels for 0%

profile of v15, /device:TPU:1, one launch (start us, length us, event | category | flops | bytes accessed | tf_op | source)
XLA Modules:
  0.0 72.1 jit_solution(6933812113443771980)
XLA Ops:
  0.0 3.8 %fusion.2 = bf16[2048,256]{1,0:T(8,128)(2,1)S(1)} fusion(bf16[1024,3072]{1,0:T(8,128)(2,1)} %param.4, bf16[1,256,1024]{2,1,0:T(8,128)(2,1)} %param.3), kind=kOutput, calls=%fused_computation.5 | convolution fusion | flops 1074266112 | bytes 5767168 | tf_op jit(solution)/shard_map/rtd,de->ret/dot_general | solution.py:153
  3.8 0.4 fusion.37
  4.2 0.6 copy-done.2
  4.8 0.3 convert_reduce_fusion
  5.1 0.1 reshape_squeeze.4
  5.3 0.2 copy.18
  5.5 0.3 copy-done.4
  5.7 3.3 %collective-permute-start = (f32[8,33,128]{2,0,1:T(8,128)S(1)}, f32[8,33,128]{2,0,1:T(8,128)S(1)}, u32[]{:S(2)}, u32[]{:S(2)}) collective-permute-start(f32[8,33,128]{2,0,1:T(8,128)S(1)} %fusion.51), channel_id=1, source_target_pairs={{0,2},{2,0},{1,3},{3,1},{4,6},{6,4},{5,7},{7,5},{8,10},{10,8},{9,1... | collective-permute-start | bytes 405512 | tf_op jit(solution)/shard_map/ppermute | solution.py:22
  9.0 3.3 %fusion.26 = bf16[1024,256]{1,0:T(8,128)(2,1)} fusion(bf16[1024,3072]{1,0:T(8,128)(2,1)} %param.4, bf16[1,256,1024]{2,1,0:T(8,128)(2,1)} %param.3), kind=kOutput, calls=%fused_computation.34 | convolution fusion | flops 538705920 | bytes 3145728 | tf_op jit(solution)/shard_map/rtd,de->ret/dot_general | solution.py:153
  12.4 1.1 %collective-permute-start.3 = (f32[2,33,128]{2,0,1:T(2,128)S(1)}, f32[2,33,128]{2,0,1:T(2,128)S(1)}, u32[]{:S(2)}, u32[]{:S(2)}) collective-permute-start(f32[2,33,128]{2,0,1:T(2,128)S(1)} %get-tuple-element.28), channel_id=1, source_target_pairs={{0,24},{8,0},{16,8},{24,16},{1,25},{9,1},{17,9},{25,17},{2,26},{10... | collective-permute-start | bytes 101384 | tf_op jit(solution)/shard_map/ppermute | solution.py:22
  13.5 0.4 collective-permute-start.1
  13.9 1.2 %collective-permute-start.2 = (f32[2,33,128]{2,0,1:T(2,128)S(1)}, f32[2,33,128]{2,0,1:T(2,128)S(1)}, u32[]{:S(2)}, u32[]{:S(2)}) collective-permute-start(f32[2,33,128]{2,0,1:T(2,128)S(1)} %get-tuple-element.29), channel_id=1, source_target_pairs={{0,16},{8,24},{16,0},{24,8},{1,17},{9,25},{17,1},{25,9},{2,18},{10... | collective-permute-start | bytes 101384 | tf_op jit(solution)/shard_map/ppermute | solution.py:22
  15.2 2.2 %collective-permute-done.1 = f32[2,33,128]{2,0,1:T(2,128)S(1)} collective-permute-done((f32[2,33,128]{2,0,1:T(2,128)S(1)}, f32[2,33,128]{2,0,1:T(2,128)S(1)}, u32[]{:S(2)}, u32[]{:S(2)}) %collective-permute-start.1) | collective-permute-done | bytes 33824 | tf_op jit(solution)/shard_map/ppermute | solution.py:22
  17.5 0.8 %collective-permute-done.2 = f32[2,33,128]{2,0,1:T(2,128)S(1)} collective-permute-done((f32[2,33,128]{2,0,1:T(2,128)S(1)}, f32[2,33,128]{2,0,1:T(2,128)S(1)}, u32[]{:S(2)}, u32[]{:S(2)}) %collective-permute-start.2) | collective-permute-done | bytes 33824 | tf_op jit(solution)/shard_map/ppermute | solution.py:22
  18.3 2.4 %collective-permute-start.4 = (f32[2,33,128]{2,0,1:T(2,128)S(1)}, f32[2,33,128]{2,0,1:T(2,128)S(1)}, u32[]{:S(2)}, u32[]{:S(2)}) collective-permute-start(f32[2,33,128]{2,0,1:T(2,128)S(1)} %add_add_fusion), channel_id=1, source_target_pairs={{0,4},{4,0},{1,5},{5,1},{2,6},{6,2},{3,7},{7,3},{8,12},{12,8},{9,1... | collective-permute-start | bytes 101384 | tf_op jit(solution)/shard_map/ppermute | solution.py:22
  20.8 1.9 %collective-permute-done.4 = f32[2,33,128]{2,0,1:T(2,128)S(1)} collective-permute-done((f32[2,33,128]{2,0,1:T(2,128)S(1)}, f32[2,33,128]{2,0,1:T(2,128)S(1)}, u32[]{:S(2)}, u32[]{:S(2)}) %collective-permute-start.4) | collective-permute-done | bytes 33824 | tf_op jit(solution)/shard_map/ppermute | solution.py:22
  22.7 1.3 %collective-permute-start.5 = (f32[2,33,128]{2,0,1:T(2,128)S(1)}, f32[2,33,128]{2,0,1:T(2,128)S(1)}, u32[]{:S(2)}, u32[]{:S(2)}) collective-permute-start(f32[2,33,128]{2,0,1:T(2,128)S(1)} %add.330), channel_id=1, source_target_pairs={{0,32},{32,64},{64,96},{96,128},{128,160},{160,192},{192,224},{224... | collective-permute-start | bytes 101384 | tf_op jit(solution)/shard_map/ppermute | solution.py:22
  24.0 2.8 %select_reduce_fusion = (f32[16,256]{1,0:T(8,128)}, bf16[16,256,256]{1,2,0:T(8,128)(2,1)S(1)}) fusion(pred[256,256]{0,1:T(8,128)(4,1)S(1)} %iota_compare_fusion, bf16[256,16,64]{0,2,1:T(8,128)(2,1)} %bitcast.116, bf16[1,256,2,16,64]{1,4,3,2,0:T(8,128)(2,1)} %bitcast.127), kind=kOutput, calls=%fused_computation.3 | convolution fusion | flops 138932224 | bytes 3227648 | tf_op jit(solution)/shard_map/rnihd,rnjhd->rnhij/dot_general | solution.py:119
  26.8 4.0 %collective-permute-start.6 = (f32[2,33,128]{2,0,1:T(2,128)S(1)}, f32[2,33,128]{2,0,1:T(2,128)S(1)}, u32[]{:S(2)}, u32[]{:S(2)}) collective-permute-start(f32[2,33,128]{2,0,1:T(2,128)S(1)} %add.330), channel_id=1, source_target_pairs={{0,224},{32,0},{64,32},{96,64},{128,96},{160,128},{192,160},{224,1... | collective-permute-start | bytes 101384 | tf_op jit(solution)/shard_map/ppermute | solution.py:22
  30.8 1.5 %fusion.10 = f32[1,1,256,16,64]{2,4,3,1,0:T(8,128)} fusion(bf16[16,256,256]{1,2,0:T(8,128)(2,1)S(1)} %get-tuple-element.36, pred[256,256]{0,1:T(8,128)(4,1)S(1)} %iota_compare_fusion, bf16[1,256,2,16,64]{1,4,3,2,0:T(8,128)(2,1)S(1)} %bitcast.128), kind=kOutput, calls=%fused_computation.17 | convolution fusion | flops 135266304 | bytes 3735552 | tf_op jit(solution)/shard_map/rnhij,rnjhd->rnihd/dot_general | solution.py:124
  32.3 2.7 %collective-permute-start.8 = (f32[2,33,128]{2,0,1:T(2,128)S(1)}, f32[2,33,128]{2,0,1:T(2,128)}, u32[]{:S(2)}, u32[]{:S(2)}) collective-permute-start(f32[2,33,128]{2,0,1:T(2,128)S(1)} %collective-permute-done.6), channel_id=1, source_target_pairs={{0,224},{32,0},{64,32},{96,64},{128,96},{160,128},{192,160},{224,1... | collective-permute-start | bytes 101384 | tf_op jit(solution)/shard_map/ppermute | solution.py:22
  35.1 0.7 %pad_maximum_fusion = f32[16,33,128]{2,0,1:T(8,128)} fusion(f32[8,33,128]{2,0,1:T(8,128)S(1)} %select_add_fusion.1, f32[8,33,128]{2,0,1:T(8,128)S(1)} %bitcast.114), kind=kLoop, calls=%fused_computation.53 | loop fusion | flops 67584 | bytes 540672 | tf_op jit(solution)/shard_map/concatenate | solution.py:80
  35.8 2.7 %collective-permute-start.12 = (f32[16,33,128]{2,0,1:T(8,128)}, f32[16,33,128]{2,0,1:T(8,128)S(1)}, u32[]{:S(2)}, u32[]{:S(2)}) collective-permute-start(f32[16,33,128]{2,0,1:T(8,128)} %pad_maximum_fusion), channel_id=1, source_target_pairs={{0,4},{4,0},{1,5},{5,1},{2,6},{6,2},{3,7},{7,3},{8,12},{12,8},{9,1... | collective-permute-start | bytes 811016 | tf_op jit(solution)/shard_map/ppermute | solution.py:22
  38.5 2.7 %collective-permute-start.10 = (f32[2,33,128]{2,0,1:T(2,128)}, f32[2,33,128]{2,0,1:T(2,128)}, u32[]{:S(2)}, u32[]{:S(2)}) collective-permute-start(f32[2,33,128]{2,0,1:T(2,128)} %collective-permute-done.8), channel_id=1, source_target_pairs={{0,224},{32,0},{64,32},{96,64},{128,96},{160,128},{192,160},{224,1... | collective-permute-start | bytes 101384 | tf_op jit(solution)/shard_map/ppermute | solution.py:22
  41.3 1.2 %collective-permute-done.10 = f32[2,33,128]{2,0,1:T(2,128)} collective-permute-done((f32[2,33,128]{2,0,1:T(2,128)}, f32[2,33,128]{2,0,1:T(2,128)}, u32[]{:S(2)}, u32[]{:S(2)}) %collective-permute-start.10) | collective-permute-done | bytes 33824 | tf_op jit(solution)/shard_map/ppermute | solution.py:22
  42.6 3.1 %collective-permute-done.11 = f32[2,33,128]{2,0,1:T(2,128)} collective-permute-done((f32[2,33,128]{2,0,1:T(2,128)}, f32[2,33,128]{2,0,1:T(2,128)}, u32[]{:S(2)}, u32[]{:S(2)}) %collective-permute-start.11) | collective-permute-done | bytes 33824 | tf_op jit(solution)/shard_map/ppermute | solution.py:22
  45.7 0.1 select_add_fusion.5
  45.8 0.7 add_bitcast_fusion
  46.5 0.1 select_add_fusion.4
  46.7 0.3 collective-permute-start.13
  46.9 3.6 %collective-permute-start.14 = (f32[2,33,128]{2,0,1:T(2,128)S(1)}, f32[2,33,128]{2,0,1:T(2,128)S(1)}, u32[]{:S(2)}, u32[]{:S(2)}) collective-permute-start(f32[2,33,128]{2,0,1:T(2,128)S(1)} %get-tuple-element.25), channel_id=1, source_target_pairs={{0,16},{8,24},{16,0},{24,8},{1,17},{9,25},{17,1},{25,9},{2,18},{10... | collective-permute-start | bytes 101384 | tf_op jit(solution)/shard_map/ppermute | solution.py:22
  50.5 0.3 collective-permute-done.13
  50.8 1.4 %collective-permute-done.14 = f32[2,33,128]{2,0,1:T(2,128)S(1)} collective-permute-done((f32[2,33,128]{2,0,1:T(2,128)S(1)}, f32[2,33,128]{2,0,1:T(2,128)S(1)}, u32[]{:S(2)}, u32[]{:S(2)}) %collective-permute-start.14) | collective-permute-done | bytes 33824 | tf_op jit(solution)/shard_map/ppermute | solution.py:22
  52.2 1.1 %collective-permute-done.15 = f32[2,33,128]{2,0,1:T(2,128)S(1)} collective-permute-done((f32[2,33,128]{2,0,1:T(2,128)S(1)}, f32[2,33,128]{2,0,1:T(2,128)S(1)}, u32[]{:S(2)}, u32[]{:S(2)}) %collective-permute-start.15) | collective-permute-done | bytes 33824 | tf_op jit(solution)/shard_map/ppermute | solution.py:22
  53.3 0.8 %pad_maximum_fusion.2 = f32[4,2,33,128]{3,1,2,0:T(2,128)S(1)} fusion(f32[1,2,33,128]{3,1,2,0:T(2,128)S(1)} %bitcast.131, f32[1,2,33,128]{3,1,2,0:T(2,128)S(1)} %bitcast.130, f32[1,2,33,128]{3,1,2,0:T(2,128)S(1)} %bitcast.129, f32[1,2,33,128]{3,1,2,0:T(2,128)} %get-tuple-element.17), kind=kLoop, calls=%fused_computation.73 | loop fusion | flops 101376 | bytes 270336 | tf_op jit(solution)/shard_map/stack | solution.py:104
  54.1 0.7 gather_fusion
  54.9 1.0 %add_select_fusion = (f32[8,33,128]{2,0,1:T(8,128)S(1)}, f32[8,33,128]{2,0,1:T(8,128)S(1)}) fusion(f32[8,33,128]{2,0,1:T(8,128)S(1)} %collective-permute-done, pred[]{:T(512)S(6)} %eq.33, f32[8,33,128]{2,0,1:T(8,128)S(1)} %bitcast.115, f32[16,33,128]{2,0,1:T(8,128)} %copy-done.1, pred[]{:T(512)S(6)} %eq.34, s32[]{:T(128)S(6)} %select_n.334, ...), kind=kLoop, calls=%fused_computation.67 | loop fusion | flops 236544 | bytes 946182 | tf_op jit(solution)/shard_map/jit(_where)/select_n | solution.py:109
  55.8 7.6 %collective-permute-start.16 = (f32[8,33,128]{2,0,1:T(8,128)S(1)}, f32[8,33,128]{2,0,1:T(8,128)S(1)}, u32[]{:S(2)}, u32[]{:S(2)}) collective-permute-start(f32[8,33,128]{2,0,1:T(8,128)S(1)} %get-tuple-element.23), channel_id=1, source_target_pairs={{0,2},{2,0},{1,3},{3,1},{4,6},{6,4},{5,7},{7,5},{8,10},{10,8},{9,1... | collective-permute-start | bytes 405512 | tf_op jit(solution)/shard_map/ppermute | solution.py:22
  63.5 0.1 broadcast_in_dim_broadcast_in_dim_reshape.6
  63.6 0.8 %collective-permute-done.16 = f32[8,33,128]{2,0,1:T(8,128)S(1)} collective-permute-done((f32[8,33,128]{2,0,1:T(8,128)S(1)}, f32[8,33,128]{2,0,1:T(8,128)S(1)}, u32[]{:S(2)}, u32[]{:S(2)}) %collective-permute-start.16) | collective-permute-done | bytes 135200 | tf_op jit(solution)/shard_map/ppermute | solution.py:22
  64.5 0.1 broadcast_in_dim_broadcast_in_dim_reshape.7
  64.6 0.8 %fusion.61 = (f32[8,64]{1,0:T(8,128)S(1)}, f32[8,64]{1,0:T(8,128)S(1)}) fusion(f32[16,64]{1,0:T(8,128)} %copy-done.4, s32[]{:T(128)S(6)} %select_n.334, f32[8,33,128]{2,0,1:T(8,128)S(1)} %get-tuple-element.22, f32[8,33,128]{2,0,1:T(8,128)S(1)} %collective-permute-done.16, s32[]{:T(128)S(6)} %select_n.335), kind=kLoop, calls=%fused_computation.102 | loop fusion | flops 2048 | bytes 12296 | tf_op jit(solution)/shard_map/add | solution.py:133
  65.4 1.3 %fusion.33 = (f32[256,8]{0,1:T(8,128)S(1)}, f32[256,8]{0,1:T(8,128)S(1)}) fusion(f32[8,64]{1,0:T(8,128)S(1)} %get-tuple-element.34, bf16[1,1,16,64,256]{4,3,2,1,0:T(8,128)(2,1)} %bitcast.117, s32[]{:T(128)S(6)} %select_n.335, f32[8,64]{1,0:T(8,128)S(1)} %get-tuple-element.33, s32[]{:T(128)S(6)} %select_n.334), kind=kLoop, calls=%fused_computation.42 | loop fusion | flops 782336 | bytes 544776 | tf_op jit(solution)/shard_map/reduce_sum | solution.py:138
  66.6 0.7 %fusion.54 = (f32[256,8]{0,1:T(8,128)S(1)}, f32[256,8]{0,1:T(8,128)S(1)}) fusion(f32[256,8]{0,1:T(8,128)S(1)} %get-tuple-element.15, f32[1,1,16,256]{3,2,1,0:T(8,128)} %bitcast.132, s32[]{:T(128)S(6)} %select_n.335, f32[256,8]{0,1:T(8,128)S(1)} %get-tuple-element.16, s32[]{:T(128)S(6)} %select_n.334), kind=kLoop, calls=%fused_computation.88 | loop fusion | flops 4096 | bytes 49160 | tf_op jit(solution)/shard_map/div | solution.py:139
  67.4 1.6 %fusion.20 = bf16[1,1,256,8,64]{2,4,3,1,0:T(8,128)(2,1)S(1)} fusion(f32[1,1,256,16,64]{2,4,3,1,0:T(8,128)} %fusion.10, s32[]{:T(128)S(6)} %select_n.335, f32[256,8]{0,1:T(8,128)S(1)} %get-tuple-element.31, f32[8,64,64]{2,1,0:T(8,128)S(1)} %broadcast_in_dim_broadcast_in_dim_reshape.7, f32[16,64,64]{2,1,0:T(8,128)S(1)} %fusion.37, ...), kind=kOutput, calls=%fused_computation.28 | convolution fusion | flops 101122048 | bytes 1582592 | tf_op jit(solution)/shard_map/rnihd,rnhde->rnihe/dot_general | solution.py:135
  68.9 1.4 %fusion.21 = bf16[1,1,256,8,64]{2,4,3,1,0:T(8,128)(2,1)S(1)} fusion(f32[1,1,256,16,64]{2,4,3,1,0:T(8,128)S(1)} %copy-done.8, s32[]{:T(128)S(6)} %select_n.334, f32[256,8]{0,1:T(8,128)S(1)} %get-tuple-element.32, f32[8,64,64]{2,1,0:T(8,128)S(1)} %broadcast_in_dim_broadcast_in_dim_reshape.6, f32[16,64,64]{2,1,0:T(8,128)S(1)} %fusion.37, ...), kind=kOutput, calls=%fused_computation.29 | convolution fusion | flops 101122048 | bytes 1582592 | tf_op jit(solution)/shard_map/rnihd,rnhde->rnihe/dot_general | solution.py:135
  70.3 0.5 fusion.29
  70.8 1.3 %fusion.15 = bf16[1,256,1024]{2,1,0:T(8,128)(2,1)} fusion(f32[256,1024]{1,0:T(8,128)S(1)} %fusion.29, bf16[256,512]{0,1:T(8,128)(2,1)S(1)} %bitcast.123, bf16[1024,1024]{1,0:T(8,128)(2,1)S(1)} %copy-done, s32[]{:T(128)S(6)} %select_n.404), kind=kOutput, calls=%fused_computation.21 | convolution fusion | flops 268959744 | bytes 2883588 | tf_op jit(solution)/shard_map/rtd,de->rte/dot_general | solution.py:185
  (44 shorter events, 0.6 us)
Async XLA Ops:
  0.0 70.3 %copy-start = (bf16[1024,1024]{1,0:T(8,128)(2,1)S(1)}, bf16[1024,1024]{1,0:T(8,128)(2,1)}, u32[]{:S(2)}) copy-start(bf16[1024,1024]{1,0:T(8,128)(2,1)} %param.5) | copy-start | bytes 6291460
  3.8 1.0 %copy-start.2 = (bf16[2048,256]{1,0:T(8,128)(2,1)}, bf16[2048,256]{1,0:T(8,128)(2,1)S(1)}, u32[]{:S(2)}) copy-start(bf16[2048,256]{1,0:T(8,128)(2,1)S(1)} %fusion.2) | copy-start | bytes 3145732
  5.1 0.6 copy-start.4
  5.7 6.6 %collective-permute-start = (f32[8,33,128]{2,0,1:T(8,128)S(1)}, f32[8,33,128]{2,0,1:T(8,128)S(1)}, u32[]{:S(2)}, u32[]{:S(2)}) collective-permute-start(f32[8,33,128]{2,0,1:T(8,128)S(1)} %fusion.51), channel_id=1, source_target_pairs={{0,2},{2,0},{1,3},{3,1},{4,6},{6,4},{5,7},{7,5},{8,10},{10,8},{9,1... | collective-permute-start | bytes 405512 | tf_op jit(solution)/shard_map/ppermute | solution.py:22
  12.4 2.9 %collective-permute-start.3 = (f32[2,33,128]{2,0,1:T(2,128)S(1)}, f32[2,33,128]{2,0,1:T(2,128)S(1)}, u32[]{:S(2)}, u32[]{:S(2)}) collective-permute-start(f32[2,33,128]{2,0,1:T(2,128)S(1)} %get-tuple-element.28), channel_id=1, source_target_pairs={{0,24},{8,0},{16,8},{24,16},{1,25},{9,1},{17,9},{25,17},{2,26},{10... | collective-permute-start | bytes 101384 | tf_op jit(solution)/shard_map/ppermute | solution.py:22
  13.5 4.0 %collective-permute-start.1 = (f32[2,33,128]{2,0,1:T(2,128)S(1)}, f32[2,33,128]{2,0,1:T(2,128)S(1)}, u32[]{:S(2)}, u32[]{:S(2)}) collective-permute-start(f32[2,33,128]{2,0,1:T(2,128)S(1)} %get-tuple-element.30), channel_id=1, source_target_pairs={{0,8},{8,16},{16,24},{24,0},{1,9},{9,17},{17,25},{25,1},{2,10},{10... | collective-permute-start | bytes 101384 | tf_op jit(solution)/shard_map/ppermute | solution.py:22
  13.9 4.3 %collective-permute-start.2 = (f32[2,33,128]{2,0,1:T(2,128)S(1)}, f32[2,33,128]{2,0,1:T(2,128)S(1)}, u32[]{:S(2)}, u32[]{:S(2)}) collective-permute-start(f32[2,33,128]{2,0,1:T(2,128)S(1)} %get-tuple-element.29), channel_id=1, source_target_pairs={{0,16},{8,24},{16,0},{24,8},{1,17},{9,25},{17,1},{25,9},{2,18},{10... | collective-permute-start | bytes 101384 | tf_op jit(solution)/shard_map/ppermute | solution.py:22
  18.3 4.4 %collective-permute-start.4 = (f32[2,33,128]{2,0,1:T(2,128)S(1)}, f32[2,33,128]{2,0,1:T(2,128)S(1)}, u32[]{:S(2)}, u32[]{:S(2)}) collective-permute-start(f32[2,33,128]{2,0,1:T(2,128)S(1)} %add_add_fusion), channel_id=1, source_target_pairs={{0,4},{4,0},{1,5},{5,1},{2,6},{6,2},{3,7},{7,3},{8,12},{12,8},{9,1... | collective-permute-start | bytes 101384 | tf_op jit(solution)/shard_map/ppermute | solution.py:22
  22.7 8.1 %collective-permute-start.5 = (f32[2,33,128]{2,0,1:T(2,128)S(1)}, f32[2,33,128]{2,0,1:T(2,128)S(1)}, u32[]{:S(2)}, u32[]{:S(2)}) collective-permute-start(f32[2,33,128]{2,0,1:T(2,128)S(1)} %add.330), channel_id=1, source_target_pairs={{0,32},{32,64},{64,96},{96,128},{128,160},{160,192},{192,224},{224... | collective-permute-start | bytes 101384 | tf_op jit(solution)/shard_map/ppermute | solution.py:22
  24.0 6.8 %copy-start.3 = (bf16[2048,256]{1,0:T(8,128)(2,1)S(1)}, bf16[2048,256]{1,0:T(8,128)(2,1)}, u32[]{:S(2)}) copy-start(bf16[2048,256]{1,0:T(8,128)(2,1)} %copy-done.2) | copy-start | bytes 3145732
  26.8 5.5 %collective-permute-start.6 = (f32[2,33,128]{2,0,1:T(2,128)S(1)}, f32[2,33,128]{2,0,1:T(2,128)S(1)}, u32[]{:S(2)}, u32[]{:S(2)}) collective-permute-start(f32[2,33,128]{2,0,1:T(2,128)S(1)} %add.330), channel_id=1, source_target_pairs={{0,224},{32,0},{64,32},{96,64},{128,96},{160,128},{192,160},{224,1... | collective-permute-start | bytes 101384 | tf_op jit(solution)/shard_map/ppermute | solution.py:22
  30.8 1.5 %copy-start.5 = (f32[2,33,128]{2,0,1:T(2,128)}, f32[2,33,128]{2,0,1:T(2,128)S(1)}, u32[]{:S(2)}) copy-start(f32[2,33,128]{2,0,1:T(2,128)S(1)} %collective-permute-done.5) | copy-start | bytes 101380
  30.8 4.3 %collective-permute-start.7 = (f32[2,33,128]{2,0,1:T(2,128)S(1)}, f32[2,33,128]{2,0,1:T(2,128)S(1)}, u32[]{:S(2)}, u32[]{:S(2)}) collective-permute-start(f32[2,33,128]{2,0,1:T(2,128)S(1)} %collective-permute-done.5), channel_id=1, source_target_pairs={{0,32},{32,64},{64,96},{96,128},{128,160},{160,192},{192,224},{224... | collective-permute-start | bytes 101384 | tf_op jit(solution)/shard_map/ppermute | solution.py:22
  32.3 3.5 %copy-start.6 = (f32[2,33,128]{2,0,1:T(2,128)}, f32[2,33,128]{2,0,1:T(2,128)S(1)}, u32[]{:S(2)}) copy-start(f32[2,33,128]{2,0,1:T(2,128)S(1)} %collective-permute-done.6) | copy-start | bytes 101380
  32.3 6.2 %collective-permute-start.8 = (f32[2,33,128]{2,0,1:T(2,128)S(1)}, f32[2,33,128]{2,0,1:T(2,128)}, u32[]{:S(2)}, u32[]{:S(2)}) collective-permute-start(f32[2,33,128]{2,0,1:T(2,128)S(1)} %collective-permute-done.6), channel_id=1, source_target_pairs={{0,224},{32,0},{64,32},{96,64},{128,96},{160,128},{192,160},{224,1... | collective-permute-start | bytes 101384 | tf_op jit(solution)/shard_map/ppermute | solution.py:22
  35.1 3.5 %copy-start.7 = (f32[2,33,128]{2,0,1:T(2,128)}, f32[2,33,128]{2,0,1:T(2,128)S(1)}, u32[]{:S(2)}) copy-start(f32[2,33,128]{2,0,1:T(2,128)S(1)} %collective-permute-done.7) | copy-start | bytes 101380
  35.1 6.2 %collective-permute-start.9 = (f32[2,33,128]{2,0,1:T(2,128)S(1)}, f32[2,33,128]{2,0,1:T(2,128)}, u32[]{:S(2)}, u32[]{:S(2)}) collective-permute-start(f32[2,33,128]{2,0,1:T(2,128)S(1)} %collective-permute-done.7), channel_id=1, source_target_pairs={{0,32},{32,64},{64,96},{96,128},{128,160},{160,192},{192,224},{224... | collective-permute-start | bytes 101384 | tf_op jit(solution)/shard_map/ppermute | solution.py:22
  35.8 10.0 %collective-permute-start.12 = (f32[16,33,128]{2,0,1:T(8,128)}, f32[16,33,128]{2,0,1:T(8,128)S(1)}, u32[]{:S(2)}, u32[]{:S(2)}) collective-permute-start(f32[16,33,128]{2,0,1:T(8,128)} %pad_maximum_fusion), channel_id=1, source_target_pairs={{0,4},{4,0},{1,5},{5,1},{2,6},{6,2},{3,7},{7,3},{8,12},{12,8},{9,1... | collective-permute-start | bytes 811016 | tf_op jit(solution)/shard_map/ppermute | solution.py:22
  38.5 4.0 %collective-permute-start.10 = (f32[2,33,128]{2,0,1:T(2,128)}, f32[2,33,128]{2,0,1:T(2,128)}, u32[]{:S(2)}, u32[]{:S(2)}) collective-permute-start(f32[2,33,128]{2,0,1:T(2,128)} %collective-permute-done.8), channel_id=1, source_target_pairs={{0,224},{32,0},{64,32},{96,64},{128,96},{160,128},{192,160},{224,1... | collective-permute-start | bytes 101384 | tf_op jit(solution)/shard_map/ppermute | solution.py:22
  41.2 4.5 %collective-permute-start.11 = (f32[2,33,128]{2,0,1:T(2,128)}, f32[2,33,128]{2,0,1:T(2,128)}, u32[]{:S(2)}, u32[]{:S(2)}) collective-permute-start(f32[2,33,128]{2,0,1:T(2,128)} %collective-permute-done.9), channel_id=1, source_target_pairs={{0,32},{32,64},{64,96},{96,128},{128,160},{160,192},{192,224},{224... | collective-permute-start | bytes 101384 | tf_op jit(solution)/shard_map/ppermute | solution.py:22
  45.8 7.5 %copy-start.1 = (f32[16,33,128]{2,0,1:T(8,128)}, f32[16,33,128]{2,0,1:T(8,128)S(1)}, u32[]{:S(2)}) copy-start(f32[16,33,128]{2,0,1:T(8,128)S(1)} %collective-permute-done.12) | copy-start | bytes 811012
  46.7 4.2 %collective-permute-start.13 = (f32[2,33,128]{2,0,1:T(2,128)S(1)}, f32[2,33,128]{2,0,1:T(2,128)S(1)}, u32[]{:S(2)}, u32[]{:S(2)}) collective-permute-start(f32[2,33,128]{2,0,1:T(2,128)S(1)} %get-tuple-element.24), channel_id=1, source_target_pairs={{0,8},{8,16},{16,24},{24,0},{1,9},{9,17},{17,25},{25,1},{2,10},{10... | collective-permute-start | bytes 101384 | tf_op jit(solution)/shard_map/ppermute | solution.py:22
  46.9 5.2 %collective-permute-start.14 = (f32[2,33,128]{2,0,1:T(2,128)S(1)}, f32[2,33,128]{2,0,1:T(2,128)S(1)}, u32[]{:S(2)}, u32[]{:S(2)}) collective-permute-start(f32[2,33,128]{2,0,1:T(2,128)S(1)} %get-tuple-element.25), channel_id=1, source_target_pairs={{0,16},{8,24},{16,0},{24,8},{1,17},{9,25},{17,1},{25,9},{2,18},{10... | collective-permute-start | bytes 101384 | tf_op jit(solution)/shard_map/ppermute | solution.py:22
  50.5 2.8 %collective-permute-start.15 = (f32[2,33,128]{2,0,1:T(2,128)S(1)}, f32[2,33,128]{2,0,1:T(2,128)S(1)}, u32[]{:S(2)}, u32[]{:S(2)}) collective-permute-start(f32[2,33,128]{2,0,1:T(2,128)S(1)} %get-tuple-element.26), channel_id=1, source_target_pairs={{0,24},{8,0},{16,8},{24,16},{1,25},{9,1},{17,9},{25,17},{2,26},{10... | collective-permute-start | bytes 101384 | tf_op jit(solution)/shard_map/ppermute | solution.py:22
  55.8 8.6 %collective-permute-start.16 = (f32[8,33,128]{2,0,1:T(8,128)S(1)}, f32[8,33,128]{2,0,1:T(8,128)S(1)}, u32[]{:S(2)}, u32[]{:S(2)}) collective-permute-start(f32[8,33,128]{2,0,1:T(8,128)S(1)} %get-tuple-element.23), channel_id=1, source_target_pairs={{0,2},{2,0},{1,3},{3,1},{4,6},{6,4},{5,7},{7,5},{8,10},{10,8},{9,1... | collective-permute-start | bytes 405512 | tf_op jit(solution)/shard_map/ppermute | solution.py:22
  64.6 4.4 %copy-start.8 = (f32[1,1,256,16,64]{2,4,3,1,0:T(8,128)S(1)}, f32[1,1,256,16,64]{2,4,3,1,0:T(8,128)}, u32[]{:S(2)}) copy-start(f32[1,1,256,16,64]{2,4,3,1,0:T(8,128)} %fusion.10) | copy-start | bytes 3145732

commit v16 on v13

--- a/solution.py
+++ b/solution.py
@@ -64,8 +64,9 @@
     n_y = lax.axis_size("seg_y")
     n_z = lax.axis_size("seg_z")
     add = lambda a, b: tmap(jnp.add, a, b)
-    own_c = part(total, core, 2)
-    got_c = swap(part(total, 1 - core, 2), "frm")
+    first, second = jnp.split(total, 2, axis=0)
+    own_c = jnp.where(core == 0, first, second)
+    got_c = swap(jnp.where(core == 0, second, first), "frm")
     lo, hi = ordered(own_c, got_c, core == 0)
     chip = add(lo, hi)
     came = [part(chip, y, n_y)] + [

time: 66 us -> 66.5 us (level)
    slice x3, local copies, waits for them, and re-layouts: 0.05 us -> 0.95 us  [heads_of(): prior_kv = prior[:, :rows_kv].reshape((half_heads,) + total_kv.shape[1:])]
    unnamed x10 -> x8, local copies, waits for them, and re-layouts: 1.27 us -> 0.6 us
where the time goes in v16:
time: 66.5 us; the launch traced here: 66.2 us
  starting transfers between devices  32.1 us (48%)
  matrix products  15.8 us (24%)
  waiting for transfers between devices  12.1 us (18%)
  local copies, waits for them, and re-layouts  3.71 us (6%)
  other arithmetic  2.17 us (3%)
    ppermute x16, starting transfers between devices, send(): return tmap(lambda t: lax.ppermute(t, axis, perm=pairs), tree)  32.1 us
    ppermute x16, waiting for transfers between devices, send(): return tmap(lambda t: lax.ppermute(t, axis, perm=pairs), tree)  12.1 us
    dot_general x2, matrix products, project(): jnp.einsum('rtd,de->ret', frames_in, w, preferred_element_type=jnp.float32)  7.03 us
    dot_general x2, matrix products, finish(): jnp.einsum('rnihd,rnhde->rnihe', pq32, before_kv, precision=lax.Precision...  2.96 us
    dot_general x1, matrix products, block_terms(): jnp.einsum('rnihd,rnjhd->rnhij', pq, pk, preferred_element_type=jnp.float32)  2.23 us
    dot_general x2, matrix products, heads_of(): jnp.einsum('rtd,de->rte', heads_out, rows_w, preferred_element_type=jnp.f...  1.74 us
    dot_general x1, matrix products, block_terms(): jnp.einsum('rnhij,rnjhd->rnihd', weights, vv, preferred_element_type=jnp....  1.45 us
  transfers between devices with their start and end apart: 16, of which 9 were waited for; matrix products, arithmetic and copies ran while one was open for 11% of the time, Pallas kernels for 0%

profile of v16, /device:TPU:1, one launch (start us, length us, event | category | flops | bytes accessed | tf_op | source)
XLA Modules:
  0.0 66.2 jit_solution(10606176580112238993)
XLA Ops:
  0.0 3.8 %fusion.2 = bf16[2048,256]{1,0:T(8,128)(2,1)S(1)} fusion(bf16[1024,3072]{1,0:T(8,128)(2,1)} %param.4, bf16[1,256,1024]{2,1,0:T(8,128)(2,1)} %param.3), kind=kOutput, calls=%fused_computation.5 | convolution fusion | flops 1074266112 | bytes 5767168 | tf_op jit(solution)/shard_map/rtd,de->ret/dot_general | solution.py:148
  3.8 0.4 fusion.37
  4.2 0.6 copy-done.1
  4.8 0.3 convert_reduce_fusion
  5.1 0.1 reshape_squeeze.4
  5.3 0.2 copy.4
  5.5 3.3 %collective-permute-start = (f32[8,33,128]{2,0,1:T(8,128)S(1)}, f32[8,33,128]{2,0,1:T(8,128)S(1)}, u32[]{:S(2)}, u32[]{:S(2)}) collective-permute-start(f32[8,33,128]{2,0,1:T(8,128)S(1)} %broadcast_select_fusion), channel_id=1, source_target_pairs={{0,2},{2,0},{1,3},{3,1},{4,6},{6,4},{5,7},{7,5},{8,10},{10,8},{9,1... | collective-permute-start | bytes 405512 | tf_op jit(solution)/shard_map/ppermute | solution.py:22
  8.8 1.0 %collective-permute-done = f32[8,33,128]{2,0,1:T(8,128)S(1)} collective-permute-done((f32[8,33,128]{2,0,1:T(8,128)S(1)}, f32[8,33,128]{2,0,1:T(8,128)S(1)}, u32[]{:S(2)}, u32[]{:S(2)}) %collective-permute-start) | collective-permute-done | bytes 135200 | tf_op jit(solution)/shard_map/ppermute | solution.py:22
  9.8 0.1 collective-permute-start.1
  9.9 2.2 %collective-permute-start.2 = (f32[2,33,128]{2,0,1:T(2,128)S(1)}, f32[2,33,128]{2,0,1:T(2,128)S(1)}, u32[]{:S(2)}, u32[]{:S(2)}) collective-permute-start(f32[2,33,128]{2,0,1:T(2,128)S(1)} %get-tuple-element.20), channel_id=1, source_target_pairs={{0,16},{8,24},{16,0},{24,8},{1,17},{9,25},{17,1},{25,9},{2,18},{10... | collective-permute-start | bytes 101384 | tf_op jit(solution)/shard_map/ppermute | solution.py:22
  12.1 1.1 %collective-permute-start.3 = (f32[2,33,128]{2,0,1:T(2,128)S(1)}, f32[2,33,128]{2,0,1:T(2,128)S(1)}, u32[]{:S(2)}, u32[]{:S(2)}) collective-permute-start(f32[2,33,128]{2,0,1:T(2,128)S(1)} %get-tuple-element.19), channel_id=1, source_target_pairs={{0,24},{8,0},{16,8},{24,16},{1,25},{9,1},{17,9},{25,17},{2,26},{10... | collective-permute-start | bytes 101384 | tf_op jit(solution)/shard_map/ppermute | solution.py:22
  13.2 3.3 %fusion.26 = bf16[1024,256]{1,0:T(8,128)(2,1)} fusion(bf16[1024,3072]{1,0:T(8,128)(2,1)} %param.4, bf16[1,256,1024]{2,1,0:T(8,128)(2,1)} %param.3), kind=kOutput, calls=%fused_computation.34 | convolution fusion | flops 538705920 | bytes 3145728 | tf_op jit(solution)/shard_map/rtd,de->ret/dot_general | solution.py:148
  16.4 0.0 collective-permute-done.1
  16.5 1.7 %collective-permute-start.4 = (f32[2,33,128]{2,0,1:T(2,128)S(1)}, f32[2,33,128]{2,0,1:T(2,128)S(1)}, u32[]{:S(2)}, u32[]{:S(2)}) collective-permute-start(f32[2,33,128]{2,0,1:T(2,128)S(1)} %add_add_fusion), channel_id=1, source_target_pairs={{0,32},{32,64},{64,96},{96,128},{128,160},{160,192},{192,224},{224... | collective-permute-start | bytes 101384 | tf_op jit(solution)/shard_map/ppermute | solution.py:22
  18.2 4.0 %collective-permute-start.5 = (f32[2,33,128]{2,0,1:T(2,128)S(1)}, f32[2,33,128]{2,0,1:T(2,128)S(1)}, u32[]{:S(2)}, u32[]{:S(2)}) collective-permute-start(f32[2,33,128]{2,0,1:T(2,128)S(1)} %add_add_fusion), channel_id=1, source_target_pairs={{0,224},{32,0},{64,32},{96,64},{128,96},{160,128},{192,160},{224,1... | collective-permute-start | bytes 101384 | tf_op jit(solution)/shard_map/ppermute | solution.py:22
  22.3 1.2 %collective-permute-done.4 = f32[2,33,128]{2,0,1:T(2,128)S(1)} collective-permute-done((f32[2,33,128]{2,0,1:T(2,128)S(1)}, f32[2,33,128]{2,0,1:T(2,128)S(1)}, u32[]{:S(2)}, u32[]{:S(2)}) %collective-permute-start.4) | collective-permute-done | bytes 33824 | tf_op jit(solution)/shard_map/ppermute | solution.py:22
  23.5 2.2 %select_reduce_fusion = (f32[16,256]{1,0:T(8,128)S(1)}, bf16[16,256,256]{1,2,0:T(8,128)(2,1)S(1)}) fusion(pred[256,256]{0,1:T(8,128)(4,1)S(1)} %iota_compare_fusion, bf16[256,16,64]{0,2,1:T(8,128)(2,1)} %bitcast.107, bf16[1,256,2,16,64]{1,4,3,2,0:T(8,128)(2,1)} %bitcast.115), kind=kOutput, calls=%fused_computation.3 | convolution fusion | flops 138932224 | bytes 3227648 | tf_op jit(solution)/shard_map/rnihd,rnjhd->rnhij/dot_general | solution.py:114
  25.7 2.8 %collective-permute-start.7 = (f32[2,33,128]{2,0,1:T(2,128)S(1)}, f32[2,33,128]{2,0,1:T(2,128)S(1)}, u32[]{:S(2)}, u32[]{:S(2)}) collective-permute-start(f32[2,33,128]{2,0,1:T(2,128)S(1)} %collective-permute-done.5), channel_id=1, source_target_pairs={{0,224},{32,0},{64,32},{96,64},{128,96},{160,128},{192,160},{224,1... | collective-permute-start | bytes 101384 | tf_op jit(solution)/shard_map/ppermute | solution.py:22
  28.5 1.4 %fusion.10 = f32[1,1,256,16,64]{2,4,3,1,0:T(8,128)} fusion(bf16[16,256,256]{1,2,0:T(8,128)(2,1)S(1)} %get-tuple-element.26, pred[256,256]{0,1:T(8,128)(4,1)S(1)} %iota_compare_fusion, bf16[1,256,2,16,64]{1,4,3,2,0:T(8,128)(2,1)S(1)} %bitcast.116), kind=kOutput, calls=%fused_computation.17 | convolution fusion | flops 135266304 | bytes 3735552 | tf_op jit(solution)/shard_map/rnhij,rnjhd->rnihd/dot_general | solution.py:119
  29.9 2.7 %collective-permute-start.9 = (f32[2,33,128]{2,0,1:T(2,128)S(1)}, f32[2,33,128]{2,0,1:T(2,128)S(1)}, u32[]{:S(2)}, u32[]{:S(2)}) collective-permute-start(f32[2,33,128]{2,0,1:T(2,128)S(1)} %collective-permute-done.7), channel_id=1, source_target_pairs={{0,224},{32,0},{64,32},{96,64},{128,96},{160,128},{192,160},{224,1... | collective-permute-start | bytes 101384 | tf_op jit(solution)/shard_map/ppermute | solution.py:22
  32.6 0.0 collective-permute-start.10
  32.7 0.9 %collective-permute-done.9 = f32[2,33,128]{2,0,1:T(2,128)S(1)} collective-permute-done((f32[2,33,128]{2,0,1:T(2,128)S(1)}, f32[2,33,128]{2,0,1:T(2,128)S(1)}, u32[]{:S(2)}, u32[]{:S(2)}) %collective-permute-start.9) | collective-permute-done | bytes 33824 | tf_op jit(solution)/shard_map/ppermute | solution.py:22
  33.6 3.3 %collective-permute-done.10 = f32[2,33,128]{2,0,1:T(2,128)} collective-permute-done((f32[2,33,128]{2,0,1:T(2,128)}, f32[2,33,128]{2,0,1:T(2,128)}, u32[]{:S(2)}, u32[]{:S(2)}) %collective-permute-start.10) | collective-permute-done | bytes 33824 | tf_op jit(solution)/shard_map/ppermute | solution.py:22
  36.9 0.1 select_add_fusion.6
  37.0 0.1 select_add_fusion.5
  37.1 0.5 collective-permute-start.11
  37.5 0.1 add_bitcast_fusion
  37.7 1.6 %collective-permute-start.12 = (f32[2,33,128]{2,0,1:T(2,128)S(1)}, f32[2,33,128]{2,0,1:T(2,128)S(1)}, u32[]{:S(2)}, u32[]{:S(2)}) collective-permute-start(f32[2,33,128]{2,0,1:T(2,128)S(1)} %get-tuple-element.17), channel_id=1, source_target_pairs={{0,16},{8,24},{16,0},{24,8},{1,17},{9,25},{17,1},{25,9},{2,18},{10... | collective-permute-start | bytes 101384 | tf_op jit(solution)/shard_map/ppermute | solution.py:22
  39.3 0.9 %collective-permute-start.13 = (f32[2,33,128]{2,0,1:T(2,128)S(1)}, f32[2,33,128]{2,0,1:T(2,128)S(1)}, u32[]{:S(2)}, u32[]{:S(2)}) collective-permute-start(f32[2,33,128]{2,0,1:T(2,128)S(1)} %get-tuple-element.16), channel_id=1, source_target_pairs={{0,24},{8,0},{16,8},{24,16},{1,25},{9,1},{17,9},{25,17},{2,26},{10... | collective-permute-start | bytes 101384 | tf_op jit(solution)/shard_map/ppermute | solution.py:22
  40.2 1.2 %collective-permute-done.11 = f32[2,33,128]{2,0,1:T(2,128)S(1)} collective-permute-done((f32[2,33,128]{2,0,1:T(2,128)S(1)}, f32[2,33,128]{2,0,1:T(2,128)S(1)}, u32[]{:S(2)}, u32[]{:S(2)}) %collective-permute-start.11) | collective-permute-done | bytes 33824 | tf_op jit(solution)/shard_map/ppermute | solution.py:22
  41.4 0.6 collective-permute-done.12
  42.0 0.3 collective-permute-done.13
  42.3 0.1 pad_maximum_fusion.1
  42.3 0.7 %gather_fusion = f32[4,2,33,128]{3,1,2,0:T(2,128)S(1)} fusion(f32[4,2,33,128]{3,1,2,0:T(2,128)S(1)} %pad_maximum_fusion.1, s32[1024]{0:T(1024)S(1)} %pad_clamp_fusion), kind=kCustom, calls=%fused_computation | custom fusion | bytes 270352 | tf_op jit(solution)/shard_map/gather | solution.py:99
  43.1 2.8 %collective-permute-start.14 = (f32[8,33,128]{2,0,1:T(8,128)S(1)}, f32[8,33,128]{2,0,1:T(8,128)S(1)}, u32[]{:S(2)}, u32[]{:S(2)}) collective-permute-start(f32[8,33,128]{2,0,1:T(8,128)S(1)} %select_add_fusion.1), channel_id=1, source_target_pairs={{0,4},{4,0},{1,5},{5,1},{2,6},{6,2},{3,7},{7,3},{8,12},{12,8},{9,1... | collective-permute-start | bytes 405512 | tf_op jit(solution)/shard_map/ppermute | solution.py:22
  45.9 2.6 %collective-permute-done.14 = f32[8,33,128]{2,0,1:T(8,128)S(1)} collective-permute-done((f32[8,33,128]{2,0,1:T(8,128)S(1)}, f32[8,33,128]{2,0,1:T(8,128)S(1)}, u32[]{:S(2)}, u32[]{:S(2)}) %collective-permute-start.14) | collective-permute-done | bytes 135200 | tf_op jit(solution)/shard_map/ppermute | solution.py:22
  48.6 0.1 add_select_fusion
  48.7 8.5 %collective-permute-start.15 = (f32[8,33,128]{2,1,0:T(8,128)S(1)}, f32[8,33,128]{2,1,0:T(8,128)}, u32[]{:S(2)}, u32[]{:S(2)}) collective-permute-start(f32[8,33,128]{2,1,0:T(8,128)S(1)} %copy.9), channel_id=1, source_target_pairs={{0,2},{2,0},{1,3},{3,1},{4,6},{6,4},{5,7},{7,5},{8,10},{10,8},{9,1... | collective-permute-start | bytes 405512 | tf_op jit(solution)/shard_map/ppermute | solution.py:22
  57.2 0.1 broadcast_in_dim_broadcast_in_dim_reshape.6
  57.3 1.0 %collective-permute-done.15 = f32[8,33,128]{2,1,0:T(8,128)} collective-permute-done((f32[8,33,128]{2,1,0:T(8,128)S(1)}, f32[8,33,128]{2,1,0:T(8,128)}, u32[]{:S(2)}, u32[]{:S(2)}) %collective-permute-start.15) | collective-permute-done | bytes 135200 | tf_op jit(solution)/shard_map/ppermute | solution.py:22
  58.3 0.9 %slice.38 = f32[8,32,128]{2,1,0:T(8,128)S(1)} slice(f32[8,33,128]{2,1,0:T(8,128)} %collective-permute-done.15), slice={[0:8], [0:32], [0:128]} | slice | bytes 262144 | tf_op jit(solution)/shard_map/slice | solution.py:173
  59.2 0.1 broadcast_in_dim_broadcast_in_dim_reshape.7
  59.3 0.8 %slice.39 = f32[8,1,64]{2,1,0:T(1,128)S(1)} slice(f32[8,33,128]{2,1,0:T(8,128)} %collective-permute-done.15), slice={[0:8], [32:33], [0:64]} | slice | bytes 4096 | tf_op jit(solution)/shard_map/slice | solution.py:174
  60.2 1.3 %fusion.33 = (f32[256,8]{0,1:T(8,128)S(1)}, f32[256,8]{0,1:T(8,128)S(1)}) fusion(f32[8,64]{1,0:T(8,128)S(1)} %get-tuple-element.24, bf16[1,1,16,64,256]{4,3,2,1,0:T(8,128)(2,1)} %bitcast.108, s32[]{:T(128)S(6)} %select_n.410, f32[8,64]{1,0:T(8,128)S(1)} %get-tuple-element.23, s32[]{:T(128)S(6)} %select_n.367), kind=kLoop, calls=%fused_computation.42 | loop fusion | flops 782336 | bytes 544776 | tf_op jit(solution)/shard_map/reduce_sum | solution.py:133
  61.5 1.6 %fusion.20 = bf16[1,1,256,8,64]{2,4,3,1,0:T(8,128)(2,1)S(1)} fusion(f32[1,1,256,16,64]{2,4,3,1,0:T(8,128)} %fusion.10, s32[]{:T(128)S(6)} %select_n.410, f32[256,8]{0,1:T(8,128)S(1)} %get-tuple-element.21, f32[8,64,64]{2,1,0:T(8,128)S(1)} %broadcast_in_dim_broadcast_in_dim_reshape.7, f32[16,64,64]{2,1,0:T(8,128)S(1)} %fusion.37, ...), kind=kOutput, calls=%fused_computation.28 | convolution fusion | flops 101122048 | bytes 1582592 | tf_op jit(solution)/shard_map/rnihd,rnhde->rnihe/dot_general | solution.py:130
  63.1 1.4 %fusion.21 = bf16[1,1,256,8,64]{2,4,3,1,0:T(8,128)(2,1)S(1)} fusion(f32[1,1,256,16,64]{2,4,3,1,0:T(8,128)S(1)} %copy-done.3, s32[]{:T(128)S(6)} %select_n.367, f32[256,8]{0,1:T(8,128)S(1)} %get-tuple-element.22, f32[8,64,64]{2,1,0:T(8,128)S(1)} %broadcast_in_dim_broadcast_in_dim_reshape.6, f32[16,64,64]{2,1,0:T(8,128)S(1)} %fusion.37, ...), kind=kOutput, calls=%fused_computation.29 | convolution fusion | flops 101122048 | bytes 1582592 | tf_op jit(solution)/shard_map/rnihd,rnhde->rnihe/dot_general | solution.py:130
  64.5 0.5 fusion.29
  64.9 1.3 %fusion.15 = bf16[1,256,1024]{2,1,0:T(8,128)(2,1)} fusion(f32[256,1024]{1,0:T(8,128)S(1)} %fusion.29, bf16[256,512]{0,1:T(8,128)(2,1)S(1)} %bitcast.111, bf16[1024,1024]{1,0:T(8,128)(2,1)S(1)} %copy-done, s32[]{:T(128)S(6)} %select_n.412), kind=kOutput, calls=%fused_computation.21 | convolution fusion | flops 268959744 | bytes 2883588 | tf_op jit(solution)/shard_map/rtd,de->rte/dot_general | solution.py:180
  (30 shorter events, 0.4 us)
Async XLA Ops:
  0.0 64.5 %copy-start = (bf16[1024,1024]{1,0:T(8,128)(2,1)S(1)}, bf16[1024,1024]{1,0:T(8,128)(2,1)}, u32[]{:S(2)}) copy-start(bf16[1024,1024]{1,0:T(8,128)(2,1)} %param.5) | copy-start | bytes 6291460
  3.8 1.0 %copy-start.1 = (bf16[2048,256]{1,0:T(8,128)(2,1)}, bf16[2048,256]{1,0:T(8,128)(2,1)S(1)}, u32[]{:S(2)}) copy-start(bf16[2048,256]{1,0:T(8,128)(2,1)S(1)} %fusion.2) | copy-start | bytes 3145732
  5.5 4.3 %collective-permute-start = (f32[8,33,128]{2,0,1:T(8,128)S(1)}, f32[8,33,128]{2,0,1:T(8,128)S(1)}, u32[]{:S(2)}, u32[]{:S(2)}) collective-permute-start(f32[8,33,128]{2,0,1:T(8,128)S(1)} %broadcast_select_fusion), channel_id=1, source_target_pairs={{0,2},{2,0},{1,3},{3,1},{4,6},{6,4},{5,7},{7,5},{8,10},{10,8},{9,1... | collective-permute-start | bytes 405512 | tf_op jit(solution)/shard_map/ppermute | solution.py:22
  9.8 6.6 %collective-permute-start.1 = (f32[2,33,128]{2,0,1:T(2,128)S(1)}, f32[2,33,128]{2,0,1:T(2,128)S(1)}, u32[]{:S(2)}, u32[]{:S(2)}) collective-permute-start(f32[2,33,128]{2,0,1:T(2,128)S(1)} %get-tuple-element.18), channel_id=1, source_target_pairs={{0,8},{8,16},{16,24},{24,0},{1,9},{9,17},{17,25},{25,1},{2,10},{10... | collective-permute-start | bytes 101384 | tf_op jit(solution)/shard_map/ppermute | solution.py:22
  9.9 6.5 %collective-permute-start.2 = (f32[2,33,128]{2,0,1:T(2,128)S(1)}, f32[2,33,128]{2,0,1:T(2,128)S(1)}, u32[]{:S(2)}, u32[]{:S(2)}) collective-permute-start(f32[2,33,128]{2,0,1:T(2,128)S(1)} %get-tuple-element.20), channel_id=1, source_target_pairs={{0,16},{8,24},{16,0},{24,8},{1,17},{9,25},{17,1},{25,9},{2,18},{10... | collective-permute-start | bytes 101384 | tf_op jit(solution)/shard_map/ppermute | solution.py:22
  12.1 4.3 %collective-permute-start.3 = (f32[2,33,128]{2,0,1:T(2,128)S(1)}, f32[2,33,128]{2,0,1:T(2,128)S(1)}, u32[]{:S(2)}, u32[]{:S(2)}) collective-permute-start(f32[2,33,128]{2,0,1:T(2,128)S(1)} %get-tuple-element.19), channel_id=1, source_target_pairs={{0,24},{8,0},{16,8},{24,16},{1,25},{9,1},{17,9},{25,17},{2,26},{10... | collective-permute-start | bytes 101384 | tf_op jit(solution)/shard_map/ppermute | solution.py:22
  16.5 7.0 %collective-permute-start.4 = (f32[2,33,128]{2,0,1:T(2,128)S(1)}, f32[2,33,128]{2,0,1:T(2,128)S(1)}, u32[]{:S(2)}, u32[]{:S(2)}) collective-permute-start(f32[2,33,128]{2,0,1:T(2,128)S(1)} %add_add_fusion), channel_id=1, source_target_pairs={{0,32},{32,64},{64,96},{96,128},{128,160},{160,192},{192,224},{224... | collective-permute-start | bytes 101384 | tf_op jit(solution)/shard_map/ppermute | solution.py:22
  18.2 7.5 %collective-permute-start.5 = (f32[2,33,128]{2,0,1:T(2,128)S(1)}, f32[2,33,128]{2,0,1:T(2,128)S(1)}, u32[]{:S(2)}, u32[]{:S(2)}) collective-permute-start(f32[2,33,128]{2,0,1:T(2,128)S(1)} %add_add_fusion), channel_id=1, source_target_pairs={{0,224},{32,0},{64,32},{96,64},{128,96},{160,128},{192,160},{224,1... | collective-permute-start | bytes 101384 | tf_op jit(solution)/shard_map/ppermute | solution.py:22
  23.5 5.0 %collective-permute-start.6 = (f32[2,33,128]{2,0,1:T(2,128)S(1)}, f32[2,33,128]{2,0,1:T(2,128)S(1)}, u32[]{:S(2)}, u32[]{:S(2)}) collective-permute-start(f32[2,33,128]{2,0,1:T(2,128)S(1)} %collective-permute-done.4), channel_id=1, source_target_pairs={{0,32},{32,64},{64,96},{96,128},{128,160},{160,192},{192,224},{224... | collective-permute-start | bytes 101384 | tf_op jit(solution)/shard_map/ppermute | solution.py:22
  23.5 5.0 %copy-start.2 = (bf16[2048,256]{1,0:T(8,128)(2,1)S(1)}, bf16[2048,256]{1,0:T(8,128)(2,1)}, u32[]{:S(2)}) copy-start(bf16[2048,256]{1,0:T(8,128)(2,1)} %copy-done.1) | copy-start | bytes 3145732
  25.7 4.2 %collective-permute-start.7 = (f32[2,33,128]{2,0,1:T(2,128)S(1)}, f32[2,33,128]{2,0,1:T(2,128)S(1)}, u32[]{:S(2)}, u32[]{:S(2)}) collective-permute-start(f32[2,33,128]{2,0,1:T(2,128)S(1)} %collective-permute-done.5), channel_id=1, source_target_pairs={{0,224},{32,0},{64,32},{96,64},{128,96},{160,128},{192,160},{224,1... | collective-permute-start | bytes 101384 | tf_op jit(solution)/shard_map/ppermute | solution.py:22
  28.5 4.1 %collective-permute-start.8 = (f32[2,33,128]{2,0,1:T(2,128)S(1)}, f32[2,33,128]{2,0,1:T(2,128)}, u32[]{:S(2)}, u32[]{:S(2)}) collective-permute-start(f32[2,33,128]{2,0,1:T(2,128)S(1)} %collective-permute-done.6), channel_id=1, source_target_pairs={{0,32},{32,64},{64,96},{96,128},{128,160},{160,192},{192,224},{224... | collective-permute-start | bytes 101384 | tf_op jit(solution)/shard_map/ppermute | solution.py:22
  29.9 3.7 %collective-permute-start.9 = (f32[2,33,128]{2,0,1:T(2,128)S(1)}, f32[2,33,128]{2,0,1:T(2,128)S(1)}, u32[]{:S(2)}, u32[]{:S(2)}) collective-permute-start(f32[2,33,128]{2,0,1:T(2,128)S(1)} %collective-permute-done.7), channel_id=1, source_target_pairs={{0,224},{32,0},{64,32},{96,64},{128,96},{160,128},{192,160},{224,1... | collective-permute-start | bytes 101384 | tf_op jit(solution)/shard_map/ppermute | solution.py:22
  32.6 4.3 %collective-permute-start.10 = (f32[2,33,128]{2,0,1:T(2,128)}, f32[2,33,128]{2,0,1:T(2,128)}, u32[]{:S(2)}, u32[]{:S(2)}) collective-permute-start(f32[2,33,128]{2,0,1:T(2,128)} %collective-permute-done.8), channel_id=1, source_target_pairs={{0,32},{32,64},{64,96},{96,128},{128,160},{160,192},{192,224},{224... | collective-permute-start | bytes 101384 | tf_op jit(solution)/shard_map/ppermute | solution.py:22
  37.1 4.3 %collective-permute-start.11 = (f32[2,33,128]{2,0,1:T(2,128)S(1)}, f32[2,33,128]{2,0,1:T(2,128)S(1)}, u32[]{:S(2)}, u32[]{:S(2)}) collective-permute-start(f32[2,33,128]{2,0,1:T(2,128)S(1)} %select_add_fusion.5), channel_id=1, source_target_pairs={{0,8},{8,16},{16,24},{24,0},{1,9},{9,17},{17,25},{25,1},{2,10},{10... | collective-permute-start | bytes 101384 | tf_op jit(solution)/shard_map/ppermute | solution.py:22
  37.7 4.4 %collective-permute-start.12 = (f32[2,33,128]{2,0,1:T(2,128)S(1)}, f32[2,33,128]{2,0,1:T(2,128)S(1)}, u32[]{:S(2)}, u32[]{:S(2)}) collective-permute-start(f32[2,33,128]{2,0,1:T(2,128)S(1)} %get-tuple-element.17), channel_id=1, source_target_pairs={{0,16},{8,24},{16,0},{24,8},{1,17},{9,25},{17,1},{25,9},{2,18},{10... | collective-permute-start | bytes 101384 | tf_op jit(solution)/shard_map/ppermute | solution.py:22
  39.3 3.0 %collective-permute-start.13 = (f32[2,33,128]{2,0,1:T(2,128)S(1)}, f32[2,33,128]{2,0,1:T(2,128)S(1)}, u32[]{:S(2)}, u32[]{:S(2)}) collective-permute-start(f32[2,33,128]{2,0,1:T(2,128)S(1)} %get-tuple-element.16), channel_id=1, source_target_pairs={{0,24},{8,0},{16,8},{24,16},{1,25},{9,1},{17,9},{25,17},{2,26},{10... | collective-permute-start | bytes 101384 | tf_op jit(solution)/shard_map/ppermute | solution.py:22
  43.1 5.5 %collective-permute-start.14 = (f32[8,33,128]{2,0,1:T(8,128)S(1)}, f32[8,33,128]{2,0,1:T(8,128)S(1)}, u32[]{:S(2)}, u32[]{:S(2)}) collective-permute-start(f32[8,33,128]{2,0,1:T(8,128)S(1)} %select_add_fusion.1), channel_id=1, source_target_pairs={{0,4},{4,0},{1,5},{5,1},{2,6},{6,2},{3,7},{7,3},{8,12},{12,8},{9,1... | collective-permute-start | bytes 405512 | tf_op jit(solution)/shard_map/ppermute | solution.py:22
  48.7 9.6 %collective-permute-start.15 = (f32[8,33,128]{2,1,0:T(8,128)S(1)}, f32[8,33,128]{2,1,0:T(8,128)}, u32[]{:S(2)}, u32[]{:S(2)}) collective-permute-start(f32[8,33,128]{2,1,0:T(8,128)S(1)} %copy.9), channel_id=1, source_target_pairs={{0,2},{2,0},{1,3},{3,1},{4,6},{6,4},{5,7},{7,5},{8,10},{10,8},{9,1... | collective-permute-start | bytes 405512 | tf_op jit(solution)/shard_map/ppermute | solution.py:22
  59.3 3.7 %copy-start.3 = (f32[1,1,256,16,64]{2,4,3,1,0:T(8,128)S(1)}, f32[1,1,256,16,64]{2,4,3,1,0:T(8,128)}, u32[]{:S(2)}) copy-start(f32[1,1,256,16,64]{2,4,3,1,0:T(8,128)} %fusion.10) | copy-start | bytes 3145732

commit v17 on v13

--- a/solution.py
+++ b/solution.py
@@ -74,15 +74,9 @@
     column = came[0]
     for c in came[1:]:
         column = add(column, c)
-    before_z = tmap(jnp.zeros_like, column)
-    left = right = column
-    for r in range(1, n_z // 2 + 1):
-        left = send(left, "seg_z", cyclic(n_z, 1))
-        before_z = add(before_z, keep(left, z >= r))
-        if r < n_z - r:
-            right = send(right, "seg_z", cyclic(n_z, -1))
-            before_z = add(before_z, keep(right, z + r >= n_z))
-    before_z, carry = lax.optimization_barrier((before_z, carry))
+    planes = lax.all_gather(column, "seg_z", axis=0)
+    earlier = lax.broadcasted_iota(jnp.int32, planes.shape, 0) < z
+    before_z = jnp.sum(jnp.where(earlier, planes, 0.0), axis=0)
 
     def for_row(t):
         out = before_z
@@ -98,6 +92,7 @@
         lambda *p: jnp.stack(p)[order].reshape((-1,) + p[0].shape[1:]),
         *pieces,
     )
+    mine, carry = lax.optimization_barrier((mine, carry))
     half = add(mine, swap(add(mine, keep(chip, xh == 0)), "seg_x"))
     got = swap(add(half, keep(own_c, core == 0)), "frm")
     own = tmap(lambda a, c: jnp.where(core == 0, a, a + c), half, got_c)

time: 66 us -> 73.9 us (1.12)
  blocking collectives: 0 us -> 21.1 us
  starting transfers between devices: 32.2 us -> 21.8 us
  matrix products: 15.8 us -> 13 us
  local copies, waits for them, and re-layouts: 3.48 us -> 4.48 us
    all_gather x0 -> x1, blocking collectives: none -> 21.1 us  [entering(): planes = lax.all_gather(column, 'seg_z', axis=0)]
    ppermute x16 -> x9, starting transfers between devices: 32.2 us -> 21.8 us  [send(): return tmap(lambda t: lax.ppermute(t, axis, perm=pairs), tree)]
    another operation x2, local copies, waits for them, and re-layouts: 0.2 us -> 1.63 us  [finish(): before_kv = jnp.cumsum(kv_blocks, axis=1) - kv_blocks + prior_kv[:, None]]
    dot_general x1, matrix products: 2.23 us -> 0.95 us  [block_terms(): jnp.einsum('rnihd,rnjhd->rnhij', pq, pk, preferred_element_type=jnp.float32)]
    reduce_sum x1, other arithmetic: 1.26 us -> 0.23 us  [finish(): jnp.sum(pq32 * before_k[:, :, None], axis=-1)]
    unnamed x10 -> x14, local copies, waits for them, and re-layouts: 1.27 us -> 0.26 us
    slice x3, local copies, waits for them, and re-layouts: 0.05 us -> 0.95 us  [heads_of(): prior_kv = prior[:, :rows_kv].reshape((half_heads,) + total_kv.shape[1:])]
    dot_general x2, matrix products: 2.96 us -> 2.14 us  [finish(): jnp.einsum('rnihd,rnhde->rnihe', pq32, before_kv, precision=lax.Precision...]
  transfers between devices with their start and end apart: 16 -> 9, of which waited for: 9 -> 7; matrix products, arithmetic and copies ran while one was open for 11% -> 8% of each run, Pallas kernels for 0% -> 0%
where the time goes in v17:
time: 73.9 us; the launch traced here: 73.7 us
  starting transfers between devices  21.8 us (29%)
  blocking collectives  21.1 us (29%)
  matrix products  13 us (18%)
  waiting for transfers between devices  11.4 us (15%)
  local copies, waits for them, and re-layouts  4.48 us (6%)
  other arithmetic  1.7 us (2%)
    ppermute x9, starting transfers between devices, send(): return tmap(lambda t: lax.ppermute(t, axis, perm=pairs), tree)  21.8 us
    all_gather x1, blocking collectives, entering(): planes = lax.all_gather(column, 'seg_z', axis=0)  21.1 us
    ppermute x9, waiting for transfers between devices, send(): return tmap(lambda t: lax.ppermute(t, axis, perm=pairs), tree)  11.4 us
    dot_general x2, matrix products, project(): jnp.einsum('rtd,de->ret', frames_in, w, preferred_element_type=jnp.float32)  6.33 us
    dot_general x2, matrix products, finish(): jnp.einsum('rnihd,rnhde->rnihe', pq32, before_kv, precision=lax.Precision...  2.14 us
    dot_general x2, matrix products, heads_of(): jnp.einsum('rtd,de->rte', heads_out, rows_w, preferred_element_type=jnp.f...  1.72 us
    another operation x2, local copies, waits for them, and re-layouts, finish(): before_kv = jnp.cumsum(kv_blocks, axis=1) - kv_blocks + prior_kv[:, None]  1.63 us
  transfers between devices with their start and end apart: 9, of which 7 were waited for; matrix products, arithmetic and copies ran while one was open for 8% of the time, Pallas kernels for 0%

profile of v17, /device:TPU:1, one launch (start us, length us, event | category | flops | bytes accessed | tf_op | source)
XLA Modules:
  0.0 73.7 jit_solution(16174487938753314446)
XLA Ops:
  0.0 0.0 copy-start
  0.0 3.8 %fusion.2 = bf16[2048,256]{1,0:T(8,128)(2,1)S(1)} fusion(bf16[1024,3072]{1,0:T(8,128)(2,1)} %param.4, bf16[1,256,1024]{2,1,0:T(8,128)(2,1)} %param.3), kind=kOutput, calls=%fused_computation.5 | convolution fusion | flops 1074266112 | bytes 5767168 | tf_op jit(solution)/shard_map/rtd,de->ret/dot_general | solution.py:142
  3.8 0.0 copy-start.4
  3.8 0.3 convert_reduce_fusion
  4.1 0.4 fusion.37
  4.5 0.2 copy-done.4
  4.8 0.1 reshape_squeeze.4
  4.9 0.2 copy.11
  5.1 3.3 %collective-permute-start = (f32[8,33,128]{2,0,1:T(8,128)S(1)}, f32[8,33,128]{2,0,1:T(8,128)S(1)}, u32[]{:S(2)}, u32[]{:S(2)}) collective-permute-start(f32[8,33,128]{2,0,1:T(8,128)S(1)} %get-tuple-element.22), channel_id=1, source_target_pairs={{0,2},{2,0},{1,3},{3,1},{4,6},{6,4},{5,7},{7,5},{8,10},{10,8},{9,1... | collective-permute-start | bytes 405512 | tf_op jit(solution)/shard_map/ppermute | solution.py:22
  8.4 0.0 copy-start.5
  8.4 2.6 %fusion.26 = bf16[1024,256]{1,0:T(8,128)(2,1)S(1)} fusion(bf16[1024,3072]{1,0:T(8,128)(2,1)} %param.4, bf16[1,256,1024]{2,1,0:T(8,128)(2,1)} %param.3), kind=kOutput, calls=%fused_computation.34 | convolution fusion | flops 538705920 | bytes 3145728 | tf_op jit(solution)/shard_map/rtd,de->ret/dot_general | solution.py:142
  11.0 0.0 copy-start.1
  11.0 0.0 copy-done.5
  11.0 1.0 %select_reduce_fusion = (f32[16,256]{1,0:T(8,128)S(1)}, bf16[16,256,256]{1,2,0:T(8,128)(2,1)S(1)}) fusion(pred[256,256]{0,1:T(8,128)(4,1)S(1)} %iota_compare_fusion, bf16[256,16,64]{0,2,1:T(8,128)(2,1)S(1)} %bitcast.109, bf16[1,256,2,16,64]{1,4,3,2,0:T(8,128)(2,1)S(1)} %bitcast.117), kind=kOutput, calls=%fused_computation.3 | convolution fusion | flops 138932224 | bytes 3227648 | tf_op jit(solution)/shard_map/rnihd,rnjhd->rnhij/dot_general | solution.py:108
  12.0 0.0 copy-done.1
  12.0 1.4 %fusion.10 = f32[1,1,256,16,64]{2,4,3,1,0:T(8,128)} fusion(bf16[16,256,256]{1,2,0:T(8,128)(2,1)S(1)} %get-tuple-element.31, pred[256,256]{0,1:T(8,128)(4,1)S(1)} %iota_compare_fusion, bf16[1,256,2,16,64]{1,4,3,2,0:T(8,128)(2,1)S(1)} %bitcast.118), kind=kOutput, calls=%fused_computation.17 | convolution fusion | flops 135266304 | bytes 3735552 | tf_op jit(solution)/shard_map/rnhij,rnjhd->rnihd/dot_general | solution.py:113
  13.4 0.0 collective-permute-done
  13.5 0.1 copy_add_fusion.1
  13.6 0.1 collective-permute-start.1
  13.7 2.7 %collective-permute-start.3 = (f32[2,33,128]{2,1,0:T(8,128)S(1)}, f32[2,33,128]{2,1,0:T(8,128)S(1)}, u32[]{:S(2)}, u32[]{:S(2)}) collective-permute-start(f32[2,33,128]{2,1,0:T(8,128)S(1)} %get-tuple-element.24), channel_id=1, source_target_pairs={{0,24},{8,0},{16,8},{24,16},{1,25},{9,1},{17,9},{25,17},{2,26},{10... | collective-permute-start | bytes 101384 | tf_op jit(solution)/shard_map/ppermute | solution.py:22
  16.3 0.0 collective-permute-start.2
  16.3 1.4 %collective-permute-done.1 = f32[2,33,128]{2,1,0:T(8,128)S(1)} collective-permute-done((f32[2,33,128]{2,1,0:T(8,128)S(1)}, f32[2,33,128]{2,1,0:T(8,128)S(1)}, u32[]{:S(2)}, u32[]{:S(2)}) %collective-permute-start.1) | collective-permute-done | bytes 33824 | tf_op jit(solution)/shard_map/ppermute | solution.py:22
  17.7 0.0 collective-permute-done.3
  17.7 3.0 %collective-permute-done.2 = f32[2,33,128]{2,1,0:T(8,128)S(1)} collective-permute-done((f32[2,33,128]{2,1,0:T(8,128)S(1)}, f32[2,33,128]{2,1,0:T(8,128)S(1)}, u32[]{:S(2)}, u32[]{:S(2)}) %collective-permute-start.2) | collective-permute-done | bytes 33824 | tf_op jit(solution)/shard_map/ppermute | solution.py:22
  20.7 21.1 %all-gather = f32[16,33,128]{2,1,0:T(8,128)S(1)} all-gather(f32[2,33,128]{2,1,0:T(8,128)S(1)} %add_add_fusion), channel_id=2, replica_groups=mesh['seg_z'=8,'seg_y'=4,'seg_x'=2,'frm'=2,'rec'=2] {'seg_z'}, dimensions={0}, use_global_device_ids=true | all-gather | bytes 304128 | tf_op jit(solution)/shard_map/all_gather | solution.py:77
  41.8 0.1 select_reduce_fusion.1
  41.9 1.3 %collective-permute-start.6 = (f32[2,33,128]{2,1,0:T(8,128)S(1)}, f32[2,33,128]{2,1,0:T(8,128)S(1)}, u32[]{:S(2)}, u32[]{:S(2)}) collective-permute-start(f32[2,33,128]{2,1,0:T(8,128)S(1)} %get-tuple-element.18), channel_id=1, source_target_pairs={{0,24},{8,0},{16,8},{24,16},{1,25},{9,1},{17,9},{25,17},{2,26},{10... | collective-permute-start | bytes 101384 | tf_op jit(solution)/shard_map/ppermute | solution.py:22
  43.3 0.6 collective-permute-start.5
  43.9 0.5 collective-permute-start.4
  44.4 0.6 collective-permute-done.6
  45.0 2.6 %collective-permute-done.5 = f32[2,33,128]{2,1,0:T(8,128)S(1)} collective-permute-done((f32[2,33,128]{2,1,0:T(8,128)S(1)}, f32[2,33,128]{2,1,0:T(8,128)S(1)}, u32[]{:S(2)}, u32[]{:S(2)}) %collective-permute-start.5) | collective-permute-done | bytes 33824 | tf_op jit(solution)/shard_map/ppermute | solution.py:22
  47.6 0.4 collective-permute-done.4
  48.1 0.6 gather_fusion
  48.7 2.8 %collective-permute-start.7 = (f32[8,33,128]{2,1,0:T(8,128)S(1)}, f32[8,33,128]{2,1,0:T(8,128)S(1)}, u32[]{:S(2)}, u32[]{:S(2)}) collective-permute-start(f32[8,33,128]{2,1,0:T(8,128)S(1)} %select_add_fusion), channel_id=1, source_target_pairs={{0,4},{4,0},{1,5},{5,1},{2,6},{6,2},{3,7},{7,3},{8,12},{12,8},{9,1... | collective-permute-start | bytes 405512 | tf_op jit(solution)/shard_map/ppermute | solution.py:22
  51.5 2.9 %collective-permute-done.7 = f32[8,33,128]{2,1,0:T(8,128)S(1)} collective-permute-done((f32[8,33,128]{2,1,0:T(8,128)S(1)}, f32[8,33,128]{2,1,0:T(8,128)S(1)}, u32[]{:S(2)}, u32[]{:S(2)}) %collective-permute-start.7) | collective-permute-done | bytes 135200 | tf_op jit(solution)/shard_map/ppermute | solution.py:22
  54.4 0.7 copy_add_fusion
  55.1 10.5 %collective-permute-start.8 = (f32[8,33,128]{2,1,0:T(8,128)}, f32[8,33,128]{2,1,0:T(8,128)}, u32[]{:S(2)}, u32[]{:S(2)}) collective-permute-start(f32[8,33,128]{2,1,0:T(8,128)} %get-tuple-element.13), channel_id=1, source_target_pairs={{0,2},{2,0},{1,3},{3,1},{4,6},{6,4},{5,7},{7,5},{8,10},{10,8},{9,1... | collective-permute-start | bytes 405512 | tf_op jit(solution)/shard_map/ppermute | solution.py:22
  65.7 0.8 %broadcast_in_dim_broadcast_in_dim_reshape.6 = f32[8,64,64]{2,1,0:T(8,128)} reshape(f32[8,32,128]{2,1,0:T(8,128)S(1)} %copy.18) | data formatting | bytes 262144 | tf_op jit(solution)/shard_map/broadcast_in_dim;broadcast_in_dim;reshape | solution.py:121
  66.5 0.5 collective-permute-done.8
  67.0 0.8 %slice.39 = f32[8,1,64]{2,1,0:T(1,128)S(1)} slice(f32[8,33,128]{2,1,0:T(8,128)} %collective-permute-done.8), slice={[0:8], [32:33], [0:64]} | slice | bytes 4096 | tf_op jit(solution)/shard_map/slice | solution.py:168
  67.8 0.9 %slice.38 = f32[8,32,128]{2,1,0:T(8,128)S(1)} slice(f32[8,33,128]{2,1,0:T(8,128)} %collective-permute-done.8), slice={[0:8], [0:32], [0:128]} | slice | bytes 262144 | tf_op jit(solution)/shard_map/slice | solution.py:167
  68.7 0.8 %broadcast_in_dim_broadcast_in_dim_reshape.7 = f32[8,64,64]{2,1,0:T(8,128)} reshape(f32[8,32,128]{2,1,0:T(8,128)S(1)} %slice.38) | data formatting | bytes 262144 | tf_op jit(solution)/shard_map/broadcast_in_dim;broadcast_in_dim;reshape | solution.py:121
  69.5 0.0 copy-done.2
  69.5 0.2 fusion.33
  69.8 1.7 %fusion.21 = bf16[1,1,256,8,64]{2,4,3,1,0:T(8,128)(2,1)S(1)} fusion(f32[1,1,256,16,64]{2,4,3,1,0:T(8,128)} %fusion.10, s32[]{:T(128)S(6)} %select_n.295, f32[256,8]{0,1:T(8,128)S(1)} %get-tuple-element.27, f32[8,64,64]{2,1,0:T(8,128)} %broadcast_in_dim_broadcast_in_dim_reshape.6, f32[16,64,64]{2,1,0:T(8,128)S(1)} %fusion.37, ...), kind=kOutput, calls=%fused_computation.29 | convolution fusion | flops 101122048 | bytes 1451520 | tf_op jit(solution)/shard_map/rnihd,rnhde->rnihe/dot_general | solution.py:124
  71.5 0.5 fusion.20
  71.9 0.5 fusion.29
  72.4 1.3 %fusion.15 = bf16[1,256,1024]{2,1,0:T(8,128)(2,1)} fusion(f32[256,1024]{1,0:T(8,128)S(1)} %fusion.29, bf16[256,512]{0,1:T(8,128)(2,1)S(1)} %bitcast.114, bf16[1024,1024]{1,0:T(8,128)(2,1)S(1)} %copy-done, s32[]{:T(128)S(6)} %select_n.353), kind=kOutput, calls=%fused_computation.21 | convolution fusion | flops 268959744 | bytes 2883588 | tf_op jit(solution)/shard_map/rtd,de->rte/dot_general | solution.py:174
  (24 shorter events, 0.4 us)
Async XLA Ops:
  0.0 71.9 %copy-start = (bf16[1024,1024]{1,0:T(8,128)(2,1)S(1)}, bf16[1024,1024]{1,0:T(8,128)(2,1)}, u32[]{:S(2)}) copy-start(bf16[1024,1024]{1,0:T(8,128)(2,1)} %param.5) | copy-start | bytes 6291460
  3.8 1.0 %copy-start.4 = (bf16[2048,256]{1,0:T(8,128)(2,1)}, bf16[2048,256]{1,0:T(8,128)(2,1)S(1)}, u32[]{:S(2)}) copy-start(bf16[2048,256]{1,0:T(8,128)(2,1)S(1)} %fusion.2) | copy-start | bytes 3145732
  5.1 8.3 %collective-permute-start = (f32[8,33,128]{2,0,1:T(8,128)S(1)}, f32[8,33,128]{2,0,1:T(8,128)S(1)}, u32[]{:S(2)}, u32[]{:S(2)}) collective-permute-start(f32[8,33,128]{2,0,1:T(8,128)S(1)} %get-tuple-element.22), channel_id=1, source_target_pairs={{0,2},{2,0},{1,3},{3,1},{4,6},{6,4},{5,7},{7,5},{8,10},{10,8},{9,1... | collective-permute-start | bytes 405512 | tf_op jit(solution)/shard_map/ppermute | solution.py:22
  8.4 2.6 %copy-start.5 = (bf16[2048,256]{1,0:T(8,128)(2,1)S(1)}, bf16[2048,256]{1,0:T(8,128)(2,1)}, u32[]{:S(2)}) copy-start(bf16[2048,256]{1,0:T(8,128)(2,1)} %copy-done.4) | copy-start | bytes 3145732
  11.0 1.0 %copy-start.1 = (bf16[1024,256]{1,0:T(8,128)(2,1)}, bf16[1024,256]{1,0:T(8,128)(2,1)S(1)}, u32[]{:S(2)}) copy-start(bf16[1024,256]{1,0:T(8,128)(2,1)S(1)} %fusion.26) | copy-start | bytes 1572868
  13.6 4.1 %collective-permute-start.1 = (f32[2,33,128]{2,1,0:T(8,128)S(1)}, f32[2,33,128]{2,1,0:T(8,128)S(1)}, u32[]{:S(2)}, u32[]{:S(2)}) collective-permute-start(f32[2,33,128]{2,1,0:T(8,128)S(1)} %get-tuple-element.23), channel_id=1, source_target_pairs={{0,8},{8,16},{16,24},{24,0},{1,9},{9,17},{17,25},{25,1},{2,10},{10... | collective-permute-start | bytes 101384 | tf_op jit(solution)/shard_map/ppermute | solution.py:22
  13.7 4.1 %collective-permute-start.3 = (f32[2,33,128]{2,1,0:T(8,128)S(1)}, f32[2,33,128]{2,1,0:T(8,128)S(1)}, u32[]{:S(2)}, u32[]{:S(2)}) collective-permute-start(f32[2,33,128]{2,1,0:T(8,128)S(1)} %get-tuple-element.24), channel_id=1, source_target_pairs={{0,24},{8,0},{16,8},{24,16},{1,25},{9,1},{17,9},{25,17},{2,26},{10... | collective-permute-start | bytes 101384 | tf_op jit(solution)/shard_map/ppermute | solution.py:22
  16.3 4.4 %collective-permute-start.2 = (f32[2,33,128]{2,1,0:T(8,128)S(1)}, f32[2,33,128]{2,1,0:T(8,128)S(1)}, u32[]{:S(2)}, u32[]{:S(2)}) collective-permute-start(f32[2,33,128]{2,1,0:T(8,128)S(1)} %get-tuple-element.25), channel_id=1, source_target_pairs={{0,16},{8,24},{16,0},{24,8},{1,17},{9,25},{17,1},{25,9},{2,18},{10... | collective-permute-start | bytes 101384 | tf_op jit(solution)/shard_map/ppermute | solution.py:22
  41.9 3.1 %collective-permute-start.6 = (f32[2,33,128]{2,1,0:T(8,128)S(1)}, f32[2,33,128]{2,1,0:T(8,128)S(1)}, u32[]{:S(2)}, u32[]{:S(2)}) collective-permute-start(f32[2,33,128]{2,1,0:T(8,128)S(1)} %get-tuple-element.18), channel_id=1, source_target_pairs={{0,24},{8,0},{16,8},{24,16},{1,25},{9,1},{17,9},{25,17},{2,26},{10... | collective-permute-start | bytes 101384 | tf_op jit(solution)/shard_map/ppermute | solution.py:22
  43.3 4.4 %collective-permute-start.5 = (f32[2,33,128]{2,1,0:T(8,128)S(1)}, f32[2,33,128]{2,1,0:T(8,128)S(1)}, u32[]{:S(2)}, u32[]{:S(2)}) collective-permute-start(f32[2,33,128]{2,1,0:T(8,128)S(1)} %get-tuple-element.19), channel_id=1, source_target_pairs={{0,16},{8,24},{16,0},{24,8},{1,17},{9,25},{17,1},{25,9},{2,18},{10... | collective-permute-start | bytes 101384 | tf_op jit(solution)/shard_map/ppermute | solution.py:22
  43.9 4.1 %collective-permute-start.4 = (f32[2,33,128]{2,1,0:T(8,128)S(1)}, f32[2,33,128]{2,1,0:T(8,128)S(1)}, u32[]{:S(2)}, u32[]{:S(2)}) collective-permute-start(f32[2,33,128]{2,1,0:T(8,128)S(1)} %select_add_fusion.3), channel_id=1, source_target_pairs={{0,8},{8,16},{16,24},{24,0},{1,9},{9,17},{17,25},{25,1},{2,10},{10... | collective-permute-start | bytes 101384 | tf_op jit(solution)/shard_map/ppermute | solution.py:22
  48.7 5.8 %collective-permute-start.7 = (f32[8,33,128]{2,1,0:T(8,128)S(1)}, f32[8,33,128]{2,1,0:T(8,128)S(1)}, u32[]{:S(2)}, u32[]{:S(2)}) collective-permute-start(f32[8,33,128]{2,1,0:T(8,128)S(1)} %select_add_fusion), channel_id=1, source_target_pairs={{0,4},{4,0},{1,5},{5,1},{2,6},{6,2},{3,7},{7,3},{8,12},{12,8},{9,1... | collective-permute-start | bytes 405512 | tf_op jit(solution)/shard_map/ppermute | solution.py:22
  55.1 14.4 %copy-start.2 = (bf16[1024,256]{1,0:T(8,128)(2,1)S(1)}, bf16[1024,256]{1,0:T(8,128)(2,1)}, u32[]{:S(2)}) copy-start(bf16[1024,256]{1,0:T(8,128)(2,1)} %copy-done.1) | copy-start | bytes 1572868
  55.1 11.9 %collective-permute-start.8 = (f32[8,33,128]{2,1,0:T(8,128)}, f32[8,33,128]{2,1,0:T(8,128)}, u32[]{:S(2)}, u32[]{:S(2)}) collective-permute-start(f32[8,33,128]{2,1,0:T(8,128)} %get-tuple-element.13), channel_id=1, source_target_pairs={{0,2},{2,0},{1,3},{3,1},{4,6},{6,4},{5,7},{7,5},{8,10},{10,8},{9,1... | collective-permute-start | bytes 405512 | tf_op jit(solution)/shard_map/ppermute | solution.py:22
  69.5 2.0 %copy-start.3 = (f32[8,64,64]{2,1,0:T(8,128)S(1)}, f32[8,64,64]{2,1,0:T(8,128)}, u32[]{:S(2)}) copy-start(f32[8,64,64]{2,1,0:T(8,128)} %broadcast_in_dim_broadcast_in_dim_reshape.7) | copy-start | bytes 393220
  69.5 2.0 %copy-start.6 = (f32[1,1,256,16,64]{2,4,3,1,0:T(8,128)S(1)}, f32[1,1,256,16,64]{2,4,3,1,0:T(8,128)}, u32[]{:S(2)}) copy-start(f32[1,1,256,16,64]{2,4,3,1,0:T(8,128)} %fusion.10) | copy-start | bytes 3145732

commit v18 on v13

--- a/solution.py
+++ b/solution.py
@@ -76,12 +76,20 @@
         column = add(column, c)
     before_z = tmap(jnp.zeros_like, column)
     left = right = column
-    for r in range(1, n_z // 2 + 1):
+    lefts = []
+    for r in range(1, n_z // 2 - 1):
         left = send(left, "seg_z", cyclic(n_z, 1))
+        lefts.append(left)
         before_z = add(before_z, keep(left, z >= r))
-        if r < n_z - r:
-            right = send(right, "seg_z", cyclic(n_z, -1))
-            before_z = add(before_z, keep(right, z + r >= n_z))
+    far = len(lefts)
+    receiver = (z + far) % n_z
+    onward = tmap(jnp.zeros_like, column)
+    for k, piece in enumerate(lefts):
+        onward = add(onward, keep(piece, receiver >= far + k + 1))
+    before_z = add(before_z, send(onward, "seg_z", cyclic(n_z, far)))
+    for r in range(1, n_z // 2):
+        right = send(right, "seg_z", cyclic(n_z, -1))
+        before_z = add(before_z, keep(right, z + r >= n_z))
     before_z, carry = lax.optimization_barrier((before_z, carry))
 
     def for_row(t):

time: 66 us -> 64.1 us (0.971)
  waiting for transfers between devices: 11.8 us -> 9.99 us
    ppermute x16 -> x15, waiting for transfers between devices: 11.8 us -> 9.99 us  [send(): return tmap(lambda t: lax.ppermute(t, axis, perm=pairs), tree)]
    ppermute x16 -> x15, starting transfers between devices: 32.2 us -> 32 us  [send(): return tmap(lambda t: lax.ppermute(t, axis, perm=pairs), tree)]
  transfers between devices with their start and end apart: 16 -> 15, of which waited for: 9 -> 10; matrix products, arithmetic and copies ran while one was open for 11% -> 11% of each run, Pallas kernels for 0% -> 0%
where the time goes in v18:
time: 64.1 us; the launch traced here: 63.8 us
  starting transfers between devices  32 us (50%)
  matrix products  15.8 us (25%)
  waiting for transfers between devices  9.99 us (16%)
  local copies, waits for them, and re-layouts  3.47 us (5%)
  other arithmetic  2.17 us (3%)
    ppermute x15, starting transfers between devices, send(): return tmap(lambda t: lax.ppermute(t, axis, perm=pairs), tree)  32 us
    ppermute x15, waiting for transfers between devices, send(): return tmap(lambda t: lax.ppermute(t, axis, perm=pairs), tree)  9.99 us
    dot_general x2, matrix products, project(): jnp.einsum('rtd,de->ret', frames_in, w, preferred_element_type=jnp.float32)  7.03 us
    dot_general x2, matrix products, finish(): jnp.einsum('rnihd,rnhde->rnihe', pq32, before_kv, precision=lax.Precision...  2.97 us
    dot_general x1, matrix products, block_terms(): jnp.einsum('rnihd,rnjhd->rnhij', pq, pk, preferred_element_type=jnp.float32)  2.22 us
    dot_general x2, matrix products, heads_of(): jnp.einsum('rtd,de->rte', heads_out, rows_w, preferred_element_type=jnp.f...  1.73 us
    dot_general x1, matrix products, block_terms(): jnp.einsum('rnhij,rnjhd->rnihd', weights, vv, preferred_element_type=jnp....  1.45 us
  transfers between devices with their start and end apart: 15, of which 10 were waited for; matrix products, arithmetic and copies ran while one was open for 11% of the time, Pallas kernels for 0%

profile of v18, /device:TPU:1, one launch (start us, length us, event | category | flops | bytes accessed | tf_op | source)
XLA Modules:
  0.0 63.8 jit_solution(3625488308875401087)
XLA Ops:
  0.0 3.8 %fusion.2 = bf16[2048,256]{1,0:T(8,128)(2,1)S(1)} fusion(bf16[1024,3072]{1,0:T(8,128)(2,1)} %param.4, bf16[1,256,1024]{2,1,0:T(8,128)(2,1)} %param.3), kind=kOutput, calls=%fused_computation.5 | convolution fusion | flops 1074266112 | bytes 5767168 | tf_op jit(solution)/shard_map/rtd,de->ret/dot_general | solution.py:155
  3.8 0.4 fusion.37
  4.2 0.6 copy-done.1
  4.8 0.3 convert_reduce_fusion
  5.1 0.1 reshape_squeeze.4
  5.3 0.2 copy.4
  5.5 3.3 %collective-permute-start = (f32[8,33,128]{2,0,1:T(8,128)S(1)}, f32[8,33,128]{2,0,1:T(8,128)S(1)}, u32[]{:S(2)}, u32[]{:S(2)}) collective-permute-start(f32[8,33,128]{2,0,1:T(8,128)S(1)} %fusion.51), channel_id=1, source_target_pairs={{0,2},{2,0},{1,3},{3,1},{4,6},{6,4},{5,7},{7,5},{8,10},{10,8},{9,1... | collective-permute-start | bytes 405512 | tf_op jit(solution)/shard_map/ppermute | solution.py:22
  8.8 3.3 %fusion.26 = bf16[1024,256]{1,0:T(8,128)(2,1)} fusion(bf16[1024,3072]{1,0:T(8,128)(2,1)} %param.4, bf16[1,256,1024]{2,1,0:T(8,128)(2,1)} %param.3), kind=kOutput, calls=%fused_computation.34 | convolution fusion | flops 538705920 | bytes 3145728 | tf_op jit(solution)/shard_map/rtd,de->ret/dot_general | solution.py:155
  12.1 0.1 collective-permute-start.1
  12.2 2.2 %collective-permute-start.2 = (f32[2,33,128]{2,0,1:T(2,128)S(1)}, f32[2,33,128]{2,0,1:T(2,128)S(1)}, u32[]{:S(2)}, u32[]{:S(2)}) collective-permute-start(f32[2,33,128]{2,0,1:T(2,128)S(1)} %get-tuple-element.20), channel_id=1, source_target_pairs={{0,16},{8,24},{16,0},{24,8},{1,17},{9,25},{17,1},{25,9},{2,18},{10... | collective-permute-start | bytes 101384 | tf_op jit(solution)/shard_map/ppermute | solution.py:22
  14.4 1.1 %collective-permute-start.3 = (f32[2,33,128]{2,0,1:T(2,128)S(1)}, f32[2,33,128]{2,0,1:T(2,128)S(1)}, u32[]{:S(2)}, u32[]{:S(2)}) collective-permute-start(f32[2,33,128]{2,0,1:T(2,128)S(1)} %get-tuple-element.19), channel_id=1, source_target_pairs={{0,24},{8,0},{16,8},{24,16},{1,25},{9,1},{17,9},{25,17},{2,26},{10... | collective-permute-start | bytes 101384 | tf_op jit(solution)/shard_map/ppermute | solution.py:22
  15.5 0.7 %collective-permute-done.1 = f32[2,33,128]{2,0,1:T(2,128)S(1)} collective-permute-done((f32[2,33,128]{2,0,1:T(2,128)S(1)}, f32[2,33,128]{2,0,1:T(2,128)S(1)}, u32[]{:S(2)}, u32[]{:S(2)}) %collective-permute-start.1) | collective-permute-done | bytes 33824 | tf_op jit(solution)/shard_map/ppermute | solution.py:22
  16.2 0.4 collective-permute-done.2
  16.6 0.9 %collective-permute-done.3 = f32[2,33,128]{2,0,1:T(2,128)S(1)} collective-permute-done((f32[2,33,128]{2,0,1:T(2,128)S(1)}, f32[2,33,128]{2,0,1:T(2,128)S(1)}, u32[]{:S(2)}, u32[]{:S(2)}) %collective-permute-start.3) | collective-permute-done | bytes 33824 | tf_op jit(solution)/shard_map/ppermute | solution.py:22
  17.5 1.4 %collective-permute-start.4 = (f32[2,33,128]{2,0,1:T(2,128)S(1)}, f32[2,33,128]{2,0,1:T(2,128)S(1)}, u32[]{:S(2)}, u32[]{:S(2)}) collective-permute-start(f32[2,33,128]{2,0,1:T(2,128)S(1)} %add_add_fusion), channel_id=1, source_target_pairs={{0,32},{32,64},{64,96},{96,128},{128,160},{160,192},{192,224},{224... | collective-permute-start | bytes 101384 | tf_op jit(solution)/shard_map/ppermute | solution.py:22
  18.9 2.2 %select_reduce_fusion = (f32[16,256]{1,0:T(8,128)S(1)}, bf16[16,256,256]{1,2,0:T(8,128)(2,1)S(1)}) fusion(pred[256,256]{0,1:T(8,128)(4,1)S(1)} %iota_compare_fusion, bf16[256,16,64]{0,2,1:T(8,128)(2,1)} %bitcast.107, bf16[1,256,2,16,64]{1,4,3,2,0:T(8,128)(2,1)} %bitcast.115), kind=kOutput, calls=%fused_computation.3 | convolution fusion | flops 138932224 | bytes 3227648 | tf_op jit(solution)/shard_map/rnihd,rnjhd->rnhij/dot_general | solution.py:121
  21.1 4.0 %collective-permute-start.7 = (f32[2,33,128]{2,0,1:T(2,128)S(1)}, f32[2,33,128]{2,0,1:T(2,128)S(1)}, u32[]{:S(2)}, u32[]{:S(2)}) collective-permute-start(f32[2,33,128]{2,0,1:T(2,128)S(1)} %add_add_fusion), channel_id=1, source_target_pairs={{0,224},{32,0},{64,32},{96,64},{128,96},{160,128},{192,160},{224,1... | collective-permute-start | bytes 101384 | tf_op jit(solution)/shard_map/ppermute | solution.py:22
  25.2 1.4 %fusion.10 = f32[1,1,256,16,64]{2,4,3,1,0:T(8,128)} fusion(bf16[16,256,256]{1,2,0:T(8,128)(2,1)S(1)} %get-tuple-element.26, pred[256,256]{0,1:T(8,128)(4,1)S(1)} %iota_compare_fusion, bf16[1,256,2,16,64]{1,4,3,2,0:T(8,128)(2,1)S(1)} %bitcast.116), kind=kOutput, calls=%fused_computation.17 | convolution fusion | flops 135266304 | bytes 3735552 | tf_op jit(solution)/shard_map/rnhij,rnjhd->rnihd/dot_general | solution.py:126
  26.7 2.7 %collective-permute-start.8 = (f32[2,33,128]{2,0,1:T(2,128)S(1)}, f32[2,33,128]{2,0,1:T(2,128)S(1)}, u32[]{:S(2)}, u32[]{:S(2)}) collective-permute-start(f32[2,33,128]{2,0,1:T(2,128)S(1)} %collective-permute-done.7), channel_id=1, source_target_pairs={{0,224},{32,0},{64,32},{96,64},{128,96},{160,128},{192,160},{224,1... | collective-permute-start | bytes 101384 | tf_op jit(solution)/shard_map/ppermute | solution.py:22
  29.4 0.1 collective-permute-start.6
  29.4 0.9 %collective-permute-done.8 = f32[2,33,128]{2,0,1:T(2,128)S(1)} collective-permute-done((f32[2,33,128]{2,0,1:T(2,128)S(1)}, f32[2,33,128]{2,0,1:T(2,128)S(1)}, u32[]{:S(2)}, u32[]{:S(2)}) %collective-permute-start.8) | collective-permute-done | bytes 33824 | tf_op jit(solution)/shard_map/ppermute | solution.py:22
  30.4 3.0 %collective-permute-start.9 = (f32[2,33,128]{2,0,1:T(2,128)S(1)}, f32[2,33,128]{2,0,1:T(2,128)}, u32[]{:S(2)}, u32[]{:S(2)}) collective-permute-start(f32[2,33,128]{2,0,1:T(2,128)S(1)} %collective-permute-done.8), channel_id=1, source_target_pairs={{0,224},{32,0},{64,32},{96,64},{128,96},{160,128},{192,160},{224,1... | collective-permute-start | bytes 101384 | tf_op jit(solution)/shard_map/ppermute | solution.py:22
  33.4 0.9 %collective-permute-done.6 = f32[2,33,128]{2,0,1:T(2,128)S(1)} collective-permute-done((f32[2,33,128]{2,0,1:T(2,128)S(1)}, f32[2,33,128]{2,0,1:T(2,128)S(1)}, u32[]{:S(2)}, u32[]{:S(2)}) %collective-permute-start.6) | collective-permute-done | bytes 33824 | tf_op jit(solution)/shard_map/ppermute | solution.py:22
  34.3 0.0 collective-permute-done.9
  34.3 0.1 select_add_fusion.6
  34.4 0.1 select_add_fusion.5
  34.5 0.3 collective-permute-start.10
  34.8 0.1 add_bitcast_fusion
  34.9 3.3 %collective-permute-start.11 = (f32[2,33,128]{2,0,1:T(2,128)S(1)}, f32[2,33,128]{2,0,1:T(2,128)S(1)}, u32[]{:S(2)}, u32[]{:S(2)}) collective-permute-start(f32[2,33,128]{2,0,1:T(2,128)S(1)} %get-tuple-element.17), channel_id=1, source_target_pairs={{0,16},{8,24},{16,0},{24,8},{1,17},{9,25},{17,1},{25,9},{2,18},{10... | collective-permute-start | bytes 101384 | tf_op jit(solution)/shard_map/ppermute | solution.py:22
  38.2 0.1 collective-permute-start.12
  38.4 0.2 collective-permute-done.10
  38.6 1.2 %collective-permute-done.11 = f32[2,33,128]{2,0,1:T(2,128)S(1)} collective-permute-done((f32[2,33,128]{2,0,1:T(2,128)S(1)}, f32[2,33,128]{2,0,1:T(2,128)S(1)}, u32[]{:S(2)}, u32[]{:S(2)}) %collective-permute-start.11) | collective-permute-done | bytes 33824 | tf_op jit(solution)/shard_map/ppermute | solution.py:22
  39.7 1.3 %collective-permute-done.12 = f32[2,33,128]{2,0,1:T(2,128)S(1)} collective-permute-done((f32[2,33,128]{2,0,1:T(2,128)S(1)}, f32[2,33,128]{2,0,1:T(2,128)S(1)}, u32[]{:S(2)}, u32[]{:S(2)}) %collective-permute-start.12) | collective-permute-done | bytes 33824 | tf_op jit(solution)/shard_map/ppermute | solution.py:22
  41.0 0.1 pad_maximum_fusion
  41.1 0.7 %gather_fusion = f32[4,2,33,128]{3,1,2,0:T(2,128)S(1)} fusion(f32[4,2,33,128]{3,1,2,0:T(2,128)S(1)} %pad_maximum_fusion, s32[1024]{0:T(1024)S(1)} %pad_clamp_fusion), kind=kCustom, calls=%fused_computation | custom fusion | bytes 270352 | tf_op jit(solution)/shard_map/gather | solution.py:106
  41.9 2.8 %collective-permute-start.13 = (f32[8,33,128]{2,0,1:T(8,128)S(1)}, f32[8,33,128]{2,0,1:T(8,128)S(1)}, u32[]{:S(2)}, u32[]{:S(2)}) collective-permute-start(f32[8,33,128]{2,0,1:T(8,128)S(1)} %select_add_fusion.1), channel_id=1, source_target_pairs={{0,4},{4,0},{1,5},{5,1},{2,6},{6,2},{3,7},{7,3},{8,12},{12,8},{9,1... | collective-permute-start | bytes 405512 | tf_op jit(solution)/shard_map/ppermute | solution.py:22
  44.7 2.6 %collective-permute-done.13 = f32[8,33,128]{2,0,1:T(8,128)S(1)} collective-permute-done((f32[8,33,128]{2,0,1:T(8,128)S(1)}, f32[8,33,128]{2,0,1:T(8,128)S(1)}, u32[]{:S(2)}, u32[]{:S(2)}) %collective-permute-start.13) | collective-permute-done | bytes 135200 | tf_op jit(solution)/shard_map/ppermute | solution.py:22
  47.4 7.7 %collective-permute-start.14 = (f32[8,33,128]{2,1,0:T(8,128)S(1)}, f32[8,33,128]{2,1,0:T(8,128)S(1)}, u32[]{:S(2)}, u32[]{:S(2)}) collective-permute-start(f32[8,33,128]{2,1,0:T(8,128)S(1)} %copy.9), channel_id=1, source_target_pairs={{0,2},{2,0},{1,3},{3,1},{4,6},{6,4},{5,7},{7,5},{8,10},{10,8},{9,1... | collective-permute-start | bytes 405512 | tf_op jit(solution)/shard_map/ppermute | solution.py:22
  55.1 0.1 broadcast_in_dim_broadcast_in_dim_reshape.6
  55.2 0.9 %collective-permute-done.14 = f32[8,33,128]{2,1,0:T(8,128)S(1)} collective-permute-done((f32[8,33,128]{2,1,0:T(8,128)S(1)}, f32[8,33,128]{2,1,0:T(8,128)S(1)}, u32[]{:S(2)}, u32[]{:S(2)}) %collective-permute-start.14) | collective-permute-done | bytes 135200 | tf_op jit(solution)/shard_map/ppermute | solution.py:22
  56.1 0.7 %copy-done.3 = f32[8,33,128]{2,1,0:T(8,128)} copy-done((f32[8,33,128]{2,1,0:T(8,128)}, f32[8,33,128]{2,1,0:T(8,128)S(1)}, u32[]{:S(2)}) %copy-start.3) | copy-done | bytes 135192
  56.8 0.1 broadcast_in_dim_broadcast_in_dim_reshape.7
  56.9 0.8 %slice.39 = f32[8,1,64]{2,1,0:T(1,128)S(1)} slice(f32[8,33,128]{2,1,0:T(8,128)} %copy-done.3), slice={[0:8], [32:33], [0:64]} | slice | bytes 4096 | tf_op jit(solution)/shard_map/slice | solution.py:181
  57.8 1.3 %fusion.33 = (f32[256,8]{0,1:T(8,128)S(1)}, f32[256,8]{0,1:T(8,128)S(1)}) fusion(f32[8,64]{1,0:T(8,128)S(1)} %get-tuple-element.24, bf16[1,1,16,64,256]{4,3,2,1,0:T(8,128)(2,1)} %bitcast.108, s32[]{:T(128)S(6)} %select_n.339, f32[8,64]{1,0:T(8,128)S(1)} %get-tuple-element.23, s32[]{:T(128)S(6)} %select_n.338), kind=kLoop, calls=%fused_computation.42 | loop fusion | flops 782336 | bytes 544776 | tf_op jit(solution)/shard_map/reduce_sum | solution.py:140
  59.1 1.6 %fusion.20 = bf16[1,1,256,8,64]{2,4,3,1,0:T(8,128)(2,1)S(1)} fusion(f32[1,1,256,16,64]{2,4,3,1,0:T(8,128)} %fusion.10, s32[]{:T(128)S(6)} %select_n.339, f32[256,8]{0,1:T(8,128)S(1)} %get-tuple-element.21, f32[8,64,64]{2,1,0:T(8,128)S(1)} %broadcast_in_dim_broadcast_in_dim_reshape.7, f32[16,64,64]{2,1,0:T(8,128)S(1)} %fusion.37, ...), kind=kOutput, calls=%fused_computation.28 | convolution fusion | flops 101122048 | bytes 1582592 | tf_op jit(solution)/shard_map/rnihd,rnhde->rnihe/dot_general | solution.py:137
  60.6 1.4 %fusion.21 = bf16[1,1,256,8,64]{2,4,3,1,0:T(8,128)(2,1)S(1)} fusion(f32[1,1,256,16,64]{2,4,3,1,0:T(8,128)S(1)} %copy-done.4, s32[]{:T(128)S(6)} %select_n.338, f32[256,8]{0,1:T(8,128)S(1)} %get-tuple-element.22, f32[8,64,64]{2,1,0:T(8,128)S(1)} %broadcast_in_dim_broadcast_in_dim_reshape.6, f32[16,64,64]{2,1,0:T(8,128)S(1)} %fusion.37, ...), kind=kOutput, calls=%fused_computation.29 | convolution fusion | flops 101122048 | bytes 1582592 | tf_op jit(solution)/shard_map/rnihd,rnhde->rnihe/dot_general | solution.py:137
  62.1 0.5 fusion.29
  62.5 1.3 %fusion.15 = bf16[1,256,1024]{2,1,0:T(8,128)(2,1)} fusion(f32[256,1024]{1,0:T(8,128)S(1)} %fusion.29, bf16[256,512]{0,1:T(8,128)(2,1)S(1)} %bitcast.111, bf16[1024,1024]{1,0:T(8,128)(2,1)S(1)} %copy-done, s32[]{:T(128)S(6)} %select_n.409), kind=kOutput, calls=%fused_computation.21 | convolution fusion | flops 268959744 | bytes 2883588 | tf_op jit(solution)/shard_map/rtd,de->rte/dot_general | solution.py:187
  (31 shorter events, 0.4 us)
Async XLA Ops:
  0.0 62.0 %copy-start = (bf16[1024,1024]{1,0:T(8,128)(2,1)S(1)}, bf16[1024,1024]{1,0:T(8,128)(2,1)}, u32[]{:S(2)}) copy-start(bf16[1024,1024]{1,0:T(8,128)(2,1)} %param.5) | copy-start | bytes 6291460
  3.8 1.0 %copy-start.1 = (bf16[2048,256]{1,0:T(8,128)(2,1)}, bf16[2048,256]{1,0:T(8,128)(2,1)S(1)}, u32[]{:S(2)}) copy-start(bf16[2048,256]{1,0:T(8,128)(2,1)S(1)} %fusion.2) | copy-start | bytes 3145732
  5.5 6.6 %collective-permute-start = (f32[8,33,128]{2,0,1:T(8,128)S(1)}, f32[8,33,128]{2,0,1:T(8,128)S(1)}, u32[]{:S(2)}, u32[]{:S(2)}) collective-permute-start(f32[8,33,128]{2,0,1:T(8,128)S(1)} %fusion.51), channel_id=1, source_target_pairs={{0,2},{2,0},{1,3},{3,1},{4,6},{6,4},{5,7},{7,5},{8,10},{10,8},{9,1... | collective-permute-start | bytes 405512 | tf_op jit(solution)/shard_map/ppermute | solution.py:22
  12.1 4.1 %collective-permute-start.1 = (f32[2,33,128]{2,0,1:T(2,128)S(1)}, f32[2,33,128]{2,0,1:T(2,128)S(1)}, u32[]{:S(2)}, u32[]{:S(2)}) collective-permute-start(f32[2,33,128]{2,0,1:T(2,128)S(1)} %get-tuple-element.18), channel_id=1, source_target_pairs={{0,8},{8,16},{16,24},{24,0},{1,9},{9,17},{17,25},{25,1},{2,10},{10... | collective-permute-start | bytes 101384 | tf_op jit(solution)/shard_map/ppermute | solution.py:22
  12.2 4.4 %collective-permute-start.2 = (f32[2,33,128]{2,0,1:T(2,128)S(1)}, f32[2,33,128]{2,0,1:T(2,128)S(1)}, u32[]{:S(2)}, u32[]{:S(2)}) collective-permute-start(f32[2,33,128]{2,0,1:T(2,128)S(1)} %get-tuple-element.20), channel_id=1, source_target_pairs={{0,16},{8,24},{16,0},{24,8},{1,17},{9,25},{17,1},{25,9},{2,18},{10... | collective-permute-start | bytes 101384 | tf_op jit(solution)/shard_map/ppermute | solution.py:22
  14.4 3.1 %collective-permute-start.3 = (f32[2,33,128]{2,0,1:T(2,128)S(1)}, f32[2,33,128]{2,0,1:T(2,128)S(1)}, u32[]{:S(2)}, u32[]{:S(2)}) collective-permute-start(f32[2,33,128]{2,0,1:T(2,128)S(1)} %get-tuple-element.19), channel_id=1, source_target_pairs={{0,24},{8,0},{16,8},{24,16},{1,25},{9,1},{17,9},{25,17},{2,26},{10... | collective-permute-start | bytes 101384 | tf_op jit(solution)/shard_map/ppermute | solution.py:22
  17.5 7.7 %collective-permute-start.4 = (f32[2,33,128]{2,0,1:T(2,128)S(1)}, f32[2,33,128]{2,0,1:T(2,128)S(1)}, u32[]{:S(2)}, u32[]{:S(2)}) collective-permute-start(f32[2,33,128]{2,0,1:T(2,128)S(1)} %add_add_fusion), channel_id=1, source_target_pairs={{0,32},{32,64},{64,96},{96,128},{128,160},{160,192},{192,224},{224... | collective-permute-start | bytes 101384 | tf_op jit(solution)/shard_map/ppermute | solution.py:22
  18.9 6.3 %copy-start.2 = (bf16[2048,256]{1,0:T(8,128)(2,1)S(1)}, bf16[2048,256]{1,0:T(8,128)(2,1)}, u32[]{:S(2)}) copy-start(bf16[2048,256]{1,0:T(8,128)(2,1)} %copy-done.1) | copy-start | bytes 3145732
  21.1 5.5 %collective-permute-start.7 = (f32[2,33,128]{2,0,1:T(2,128)S(1)}, f32[2,33,128]{2,0,1:T(2,128)S(1)}, u32[]{:S(2)}, u32[]{:S(2)}) collective-permute-start(f32[2,33,128]{2,0,1:T(2,128)S(1)} %add_add_fusion), channel_id=1, source_target_pairs={{0,224},{32,0},{64,32},{96,64},{128,96},{160,128},{192,160},{224,1... | collective-permute-start | bytes 101384 | tf_op jit(solution)/shard_map/ppermute | solution.py:22
  25.2 4.1 %collective-permute-start.5 = (f32[2,33,128]{2,0,1:T(2,128)S(1)}, f32[2,33,128]{2,0,1:T(2,128)S(1)}, u32[]{:S(2)}, u32[]{:S(2)}) collective-permute-start(f32[2,33,128]{2,0,1:T(2,128)S(1)} %collective-permute-done.4), channel_id=1, source_target_pairs={{0,32},{32,64},{64,96},{96,128},{128,160},{160,192},{192,224},{224... | collective-permute-start | bytes 101384 | tf_op jit(solution)/shard_map/ppermute | solution.py:22
  26.7 3.7 %collective-permute-start.8 = (f32[2,33,128]{2,0,1:T(2,128)S(1)}, f32[2,33,128]{2,0,1:T(2,128)S(1)}, u32[]{:S(2)}, u32[]{:S(2)}) collective-permute-start(f32[2,33,128]{2,0,1:T(2,128)S(1)} %collective-permute-done.7), channel_id=1, source_target_pairs={{0,224},{32,0},{64,32},{96,64},{128,96},{160,128},{192,160},{224,1... | collective-permute-start | bytes 101384 | tf_op jit(solution)/shard_map/ppermute | solution.py:22
  29.4 5.0 %collective-permute-start.6 = (f32[2,33,128]{2,0,1:T(2,128)S(1)}, f32[2,33,128]{2,0,1:T(2,128)S(1)}, u32[]{:S(2)}, u32[]{:S(2)}) collective-permute-start(f32[2,33,128]{2,0,1:T(2,128)S(1)} %select_add_fusion.7), channel_id=1, source_target_pairs={{0,64},{32,96},{64,128},{96,160},{128,192},{160,224},{192,0},{224,... | collective-permute-start | bytes 101384 | tf_op jit(solution)/shard_map/ppermute | solution.py:22
  30.4 4.0 %collective-permute-start.9 = (f32[2,33,128]{2,0,1:T(2,128)S(1)}, f32[2,33,128]{2,0,1:T(2,128)}, u32[]{:S(2)}, u32[]{:S(2)}) collective-permute-start(f32[2,33,128]{2,0,1:T(2,128)S(1)} %collective-permute-done.8), channel_id=1, source_target_pairs={{0,224},{32,0},{64,32},{96,64},{128,96},{160,128},{192,160},{224,1... | collective-permute-start | bytes 101384 | tf_op jit(solution)/shard_map/ppermute | solution.py:22
  34.5 4.1 %collective-permute-start.10 = (f32[2,33,128]{2,0,1:T(2,128)S(1)}, f32[2,33,128]{2,0,1:T(2,128)S(1)}, u32[]{:S(2)}, u32[]{:S(2)}) collective-permute-start(f32[2,33,128]{2,0,1:T(2,128)S(1)} %select_add_fusion.5), channel_id=1, source_target_pairs={{0,8},{8,16},{16,24},{24,0},{1,9},{9,17},{17,25},{25,1},{2,10},{10... | collective-permute-start | bytes 101384 | tf_op jit(solution)/shard_map/ppermute | solution.py:22
  34.9 4.8 %collective-permute-start.11 = (f32[2,33,128]{2,0,1:T(2,128)S(1)}, f32[2,33,128]{2,0,1:T(2,128)S(1)}, u32[]{:S(2)}, u32[]{:S(2)}) collective-permute-start(f32[2,33,128]{2,0,1:T(2,128)S(1)} %get-tuple-element.17), channel_id=1, source_target_pairs={{0,16},{8,24},{16,0},{24,8},{1,17},{9,25},{17,1},{25,9},{2,18},{10... | collective-permute-start | bytes 101384 | tf_op jit(solution)/shard_map/ppermute | solution.py:22
  38.2 2.8 %collective-permute-start.12 = (f32[2,33,128]{2,0,1:T(2,128)S(1)}, f32[2,33,128]{2,0,1:T(2,128)S(1)}, u32[]{:S(2)}, u32[]{:S(2)}) collective-permute-start(f32[2,33,128]{2,0,1:T(2,128)S(1)} %get-tuple-element.16), channel_id=1, source_target_pairs={{0,24},{8,0},{16,8},{24,16},{1,25},{9,1},{17,9},{25,17},{2,26},{10... | collective-permute-start | bytes 101384 | tf_op jit(solution)/shard_map/ppermute | solution.py:22
  41.9 5.5 %collective-permute-start.13 = (f32[8,33,128]{2,0,1:T(8,128)S(1)}, f32[8,33,128]{2,0,1:T(8,128)S(1)}, u32[]{:S(2)}, u32[]{:S(2)}) collective-permute-start(f32[8,33,128]{2,0,1:T(8,128)S(1)} %select_add_fusion.1), channel_id=1, source_target_pairs={{0,4},{4,0},{1,5},{5,1},{2,6},{6,2},{3,7},{7,3},{8,12},{12,8},{9,1... | collective-permute-start | bytes 405512 | tf_op jit(solution)/shard_map/ppermute | solution.py:22
  47.4 8.7 %collective-permute-start.14 = (f32[8,33,128]{2,1,0:T(8,128)S(1)}, f32[8,33,128]{2,1,0:T(8,128)S(1)}, u32[]{:S(2)}, u32[]{:S(2)}) collective-permute-start(f32[8,33,128]{2,1,0:T(8,128)S(1)} %copy.9), channel_id=1, source_target_pairs={{0,2},{2,0},{1,3},{3,1},{4,6},{6,4},{5,7},{7,5},{8,10},{10,8},{9,1... | collective-permute-start | bytes 405512 | tf_op jit(solution)/shard_map/ppermute | solution.py:22
  56.1 0.7 %copy-start.3 = (f32[8,33,128]{2,1,0:T(8,128)}, f32[8,33,128]{2,1,0:T(8,128)S(1)}, u32[]{:S(2)}) copy-start(f32[8,33,128]{2,1,0:T(8,128)S(1)} %collective-permute-done.14) | copy-start | bytes 405508
  56.9 3.7 %copy-start.4 = (f32[1,1,256,16,64]{2,4,3,1,0:T(8,128)S(1)}, f32[1,1,256,16,64]{2,4,3,1,0:T(8,128)}, u32[]{:S(2)}) copy-start(f32[1,1,256,16,64]{2,4,3,1,0:T(8,128)} %fusion.10) | copy-start | bytes 3145732

commit v19 on v17

--- a/solution.py
+++ b/solution.py
@@ -74,9 +74,18 @@
     column = came[0]
     for c in came[1:]:
         column = add(column, c)
-    planes = lax.all_gather(column, "seg_z", axis=0)
-    earlier = lax.broadcasted_iota(jnp.int32, planes.shape, 0) < z
-    before_z = jnp.sum(jnp.where(earlier, planes, 0.0), axis=0)
+    assert n_z == 8
+    left = send(column, "seg_z", cyclic(n_z, 1))
+    right = send(column, "seg_z", cyclic(n_z, -1))
+    before_z = add(keep(left, z >= 1), keep(right, z + 1 >= n_z))
+    to = lambda s: (z + s) % n_z
+    two = send(keep(column, to(2) >= 2), "seg_z", cyclic(n_z, 2))
+    three = add(keep(column, to(3) >= 3), keep(left, to(3) >= 4))
+    three = send(three, "seg_z", cyclic(n_z, 3))
+    back = add(keep(column, to(-2) + 2 >= n_z), keep(right, to(-2) + 3 >= n_z))
+    back = send(back, "seg_z", cyclic(n_z, -2))
+    before_z = add(before_z, add(two, add(three, back)))
+    before_z, carry = lax.optimization_barrier((before_z, carry))
 
     def for_row(t):
         out = before_z
@@ -92,7 +101,6 @@
         lambda *p: jnp.stack(p)[order].reshape((-1,) + p[0].shape[1:]),
         *pieces,
     )
-    mine, carry = lax.optimization_barrier((mine, carry))
     half = add(mine, swap(add(mine, keep(chip, xh == 0)), "seg_x"))
     got = swap(add(half, keep(own_c, core == 0)), "frm")
     own = tmap(lambda a, c: jnp.where(core == 0, a, a + c), half, got_c)

time: 73.9 us -> 63.3 us (0.86)
  blocking collectives: 21.1 us -> 0 us
  starting transfers between devices: 21.8 us -> 29.7 us
  matrix products: 13 us -> 18.8 us
  waiting for transfers between devices: 11.4 us -> 8.02 us
  other arithmetic: 1.7 us -> 2.81 us
  local copies, waits for them, and re-layouts: 4.48 us -> 3.48 us
    all_gather x1 -> x0, blocking collectives: 21.1 us -> none  [entering(): planes = lax.all_gather(column, 'seg_z', axis=0)]
    ppermute x9 -> x14, starting transfers between devices: 21.8 us -> 29.7 us  [send(): return tmap(lambda t: lax.ppermute(t, axis, perm=pairs), tree)]
    ppermute x9 -> x14, waiting for transfers between devices: 11.4 us -> 8.02 us  [send(): return tmap(lambda t: lax.ppermute(t, axis, perm=pairs), tree)]
    dot_general x1, matrix products: 0.95 us -> 3.47 us  [block_terms(): jnp.einsum('rnihd,rnjhd->rnhij', pq, pk, preferred_element_type=jnp.float32)]
    dot_general x1, matrix products: 1.44 us -> 3.2 us  [block_terms(): jnp.einsum('rnhij,rnjhd->rnihd', weights, vv, preferred_element_type=jnp....]
    another operation x2, local copies, waits for them, and re-layouts: 1.63 us -> 0.2 us  [finish(): before_kv = jnp.cumsum(kv_blocks, axis=1) - kv_blocks + prior_kv[:, None]]
    reduce_sum x1, other arithmetic: 0.23 us -> 1.26 us  [finish(): jnp.sum(pq32 * before_k[:, :, None], axis=-1)]
    unnamed x14 -> x8, local copies, waits for them, and re-layouts: 0.26 us -> 1.28 us
  transfers between devices with their start and end apart: 9 -> 14, of which waited for: 7 -> 7; matrix products, arithmetic and copies ran while one was open for 8% -> 17% of each run, Pallas kernels for 0% -> 0%
where the time goes in v19:
time: 63.3 us; the launch traced here: 63.1 us
  starting transfers between devices  29.7 us (47%)
  matrix products  18.8 us (30%)
  waiting for transfers between devices  8.02 us (13%)
  local copies, waits for them, and re-layouts  3.48 us (5%)
  other arithmetic  2.81 us (4%)
    ppermute x14, starting transfers between devices, send(): return tmap(lambda t: lax.ppermute(t, axis, perm=pairs), tree)  29.7 us
    ppermute x14, waiting for transfers between devices, send(): return tmap(lambda t: lax.ppermute(t, axis, perm=pairs), tree)  8.02 us
    dot_general x2, matrix products, project(): jnp.einsum('rtd,de->ret', frames_in, w, preferred_element_type=jnp.float32)  7.03 us
    dot_general x1, matrix products, block_terms(): jnp.einsum('rnihd,rnjhd->rnhij', pq, pk, preferred_element_type=jnp.float32)  3.47 us
    dot_general x1, matrix products, block_terms(): jnp.einsum('rnhij,rnjhd->rnihd', weights, vv, preferred_element_type=jnp....  3.2 us
    dot_general x2, matrix products, finish(): jnp.einsum('rnihd,rnhde->rnihe', pq32, before_kv, precision=lax.Precision...  2.96 us
    dot_general x2, matrix products, heads_of(): jnp.einsum('rtd,de->rte', heads_out, rows_w, preferred_element_type=jnp.f...  1.73 us
    unnamed x8, local copies, waits for them, and re-layouts  1.28 us
  transfers between devices with their start and end apart: 14, of which 7 were waited for; matrix products, arithmetic and copies ran while one was open for 17% of the time, Pallas kernels for 0%

profile of v19, /device:TPU:1, one launch (start us, length us, event | category | flops | bytes accessed | tf_op | source)
XLA Modules:
  0.0 63.1 jit_solution(8469646345758692694)
XLA Ops:
  0.0 3.8 %fusion.2 = bf16[2048,256]{1,0:T(8,128)(2,1)S(1)} fusion(bf16[1024,3072]{1,0:T(8,128)(2,1)} %param.4, bf16[1,256,1024]{2,1,0:T(8,128)(2,1)} %param.3), kind=kOutput, calls=%fused_computation.5 | convolution fusion | flops 1074266112 | bytes 5767168 | tf_op jit(solution)/shard_map/rtd,de->ret/dot_general | solution.py:150
  3.8 0.4 fusion.37
  4.2 0.6 copy-done.1
  4.8 0.3 convert_reduce_fusion
  5.1 0.1 reshape_squeeze.4
  5.3 0.2 copy.4
  5.5 3.3 %collective-permute-start = (f32[8,33,128]{2,0,1:T(8,128)S(1)}, f32[8,33,128]{2,0,1:T(8,128)S(1)}, u32[]{:S(2)}, u32[]{:S(2)}) collective-permute-start(f32[8,33,128]{2,0,1:T(8,128)S(1)} %fusion.51), channel_id=1, source_target_pairs={{0,2},{2,0},{1,3},{3,1},{4,6},{6,4},{5,7},{7,5},{8,10},{10,8},{9,1... | collective-permute-start | bytes 405512 | tf_op jit(solution)/shard_map/ppermute | solution.py:22
  8.8 3.3 %fusion.26 = bf16[1024,256]{1,0:T(8,128)(2,1)} fusion(bf16[1024,3072]{1,0:T(8,128)(2,1)} %param.4, bf16[1,256,1024]{2,1,0:T(8,128)(2,1)} %param.3), kind=kOutput, calls=%fused_computation.34 | convolution fusion | flops 538705920 | bytes 3145728 | tf_op jit(solution)/shard_map/rtd,de->ret/dot_general | solution.py:150
  12.1 0.0 collective-permute-done
  12.2 0.1 collective-permute-start.1
  12.3 2.2 %collective-permute-start.2 = (f32[2,33,128]{2,0,1:T(2,128)S(1)}, f32[2,33,128]{2,0,1:T(2,128)S(1)}, u32[]{:S(2)}, u32[]{:S(2)}) collective-permute-start(f32[2,33,128]{2,0,1:T(2,128)S(1)} %get-tuple-element.22), channel_id=1, source_target_pairs={{0,16},{8,24},{16,0},{24,8},{1,17},{9,25},{17,1},{25,9},{2,18},{10... | collective-permute-start | bytes 101384 | tf_op jit(solution)/shard_map/ppermute | solution.py:22
  14.4 1.1 %collective-permute-start.3 = (f32[2,33,128]{2,0,1:T(2,128)S(1)}, f32[2,33,128]{2,0,1:T(2,128)S(1)}, u32[]{:S(2)}, u32[]{:S(2)}) collective-permute-start(f32[2,33,128]{2,0,1:T(2,128)S(1)} %get-tuple-element.21), channel_id=1, source_target_pairs={{0,24},{8,0},{16,8},{24,16},{1,25},{9,1},{17,9},{25,17},{2,26},{10... | collective-permute-start | bytes 101384 | tf_op jit(solution)/shard_map/ppermute | solution.py:22
  15.5 3.5 %select_reduce_fusion = (f32[16,256]{1,0:T(8,128)S(1)}, bf16[16,256,256]{1,2,0:T(8,128)(2,1)}) fusion(pred[256,256]{0,1:T(8,128)(4,1)S(1)} %iota_compare_fusion, bf16[256,16,64]{0,2,1:T(8,128)(2,1)} %bitcast.107, bf16[1,256,2,16,64]{1,4,3,2,0:T(8,128)(2,1)} %bitcast.115), kind=kOutput, calls=%fused_computation.3 | convolution fusion | flops 138932224 | bytes 3227648 | tf_op jit(solution)/shard_map/rnihd,rnjhd->rnhij/dot_general | solution.py:116
  19.0 0.0 collective-permute-done.1
  19.0 0.0 collective-permute-done.2
  19.0 1.7 %collective-permute-start.4 = (f32[2,33,128]{2,0,1:T(2,128)S(1)}, f32[2,33,128]{2,0,1:T(2,128)S(1)}, u32[]{:S(2)}, u32[]{:S(2)}) collective-permute-start(f32[2,33,128]{2,0,1:T(2,128)S(1)} %get-tuple-element.14), channel_id=1, source_target_pairs={{0,32},{32,64},{64,96},{96,128},{128,160},{160,192},{192,224},{224... | collective-permute-start | bytes 101384 | tf_op jit(solution)/shard_map/ppermute | solution.py:22
  20.8 4.0 %collective-permute-start.5 = (f32[2,33,128]{2,0,1:T(2,128)S(1)}, f32[2,33,128]{2,0,1:T(2,128)S(1)}, u32[]{:S(2)}, u32[]{:S(2)}) collective-permute-start(f32[2,33,128]{2,0,1:T(2,128)S(1)} %get-tuple-element.14), channel_id=1, source_target_pairs={{0,224},{32,0},{64,32},{96,64},{128,96},{160,128},{192,160},{224,1... | collective-permute-start | bytes 101384 | tf_op jit(solution)/shard_map/ppermute | solution.py:22
  24.8 3.2 %fusion.10 = f32[1,1,256,16,64]{2,4,3,1,0:T(8,128)} fusion(bf16[16,256,256]{1,2,0:T(8,128)(2,1)} %get-tuple-element.30, pred[256,256]{0,1:T(8,128)(4,1)S(1)} %iota_compare_fusion, bf16[1,256,2,16,64]{1,4,3,2,0:T(8,128)(2,1)} %bitcast.116), kind=kOutput, calls=%fused_computation.17 | convolution fusion | flops 135266304 | bytes 3735552 | tf_op jit(solution)/shard_map/rnhij,rnjhd->rnihd/dot_general | solution.py:121
  28.0 0.0 collective-permute-start.6
  28.0 0.0 collective-permute-done.4
  28.0 0.7 %select_add_fusion.6 = (f32[2,33,128]{2,0,1:T(2,128)}, f32[2,33,128]{2,0,1:T(2,128)}) fusion(f32[2,33,128]{2,0,1:T(2,128)S(1)} %collective-permute-done.5, f32[2,33,128]{2,0,1:T(2,128)S(1)} %get-tuple-element.14, pred[]{:T(512)S(6)} %ge.40, pred[]{:T(512)S(6)} %ge.39, f32[2,33,128]{2,0,1:T(2,128)S(1)} %collective-permute-done.4, pred[]{:T(512)S(6)} %ge.38, ...), kind=kLoop, calls=%fused_computation.78 | loop fusion | flops 50688 | bytes 168964 | tf_op jit(solution)/shard_map/add | solution.py:18
  28.7 3.4 %collective-permute-start.7 = (f32[2,33,128]{2,0,1:T(2,128)}, f32[2,33,128]{2,0,1:T(2,128)S(1)}, u32[]{:S(2)}, u32[]{:S(2)}) collective-permute-start(f32[2,33,128]{2,0,1:T(2,128)} %get-tuple-element.24), channel_id=1, source_target_pairs={{0,96},{32,128},{64,160},{96,192},{128,224},{160,0},{192,32},{224,... | collective-permute-start | bytes 101384 | tf_op jit(solution)/shard_map/ppermute | solution.py:22
  32.1 1.7 %collective-permute-start.8 = (f32[2,33,128]{2,0,1:T(2,128)}, f32[2,33,128]{2,0,1:T(2,128)S(1)}, u32[]{:S(2)}, u32[]{:S(2)}) collective-permute-start(f32[2,33,128]{2,0,1:T(2,128)} %get-tuple-element.23), channel_id=1, source_target_pairs={{0,192},{32,224},{64,0},{96,32},{128,64},{160,96},{192,128},{224,1... | collective-permute-start | bytes 101384 | tf_op jit(solution)/shard_map/ppermute | solution.py:22
  33.9 1.7 %collective-permute-done.7 = f32[2,33,128]{2,0,1:T(2,128)S(1)} collective-permute-done((f32[2,33,128]{2,0,1:T(2,128)}, f32[2,33,128]{2,0,1:T(2,128)S(1)}, u32[]{:S(2)}, u32[]{:S(2)}) %collective-permute-start.7) | collective-permute-done | bytes 33824 | tf_op jit(solution)/shard_map/ppermute | solution.py:22
  35.6 0.7 %collective-permute-done.8 = f32[2,33,128]{2,0,1:T(2,128)S(1)} collective-permute-done((f32[2,33,128]{2,0,1:T(2,128)}, f32[2,33,128]{2,0,1:T(2,128)S(1)}, u32[]{:S(2)}, u32[]{:S(2)}) %collective-permute-start.8) | collective-permute-done | bytes 33824 | tf_op jit(solution)/shard_map/ppermute | solution.py:22
  36.4 0.1 select_add_fusion.5
  36.4 0.7 %collective-permute-start.9 = (f32[2,33,128]{2,0,1:T(2,128)S(1)}, f32[2,33,128]{2,0,1:T(2,128)S(1)}, u32[]{:S(2)}, u32[]{:S(2)}) collective-permute-start(f32[2,33,128]{2,0,1:T(2,128)S(1)} %select_add_fusion.5), channel_id=1, source_target_pairs={{0,8},{8,16},{16,24},{24,0},{1,9},{9,17},{17,25},{25,1},{2,10},{10... | collective-permute-start | bytes 101384 | tf_op jit(solution)/shard_map/ppermute | solution.py:22
  37.1 0.1 add_bitcast_fusion
  37.2 1.4 %collective-permute-start.10 = (f32[2,33,128]{2,0,1:T(2,128)S(1)}, f32[2,33,128]{2,0,1:T(2,128)S(1)}, u32[]{:S(2)}, u32[]{:S(2)}) collective-permute-start(f32[2,33,128]{2,0,1:T(2,128)S(1)} %get-tuple-element.19), channel_id=1, source_target_pairs={{0,16},{8,24},{16,0},{24,8},{1,17},{9,25},{17,1},{25,9},{2,18},{10... | collective-permute-start | bytes 101384 | tf_op jit(solution)/shard_map/ppermute | solution.py:22
  38.6 1.1 %collective-permute-start.11 = (f32[2,33,128]{2,0,1:T(2,128)S(1)}, f32[2,33,128]{2,0,1:T(2,128)S(1)}, u32[]{:S(2)}, u32[]{:S(2)}) collective-permute-start(f32[2,33,128]{2,0,1:T(2,128)S(1)} %get-tuple-element.18), channel_id=1, source_target_pairs={{0,24},{8,0},{16,8},{24,16},{1,25},{9,1},{17,9},{25,17},{2,26},{10... | collective-permute-start | bytes 101384 | tf_op jit(solution)/shard_map/ppermute | solution.py:22
  39.7 1.0 %collective-permute-done.9 = f32[2,33,128]{2,0,1:T(2,128)S(1)} collective-permute-done((f32[2,33,128]{2,0,1:T(2,128)S(1)}, f32[2,33,128]{2,0,1:T(2,128)S(1)}, u32[]{:S(2)}, u32[]{:S(2)}) %collective-permute-start.9) | collective-permute-done | bytes 33824 | tf_op jit(solution)/shard_map/ppermute | solution.py:22
  40.7 0.9 %collective-permute-done.10 = f32[2,33,128]{2,0,1:T(2,128)S(1)} collective-permute-done((f32[2,33,128]{2,0,1:T(2,128)S(1)}, f32[2,33,128]{2,0,1:T(2,128)S(1)}, u32[]{:S(2)}, u32[]{:S(2)}) %collective-permute-start.10) | collective-permute-done | bytes 33824 | tf_op jit(solution)/shard_map/ppermute | solution.py:22
  41.6 0.2 collective-permute-done.11
  41.8 0.1 pad_maximum_fusion
  41.9 0.7 %gather_fusion = f32[4,2,33,128]{3,1,2,0:T(2,128)S(1)} fusion(f32[4,2,33,128]{3,1,2,0:T(2,128)S(1)} %pad_maximum_fusion, s32[1024]{0:T(1024)S(1)} %pad_clamp_fusion), kind=kCustom, calls=%fused_computation | custom fusion | bytes 270352 | tf_op jit(solution)/shard_map/gather | solution.py:101
  42.7 2.8 %collective-permute-start.12 = (f32[8,33,128]{2,0,1:T(8,128)S(1)}, f32[8,33,128]{2,0,1:T(8,128)S(1)}, u32[]{:S(2)}, u32[]{:S(2)}) collective-permute-start(f32[8,33,128]{2,0,1:T(8,128)S(1)} %select_add_fusion.1), channel_id=1, source_target_pairs={{0,4},{4,0},{1,5},{5,1},{2,6},{6,2},{3,7},{7,3},{8,12},{12,8},{9,1... | collective-permute-start | bytes 405512 | tf_op jit(solution)/shard_map/ppermute | solution.py:22
  45.5 2.6 %collective-permute-done.12 = f32[8,33,128]{2,0,1:T(8,128)S(1)} collective-permute-done((f32[8,33,128]{2,0,1:T(8,128)S(1)}, f32[8,33,128]{2,0,1:T(8,128)S(1)}, u32[]{:S(2)}, u32[]{:S(2)}) %collective-permute-start.12) | collective-permute-done | bytes 135200 | tf_op jit(solution)/shard_map/ppermute | solution.py:22
  48.2 6.2 %collective-permute-start.13 = (f32[8,33,128]{2,1,0:T(8,128)S(1)}, f32[8,33,128]{2,1,0:T(8,128)S(1)}, u32[]{:S(2)}, u32[]{:S(2)}) collective-permute-start(f32[8,33,128]{2,1,0:T(8,128)S(1)} %copy.9), channel_id=1, source_target_pairs={{0,2},{2,0},{1,3},{3,1},{4,6},{6,4},{5,7},{7,5},{8,10},{10,8},{9,1... | collective-permute-start | bytes 405512 | tf_op jit(solution)/shard_map/ppermute | solution.py:22
  54.4 0.1 broadcast_in_dim_broadcast_in_dim_reshape.6
  54.5 0.9 %collective-permute-done.13 = f32[8,33,128]{2,1,0:T(8,128)S(1)} collective-permute-done((f32[8,33,128]{2,1,0:T(8,128)S(1)}, f32[8,33,128]{2,1,0:T(8,128)S(1)}, u32[]{:S(2)}, u32[]{:S(2)}) %collective-permute-start.13) | collective-permute-done | bytes 135200 | tf_op jit(solution)/shard_map/ppermute | solution.py:22
  55.4 0.7 %copy-done.2 = f32[8,33,128]{2,1,0:T(8,128)} copy-done((f32[8,33,128]{2,1,0:T(8,128)}, f32[8,33,128]{2,1,0:T(8,128)S(1)}, u32[]{:S(2)}) %copy-start.2) | copy-done | bytes 135192
  56.1 0.1 broadcast_in_dim_broadcast_in_dim_reshape.7
  56.2 0.8 %slice.39 = f32[8,1,64]{2,1,0:T(1,128)S(1)} slice(f32[8,33,128]{2,1,0:T(8,128)} %copy-done.2), slice={[0:8], [32:33], [0:64]} | slice | bytes 4096 | tf_op jit(solution)/shard_map/slice | solution.py:176
  57.1 1.3 %fusion.33 = (f32[256,8]{0,1:T(8,128)S(1)}, f32[256,8]{0,1:T(8,128)S(1)}) fusion(f32[8,64]{1,0:T(8,128)S(1)} %get-tuple-element.28, bf16[1,1,16,64,256]{4,3,2,1,0:T(8,128)(2,1)} %bitcast.108, s32[]{:T(128)S(6)} %select_n.351, f32[8,64]{1,0:T(8,128)S(1)} %get-tuple-element.27, s32[]{:T(128)S(6)} %select_n.350), kind=kLoop, calls=%fused_computation.42 | loop fusion | flops 782336 | bytes 544776 | tf_op jit(solution)/shard_map/reduce_sum | solution.py:135
  58.4 1.6 %fusion.20 = bf16[1,1,256,8,64]{2,4,3,1,0:T(8,128)(2,1)S(1)} fusion(f32[1,1,256,16,64]{2,4,3,1,0:T(8,128)} %fusion.10, s32[]{:T(128)S(6)} %select_n.351, f32[256,8]{0,1:T(8,128)S(1)} %get-tuple-element.25, f32[8,64,64]{2,1,0:T(8,128)S(1)} %broadcast_in_dim_broadcast_in_dim_reshape.7, f32[16,64,64]{2,1,0:T(8,128)S(1)} %fusion.37, ...), kind=kOutput, calls=%fused_computation.28 | convolution fusion | flops 101122048 | bytes 1582592 | tf_op jit(solution)/shard_map/rnihd,rnhde->rnihe/dot_general | solution.py:132
  59.9 1.4 %fusion.21 = bf16[1,1,256,8,64]{2,4,3,1,0:T(8,128)(2,1)S(1)} fusion(f32[1,1,256,16,64]{2,4,3,1,0:T(8,128)S(1)} %copy-done.3, s32[]{:T(128)S(6)} %select_n.350, f32[256,8]{0,1:T(8,128)S(1)} %get-tuple-element.26, f32[8,64,64]{2,1,0:T(8,128)S(1)} %broadcast_in_dim_broadcast_in_dim_reshape.6, f32[16,64,64]{2,1,0:T(8,128)S(1)} %fusion.37, ...), kind=kOutput, calls=%fused_computation.29 | convolution fusion | flops 101122048 | bytes 1582592 | tf_op jit(solution)/shard_map/rnihd,rnhde->rnihe/dot_general | solution.py:132
  61.4 0.5 fusion.29
  61.8 1.3 %fusion.15 = bf16[1,256,1024]{2,1,0:T(8,128)(2,1)} fusion(f32[256,1024]{1,0:T(8,128)S(1)} %fusion.29, bf16[256,512]{0,1:T(8,128)(2,1)S(1)} %bitcast.111, bf16[1024,1024]{1,0:T(8,128)(2,1)S(1)} %copy-done, s32[]{:T(128)S(6)} %select_n.423), kind=kOutput, calls=%fused_computation.21 | convolution fusion | flops 268959744 | bytes 2883588 | tf_op jit(solution)/shard_map/rtd,de->rte/dot_general | solution.py:182
  (27 shorter events, 0.5 us)
Async XLA Ops:
  0.0 61.4 %copy-start = (bf16[1024,1024]{1,0:T(8,128)(2,1)S(1)}, bf16[1024,1024]{1,0:T(8,128)(2,1)}, u32[]{:S(2)}) copy-start(bf16[1024,1024]{1,0:T(8,128)(2,1)} %param.5) | copy-start | bytes 6291460
  3.8 1.0 %copy-start.1 = (bf16[2048,256]{1,0:T(8,128)(2,1)}, bf16[2048,256]{1,0:T(8,128)(2,1)S(1)}, u32[]{:S(2)}) copy-start(bf16[2048,256]{1,0:T(8,128)(2,1)S(1)} %fusion.2) | copy-start | bytes 3145732
  5.5 6.6 %collective-permute-start = (f32[8,33,128]{2,0,1:T(8,128)S(1)}, f32[8,33,128]{2,0,1:T(8,128)S(1)}, u32[]{:S(2)}, u32[]{:S(2)}) collective-permute-start(f32[8,33,128]{2,0,1:T(8,128)S(1)} %fusion.51), channel_id=1, source_target_pairs={{0,2},{2,0},{1,3},{3,1},{4,6},{6,4},{5,7},{7,5},{8,10},{10,8},{9,1... | collective-permute-start | bytes 405512 | tf_op jit(solution)/shard_map/ppermute | solution.py:22
  12.2 6.8 %collective-permute-start.1 = (f32[2,33,128]{2,0,1:T(2,128)S(1)}, f32[2,33,128]{2,0,1:T(2,128)S(1)}, u32[]{:S(2)}, u32[]{:S(2)}) collective-permute-start(f32[2,33,128]{2,0,1:T(2,128)S(1)} %get-tuple-element.20), channel_id=1, source_target_pairs={{0,8},{8,16},{16,24},{24,0},{1,9},{9,17},{17,25},{25,1},{2,10},{10... | collective-permute-start | bytes 101384 | tf_op jit(solution)/shard_map/ppermute | solution.py:22
  12.3 6.7 %collective-permute-start.2 = (f32[2,33,128]{2,0,1:T(2,128)S(1)}, f32[2,33,128]{2,0,1:T(2,128)S(1)}, u32[]{:S(2)}, u32[]{:S(2)}) collective-permute-start(f32[2,33,128]{2,0,1:T(2,128)S(1)} %get-tuple-element.22), channel_id=1, source_target_pairs={{0,16},{8,24},{16,0},{24,8},{1,17},{9,25},{17,1},{25,9},{2,18},{10... | collective-permute-start | bytes 101384 | tf_op jit(solution)/shard_map/ppermute | solution.py:22
  14.4 4.5 %collective-permute-start.3 = (f32[2,33,128]{2,0,1:T(2,128)S(1)}, f32[2,33,128]{2,0,1:T(2,128)S(1)}, u32[]{:S(2)}, u32[]{:S(2)}) collective-permute-start(f32[2,33,128]{2,0,1:T(2,128)S(1)} %get-tuple-element.21), channel_id=1, source_target_pairs={{0,24},{8,0},{16,8},{24,16},{1,25},{9,1},{17,9},{25,17},{2,26},{10... | collective-permute-start | bytes 101384 | tf_op jit(solution)/shard_map/ppermute | solution.py:22
  19.0 8.9 %collective-permute-start.4 = (f32[2,33,128]{2,0,1:T(2,128)S(1)}, f32[2,33,128]{2,0,1:T(2,128)S(1)}, u32[]{:S(2)}, u32[]{:S(2)}) collective-permute-start(f32[2,33,128]{2,0,1:T(2,128)S(1)} %get-tuple-element.14), channel_id=1, source_target_pairs={{0,32},{32,64},{64,96},{96,128},{128,160},{160,192},{192,224},{224... | collective-permute-start | bytes 101384 | tf_op jit(solution)/shard_map/ppermute | solution.py:22
  20.8 7.2 %collective-permute-start.5 = (f32[2,33,128]{2,0,1:T(2,128)S(1)}, f32[2,33,128]{2,0,1:T(2,128)S(1)}, u32[]{:S(2)}, u32[]{:S(2)}) collective-permute-start(f32[2,33,128]{2,0,1:T(2,128)S(1)} %get-tuple-element.14), channel_id=1, source_target_pairs={{0,224},{32,0},{64,32},{96,64},{128,96},{160,128},{192,160},{224,1... | collective-permute-start | bytes 101384 | tf_op jit(solution)/shard_map/ppermute | solution.py:22
  28.0 5.9 %collective-permute-start.6 = (f32[2,33,128]{2,0,1:T(2,128)S(1)}, f32[2,33,128]{2,0,1:T(2,128)S(1)}, u32[]{:S(2)}, u32[]{:S(2)}) collective-permute-start(f32[2,33,128]{2,0,1:T(2,128)S(1)} %get-tuple-element.13), channel_id=1, source_target_pairs={{0,64},{32,96},{64,128},{96,160},{128,192},{160,224},{192,0},{224,... | collective-permute-start | bytes 101384 | tf_op jit(solution)/shard_map/ppermute | solution.py:22
  28.7 7.0 %collective-permute-start.7 = (f32[2,33,128]{2,0,1:T(2,128)}, f32[2,33,128]{2,0,1:T(2,128)S(1)}, u32[]{:S(2)}, u32[]{:S(2)}) collective-permute-start(f32[2,33,128]{2,0,1:T(2,128)} %get-tuple-element.24), channel_id=1, source_target_pairs={{0,96},{32,128},{64,160},{96,192},{128,224},{160,0},{192,32},{224,... | collective-permute-start | bytes 101384 | tf_op jit(solution)/shard_map/ppermute | solution.py:22
  32.1 4.2 %collective-permute-start.8 = (f32[2,33,128]{2,0,1:T(2,128)}, f32[2,33,128]{2,0,1:T(2,128)S(1)}, u32[]{:S(2)}, u32[]{:S(2)}) collective-permute-start(f32[2,33,128]{2,0,1:T(2,128)} %get-tuple-element.23), channel_id=1, source_target_pairs={{0,192},{32,224},{64,0},{96,32},{128,64},{160,96},{192,128},{224,1... | collective-permute-start | bytes 101384 | tf_op jit(solution)/shard_map/ppermute | solution.py:22
  36.4 4.2 %collective-permute-start.9 = (f32[2,33,128]{2,0,1:T(2,128)S(1)}, f32[2,33,128]{2,0,1:T(2,128)S(1)}, u32[]{:S(2)}, u32[]{:S(2)}) collective-permute-start(f32[2,33,128]{2,0,1:T(2,128)S(1)} %select_add_fusion.5), channel_id=1, source_target_pairs={{0,8},{8,16},{16,24},{24,0},{1,9},{9,17},{17,25},{25,1},{2,10},{10... | collective-permute-start | bytes 101384 | tf_op jit(solution)/shard_map/ppermute | solution.py:22
  37.2 4.4 %collective-permute-start.10 = (f32[2,33,128]{2,0,1:T(2,128)S(1)}, f32[2,33,128]{2,0,1:T(2,128)S(1)}, u32[]{:S(2)}, u32[]{:S(2)}) collective-permute-start(f32[2,33,128]{2,0,1:T(2,128)S(1)} %get-tuple-element.19), channel_id=1, source_target_pairs={{0,16},{8,24},{16,0},{24,8},{1,17},{9,25},{17,1},{25,9},{2,18},{10... | collective-permute-start | bytes 101384 | tf_op jit(solution)/shard_map/ppermute | solution.py:22
  38.6 3.2 %collective-permute-start.11 = (f32[2,33,128]{2,0,1:T(2,128)S(1)}, f32[2,33,128]{2,0,1:T(2,128)S(1)}, u32[]{:S(2)}, u32[]{:S(2)}) collective-permute-start(f32[2,33,128]{2,0,1:T(2,128)S(1)} %get-tuple-element.18), channel_id=1, source_target_pairs={{0,24},{8,0},{16,8},{24,16},{1,25},{9,1},{17,9},{25,17},{2,26},{10... | collective-permute-start | bytes 101384 | tf_op jit(solution)/shard_map/ppermute | solution.py:22
  42.7 5.5 %collective-permute-start.12 = (f32[8,33,128]{2,0,1:T(8,128)S(1)}, f32[8,33,128]{2,0,1:T(8,128)S(1)}, u32[]{:S(2)}, u32[]{:S(2)}) collective-permute-start(f32[8,33,128]{2,0,1:T(8,128)S(1)} %select_add_fusion.1), channel_id=1, source_target_pairs={{0,4},{4,0},{1,5},{5,1},{2,6},{6,2},{3,7},{7,3},{8,12},{12,8},{9,1... | collective-permute-start | bytes 405512 | tf_op jit(solution)/shard_map/ppermute | solution.py:22
  48.2 7.2 %collective-permute-start.13 = (f32[8,33,128]{2,1,0:T(8,128)S(1)}, f32[8,33,128]{2,1,0:T(8,128)S(1)}, u32[]{:S(2)}, u32[]{:S(2)}) collective-permute-start(f32[8,33,128]{2,1,0:T(8,128)S(1)} %copy.9), channel_id=1, source_target_pairs={{0,2},{2,0},{1,3},{3,1},{4,6},{6,4},{5,7},{7,5},{8,10},{10,8},{9,1... | collective-permute-start | bytes 405512 | tf_op jit(solution)/shard_map/ppermute | solution.py:22
  55.4 0.7 %copy-start.2 = (f32[8,33,128]{2,1,0:T(8,128)}, f32[8,33,128]{2,1,0:T(8,128)S(1)}, u32[]{:S(2)}) copy-start(f32[8,33,128]{2,1,0:T(8,128)S(1)} %collective-permute-done.13) | copy-start | bytes 405508
  56.2 3.7 %copy-start.3 = (f32[1,1,256,16,64]{2,4,3,1,0:T(8,128)S(1)}, f32[1,1,256,16,64]{2,4,3,1,0:T(8,128)}, u32[]{:S(2)}) copy-start(f32[1,1,256,16,64]{2,4,3,1,0:T(8,128)} %fusion.10) | copy-start | bytes 3145732

commit v20 on v19

--- a/solution.py
+++ b/solution.py
@@ -76,15 +76,15 @@
         column = add(column, c)
     assert n_z == 8
     left = send(column, "seg_z", cyclic(n_z, 1))
+    far = send(column, "seg_z", cyclic(n_z, 2))
     right = send(column, "seg_z", cyclic(n_z, -1))
-    before_z = add(keep(left, z >= 1), keep(right, z + 1 >= n_z))
+    before_z = add(add(keep(left, z >= 1), keep(far, z >= 2)), keep(right, z + 1 >= n_z))
     to = lambda s: (z + s) % n_z
-    two = send(keep(column, to(2) >= 2), "seg_z", cyclic(n_z, 2))
-    three = add(keep(column, to(3) >= 3), keep(left, to(3) >= 4))
-    three = send(three, "seg_z", cyclic(n_z, 3))
+    onward = add(keep(left, to(2) >= 3), keep(far, to(2) >= 4))
+    onward = send(onward, "seg_z", cyclic(n_z, 2))
     back = add(keep(column, to(-2) + 2 >= n_z), keep(right, to(-2) + 3 >= n_z))
     back = send(back, "seg_z", cyclic(n_z, -2))
-    before_z = add(before_z, add(two, add(three, back)))
+    before_z = add(before_z, add(onward, back))
     before_z, carry = lax.optimization_barrier((before_z, carry))
 
     def for_row(t):

time: 63.3 us -> 66.5 us (1.051)
  waiting for transfers between devices: 8.02 us -> 12.1 us
  starting transfers between devices: 29.7 us -> 28.8 us
    ppermute x14, waiting for transfers between devices: 8.02 us -> 12.1 us  [send(): return tmap(lambda t: lax.ppermute(t, axis, perm=pairs), tree)]
    ppermute x14, starting transfers between devices: 29.7 us -> 28.8 us  [send(): return tmap(lambda t: lax.ppermute(t, axis, perm=pairs), tree)]
  transfers between devices with their start and end apart: 14 -> 14, of which waited for: 7 -> 8; matrix products, arithmetic and copies ran while one was open for 17% -> 16% of each run, Pallas kernels for 0% -> 0%
where the time goes in v20:
time: 66.5 us; the launch traced here: 66.2 us
  starting transfers between devices  28.8 us (43%)
  matrix products  18.7 us (28%)
  waiting for transfers between devices  12.1 us (18%)
  local copies, waits for them, and re-layouts  3.49 us (5%)
  other arithmetic  2.78 us (4%)
    ppermute x14, starting transfers between devices, send(): return tmap(lambda t: lax.ppermute(t, axis, perm=pairs), tree)  28.8 us
    ppermute x14, waiting for transfers between devices, send(): return tmap(lambda t: lax.ppermute(t, axis, perm=pairs), tree)  12.1 us
    dot_general x2, matrix products, project(): jnp.einsum('rtd,de->ret', frames_in, w, preferred_element_type=jnp.float32)  7.03 us
    dot_general x1, matrix products, block_terms(): jnp.einsum('rnihd,rnjhd->rnhij', pq, pk, preferred_element_type=jnp.float32)  3.46 us
    dot_general x1, matrix products, block_terms(): jnp.einsum('rnhij,rnjhd->rnihd', weights, vv, preferred_element_type=jnp....  3.2 us
    dot_general x2, matrix products, finish(): jnp.einsum('rnihd,rnhde->rnihe', pq32, before_kv, precision=lax.Precision...  2.93 us
    dot_general x2, matrix products, heads_of(): jnp.einsum('rtd,de->rte', heads_out, rows_w, preferred_element_type=jnp.f...  1.72 us
  transfers between devices with their start and end apart: 14, of which 8 were waited for; matrix products, arithmetic and copies ran while one was open for 16% of the time, Pallas kernels for 0%

profile of v20, /device:TPU:1, one launch (start us, length us, event | category | flops | bytes accessed | tf_op | source)
XLA Modules:
  0.0 66.2 jit_solution(17449123171983131719)
XLA Ops:
  0.0 3.8 %fusion.2 = bf16[2048,256]{1,0:T(8,128)(2,1)S(1)} fusion(bf16[1024,3072]{1,0:T(8,128)(2,1)} %param.4, bf16[1,256,1024]{2,1,0:T(8,128)(2,1)} %param.3), kind=kOutput, calls=%fused_computation.5 | convolution fusion | flops 1074266112 | bytes 5767168 | tf_op jit(solution)/shard_map/rtd,de->ret/dot_general | solution.py:150
  3.8 0.4 fusion.37
  4.2 0.6 copy-done.1
  4.8 0.3 convert_reduce_fusion
  5.1 0.1 reshape_squeeze.4
  5.3 0.2 copy.4
  5.5 3.3 %collective-permute-start = (f32[8,33,128]{2,0,1:T(8,128)S(1)}, f32[8,33,128]{2,0,1:T(8,128)S(1)}, u32[]{:S(2)}, u32[]{:S(2)}) collective-permute-start(f32[8,33,128]{2,0,1:T(8,128)S(1)} %fusion.51), channel_id=1, source_target_pairs={{0,2},{2,0},{1,3},{3,1},{4,6},{6,4},{5,7},{7,5},{8,10},{10,8},{9,1... | collective-permute-start | bytes 405512 | tf_op jit(solution)/shard_map/ppermute | solution.py:22
  8.8 3.3 %fusion.26 = bf16[1024,256]{1,0:T(8,128)(2,1)} fusion(bf16[1024,3072]{1,0:T(8,128)(2,1)} %param.4, bf16[1,256,1024]{2,1,0:T(8,128)(2,1)} %param.3), kind=kOutput, calls=%fused_computation.34 | convolution fusion | flops 538705920 | bytes 3145728 | tf_op jit(solution)/shard_map/rtd,de->ret/dot_general | solution.py:150
  12.1 0.0 collective-permute-done
  12.2 0.1 collective-permute-start.1
  12.2 2.2 %collective-permute-start.2 = (f32[2,33,128]{2,0,1:T(2,128)S(1)}, f32[2,33,128]{2,0,1:T(2,128)S(1)}, u32[]{:S(2)}, u32[]{:S(2)}) collective-permute-start(f32[2,33,128]{2,0,1:T(2,128)S(1)} %get-tuple-element.20), channel_id=1, source_target_pairs={{0,16},{8,24},{16,0},{24,8},{1,17},{9,25},{17,1},{25,9},{2,18},{10... | collective-permute-start | bytes 101384 | tf_op jit(solution)/shard_map/ppermute | solution.py:22
  14.4 1.1 %collective-permute-start.3 = (f32[2,33,128]{2,0,1:T(2,128)S(1)}, f32[2,33,128]{2,0,1:T(2,128)S(1)}, u32[]{:S(2)}, u32[]{:S(2)}) collective-permute-start(f32[2,33,128]{2,0,1:T(2,128)S(1)} %get-tuple-element.19), channel_id=1, source_target_pairs={{0,24},{8,0},{16,8},{24,16},{1,25},{9,1},{17,9},{25,17},{2,26},{10... | collective-permute-start | bytes 101384 | tf_op jit(solution)/shard_map/ppermute | solution.py:22
  15.5 3.5 %select_reduce_fusion = (f32[16,256]{1,0:T(8,128)S(1)}, bf16[16,256,256]{1,2,0:T(8,128)(2,1)}) fusion(pred[256,256]{0,1:T(8,128)(4,1)S(1)} %iota_compare_fusion, bf16[256,16,64]{0,2,1:T(8,128)(2,1)} %bitcast.107, bf16[1,256,2,16,64]{1,4,3,2,0:T(8,128)(2,1)} %bitcast.115), kind=kOutput, calls=%fused_computation.3 | convolution fusion | flops 138932224 | bytes 3227648 | tf_op jit(solution)/shard_map/rnihd,rnjhd->rnhij/dot_general | solution.py:116
  19.0 0.0 collective-permute-done.1
  19.0 0.0 collective-permute-done.2
  19.0 0.0 collective-permute-done.3
  19.0 5.7 %collective-permute-start.6 = (f32[2,33,128]{2,0,1:T(2,128)S(1)}, f32[2,33,128]{2,0,1:T(2,128)S(1)}, u32[]{:S(2)}, u32[]{:S(2)}) collective-permute-start(f32[2,33,128]{2,0,1:T(2,128)S(1)} %add_add_fusion.1), channel_id=1, source_target_pairs={{0,224},{32,0},{64,32},{96,64},{128,96},{160,128},{192,160},{224,1... | collective-permute-start | bytes 101384 | tf_op jit(solution)/shard_map/ppermute | solution.py:22
  24.7 3.2 %fusion.10 = f32[1,1,256,16,64]{2,4,3,1,0:T(8,128)} fusion(bf16[16,256,256]{1,2,0:T(8,128)(2,1)} %get-tuple-element.26, pred[256,256]{0,1:T(8,128)(4,1)S(1)} %iota_compare_fusion, bf16[1,256,2,16,64]{1,4,3,2,0:T(8,128)(2,1)} %bitcast.116), kind=kOutput, calls=%fused_computation.17 | convolution fusion | flops 135266304 | bytes 3735552 | tf_op jit(solution)/shard_map/rnhij,rnjhd->rnihd/dot_general | solution.py:121
  27.9 0.0 collective-permute-done.6
  27.9 3.6 %collective-permute-start.8 = (f32[2,33,128]{2,0,1:T(2,128)S(1)}, f32[2,33,128]{2,0,1:T(2,128)S(1)}, u32[]{:S(2)}, u32[]{:S(2)}) collective-permute-start(f32[2,33,128]{2,0,1:T(2,128)S(1)} %select_add_fusion.6), channel_id=1, source_target_pairs={{0,192},{32,224},{64,0},{96,32},{128,64},{160,96},{192,128},{224,1... | collective-permute-start | bytes 101384 | tf_op jit(solution)/shard_map/ppermute | solution.py:22
  31.6 0.3 collective-permute-done.4
  31.9 1.2 %collective-permute-done.5 = f32[2,33,128]{2,0,1:T(2,128)S(1)} collective-permute-done((f32[2,33,128]{2,0,1:T(2,128)S(1)}, f32[2,33,128]{2,0,1:T(2,128)S(1)}, u32[]{:S(2)}, u32[]{:S(2)}) %collective-permute-start.5) | collective-permute-done | bytes 33824 | tf_op jit(solution)/shard_map/ppermute | solution.py:22
  33.0 0.6 select_add_fusion.7
  33.8 5.0 %collective-permute-done.7 = f32[2,33,128]{2,0,1:T(2,128)S(1)} collective-permute-done((f32[2,33,128]{2,0,1:T(2,128)}, f32[2,33,128]{2,0,1:T(2,128)S(1)}, u32[]{:S(2)}, u32[]{:S(2)}) %collective-permute-start.7) | collective-permute-done | bytes 33824 | tf_op jit(solution)/shard_map/ppermute | solution.py:22
  38.8 0.1 add_add_fusion
  38.9 0.1 select_add_fusion.5
  38.9 0.7 collective-permute-start.9
  39.6 0.1 add_bitcast_fusion
  39.7 1.1 %collective-permute-start.10 = (f32[2,33,128]{2,0,1:T(2,128)S(1)}, f32[2,33,128]{2,0,1:T(2,128)S(1)}, u32[]{:S(2)}, u32[]{:S(2)}) collective-permute-start(f32[2,33,128]{2,0,1:T(2,128)S(1)} %get-tuple-element.17), channel_id=1, source_target_pairs={{0,16},{8,24},{16,0},{24,8},{1,17},{9,25},{17,1},{25,9},{2,18},{10... | collective-permute-start | bytes 101384 | tf_op jit(solution)/shard_map/ppermute | solution.py:22
  40.8 1.4 %collective-permute-start.11 = (f32[2,33,128]{2,0,1:T(2,128)S(1)}, f32[2,33,128]{2,0,1:T(2,128)S(1)}, u32[]{:S(2)}, u32[]{:S(2)}) collective-permute-start(f32[2,33,128]{2,0,1:T(2,128)S(1)} %get-tuple-element.16), channel_id=1, source_target_pairs={{0,24},{8,0},{16,8},{24,16},{1,25},{9,1},{17,9},{25,17},{2,26},{10... | collective-permute-start | bytes 101384 | tf_op jit(solution)/shard_map/ppermute | solution.py:22
  42.2 0.9 %collective-permute-done.9 = f32[2,33,128]{2,0,1:T(2,128)S(1)} collective-permute-done((f32[2,33,128]{2,0,1:T(2,128)S(1)}, f32[2,33,128]{2,0,1:T(2,128)S(1)}, u32[]{:S(2)}, u32[]{:S(2)}) %collective-permute-start.9) | collective-permute-done | bytes 33824 | tf_op jit(solution)/shard_map/ppermute | solution.py:22
  43.2 0.9 %collective-permute-done.10 = f32[2,33,128]{2,0,1:T(2,128)S(1)} collective-permute-done((f32[2,33,128]{2,0,1:T(2,128)S(1)}, f32[2,33,128]{2,0,1:T(2,128)S(1)}, u32[]{:S(2)}, u32[]{:S(2)}) %collective-permute-start.10) | collective-permute-done | bytes 33824 | tf_op jit(solution)/shard_map/ppermute | solution.py:22
  44.1 0.2 collective-permute-done.11
  44.3 0.1 pad_maximum_fusion
  44.4 0.7 %gather_fusion = f32[4,2,33,128]{3,1,2,0:T(2,128)S(1)} fusion(f32[4,2,33,128]{3,1,2,0:T(2,128)S(1)} %pad_maximum_fusion, s32[1024]{0:T(1024)S(1)} %pad_clamp_fusion), kind=kCustom, calls=%fused_computation | custom fusion | bytes 270352 | tf_op jit(solution)/shard_map/gather | solution.py:101
  45.2 2.8 %collective-permute-start.12 = (f32[8,33,128]{2,0,1:T(8,128)S(1)}, f32[8,33,128]{2,0,1:T(8,128)S(1)}, u32[]{:S(2)}, u32[]{:S(2)}) collective-permute-start(f32[8,33,128]{2,0,1:T(8,128)S(1)} %select_add_fusion.1), channel_id=1, source_target_pairs={{0,4},{4,0},{1,5},{5,1},{2,6},{6,2},{3,7},{7,3},{8,12},{12,8},{9,1... | collective-permute-start | bytes 405512 | tf_op jit(solution)/shard_map/ppermute | solution.py:22
  48.0 2.6 %collective-permute-done.12 = f32[8,33,128]{2,0,1:T(8,128)S(1)} collective-permute-done((f32[8,33,128]{2,0,1:T(8,128)S(1)}, f32[8,33,128]{2,0,1:T(8,128)S(1)}, u32[]{:S(2)}, u32[]{:S(2)}) %collective-permute-start.12) | collective-permute-done | bytes 135200 | tf_op jit(solution)/shard_map/ppermute | solution.py:22
  50.7 6.8 %collective-permute-start.13 = (f32[8,33,128]{2,1,0:T(8,128)S(1)}, f32[8,33,128]{2,1,0:T(8,128)S(1)}, u32[]{:S(2)}, u32[]{:S(2)}) collective-permute-start(f32[8,33,128]{2,1,0:T(8,128)S(1)} %copy.9), channel_id=1, source_target_pairs={{0,2},{2,0},{1,3},{3,1},{4,6},{6,4},{5,7},{7,5},{8,10},{10,8},{9,1... | collective-permute-start | bytes 405512 | tf_op jit(solution)/shard_map/ppermute | solution.py:22
  57.6 0.1 broadcast_in_dim_broadcast_in_dim_reshape.6
  57.7 0.9 %collective-permute-done.13 = f32[8,33,128]{2,1,0:T(8,128)S(1)} collective-permute-done((f32[8,33,128]{2,1,0:T(8,128)S(1)}, f32[8,33,128]{2,1,0:T(8,128)S(1)}, u32[]{:S(2)}, u32[]{:S(2)}) %collective-permute-start.13) | collective-permute-done | bytes 135200 | tf_op jit(solution)/shard_map/ppermute | solution.py:22
  58.6 0.7 %copy-done.2 = f32[8,33,128]{2,1,0:T(8,128)} copy-done((f32[8,33,128]{2,1,0:T(8,128)}, f32[8,33,128]{2,1,0:T(8,128)S(1)}, u32[]{:S(2)}) %copy-start.2) | copy-done | bytes 135192
  59.3 0.1 broadcast_in_dim_broadcast_in_dim_reshape.7
  59.4 0.8 %slice.39 = f32[8,1,64]{2,1,0:T(1,128)S(1)} slice(f32[8,33,128]{2,1,0:T(8,128)} %copy-done.2), slice={[0:8], [32:33], [0:64]} | slice | bytes 4096 | tf_op jit(solution)/shard_map/slice | solution.py:176
  60.2 1.3 %fusion.33 = (f32[256,8]{0,1:T(8,128)S(1)}, f32[256,8]{0,1:T(8,128)S(1)}) fusion(f32[8,64]{1,0:T(8,128)S(1)} %get-tuple-element.24, bf16[1,1,16,64,256]{4,3,2,1,0:T(8,128)(2,1)} %bitcast.108, s32[]{:T(128)S(6)} %select_n.347, f32[8,64]{1,0:T(8,128)S(1)} %get-tuple-element.23, s32[]{:T(128)S(6)} %select_n.346), kind=kLoop, calls=%fused_computation.42 | loop fusion | flops 782336 | bytes 544776 | tf_op jit(solution)/shard_map/reduce_sum | solution.py:135
  61.5 1.6 %fusion.20 = bf16[1,1,256,8,64]{2,4,3,1,0:T(8,128)(2,1)S(1)} fusion(f32[1,1,256,16,64]{2,4,3,1,0:T(8,128)} %fusion.10, s32[]{:T(128)S(6)} %select_n.347, f32[256,8]{0,1:T(8,128)S(1)} %get-tuple-element.21, f32[8,64,64]{2,1,0:T(8,128)S(1)} %broadcast_in_dim_broadcast_in_dim_reshape.7, f32[16,64,64]{2,1,0:T(8,128)S(1)} %fusion.37, ...), kind=kOutput, calls=%fused_computation.28 | convolution fusion | flops 101122048 | bytes 1582592 | tf_op jit(solution)/shard_map/rnihd,rnhde->rnihe/dot_general | solution.py:132
  63.1 1.4 %fusion.21 = bf16[1,1,256,8,64]{2,4,3,1,0:T(8,128)(2,1)S(1)} fusion(f32[1,1,256,16,64]{2,4,3,1,0:T(8,128)S(1)} %copy-done.3, s32[]{:T(128)S(6)} %select_n.346, f32[256,8]{0,1:T(8,128)S(1)} %get-tuple-element.22, f32[8,64,64]{2,1,0:T(8,128)S(1)} %broadcast_in_dim_broadcast_in_dim_reshape.6, f32[16,64,64]{2,1,0:T(8,128)S(1)} %fusion.37, ...), kind=kOutput, calls=%fused_computation.29 | convolution fusion | flops 101122048 | bytes 1582592 | tf_op jit(solution)/shard_map/rnihd,rnhde->rnihe/dot_general | solution.py:132
  64.5 0.5 fusion.29
  65.0 1.3 %fusion.15 = bf16[1,256,1024]{2,1,0:T(8,128)(2,1)} fusion(f32[256,1024]{1,0:T(8,128)S(1)} %fusion.29, bf16[256,512]{0,1:T(8,128)(2,1)S(1)} %bitcast.111, bf16[1024,1024]{1,0:T(8,128)(2,1)S(1)} %copy-done, s32[]{:T(128)S(6)} %select_n.418), kind=kOutput, calls=%fused_computation.21 | convolution fusion | flops 268959744 | bytes 2883588 | tf_op jit(solution)/shard_map/rtd,de->rte/dot_general | solution.py:182
  (28 shorter events, 0.4 us)
Async XLA Ops:
  0.0 64.5 %copy-start = (bf16[1024,1024]{1,0:T(8,128)(2,1)S(1)}, bf16[1024,1024]{1,0:T(8,128)(2,1)}, u32[]{:S(2)}) copy-start(bf16[1024,1024]{1,0:T(8,128)(2,1)} %param.5) | copy-start | bytes 6291460
  3.8 1.0 %copy-start.1 = (bf16[2048,256]{1,0:T(8,128)(2,1)}, bf16[2048,256]{1,0:T(8,128)(2,1)S(1)}, u32[]{:S(2)}) copy-start(bf16[2048,256]{1,0:T(8,128)(2,1)S(1)} %fusion.2) | copy-start | bytes 3145732
  5.5 6.6 %collective-permute-start = (f32[8,33,128]{2,0,1:T(8,128)S(1)}, f32[8,33,128]{2,0,1:T(8,128)S(1)}, u32[]{:S(2)}, u32[]{:S(2)}) collective-permute-start(f32[8,33,128]{2,0,1:T(8,128)S(1)} %fusion.51), channel_id=1, source_target_pairs={{0,2},{2,0},{1,3},{3,1},{4,6},{6,4},{5,7},{7,5},{8,10},{10,8},{9,1... | collective-permute-start | bytes 405512 | tf_op jit(solution)/shard_map/ppermute | solution.py:22
  12.2 6.8 %collective-permute-start.1 = (f32[2,33,128]{2,0,1:T(2,128)S(1)}, f32[2,33,128]{2,0,1:T(2,128)S(1)}, u32[]{:S(2)}, u32[]{:S(2)}) collective-permute-start(f32[2,33,128]{2,0,1:T(2,128)S(1)} %get-tuple-element.18), channel_id=1, source_target_pairs={{0,8},{8,16},{16,24},{24,0},{1,9},{9,17},{17,25},{25,1},{2,10},{10... | collective-permute-start | bytes 101384 | tf_op jit(solution)/shard_map/ppermute | solution.py:22
  12.2 6.7 %collective-permute-start.2 = (f32[2,33,128]{2,0,1:T(2,128)S(1)}, f32[2,33,128]{2,0,1:T(2,128)S(1)}, u32[]{:S(2)}, u32[]{:S(2)}) collective-permute-start(f32[2,33,128]{2,0,1:T(2,128)S(1)} %get-tuple-element.20), channel_id=1, source_target_pairs={{0,16},{8,24},{16,0},{24,8},{1,17},{9,25},{17,1},{25,9},{2,18},{10... | collective-permute-start | bytes 101384 | tf_op jit(solution)/shard_map/ppermute | solution.py:22
  14.4 4.5 %collective-permute-start.3 = (f32[2,33,128]{2,0,1:T(2,128)S(1)}, f32[2,33,128]{2,0,1:T(2,128)S(1)}, u32[]{:S(2)}, u32[]{:S(2)}) collective-permute-start(f32[2,33,128]{2,0,1:T(2,128)S(1)} %get-tuple-element.19), channel_id=1, source_target_pairs={{0,24},{8,0},{16,8},{24,16},{1,25},{9,1},{17,9},{25,17},{2,26},{10... | collective-permute-start | bytes 101384 | tf_op jit(solution)/shard_map/ppermute | solution.py:22
  19.0 8.9 %collective-permute-start.6 = (f32[2,33,128]{2,0,1:T(2,128)S(1)}, f32[2,33,128]{2,0,1:T(2,128)S(1)}, u32[]{:S(2)}, u32[]{:S(2)}) collective-permute-start(f32[2,33,128]{2,0,1:T(2,128)S(1)} %add_add_fusion.1), channel_id=1, source_target_pairs={{0,224},{32,0},{64,32},{96,64},{128,96},{160,128},{192,160},{224,1... | collective-permute-start | bytes 101384 | tf_op jit(solution)/shard_map/ppermute | solution.py:22
  27.9 4.0 %collective-permute-start.4 = (f32[2,33,128]{2,0,1:T(2,128)S(1)}, f32[2,33,128]{2,0,1:T(2,128)S(1)}, u32[]{:S(2)}, u32[]{:S(2)}) collective-permute-start(f32[2,33,128]{2,0,1:T(2,128)S(1)} %add_add_fusion.1), channel_id=1, source_target_pairs={{0,32},{32,64},{64,96},{96,128},{128,160},{160,192},{192,224},{224... | collective-permute-start | bytes 101384 | tf_op jit(solution)/shard_map/ppermute | solution.py:22
  27.9 5.2 %collective-permute-start.5 = (f32[2,33,128]{2,0,1:T(2,128)S(1)}, f32[2,33,128]{2,0,1:T(2,128)S(1)}, u32[]{:S(2)}, u32[]{:S(2)}) collective-permute-start(f32[2,33,128]{2,0,1:T(2,128)S(1)} %add_add_fusion.1), channel_id=1, source_target_pairs={{0,64},{32,96},{64,128},{96,160},{128,192},{160,224},{192,0},{224,... | collective-permute-start | bytes 101384 | tf_op jit(solution)/shard_map/ppermute | solution.py:22
  27.9 5.9 %collective-permute-start.8 = (f32[2,33,128]{2,0,1:T(2,128)S(1)}, f32[2,33,128]{2,0,1:T(2,128)S(1)}, u32[]{:S(2)}, u32[]{:S(2)}) collective-permute-start(f32[2,33,128]{2,0,1:T(2,128)S(1)} %select_add_fusion.6), channel_id=1, source_target_pairs={{0,192},{32,224},{64,0},{96,32},{128,64},{160,96},{192,128},{224,1... | collective-permute-start | bytes 101384 | tf_op jit(solution)/shard_map/ppermute | solution.py:22
  33.7 5.1 %collective-permute-start.7 = (f32[2,33,128]{2,0,1:T(2,128)}, f32[2,33,128]{2,0,1:T(2,128)S(1)}, u32[]{:S(2)}, u32[]{:S(2)}) collective-permute-start(f32[2,33,128]{2,0,1:T(2,128)} %select_add_fusion.7), channel_id=1, source_target_pairs={{0,64},{32,96},{64,128},{96,160},{128,192},{160,224},{192,0},{224,... | collective-permute-start | bytes 101384 | tf_op jit(solution)/shard_map/ppermute | solution.py:22
  38.9 4.2 %collective-permute-start.9 = (f32[2,33,128]{2,0,1:T(2,128)S(1)}, f32[2,33,128]{2,0,1:T(2,128)S(1)}, u32[]{:S(2)}, u32[]{:S(2)}) collective-permute-start(f32[2,33,128]{2,0,1:T(2,128)S(1)} %select_add_fusion.5), channel_id=1, source_target_pairs={{0,8},{8,16},{16,24},{24,0},{1,9},{9,17},{17,25},{25,1},{2,10},{10... | collective-permute-start | bytes 101384 | tf_op jit(solution)/shard_map/ppermute | solution.py:22
  39.7 4.4 %collective-permute-start.10 = (f32[2,33,128]{2,0,1:T(2,128)S(1)}, f32[2,33,128]{2,0,1:T(2,128)S(1)}, u32[]{:S(2)}, u32[]{:S(2)}) collective-permute-start(f32[2,33,128]{2,0,1:T(2,128)S(1)} %get-tuple-element.17), channel_id=1, source_target_pairs={{0,16},{8,24},{16,0},{24,8},{1,17},{9,25},{17,1},{25,9},{2,18},{10... | collective-permute-start | bytes 101384 | tf_op jit(solution)/shard_map/ppermute | solution.py:22
  40.8 3.5 %collective-permute-start.11 = (f32[2,33,128]{2,0,1:T(2,128)S(1)}, f32[2,33,128]{2,0,1:T(2,128)S(1)}, u32[]{:S(2)}, u32[]{:S(2)}) collective-permute-start(f32[2,33,128]{2,0,1:T(2,128)S(1)} %get-tuple-element.16), channel_id=1, source_target_pairs={{0,24},{8,0},{16,8},{24,16},{1,25},{9,1},{17,9},{25,17},{2,26},{10... | collective-permute-start | bytes 101384 | tf_op jit(solution)/shard_map/ppermute | solution.py:22
  45.2 5.5 %collective-permute-start.12 = (f32[8,33,128]{2,0,1:T(8,128)S(1)}, f32[8,33,128]{2,0,1:T(8,128)S(1)}, u32[]{:S(2)}, u32[]{:S(2)}) collective-permute-start(f32[8,33,128]{2,0,1:T(8,128)S(1)} %select_add_fusion.1), channel_id=1, source_target_pairs={{0,4},{4,0},{1,5},{5,1},{2,6},{6,2},{3,7},{7,3},{8,12},{12,8},{9,1... | collective-permute-start | bytes 405512 | tf_op jit(solution)/shard_map/ppermute | solution.py:22
  50.7 7.9 %collective-permute-start.13 = (f32[8,33,128]{2,1,0:T(8,128)S(1)}, f32[8,33,128]{2,1,0:T(8,128)S(1)}, u32[]{:S(2)}, u32[]{:S(2)}) collective-permute-start(f32[8,33,128]{2,1,0:T(8,128)S(1)} %copy.9), channel_id=1, source_target_pairs={{0,2},{2,0},{1,3},{3,1},{4,6},{6,4},{5,7},{7,5},{8,10},{10,8},{9,1... | collective-permute-start | bytes 405512 | tf_op jit(solution)/shard_map/ppermute | solution.py:22
  58.6 0.7 %copy-start.2 = (f32[8,33,128]{2,1,0:T(8,128)}, f32[8,33,128]{2,1,0:T(8,128)S(1)}, u32[]{:S(2)}) copy-start(f32[8,33,128]{2,1,0:T(8,128)S(1)} %collective-permute-done.13) | copy-start | bytes 405508
  59.4 3.7 %copy-start.3 = (f32[1,1,256,16,64]{2,4,3,1,0:T(8,128)S(1)}, f32[1,1,256,16,64]{2,4,3,1,0:T(8,128)}, u32[]{:S(2)}) copy-start(f32[1,1,256,16,64]{2,4,3,1,0:T(8,128)} %fusion.10) | copy-start | bytes 3145732

commit v21 on v19

--- a/solution.py
+++ b/solution.py
@@ -96,11 +96,13 @@
     pieces = [for_row(y)] + [
         send(for_row((y + s) % n_y), "seg_y", cyclic(n_y, s)) for s in range(1, n_y)
     ]
-    order = (y - jnp.arange(n_y)) % n_y
-    mine = tmap(
-        lambda *p: jnp.stack(p)[order].reshape((-1,) + p[0].shape[1:]),
-        *pieces,
-    )
+    def placed(j):
+        out = keep(pieces[0], y == j)
+        for s in range(1, n_y):
+            out = add(out, keep(pieces[s], (y - s) % n_y == j))
+        return out
+
+    mine = tmap(lambda *p: jnp.concatenate(p, axis=0), *[placed(j) for j in range(n_y)])
     half = add(mine, swap(add(mine, keep(chip, xh == 0)), "seg_x"))
     got = swap(add(half, keep(own_c, core == 0)), "frm")
     own = tmap(lambda a, c: jnp.where(core == 0, a, a + c), half, got_c)

time: 63.3 us -> 65 us (1.027)
  waiting for transfers between devices: 8.02 us -> 9.23 us
  other arithmetic: 2.81 us -> 3.75 us
  starting transfers between devices: 29.7 us -> 28.8 us
    ppermute x14, waiting for transfers between devices: 8.02 us -> 9.23 us  [send(): return tmap(lambda t: lax.ppermute(t, axis, perm=pairs), tree)]
    add x5 -> x7, other arithmetic: 0.85 us -> 1.93 us  [tmap(): return jax.tree.map(f, *trees)]
    slice x3, local copies, waits for them, and re-layouts: 0.05 us -> 0.95 us  [heads_of(): prior_kv = prior[:, :rows_kv].reshape((half_heads,) + total_kv.shape[1:])]
    ppermute x14, starting transfers between devices: 29.7 us -> 28.8 us  [send(): return tmap(lambda t: lax.ppermute(t, axis, perm=pairs), tree)]
    gather x2 -> x0, local copies, waits for them, and re-layouts: 0.74 us -> none  [entering(): jnp.stack(p)[order].reshape((-1,) + p[0].shape[1:])]
    unnamed x8, local copies, waits for them, and re-layouts: 1.28 us -> 0.62 us
  transfers between devices with their start and end apart: 14 -> 14, of which waited for: 7 -> 8; matrix products, arithmetic and copies ran while one was open for 17% -> 18% of each run, Pallas kernels for 0% -> 0%
where the time goes in v21:
time: 65 us; the launch traced here: 64.4 us
  starting transfers between devices  28.8 us (44%)
  matrix products  19.4 us (30%)
  waiting for transfers between devices  9.23 us (14%)
  other arithmetic  3.75 us (6%)
  local copies, waits for them, and re-layouts  2.99 us (5%)
    ppermute x14, starting transfers between devices, send(): return tmap(lambda t: lax.ppermute(t, axis, perm=pairs), tree)  28.8 us
    ppermute x14, waiting for transfers between devices, send(): return tmap(lambda t: lax.ppermute(t, axis, perm=pairs), tree)  9.23 us
    dot_general x2, matrix products, project(): jnp.einsum('rtd,de->ret', frames_in, w, preferred_element_type=jnp.float32)  7.03 us
    dot_general x1, matrix products, block_terms(): jnp.einsum('rnihd,rnjhd->rnhij', pq, pk, preferred_element_type=jnp.float32)  4.04 us
    dot_general x1, matrix products, block_terms(): jnp.einsum('rnhij,rnjhd->rnihd', weights, vv, preferred_element_type=jnp....  3.21 us
    dot_general x2, matrix products, finish(): jnp.einsum('rnihd,rnhde->rnihe', pq32, before_kv, precision=lax.Precision...  2.96 us
    add x7, other arithmetic, tmap(): return jax.tree.map(f, *trees)  1.93 us
    dot_general x2, matrix products, heads_of(): jnp.einsum('rtd,de->rte', heads_out, rows_w, preferred_element_type=jnp.f...  1.73 us
  transfers between devices with their start and end apart: 14, of which 8 were waited for; matrix products, arithmetic and copies ran while one was open for 18% of the time, Pallas kernels for 0%

profile of v21, /device:TPU:1, one launch (start us, length us, event | category | flops | bytes accessed | tf_op | source)
XLA Modules:
  0.0 64.4 jit_solution(8901106436438627953)
XLA Ops:
  0.0 3.8 %fusion.2 = bf16[2048,256]{1,0:T(8,128)(2,1)S(1)} fusion(bf16[1024,3072]{1,0:T(8,128)(2,1)} %param.4, bf16[1,256,1024]{2,1,0:T(8,128)(2,1)} %param.3), kind=kOutput, calls=%fused_computation.4 | convolution fusion | flops 1074266112 | bytes 5767168 | tf_op jit(solution)/shard_map/rtd,de->ret/dot_general | solution.py:152
  3.8 0.4 fusion.37
  4.2 0.6 copy-done.1
  4.8 0.3 convert_reduce_fusion
  5.1 0.1 reshape_squeeze.4
  5.3 0.2 copy.4
  5.5 3.3 %collective-permute-start = (f32[8,33,128]{2,0,1:T(8,128)S(1)}, f32[8,33,128]{2,0,1:T(8,128)S(1)}, u32[]{:S(2)}, u32[]{:S(2)}) collective-permute-start(f32[8,33,128]{2,0,1:T(8,128)S(1)} %fusion.51), channel_id=1, source_target_pairs={{0,2},{2,0},{1,3},{3,1},{4,6},{6,4},{5,7},{7,5},{8,10},{10,8},{9,1... | collective-permute-start | bytes 405512 | tf_op jit(solution)/shard_map/ppermute | solution.py:22
  8.8 3.3 %fusion.26 = bf16[1024,256]{1,0:T(8,128)(2,1)} fusion(bf16[1024,3072]{1,0:T(8,128)(2,1)} %param.4, bf16[1,256,1024]{2,1,0:T(8,128)(2,1)} %param.3), kind=kOutput, calls=%fused_computation.33 | convolution fusion | flops 538705920 | bytes 3145728 | tf_op jit(solution)/shard_map/rtd,de->ret/dot_general | solution.py:152
  12.0 0.0 collective-permute-done
  12.1 0.1 collective-permute-start.1
  12.2 2.2 %collective-permute-start.2 = (f32[2,33,128]{2,0,1:T(2,128)S(1)}, f32[2,33,128]{2,0,1:T(2,128)S(1)}, u32[]{:S(2)}, u32[]{:S(2)}) collective-permute-start(f32[2,33,128]{2,0,1:T(2,128)S(1)} %get-tuple-element.27), channel_id=1, source_target_pairs={{0,16},{8,24},{16,0},{24,8},{1,17},{9,25},{17,1},{25,9},{2,18},{10... | collective-permute-start | bytes 101384 | tf_op jit(solution)/shard_map/ppermute | solution.py:22
  14.4 1.1 %collective-permute-start.3 = (f32[2,33,128]{2,0,1:T(2,128)S(1)}, f32[2,33,128]{2,0,1:T(2,128)S(1)}, u32[]{:S(2)}, u32[]{:S(2)}) collective-permute-start(f32[2,33,128]{2,0,1:T(2,128)S(1)} %get-tuple-element.26), channel_id=1, source_target_pairs={{0,24},{8,0},{16,8},{24,16},{1,25},{9,1},{17,9},{25,17},{2,26},{10... | collective-permute-start | bytes 101384 | tf_op jit(solution)/shard_map/ppermute | solution.py:22
  15.5 0.7 %collective-permute-done.1 = f32[2,33,128]{2,0,1:T(2,128)S(1)} collective-permute-done((f32[2,33,128]{2,0,1:T(2,128)S(1)}, f32[2,33,128]{2,0,1:T(2,128)S(1)}, u32[]{:S(2)}, u32[]{:S(2)}) %collective-permute-start.1) | collective-permute-done | bytes 33824 | tf_op jit(solution)/shard_map/ppermute | solution.py:22
  16.2 0.4 collective-permute-done.2
  16.6 0.9 %collective-permute-done.3 = f32[2,33,128]{2,0,1:T(2,128)S(1)} collective-permute-done((f32[2,33,128]{2,0,1:T(2,128)S(1)}, f32[2,33,128]{2,0,1:T(2,128)S(1)}, u32[]{:S(2)}, u32[]{:S(2)}) %collective-permute-start.3) | collective-permute-done | bytes 33824 | tf_op jit(solution)/shard_map/ppermute | solution.py:22
  17.5 1.4 %collective-permute-start.4 = (f32[2,33,128]{2,0,1:T(2,128)S(1)}, f32[2,33,128]{2,0,1:T(2,128)S(1)}, u32[]{:S(2)}, u32[]{:S(2)}) collective-permute-start(f32[2,33,128]{2,0,1:T(2,128)S(1)} %get-tuple-element.16), channel_id=1, source_target_pairs={{0,32},{32,64},{64,96},{96,128},{128,160},{160,192},{192,224},{224... | collective-permute-start | bytes 101384 | tf_op jit(solution)/shard_map/ppermute | solution.py:22
  18.9 4.0 %collective-permute-start.5 = (f32[2,33,128]{2,0,1:T(2,128)S(1)}, f32[2,33,128]{2,0,1:T(2,128)S(1)}, u32[]{:S(2)}, u32[]{:S(2)}) collective-permute-start(f32[2,33,128]{2,0,1:T(2,128)S(1)} %get-tuple-element.16), channel_id=1, source_target_pairs={{0,224},{32,0},{64,32},{96,64},{128,96},{160,128},{192,160},{224,1... | collective-permute-start | bytes 101384 | tf_op jit(solution)/shard_map/ppermute | solution.py:22
  23.0 4.0 %select_reduce_fusion = (f32[16,256]{1,0:T(8,128)}, bf16[16,256,256]{1,2,0:T(8,128)(2,1)}) fusion(pred[256,256]{0,1:T(8,128)(4,1)S(1)} %iota_compare_fusion, bf16[256,16,64]{0,2,1:T(8,128)(2,1)} %bitcast.97, bf16[1,256,2,16,64]{1,4,3,2,0:T(8,128)(2,1)} %bitcast.105), kind=kOutput, calls=%fused_computation.2 | convolution fusion | flops 138932224 | bytes 3227648 | tf_op jit(solution)/shard_map/rnihd,rnjhd->rnhij/dot_general | solution.py:118
  27.0 0.0 collective-permute-start.6
  27.0 0.7 %select_add_fusion.11 = (f32[2,33,128]{2,0,1:T(2,128)}, f32[2,33,128]{2,0,1:T(2,128)}) fusion(f32[2,33,128]{2,0,1:T(2,128)S(1)} %collective-permute-done.5, f32[2,33,128]{2,0,1:T(2,128)S(1)} %get-tuple-element.16, pred[]{:T(512)S(6)} %ge.40, pred[]{:T(512)S(6)} %ge.39, f32[2,33,128]{2,0,1:T(2,128)S(1)} %collective-permute-done.4, pred[]{:T(512)S(6)} %ge.38, ...), kind=kLoop, calls=%fused_computation.82 | loop fusion | flops 50688 | bytes 168964 | tf_op jit(solution)/shard_map/add | solution.py:18
  27.7 3.4 %collective-permute-start.7 = (f32[2,33,128]{2,0,1:T(2,128)}, f32[2,33,128]{2,0,1:T(2,128)S(1)}, u32[]{:S(2)}, u32[]{:S(2)}) collective-permute-start(f32[2,33,128]{2,0,1:T(2,128)} %get-tuple-element.29), channel_id=1, source_target_pairs={{0,96},{32,128},{64,160},{96,192},{128,224},{160,0},{192,32},{224,... | collective-permute-start | bytes 101384 | tf_op jit(solution)/shard_map/ppermute | solution.py:22
  31.2 1.6 %collective-permute-start.8 = (f32[2,33,128]{2,0,1:T(2,128)}, f32[2,33,128]{2,0,1:T(2,128)}, u32[]{:S(2)}, u32[]{:S(2)}) collective-permute-start(f32[2,33,128]{2,0,1:T(2,128)} %get-tuple-element.28), channel_id=1, source_target_pairs={{0,192},{32,224},{64,0},{96,32},{128,64},{160,96},{192,128},{224,1... | collective-permute-start | bytes 101384 | tf_op jit(solution)/shard_map/ppermute | solution.py:22
  32.8 3.2 %fusion.10 = f32[1,1,256,16,64]{2,4,3,1,0:T(8,128)} fusion(bf16[16,256,256]{1,2,0:T(8,128)(2,1)} %get-tuple-element.35, pred[256,256]{0,1:T(8,128)(4,1)S(1)} %iota_compare_fusion, bf16[1,256,2,16,64]{1,4,3,2,0:T(8,128)(2,1)} %bitcast.106), kind=kOutput, calls=%fused_computation.16 | convolution fusion | flops 135266304 | bytes 3735552 | tf_op jit(solution)/shard_map/rnhij,rnjhd->rnihd/dot_general | solution.py:123
  36.0 0.8 %add_add_fusion = f32[2,33,128]{2,0,1:T(2,128)S(1)} fusion(f32[2,33,128]{2,0,1:T(2,128)S(1)} %collective-permute-done.6, f32[2,33,128]{2,0,1:T(2,128)S(1)} %collective-permute-done.7, f32[2,33,128]{2,0,1:T(2,128)} %collective-permute-done.8, f32[2,33,128]{2,0,1:T(2,128)S(1)} %collective-permute-done.5, f32[2,33,128]{2,0,1:T(2,128)S(1)} %collective-permute-done.4, ...), kind=kLoop, calls=%fused_computation.81 | loop fusion | flops 50688 | bytes 202754 | tf_op jit(solution)/shard_map/add | solution.py:18
  36.8 0.1 select_add_fusion.9
  37.0 1.6 %collective-permute-start.10 = (f32[2,33,128]{2,0,1:T(2,128)S(1)}, f32[2,33,128]{2,0,1:T(2,128)S(1)}, u32[]{:S(2)}, u32[]{:S(2)}) collective-permute-start(f32[2,33,128]{2,0,1:T(2,128)S(1)} %get-tuple-element.21), channel_id=1, source_target_pairs={{0,16},{8,24},{16,0},{24,8},{1,17},{9,25},{17,1},{25,9},{2,18},{10... | collective-permute-start | bytes 101384 | tf_op jit(solution)/shard_map/ppermute | solution.py:22
  38.6 1.1 %collective-permute-start.11 = (f32[2,33,128]{2,0,1:T(2,128)S(1)}, f32[2,33,128]{2,0,1:T(2,128)S(1)}, u32[]{:S(2)}, u32[]{:S(2)}) collective-permute-start(f32[2,33,128]{2,0,1:T(2,128)S(1)} %get-tuple-element.20), channel_id=1, source_target_pairs={{0,24},{8,0},{16,8},{24,16},{1,25},{9,1},{17,9},{25,17},{2,26},{10... | collective-permute-start | bytes 101384 | tf_op jit(solution)/shard_map/ppermute | solution.py:22
  39.7 0.4 collective-permute-start.9
  40.0 1.3 %collective-permute-done.10 = f32[2,33,128]{2,0,1:T(2,128)S(1)} collective-permute-done((f32[2,33,128]{2,0,1:T(2,128)S(1)}, f32[2,33,128]{2,0,1:T(2,128)S(1)}, u32[]{:S(2)}, u32[]{:S(2)}) %collective-permute-start.10) | collective-permute-done | bytes 33824 | tf_op jit(solution)/shard_map/ppermute | solution.py:22
  41.3 0.2 collective-permute-done.11
  41.6 2.1 %collective-permute-done.9 = f32[2,33,128]{2,0,1:T(2,128)S(1)} collective-permute-done((f32[2,33,128]{2,0,1:T(2,128)S(1)}, f32[2,33,128]{2,0,1:T(2,128)S(1)}, u32[]{:S(2)}, u32[]{:S(2)}) %collective-permute-start.9) | collective-permute-done | bytes 33824 | tf_op jit(solution)/shard_map/ppermute | solution.py:22
  43.6 0.1 select_add_fusion.6
  43.8 0.1 select_add_fusion.5
  43.9 0.1 select_add_fusion.1
  43.9 2.8 %collective-permute-start.12 = (f32[8,33,128]{2,0,1:T(8,128)S(1)}, f32[8,33,128]{2,0,1:T(8,128)S(1)}, u32[]{:S(2)}, u32[]{:S(2)}) collective-permute-start(f32[8,33,128]{2,0,1:T(8,128)S(1)} %select_add_fusion.1), channel_id=1, source_target_pairs={{0,4},{4,0},{1,5},{5,1},{2,6},{6,2},{3,7},{7,3},{8,12},{12,8},{9,1... | collective-permute-start | bytes 405512 | tf_op jit(solution)/shard_map/ppermute | solution.py:22
  46.8 2.6 %collective-permute-done.12 = f32[8,33,128]{2,0,1:T(8,128)S(1)} collective-permute-done((f32[8,33,128]{2,0,1:T(8,128)S(1)}, f32[8,33,128]{2,0,1:T(8,128)S(1)}, u32[]{:S(2)}, u32[]{:S(2)}) %collective-permute-start.12) | collective-permute-done | bytes 135200 | tf_op jit(solution)/shard_map/ppermute | solution.py:22
  49.4 0.1 add_select_fusion
  49.5 5.8 %collective-permute-start.13 = (f32[8,33,128]{2,1,0:T(8,128)S(1)}, f32[8,33,128]{2,1,0:T(8,128)}, u32[]{:S(2)}, u32[]{:S(2)}) collective-permute-start(f32[8,33,128]{2,1,0:T(8,128)S(1)} %copy.8), channel_id=1, source_target_pairs={{0,2},{2,0},{1,3},{3,1},{4,6},{6,4},{5,7},{7,5},{8,10},{10,8},{9,1... | collective-permute-start | bytes 405512 | tf_op jit(solution)/shard_map/ppermute | solution.py:22
  55.3 0.1 broadcast_in_dim_broadcast_in_dim_reshape.6
  55.5 1.0 %collective-permute-done.13 = f32[8,33,128]{2,1,0:T(8,128)} collective-permute-done((f32[8,33,128]{2,1,0:T(8,128)S(1)}, f32[8,33,128]{2,1,0:T(8,128)}, u32[]{:S(2)}, u32[]{:S(2)}) %collective-permute-start.13) | collective-permute-done | bytes 135200 | tf_op jit(solution)/shard_map/ppermute | solution.py:22
  56.5 0.9 %slice.36 = f32[8,32,128]{2,1,0:T(8,128)S(1)} slice(f32[8,33,128]{2,1,0:T(8,128)} %collective-permute-done.13), slice={[0:8], [0:32], [0:128]} | slice | bytes 262144 | tf_op jit(solution)/shard_map/slice | solution.py:177
  57.4 0.1 broadcast_in_dim_broadcast_in_dim_reshape.7
  57.5 0.8 %slice.37 = f32[8,1,64]{2,1,0:T(1,128)S(1)} slice(f32[8,33,128]{2,1,0:T(8,128)} %collective-permute-done.13), slice={[0:8], [32:33], [0:64]} | slice | bytes 4096 | tf_op jit(solution)/shard_map/slice | solution.py:178
  58.4 1.3 %fusion.33 = (f32[256,8]{0,1:T(8,128)S(1)}, f32[256,8]{0,1:T(8,128)S(1)}) fusion(f32[8,64]{1,0:T(8,128)S(1)} %get-tuple-element.33, bf16[1,1,16,64,256]{4,3,2,1,0:T(8,128)(2,1)} %bitcast.98, s32[]{:T(128)S(6)} %select_n.448, f32[8,64]{1,0:T(8,128)S(1)} %get-tuple-element.32, s32[]{:T(128)S(6)} %select_n.447), kind=kLoop, calls=%fused_computation.41 | loop fusion | flops 782336 | bytes 544776 | tf_op jit(solution)/shard_map/reduce_sum | solution.py:137
  59.7 1.6 %fusion.20 = bf16[1,1,256,8,64]{2,4,3,1,0:T(8,128)(2,1)S(1)} fusion(f32[1,1,256,16,64]{2,4,3,1,0:T(8,128)} %fusion.10, s32[]{:T(128)S(6)} %select_n.448, f32[256,8]{0,1:T(8,128)S(1)} %get-tuple-element.30, f32[8,64,64]{2,1,0:T(8,128)S(1)} %broadcast_in_dim_broadcast_in_dim_reshape.7, f32[16,64,64]{2,1,0:T(8,128)S(1)} %fusion.37, ...), kind=kOutput, calls=%fused_computation.27 | convolution fusion | flops 101122048 | bytes 1582592 | tf_op jit(solution)/shard_map/rnihd,rnhde->rnihe/dot_general | solution.py:134
  61.2 1.4 %fusion.21 = bf16[1,1,256,8,64]{2,4,3,1,0:T(8,128)(2,1)S(1)} fusion(f32[1,1,256,16,64]{2,4,3,1,0:T(8,128)S(1)} %copy-done.3, s32[]{:T(128)S(6)} %select_n.447, f32[256,8]{0,1:T(8,128)S(1)} %get-tuple-element.31, f32[8,64,64]{2,1,0:T(8,128)S(1)} %broadcast_in_dim_broadcast_in_dim_reshape.6, f32[16,64,64]{2,1,0:T(8,128)S(1)} %fusion.37, ...), kind=kOutput, calls=%fused_computation.28 | convolution fusion | flops 101122048 | bytes 1582592 | tf_op jit(solution)/shard_map/rnihd,rnhde->rnihe/dot_general | solution.py:134
  62.7 0.5 fusion.29
  63.1 1.3 %fusion.15 = bf16[1,256,1024]{2,1,0:T(8,128)(2,1)} fusion(f32[256,1024]{1,0:T(8,128)S(1)} %fusion.29, bf16[256,512]{0,1:T(8,128)(2,1)S(1)} %bitcast.101, bf16[1024,1024]{1,0:T(8,128)(2,1)S(1)} %copy-done, s32[]{:T(128)S(6)} %select_n.550), kind=kOutput, calls=%fused_computation.20 | convolution fusion | flops 268959744 | bytes 2883588 | tf_op jit(solution)/shard_map/rtd,de->rte/dot_general | solution.py:184
  (23 shorter events, 0.3 us)
Async XLA Ops:
  0.0 62.6 %copy-start = (bf16[1024,1024]{1,0:T(8,128)(2,1)S(1)}, bf16[1024,1024]{1,0:T(8,128)(2,1)}, u32[]{:S(2)}) copy-start(bf16[1024,1024]{1,0:T(8,128)(2,1)} %param.5) | copy-start | bytes 6291460
  3.8 1.0 %copy-start.1 = (bf16[2048,256]{1,0:T(8,128)(2,1)}, bf16[2048,256]{1,0:T(8,128)(2,1)S(1)}, u32[]{:S(2)}) copy-start(bf16[2048,256]{1,0:T(8,128)(2,1)S(1)} %fusion.2) | copy-start | bytes 3145732
  5.5 6.6 %collective-permute-start = (f32[8,33,128]{2,0,1:T(8,128)S(1)}, f32[8,33,128]{2,0,1:T(8,128)S(1)}, u32[]{:S(2)}, u32[]{:S(2)}) collective-permute-start(f32[8,33,128]{2,0,1:T(8,128)S(1)} %fusion.51), channel_id=1, source_target_pairs={{0,2},{2,0},{1,3},{3,1},{4,6},{6,4},{5,7},{7,5},{8,10},{10,8},{9,1... | collective-permute-start | bytes 405512 | tf_op jit(solution)/shard_map/ppermute | solution.py:22
  12.1 4.1 %collective-permute-start.1 = (f32[2,33,128]{2,0,1:T(2,128)S(1)}, f32[2,33,128]{2,0,1:T(2,128)S(1)}, u32[]{:S(2)}, u32[]{:S(2)}) collective-permute-start(f32[2,33,128]{2,0,1:T(2,128)S(1)} %get-tuple-element.25), channel_id=1, source_target_pairs={{0,8},{8,16},{16,24},{24,0},{1,9},{9,17},{17,25},{25,1},{2,10},{10... | collective-permute-start | bytes 101384 | tf_op jit(solution)/shard_map/ppermute | solution.py:22
  12.2 4.4 %collective-permute-start.2 = (f32[2,33,128]{2,0,1:T(2,128)S(1)}, f32[2,33,128]{2,0,1:T(2,128)S(1)}, u32[]{:S(2)}, u32[]{:S(2)}) collective-permute-start(f32[2,33,128]{2,0,1:T(2,128)S(1)} %get-tuple-element.27), channel_id=1, source_target_pairs={{0,16},{8,24},{16,0},{24,8},{1,17},{9,25},{17,1},{25,9},{2,18},{10... | collective-permute-start | bytes 101384 | tf_op jit(solution)/shard_map/ppermute | solution.py:22
  14.4 3.1 %collective-permute-start.3 = (f32[2,33,128]{2,0,1:T(2,128)S(1)}, f32[2,33,128]{2,0,1:T(2,128)S(1)}, u32[]{:S(2)}, u32[]{:S(2)}) collective-permute-start(f32[2,33,128]{2,0,1:T(2,128)S(1)} %get-tuple-element.26), channel_id=1, source_target_pairs={{0,24},{8,0},{16,8},{24,16},{1,25},{9,1},{17,9},{25,17},{2,26},{10... | collective-permute-start | bytes 101384 | tf_op jit(solution)/shard_map/ppermute | solution.py:22
  17.5 9.5 %collective-permute-start.4 = (f32[2,33,128]{2,0,1:T(2,128)S(1)}, f32[2,33,128]{2,0,1:T(2,128)S(1)}, u32[]{:S(2)}, u32[]{:S(2)}) collective-permute-start(f32[2,33,128]{2,0,1:T(2,128)S(1)} %get-tuple-element.16), channel_id=1, source_target_pairs={{0,32},{32,64},{64,96},{96,128},{128,160},{160,192},{192,224},{224... | collective-permute-start | bytes 101384 | tf_op jit(solution)/shard_map/ppermute | solution.py:22
  18.9 8.1 %collective-permute-start.5 = (f32[2,33,128]{2,0,1:T(2,128)S(1)}, f32[2,33,128]{2,0,1:T(2,128)S(1)}, u32[]{:S(2)}, u32[]{:S(2)}) collective-permute-start(f32[2,33,128]{2,0,1:T(2,128)S(1)} %get-tuple-element.16), channel_id=1, source_target_pairs={{0,224},{32,0},{64,32},{96,64},{128,96},{160,128},{192,160},{224,1... | collective-permute-start | bytes 101384 | tf_op jit(solution)/shard_map/ppermute | solution.py:22
  27.0 9.0 %collective-permute-start.6 = (f32[2,33,128]{2,0,1:T(2,128)S(1)}, f32[2,33,128]{2,0,1:T(2,128)S(1)}, u32[]{:S(2)}, u32[]{:S(2)}) collective-permute-start(f32[2,33,128]{2,0,1:T(2,128)S(1)} %get-tuple-element.15), channel_id=1, source_target_pairs={{0,64},{32,96},{64,128},{96,160},{128,192},{160,224},{192,0},{224,... | collective-permute-start | bytes 101384 | tf_op jit(solution)/shard_map/ppermute | solution.py:22
  27.7 8.3 %collective-permute-start.7 = (f32[2,33,128]{2,0,1:T(2,128)}, f32[2,33,128]{2,0,1:T(2,128)S(1)}, u32[]{:S(2)}, u32[]{:S(2)}) collective-permute-start(f32[2,33,128]{2,0,1:T(2,128)} %get-tuple-element.29), channel_id=1, source_target_pairs={{0,96},{32,128},{64,160},{96,192},{128,224},{160,0},{192,32},{224,... | collective-permute-start | bytes 101384 | tf_op jit(solution)/shard_map/ppermute | solution.py:22
  31.2 4.9 %collective-permute-start.8 = (f32[2,33,128]{2,0,1:T(2,128)}, f32[2,33,128]{2,0,1:T(2,128)}, u32[]{:S(2)}, u32[]{:S(2)}) collective-permute-start(f32[2,33,128]{2,0,1:T(2,128)} %get-tuple-element.28), channel_id=1, source_target_pairs={{0,192},{32,224},{64,0},{96,32},{128,64},{160,96},{192,128},{224,1... | collective-permute-start | bytes 101384 | tf_op jit(solution)/shard_map/ppermute | solution.py:22
  37.0 4.4 %collective-permute-start.10 = (f32[2,33,128]{2,0,1:T(2,128)S(1)}, f32[2,33,128]{2,0,1:T(2,128)S(1)}, u32[]{:S(2)}, u32[]{:S(2)}) collective-permute-start(f32[2,33,128]{2,0,1:T(2,128)S(1)} %get-tuple-element.21), channel_id=1, source_target_pairs={{0,16},{8,24},{16,0},{24,8},{1,17},{9,25},{17,1},{25,9},{2,18},{10... | collective-permute-start | bytes 101384 | tf_op jit(solution)/shard_map/ppermute | solution.py:22
  38.6 3.0 %collective-permute-start.11 = (f32[2,33,128]{2,0,1:T(2,128)S(1)}, f32[2,33,128]{2,0,1:T(2,128)S(1)}, u32[]{:S(2)}, u32[]{:S(2)}) collective-permute-start(f32[2,33,128]{2,0,1:T(2,128)S(1)} %get-tuple-element.20), channel_id=1, source_target_pairs={{0,24},{8,0},{16,8},{24,16},{1,25},{9,1},{17,9},{25,17},{2,26},{10... | collective-permute-start | bytes 101384 | tf_op jit(solution)/shard_map/ppermute | solution.py:22
  39.7 4.0 %collective-permute-start.9 = (f32[2,33,128]{2,0,1:T(2,128)S(1)}, f32[2,33,128]{2,0,1:T(2,128)S(1)}, u32[]{:S(2)}, u32[]{:S(2)}) collective-permute-start(f32[2,33,128]{2,0,1:T(2,128)S(1)} %get-tuple-element.19), channel_id=1, source_target_pairs={{0,8},{8,16},{16,24},{24,0},{1,9},{9,17},{17,25},{25,1},{2,10},{10... | collective-permute-start | bytes 101384 | tf_op jit(solution)/shard_map/ppermute | solution.py:22
  43.7 15.9 %copy-start.2 = (f32[16,256]{1,0:T(8,128)S(1)}, f32[16,256]{1,0:T(8,128)}, u32[]{:S(2)}) copy-start(f32[16,256]{1,0:T(8,128)} %get-tuple-element.34) | copy-start | bytes 49156
  43.9 5.5 %collective-permute-start.12 = (f32[8,33,128]{2,0,1:T(8,128)S(1)}, f32[8,33,128]{2,0,1:T(8,128)S(1)}, u32[]{:S(2)}, u32[]{:S(2)}) collective-permute-start(f32[8,33,128]{2,0,1:T(8,128)S(1)} %select_add_fusion.1), channel_id=1, source_target_pairs={{0,4},{4,0},{1,5},{5,1},{2,6},{6,2},{3,7},{7,3},{8,12},{12,8},{9,1... | collective-permute-start | bytes 405512 | tf_op jit(solution)/shard_map/ppermute | solution.py:22
  49.5 6.9 %collective-permute-start.13 = (f32[8,33,128]{2,1,0:T(8,128)S(1)}, f32[8,33,128]{2,1,0:T(8,128)}, u32[]{:S(2)}, u32[]{:S(2)}) collective-permute-start(f32[8,33,128]{2,1,0:T(8,128)S(1)} %copy.8), channel_id=1, source_target_pairs={{0,2},{2,0},{1,3},{3,1},{4,6},{6,4},{5,7},{7,5},{8,10},{10,8},{9,1... | collective-permute-start | bytes 405512 | tf_op jit(solution)/shard_map/ppermute | solution.py:22
  57.5 3.7 %copy-start.3 = (f32[1,1,256,16,64]{2,4,3,1,0:T(8,128)S(1)}, f32[1,1,256,16,64]{2,4,3,1,0:T(8,128)}, u32[]{:S(2)}) copy-start(f32[1,1,256,16,64]{2,4,3,1,0:T(8,128)} %fusion.10) | copy-start | bytes 3145732

commit v22 on v19

--- a/solution.py
+++ b/solution.py
@@ -56,7 +56,7 @@
     return [(i, (i + s) % n) for i in range(n)]
 
 
-def entering(total, carry):
+def entering(total, carry, late, use_late):
     core = lax.axis_index("frm")
     xh = lax.axis_index("seg_x")
     y = lax.axis_index("seg_y")
@@ -74,6 +74,8 @@
     column = came[0]
     for c in came[1:]:
         column = add(column, c)
+    column, late = lax.optimization_barrier((column, late))
+    carry = use_late(late, carry)
     assert n_z == 8
     left = send(column, "seg_z", cyclic(n_z, 1))
     right = send(column, "seg_z", cyclic(n_z, -1))
@@ -152,19 +154,32 @@
         return jnp.transpose(out, (0, 4, 1, 2, 3))
 
     keys_values = project(w_qkv[:, width:], 2)
-    queries = project(w_qkv[:, :width], 1)
-    phi_q = features(queries[:, :, 0].astype(jnp.float32)).astype(jnp.bfloat16)
     phi_k = features(keys_values[:, :, 0].astype(jnp.float32)).astype(jnp.bfloat16)
     values = keys_values[:, :, 1]
-    pq, num_local, den_local, kv_blocks, k_blocks = block_terms(phi_q, phi_k, values, SPAN)
+    kv_blocks = jnp.einsum(
+        "rnjhd,rnjhe->rnhde",
+        phi_k.reshape(rows, -1, SPAN, HEADS, head_dim),
+        values.reshape(rows, -1, SPAN, HEADS, head_dim),
+        preferred_element_type=jnp.float32,
+    )
+    k_blocks = jnp.sum(phi_k.reshape(rows, -1, SPAN, HEADS, head_dim), axis=2, dtype=jnp.float32)
+
+    def local(frames, _):
+        queries = jnp.einsum("rtd,de->ret", frames, w_qkv[:, :width], preferred_element_type=jnp.float32)
+        queries = queries.astype(jnp.bfloat16).reshape(rows, 1, HEADS, head_dim, tok_local)
+        queries = jnp.transpose(queries, (0, 4, 1, 2, 3))
+        phi_q = features(queries[:, :, 0].astype(jnp.float32)).astype(jnp.bfloat16)
+        pq, num_local, den_local, _, _ = block_terms(phi_q, phi_k, values, SPAN)
+        return pq, num_local, den_local
+
     total_kv = jnp.sum(kv_blocks, axis=1)[0]
     total_k = jnp.sum(k_blocks, axis=1)[0]
     lanes = 128
     dense = total_kv.reshape(HEADS, -1, lanes)
     rows_kv = dense.shape[1]
     norm = jnp.pad(total_k, ((0, 0), (0, lanes - total_k.shape[1])))[:, None]
-    (own, other), (num_local, den_local) = entering(
-        jnp.concatenate([dense, norm], axis=1), (num_local, den_local)
+    (own, other), (pq, num_local, den_local) = entering(
+        jnp.concatenate([dense, norm], axis=1), None, frames_in, local
     )
     core = lax.axis_index("frm")
     half_heads = HEADS // 2

time: 63.3 us -> 64.1 us (1.013)
  waiting for transfers between devices: 8.02 us -> 11.6 us
  local copies, waits for them, and re-layouts: 3.48 us -> 6.96 us
  matrix products: 18.8 us -> 15.5 us
  other arithmetic: 2.81 us -> 1.13 us
  starting transfers between devices: 29.7 us -> 28.2 us
    ppermute x14, waiting for transfers between devices: 8.02 us -> 11.6 us  [send(): return tmap(lambda t: lax.ppermute(t, axis, perm=pairs), tree)]
    dot_general x1 -> x2, matrix products: 0.38 us -> 3.75 us  [the longest x1 3.38 us: local(): jnp.einsum('rtd,de->ret', frames, w_qkv[:, :width], preferred_element_typ...]
    dot_general x2 -> x1, matrix products: 7.03 us -> 3.78 us  [project(): jnp.einsum('rtd,de->ret', frames_in, w, preferred_element_type=jnp.float32)]
    dot_general x1, matrix products: 3.2 us -> 1.44 us  [block_terms(): jnp.einsum('rnhij,rnjhd->rnihd', weights, vv, preferred_element_type=jnp....]
    ppermute x14, starting transfers between devices: 29.7 us -> 28.2 us  [send(): return tmap(lambda t: lax.ppermute(t, axis, perm=pairs), tree)]
    another operation x2, local copies, waits for them, and re-layouts: 0.2 us -> 1.61 us  [finish(): before_kv = jnp.cumsum(kv_blocks, axis=1) - kv_blocks + prior_kv[:, None]]
    another operation x0 -> x1, local copies, waits for them, and re-layouts: none -> 1.24 us
    reduce_sum x1, other arithmetic: 1.26 us -> 0.23 us  [finish(): jnp.sum(pq32 * before_k[:, :, None], axis=-1)]
  transfers between devices with their start and end apart: 14 -> 14, of which waited for: 7 -> 10; matrix products, arithmetic and copies ran while one was open for 17% -> 15% of each run, Pallas kernels for 0% -> 0%
where the time goes in v22:
time: 64.1 us; the launch traced here: 63.8 us
  starting transfers between devices  28.2 us (44%)
  matrix products  15.5 us (24%)
  waiting for transfers between devices  11.6 us (18%)
  local copies, waits for them, and re-layouts  6.96 us (11%)
  other arithmetic  1.13 us (2%)
    ppermute x14, starting transfers between devices, send(): return tmap(lambda t: lax.ppermute(t, axis, perm=pairs), tree)  28.2 us
    ppermute x14, waiting for transfers between devices, send(): return tmap(lambda t: lax.ppermute(t, axis, perm=pairs), tree)  11.6 us
    dot_general x1, matrix products, project(): jnp.einsum('rtd,de->ret', frames_in, w, preferred_element_type=jnp.float32)  3.78 us
    dot_general x1, matrix products, local(): jnp.einsum('rtd,de->ret', frames, w_qkv[:, :width], preferred_element_typ...  3.38 us
    dot_general x1, matrix products, block_terms(): jnp.einsum('rnihd,rnjhd->rnhij', pq, pk, preferred_element_type=jnp.float32)  2.66 us
    dot_general x2, matrix products, finish(): jnp.einsum('rnihd,rnhde->rnihe', pq32, before_kv, precision=lax.Precision...  2.12 us
    dot_general x2, matrix products, heads_of(): jnp.einsum('rtd,de->rte', heads_out, rows_w, preferred_element_type=jnp.f...  1.74 us
    another operation x2, local copies, waits for them, and re-layouts, finish(): before_kv = jnp.cumsum(kv_blocks, axis=1) - kv_blocks + prior_kv[:, None]  1.61 us
  transfers between devices with their start and end apart: 14, of which 10 were waited for; matrix products, arithmetic and copies ran while one was open for 15% of the time, Pallas kernels for 0%

profile of v22, /device:TPU:1, one launch (start us, length us, event | category | flops | bytes accessed | tf_op | source)
XLA Modules:
  0.0 63.8 jit_solution(3133307023536082347)
XLA Ops:
  0.0 3.8 %fusion.2 = bf16[2048,256]{1,0:T(8,128)(2,1)S(1)} fusion(bf16[1024,3072]{1,0:T(8,128)(2,1)} %param.4, bf16[1,256,1024]{2,1,0:T(8,128)(2,1)} %param.3), kind=kOutput, calls=%fused_computation.5 | convolution fusion | flops 1074266112 | bytes 5767168 | tf_op jit(solution)/shard_map/rtd,de->ret/dot_general | solution.py:152
  3.8 0.4 fusion.39
  4.2 0.6 copy-done.4
  4.8 0.3 convert_reduce_fusion
  5.1 0.1 reshape_squeeze.2
  5.3 0.2 copy.12
  5.5 3.3 %collective-permute-start = (f32[8,33,128]{2,0,1:T(8,128)S(1)}, f32[8,33,128]{2,0,1:T(8,128)S(1)}, u32[]{:S(2)}, u32[]{:S(2)}) collective-permute-start(f32[8,33,128]{2,0,1:T(8,128)S(1)} %fusion.52), channel_id=1, source_target_pairs={{0,2},{2,0},{1,3},{3,1},{4,6},{6,4},{5,7},{7,5},{8,10},{10,8},{9,1... | collective-permute-start | bytes 405512 | tf_op jit(solution)/shard_map/ppermute | solution.py:22
  8.8 1.0 %collective-permute-done = f32[8,33,128]{2,0,1:T(8,128)S(1)} collective-permute-done((f32[8,33,128]{2,0,1:T(8,128)S(1)}, f32[8,33,128]{2,0,1:T(8,128)S(1)}, u32[]{:S(2)}, u32[]{:S(2)}) %collective-permute-start) | collective-permute-done | bytes 135200 | tf_op jit(solution)/shard_map/ppermute | solution.py:22
  9.8 1.1 %collective-permute-start.3 = (f32[2,33,128]{2,0,1:T(2,128)S(1)}, f32[2,33,128]{2,0,1:T(2,128)S(1)}, u32[]{:S(2)}, u32[]{:S(2)}) collective-permute-start(f32[2,33,128]{2,0,1:T(2,128)S(1)} %get-tuple-element.25), channel_id=1, source_target_pairs={{0,24},{8,0},{16,8},{24,16},{1,25},{9,1},{17,9},{25,17},{2,26},{10... | collective-permute-start | bytes 101384 | tf_op jit(solution)/shard_map/ppermute | solution.py:22
  10.9 0.4 collective-permute-start.2
  11.3 0.7 %collective-permute-start.1 = (f32[2,33,128]{2,0,1:T(2,128)S(1)}, f32[2,33,128]{2,0,1:T(2,128)S(1)}, u32[]{:S(2)}, u32[]{:S(2)}) collective-permute-start(f32[2,33,128]{2,0,1:T(2,128)S(1)} %get-tuple-element.24), channel_id=1, source_target_pairs={{0,8},{8,16},{16,24},{24,0},{1,9},{9,17},{17,25},{25,1},{2,10},{10... | collective-permute-start | bytes 101384 | tf_op jit(solution)/shard_map/ppermute | solution.py:22
  12.1 0.5 collective-permute-done.3
  12.7 2.6 %collective-permute-done.2 = f32[2,33,128]{2,0,1:T(2,128)S(1)} collective-permute-done((f32[2,33,128]{2,0,1:T(2,128)S(1)}, f32[2,33,128]{2,0,1:T(2,128)S(1)}, u32[]{:S(2)}, u32[]{:S(2)}) %collective-permute-start.2) | collective-permute-done | bytes 33824 | tf_op jit(solution)/shard_map/ppermute | solution.py:22
  15.2 0.3 collective-permute-done.1
  15.6 5.7 %collective-permute-start.5 = (f32[2,33,128]{2,0,1:T(2,128)S(1)}, f32[2,33,128]{2,0,1:T(2,128)S(1)}, u32[]{:S(2)}, u32[]{:S(2)}) collective-permute-start(f32[2,33,128]{2,0,1:T(2,128)S(1)} %add_add_fusion.1), channel_id=1, source_target_pairs={{0,224},{32,0},{64,32},{96,64},{128,96},{160,128},{192,160},{224,1... | collective-permute-start | bytes 101384 | tf_op jit(solution)/shard_map/ppermute | solution.py:22
  21.3 3.4 %fusion.33 = bf16[1024,256]{0,1:T(8,128)(2,1)} fusion(bf16[1024,3072]{1,0:T(8,128)(2,1)} %param.4, bf16[1,256,1024]{2,1,0:T(8,128)(2,1)} %param.3), kind=kOutput, calls=%fused_computation.40 | convolution fusion | flops 538705920 | bytes 3145728 | tf_op jit(solution)/shard_map/rtd,de->ret/dot_general | solution.py:168
  24.7 1.2 %copy.13 = bf16[1024,256]{1,0:T(8,128)(2,1)S(1)} copy(bf16[1024,256]{0,1:T(8,128)(2,1)} %fusion.33) | data formatting | bytes 1048576 | tf_op jit(solution)/shard_map/convert.3
  25.9 2.7 %select_reduce_fusion = (f32[16,256]{1,0:T(8,128)}, bf16[16,256,256]{1,2,0:T(8,128)(2,1)S(1)}) fusion(pred[256,256]{0,1:T(8,128)(4,1)S(1)} %iota_compare_fusion, bf16[256,16,64]{0,2,1:T(8,128)(2,1)S(1)} %bitcast.98, bf16[1,256,2,16,64]{1,4,3,2,0:T(8,128)(2,1)} %bitcast.108), kind=kOutput, calls=%fused_computation.3 | convolution fusion | flops 138932224 | bytes 3227648 | tf_op jit(solution)/shard_map/rnihd,rnjhd->rnhij/dot_general | solution.py:118
  28.6 0.1 select_add_fusion.6
  28.6 0.1 collective-permute-start.6
  28.7 3.5 %collective-permute-start.7 = (f32[2,33,128]{2,0,1:T(2,128)S(1)}, f32[2,33,128]{2,0,1:T(2,128)S(1)}, u32[]{:S(2)}, u32[]{:S(2)}) collective-permute-start(f32[2,33,128]{2,0,1:T(2,128)S(1)} %get-tuple-element.28), channel_id=1, source_target_pairs={{0,96},{32,128},{64,160},{96,192},{128,224},{160,0},{192,32},{224,... | collective-permute-start | bytes 101384 | tf_op jit(solution)/shard_map/ppermute | solution.py:22
  32.3 1.7 %collective-permute-start.8 = (f32[2,33,128]{2,0,1:T(2,128)S(1)}, f32[2,33,128]{2,0,1:T(2,128)S(1)}, u32[]{:S(2)}, u32[]{:S(2)}) collective-permute-start(f32[2,33,128]{2,0,1:T(2,128)S(1)} %get-tuple-element.27), channel_id=1, source_target_pairs={{0,192},{32,224},{64,0},{96,32},{128,64},{160,96},{192,128},{224,1... | collective-permute-start | bytes 101384 | tf_op jit(solution)/shard_map/ppermute | solution.py:22
  34.0 1.4 %fusion.10 = f32[1,1,256,16,64]{2,4,3,1,0:T(8,128)} fusion(bf16[16,256,256]{1,2,0:T(8,128)(2,1)S(1)} %get-tuple-element.35, pred[256,256]{0,1:T(8,128)(4,1)S(1)} %iota_compare_fusion, bf16[1,256,2,16,64]{1,4,3,2,0:T(8,128)(2,1)S(1)} %bitcast.109), kind=kOutput, calls=%fused_computation.17 | convolution fusion | flops 135266304 | bytes 3735552 | tf_op jit(solution)/shard_map/rnhij,rnjhd->rnihd/dot_general | solution.py:123
  35.5 0.8 %collective-permute-done.8 = f32[2,33,128]{2,0,1:T(2,128)S(1)} collective-permute-done((f32[2,33,128]{2,0,1:T(2,128)S(1)}, f32[2,33,128]{2,0,1:T(2,128)S(1)}, u32[]{:S(2)}, u32[]{:S(2)}) %collective-permute-start.8) | collective-permute-done | bytes 33824 | tf_op jit(solution)/shard_map/ppermute | solution.py:22
  36.3 0.1 add_bitcast_fusion
  36.5 0.8 %collective-permute-start.11 = (f32[2,33,128]{2,0,1:T(2,128)S(1)}, f32[2,33,128]{2,0,1:T(2,128)S(1)}, u32[]{:S(2)}, u32[]{:S(2)}) collective-permute-start(f32[2,33,128]{2,0,1:T(2,128)S(1)} %get-tuple-element.22), channel_id=1, source_target_pairs={{0,24},{8,0},{16,8},{24,16},{1,25},{9,1},{17,9},{25,17},{2,26},{10... | collective-permute-start | bytes 101384 | tf_op jit(solution)/shard_map/ppermute | solution.py:22
  37.3 1.0 %collective-permute-start.10 = (f32[2,33,128]{2,0,1:T(2,128)S(1)}, f32[2,33,128]{2,0,1:T(2,128)S(1)}, u32[]{:S(2)}, u32[]{:S(2)}) collective-permute-start(f32[2,33,128]{2,0,1:T(2,128)S(1)} %get-tuple-element.23), channel_id=1, source_target_pairs={{0,16},{8,24},{16,0},{24,8},{1,17},{9,25},{17,1},{25,9},{2,18},{10... | collective-permute-start | bytes 101384 | tf_op jit(solution)/shard_map/ppermute | solution.py:22
  38.3 0.1 select_add_fusion.5
  38.3 0.8 %collective-permute-start.9 = (f32[2,33,128]{2,0,1:T(2,128)S(1)}, f32[2,33,128]{2,0,1:T(2,128)S(1)}, u32[]{:S(2)}, u32[]{:S(2)}) collective-permute-start(f32[2,33,128]{2,0,1:T(2,128)S(1)} %select_add_fusion.5), channel_id=1, source_target_pairs={{0,8},{8,16},{16,24},{24,0},{1,9},{9,17},{17,25},{25,1},{2,10},{10... | collective-permute-start | bytes 101384 | tf_op jit(solution)/shard_map/ppermute | solution.py:22
  39.2 0.4 collective-permute-done.11
  39.6 2.0 %collective-permute-done.10 = f32[2,33,128]{2,0,1:T(2,128)S(1)} collective-permute-done((f32[2,33,128]{2,0,1:T(2,128)S(1)}, f32[2,33,128]{2,0,1:T(2,128)S(1)}, u32[]{:S(2)}, u32[]{:S(2)}) %collective-permute-start.10) | collective-permute-done | bytes 33824 | tf_op jit(solution)/shard_map/ppermute | solution.py:22
  41.6 0.8 %collective-permute-done.9 = f32[2,33,128]{2,0,1:T(2,128)S(1)} collective-permute-done((f32[2,33,128]{2,0,1:T(2,128)S(1)}, f32[2,33,128]{2,0,1:T(2,128)S(1)}, u32[]{:S(2)}, u32[]{:S(2)}) %collective-permute-start.9) | collective-permute-done | bytes 33824 | tf_op jit(solution)/shard_map/ppermute | solution.py:22
  42.4 0.1 pad_maximum_fusion
  42.4 0.7 %gather_fusion = f32[4,2,33,128]{3,1,2,0:T(2,128)S(1)} fusion(f32[4,2,33,128]{3,1,2,0:T(2,128)S(1)} %pad_maximum_fusion, s32[1024]{0:T(1024)S(1)} %pad_clamp_fusion), kind=kCustom, calls=%fused_computation | custom fusion | bytes 270352 | tf_op jit(solution)/shard_map/gather | solution.py:103
  43.2 2.8 %collective-permute-start.12 = (f32[8,33,128]{2,0,1:T(8,128)S(1)}, f32[8,33,128]{2,0,1:T(8,128)S(1)}, u32[]{:S(2)}, u32[]{:S(2)}) collective-permute-start(f32[8,33,128]{2,0,1:T(8,128)S(1)} %select_add_fusion.1), channel_id=1, source_target_pairs={{0,4},{4,0},{1,5},{5,1},{2,6},{6,2},{3,7},{7,3},{8,12},{12,8},{9,1... | collective-permute-start | bytes 405512 | tf_op jit(solution)/shard_map/ppermute | solution.py:22
  46.1 2.6 %collective-permute-done.12 = f32[8,33,128]{2,0,1:T(8,128)S(1)} collective-permute-done((f32[8,33,128]{2,0,1:T(8,128)S(1)}, f32[8,33,128]{2,0,1:T(8,128)S(1)}, u32[]{:S(2)}, u32[]{:S(2)}) %collective-permute-start.12) | collective-permute-done | bytes 135200 | tf_op jit(solution)/shard_map/ppermute | solution.py:22
  48.7 0.7 %copy.18 = f32[8,33,128]{2,1,0:T(8,128)} copy(f32[8,33,128]{2,0,1:T(8,128)S(1)} %get-tuple-element.20) | data formatting | bytes 270336 | tf_op jit(solution)/shard_map/add | solution.py:18
  49.4 6.3 %collective-permute-start.13 = (f32[8,33,128]{2,1,0:T(8,128)}, f32[8,33,128]{2,1,0:T(8,128)}, u32[]{:S(2)}, u32[]{:S(2)}) collective-permute-start(f32[8,33,128]{2,1,0:T(8,128)} %copy.18), channel_id=1, source_target_pairs={{0,2},{2,0},{1,3},{3,1},{4,6},{6,4},{5,7},{7,5},{8,10},{10,8},{9,1... | collective-permute-start | bytes 405512 | tf_op jit(solution)/shard_map/ppermute | solution.py:22
  55.8 0.8 %broadcast_in_dim_broadcast_in_dim_reshape.6 = f32[8,64,64]{2,1,0:T(8,128)} reshape(f32[8,32,128]{2,1,0:T(8,128)S(1)} %copy.16) | data formatting | bytes 262144 | tf_op jit(solution)/shard_map/broadcast_in_dim;broadcast_in_dim;reshape | solution.py:131
  56.6 0.5 collective-permute-done.13
  57.1 0.8 %slice.39 = f32[8,1,64]{2,1,0:T(1,128)S(1)} slice(f32[8,33,128]{2,1,0:T(8,128)} %collective-permute-done.13), slice={[0:8], [32:33], [0:64]} | slice | bytes 4096 | tf_op jit(solution)/shard_map/slice | solution.py:191
  57.9 0.9 %slice.38 = f32[8,32,128]{2,1,0:T(8,128)S(1)} slice(f32[8,33,128]{2,1,0:T(8,128)} %collective-permute-done.13), slice={[0:8], [0:32], [0:128]} | slice | bytes 262144 | tf_op jit(solution)/shard_map/slice | solution.py:190
  58.8 0.8 %broadcast_in_dim_broadcast_in_dim_reshape.7 = f32[8,64,64]{2,1,0:T(8,128)} reshape(f32[8,32,128]{2,1,0:T(8,128)S(1)} %slice.38) | data formatting | bytes 262144 | tf_op jit(solution)/shard_map/broadcast_in_dim;broadcast_in_dim;reshape | solution.py:131
  59.6 0.2 multiply_reduce_fusion
  59.9 1.7 %fusion.21 = bf16[1,1,256,8,64]{2,4,3,1,0:T(8,128)(2,1)S(1)} fusion(f32[1,1,256,16,64]{2,4,3,1,0:T(8,128)} %fusion.10, s32[]{:T(128)S(6)} %select_n.352, f32[256,8]{0,1:T(8,128)S(1)} %get-tuple-element.31, f32[8,64,64]{2,1,0:T(8,128)} %broadcast_in_dim_broadcast_in_dim_reshape.6, f32[16,64,64]{2,1,0:T(8,128)S(1)} %copy-done.2, ...), kind=kOutput, calls=%fused_computation.29 | convolution fusion | flops 101122048 | bytes 1451520 | tf_op jit(solution)/shard_map/rnihd,rnhde->rnihe/dot_general | solution.py:134
  61.6 0.5 fusion.20
  62.0 0.5 fusion.29
  62.5 1.3 %fusion.15 = bf16[1,256,1024]{2,1,0:T(8,128)(2,1)} fusion(f32[256,1024]{1,0:T(8,128)S(1)} %fusion.29, bf16[256,512]{0,1:T(8,128)(2,1)S(1)} %bitcast.105, bf16[1024,1024]{1,0:T(8,128)(2,1)S(1)} %copy-done, s32[]{:T(128)S(6)} %select_n.426), kind=kOutput, calls=%fused_computation.21 | convolution fusion | flops 268959744 | bytes 2883588 | tf_op jit(solution)/shard_map/rtd,de->rte/dot_general | solution.py:197
  (36 shorter events, 0.4 us)
Async XLA Ops:
  0.0 62.0 %copy-start = (bf16[1024,1024]{1,0:T(8,128)(2,1)S(1)}, bf16[1024,1024]{1,0:T(8,128)(2,1)}, u32[]{:S(2)}) copy-start(bf16[1024,1024]{1,0:T(8,128)(2,1)} %param.5) | copy-start | bytes 6291460
  3.8 1.0 %copy-start.4 = (bf16[2048,256]{1,0:T(8,128)(2,1)}, bf16[2048,256]{1,0:T(8,128)(2,1)S(1)}, u32[]{:S(2)}) copy-start(bf16[2048,256]{1,0:T(8,128)(2,1)S(1)} %fusion.2) | copy-start | bytes 3145732
  4.8 4.0 %copy-start.1 = (f32[16,64,64]{2,1,0:T(8,128)}, f32[16,64,64]{2,1,0:T(8,128)S(1)}, u32[]{:S(2)}) copy-start(f32[16,64,64]{2,1,0:T(8,128)S(1)} %fusion.39) | copy-start | bytes 786436
  5.5 4.3 %collective-permute-start = (f32[8,33,128]{2,0,1:T(8,128)S(1)}, f32[8,33,128]{2,0,1:T(8,128)S(1)}, u32[]{:S(2)}, u32[]{:S(2)}) collective-permute-start(f32[8,33,128]{2,0,1:T(8,128)S(1)} %fusion.52), channel_id=1, source_target_pairs={{0,2},{2,0},{1,3},{3,1},{4,6},{6,4},{5,7},{7,5},{8,10},{10,8},{9,1... | collective-permute-start | bytes 405512 | tf_op jit(solution)/shard_map/ppermute | solution.py:22
  9.8 2.9 %collective-permute-start.3 = (f32[2,33,128]{2,0,1:T(2,128)S(1)}, f32[2,33,128]{2,0,1:T(2,128)S(1)}, u32[]{:S(2)}, u32[]{:S(2)}) collective-permute-start(f32[2,33,128]{2,0,1:T(2,128)S(1)} %get-tuple-element.25), channel_id=1, source_target_pairs={{0,24},{8,0},{16,8},{24,16},{1,25},{9,1},{17,9},{25,17},{2,26},{10... | collective-permute-start | bytes 101384 | tf_op jit(solution)/shard_map/ppermute | solution.py:22
  10.9 4.3 %collective-permute-start.2 = (f32[2,33,128]{2,0,1:T(2,128)S(1)}, f32[2,33,128]{2,0,1:T(2,128)S(1)}, u32[]{:S(2)}, u32[]{:S(2)}) collective-permute-start(f32[2,33,128]{2,0,1:T(2,128)S(1)} %get-tuple-element.26), channel_id=1, source_target_pairs={{0,16},{8,24},{16,0},{24,8},{1,17},{9,25},{17,1},{25,9},{2,18},{10... | collective-permute-start | bytes 101384 | tf_op jit(solution)/shard_map/ppermute | solution.py:22
  11.3 4.3 %collective-permute-start.1 = (f32[2,33,128]{2,0,1:T(2,128)S(1)}, f32[2,33,128]{2,0,1:T(2,128)S(1)}, u32[]{:S(2)}, u32[]{:S(2)}) collective-permute-start(f32[2,33,128]{2,0,1:T(2,128)S(1)} %get-tuple-element.24), channel_id=1, source_target_pairs={{0,8},{8,16},{16,24},{24,0},{1,9},{9,17},{17,25},{25,1},{2,10},{10... | collective-permute-start | bytes 101384 | tf_op jit(solution)/shard_map/ppermute | solution.py:22
  15.6 13.0 %collective-permute-start.5 = (f32[2,33,128]{2,0,1:T(2,128)S(1)}, f32[2,33,128]{2,0,1:T(2,128)S(1)}, u32[]{:S(2)}, u32[]{:S(2)}) collective-permute-start(f32[2,33,128]{2,0,1:T(2,128)S(1)} %add_add_fusion.1), channel_id=1, source_target_pairs={{0,224},{32,0},{64,32},{96,64},{128,96},{160,128},{192,160},{224,1... | collective-permute-start | bytes 101384 | tf_op jit(solution)/shard_map/ppermute | solution.py:22
  21.3 7.3 %collective-permute-start.4 = (f32[2,33,128]{2,0,1:T(2,128)S(1)}, f32[2,33,128]{2,0,1:T(2,128)S(1)}, u32[]{:S(2)}, u32[]{:S(2)}) collective-permute-start(f32[2,33,128]{2,0,1:T(2,128)S(1)} %add_add_fusion.1), channel_id=1, source_target_pairs={{0,32},{32,64},{64,96},{96,128},{128,160},{160,192},{192,224},{224... | collective-permute-start | bytes 101384 | tf_op jit(solution)/shard_map/ppermute | solution.py:22
  25.9 8.1 %copy-start.5 = (bf16[2048,256]{1,0:T(8,128)(2,1)S(1)}, bf16[2048,256]{1,0:T(8,128)(2,1)}, u32[]{:S(2)}) copy-start(bf16[2048,256]{1,0:T(8,128)(2,1)} %copy-done.4) | copy-start | bytes 3145732
  28.6 6.8 %collective-permute-start.6 = (f32[2,33,128]{2,0,1:T(2,128)S(1)}, f32[2,33,128]{2,0,1:T(2,128)S(1)}, u32[]{:S(2)}, u32[]{:S(2)}) collective-permute-start(f32[2,33,128]{2,0,1:T(2,128)S(1)} %get-tuple-element.29), channel_id=1, source_target_pairs={{0,64},{32,96},{64,128},{96,160},{128,192},{160,224},{192,0},{224,... | collective-permute-start | bytes 101384 | tf_op jit(solution)/shard_map/ppermute | solution.py:22
  28.7 6.7 %collective-permute-start.7 = (f32[2,33,128]{2,0,1:T(2,128)S(1)}, f32[2,33,128]{2,0,1:T(2,128)S(1)}, u32[]{:S(2)}, u32[]{:S(2)}) collective-permute-start(f32[2,33,128]{2,0,1:T(2,128)S(1)} %get-tuple-element.28), channel_id=1, source_target_pairs={{0,96},{32,128},{64,160},{96,192},{128,224},{160,0},{192,32},{224,... | collective-permute-start | bytes 101384 | tf_op jit(solution)/shard_map/ppermute | solution.py:22
  32.3 4.0 %collective-permute-start.8 = (f32[2,33,128]{2,0,1:T(2,128)S(1)}, f32[2,33,128]{2,0,1:T(2,128)S(1)}, u32[]{:S(2)}, u32[]{:S(2)}) collective-permute-start(f32[2,33,128]{2,0,1:T(2,128)S(1)} %get-tuple-element.27), channel_id=1, source_target_pairs={{0,192},{32,224},{64,0},{96,32},{128,64},{160,96},{192,128},{224,1... | collective-permute-start | bytes 101384 | tf_op jit(solution)/shard_map/ppermute | solution.py:22
  36.5 3.1 %collective-permute-start.11 = (f32[2,33,128]{2,0,1:T(2,128)S(1)}, f32[2,33,128]{2,0,1:T(2,128)S(1)}, u32[]{:S(2)}, u32[]{:S(2)}) collective-permute-start(f32[2,33,128]{2,0,1:T(2,128)S(1)} %get-tuple-element.22), channel_id=1, source_target_pairs={{0,24},{8,0},{16,8},{24,16},{1,25},{9,1},{17,9},{25,17},{2,26},{10... | collective-permute-start | bytes 101384 | tf_op jit(solution)/shard_map/ppermute | solution.py:22
  37.3 4.3 %collective-permute-start.10 = (f32[2,33,128]{2,0,1:T(2,128)S(1)}, f32[2,33,128]{2,0,1:T(2,128)S(1)}, u32[]{:S(2)}, u32[]{:S(2)}) collective-permute-start(f32[2,33,128]{2,0,1:T(2,128)S(1)} %get-tuple-element.23), channel_id=1, source_target_pairs={{0,16},{8,24},{16,0},{24,8},{1,17},{9,25},{17,1},{25,9},{2,18},{10... | collective-permute-start | bytes 101384 | tf_op jit(solution)/shard_map/ppermute | solution.py:22
  38.3 4.1 %collective-permute-start.9 = (f32[2,33,128]{2,0,1:T(2,128)S(1)}, f32[2,33,128]{2,0,1:T(2,128)S(1)}, u32[]{:S(2)}, u32[]{:S(2)}) collective-permute-start(f32[2,33,128]{2,0,1:T(2,128)S(1)} %select_add_fusion.5), channel_id=1, source_target_pairs={{0,8},{8,16},{16,24},{24,0},{1,9},{9,17},{17,25},{25,1},{2,10},{10... | collective-permute-start | bytes 101384 | tf_op jit(solution)/shard_map/ppermute | solution.py:22
  43.1 16.7 %copy-start.6 = (f32[16,256]{1,0:T(8,128)S(1)}, f32[16,256]{1,0:T(8,128)}, u32[]{:S(2)}) copy-start(f32[16,256]{1,0:T(8,128)} %get-tuple-element.34) | copy-start | bytes 49156
  43.2 5.5 %collective-permute-start.12 = (f32[8,33,128]{2,0,1:T(8,128)S(1)}, f32[8,33,128]{2,0,1:T(8,128)S(1)}, u32[]{:S(2)}, u32[]{:S(2)}) collective-permute-start(f32[8,33,128]{2,0,1:T(8,128)S(1)} %select_add_fusion.1), channel_id=1, source_target_pairs={{0,4},{4,0},{1,5},{5,1},{2,6},{6,2},{3,7},{7,3},{8,12},{12,8},{9,1... | collective-permute-start | bytes 405512 | tf_op jit(solution)/shard_map/ppermute | solution.py:22
  48.7 11.1 %copy-start.2 = (f32[16,64,64]{2,1,0:T(8,128)S(1)}, f32[16,64,64]{2,1,0:T(8,128)}, u32[]{:S(2)}) copy-start(f32[16,64,64]{2,1,0:T(8,128)} %copy-done.1) | copy-start | bytes 786436
  49.4 7.6 %collective-permute-start.13 = (f32[8,33,128]{2,1,0:T(8,128)}, f32[8,33,128]{2,1,0:T(8,128)}, u32[]{:S(2)}, u32[]{:S(2)}) collective-permute-start(f32[8,33,128]{2,1,0:T(8,128)} %copy.18), channel_id=1, source_target_pairs={{0,2},{2,0},{1,3},{3,1},{4,6},{6,4},{5,7},{7,5},{8,10},{10,8},{9,1... | collective-permute-start | bytes 405512 | tf_op jit(solution)/shard_map/ppermute | solution.py:22
  59.6 2.0 %copy-start.3 = (f32[8,64,64]{2,1,0:T(8,128)S(1)}, f32[8,64,64]{2,1,0:T(8,128)}, u32[]{:S(2)}) copy-start(f32[8,64,64]{2,1,0:T(8,128)} %broadcast_in_dim_broadcast_in_dim_reshape.7) | copy-start | bytes 393220
  59.6 2.0 %copy-start.7 = (f32[1,1,256,16,64]{2,4,3,1,0:T(8,128)S(1)}, f32[1,1,256,16,64]{2,4,3,1,0:T(8,128)}, u32[]{:S(2)}) copy-start(f32[1,1,256,16,64]{2,4,3,1,0:T(8,128)} %fusion.10) | copy-start | bytes 3145732

commit v23 on v19

--- a/solution.py
+++ b/solution.py
@@ -85,7 +85,6 @@
     back = add(keep(column, to(-2) + 2 >= n_z), keep(right, to(-2) + 3 >= n_z))
     back = send(back, "seg_z", cyclic(n_z, -2))
     before_z = add(before_z, add(two, add(three, back)))
-    before_z, carry = lax.optimization_barrier((before_z, carry))
 
     def for_row(t):
         out = before_z
@@ -101,6 +100,7 @@
         lambda *p: jnp.stack(p)[order].reshape((-1,) + p[0].shape[1:]),
         *pieces,
     )
+    mine, carry = lax.optimization_barrier((mine, carry))
     half = add(mine, swap(add(mine, keep(chip, xh == 0)), "seg_x"))
     got = swap(add(half, keep(own_c, core == 0)), "frm")
     own = tmap(lambda a, c: jnp.where(core == 0, a, a + c), half, got_c)

time: 63.3 us -> 67.7 us (1.070)
  waiting for transfers between devices: 8.02 us -> 15 us
  starting transfers between devices: 29.7 us -> 25.7 us
  other arithmetic: 2.81 us -> 4.44 us
  local copies, waits for them, and re-layouts: 3.48 us -> 2.64 us
    ppermute x14, waiting for transfers between devices: 8.02 us -> 15 us  [send(): return tmap(lambda t: lax.ppermute(t, axis, perm=pairs), tree)]
    ppermute x14, starting transfers between devices: 29.7 us -> 25.7 us  [send(): return tmap(lambda t: lax.ppermute(t, axis, perm=pairs), tree)]
    another operation x2, other arithmetic: 0.19 us -> 1.71 us  [entering(): jnp.stack(p)[order].reshape((-1,) + p[0].shape[1:])]
    slice x1, local copies, waits for them, and re-layouts: 0.85 us -> 0.01 us  [heads_of(): prior_k = prior[:, rows_kv, :total_k.shape[1]]]
  transfers between devices with their start and end apart: 14 -> 14, of which waited for: 7 -> 8; matrix products, arithmetic and copies ran while one was open for 17% -> 17% of each run, Pallas kernels for 0% -> 0%
where the time goes in v23:
time: 67.7 us; the launch traced here: 67.4 us
  starting transfers between devices  25.7 us (38%)
  matrix products  19.3 us (29%)
  waiting for transfers between devices  15 us (22%)
  other arithmetic  4.44 us (7%)
  local copies, waits for them, and re-layouts  2.64 us (4%)
    ppermute x14, starting transfers between devices, send(): return tmap(lambda t: lax.ppermute(t, axis, perm=pairs), tree)  25.7 us
    ppermute x14, waiting for transfers between devices, send(): return tmap(lambda t: lax.ppermute(t, axis, perm=pairs), tree)  15 us
    dot_general x2, matrix products, project(): jnp.einsum('rtd,de->ret', frames_in, w, preferred_element_type=jnp.float32)  7.03 us
    dot_general x1, matrix products, block_terms(): jnp.einsum('rnihd,rnjhd->rnhij', pq, pk, preferred_element_type=jnp.float32)  4.06 us
    dot_general x1, matrix products, block_terms(): jnp.einsum('rnhij,rnjhd->rnihd', weights, vv, preferred_element_type=jnp....  3.19 us
    dot_general x2, matrix products, finish(): jnp.einsum('rnihd,rnhde->rnihe', pq32, before_kv, precision=lax.Precision...  2.94 us
    dot_general x2, matrix products, heads_of(): jnp.einsum('rtd,de->rte', heads_out, rows_w, preferred_element_type=jnp.f...  1.72 us
    another operation x2, other arithmetic, entering(): jnp.stack(p)[order].reshape((-1,) + p[0].shape[1:])  1.71 us
  transfers between devices with their start and end apart: 14, of which 8 were waited for; matrix products, arithmetic and copies ran while one was open for 17% of the time, Pallas kernels for 0%

profile of v23, /device:TPU:1, one launch (start us, length us, event | category | flops | bytes accessed | tf_op | source)
XLA Modules:
  0.0 67.4 jit_solution(6748492696178035924)
XLA Ops:
  0.0 3.8 %fusion.2 = bf16[2048,256]{1,0:T(8,128)(2,1)S(1)} fusion(bf16[1024,3072]{1,0:T(8,128)(2,1)} %param.4, bf16[1,256,1024]{2,1,0:T(8,128)(2,1)} %param.3), kind=kOutput, calls=%fused_computation.5 | convolution fusion | flops 1074266112 | bytes 5767168 | tf_op jit(solution)/shard_map/rtd,de->ret/dot_general | solution.py:150
  3.8 0.3 convert_reduce_fusion
  4.1 0.7 copy-done.1
  4.8 0.4 fusion.37
  5.2 0.1 reshape_squeeze.4
  5.3 0.2 copy.4
  5.5 3.3 %collective-permute-start = (f32[8,33,128]{2,0,1:T(8,128)S(1)}, f32[8,33,128]{2,0,1:T(8,128)S(1)}, u32[]{:S(2)}, u32[]{:S(2)}) collective-permute-start(f32[8,33,128]{2,0,1:T(8,128)S(1)} %fusion.51), channel_id=1, source_target_pairs={{0,2},{2,0},{1,3},{3,1},{4,6},{6,4},{5,7},{7,5},{8,10},{10,8},{9,1... | collective-permute-start | bytes 405512 | tf_op jit(solution)/shard_map/ppermute | solution.py:22
  8.8 3.3 %fusion.26 = bf16[1024,256]{1,0:T(8,128)(2,1)} fusion(bf16[1024,3072]{1,0:T(8,128)(2,1)} %param.4, bf16[1,256,1024]{2,1,0:T(8,128)(2,1)} %param.3), kind=kOutput, calls=%fused_computation.34 | convolution fusion | flops 538705920 | bytes 3145728 | tf_op jit(solution)/shard_map/rtd,de->ret/dot_general | solution.py:150
  12.1 0.0 collective-permute-done
  12.2 0.1 collective-permute-start.1
  12.3 2.7 %collective-permute-start.3 = (f32[2,33,128]{2,0,1:T(2,128)S(1)}, f32[2,33,128]{2,0,1:T(2,128)S(1)}, u32[]{:S(2)}, u32[]{:S(2)}) collective-permute-start(f32[2,33,128]{2,0,1:T(2,128)S(1)} %get-tuple-element.23), channel_id=1, source_target_pairs={{0,24},{8,0},{16,8},{24,16},{1,25},{9,1},{17,9},{25,17},{2,26},{10... | collective-permute-start | bytes 101384 | tf_op jit(solution)/shard_map/ppermute | solution.py:22
  15.0 0.0 collective-permute-start.2
  15.0 4.1 %select_reduce_fusion = (f32[16,256]{1,0:T(8,128)}, bf16[16,256,256]{1,2,0:T(8,128)(2,1)}) fusion(pred[256,256]{0,1:T(8,128)(4,1)S(1)} %iota_compare_fusion, bf16[256,16,64]{0,2,1:T(8,128)(2,1)} %bitcast.107, bf16[1,256,2,16,64]{1,4,3,2,0:T(8,128)(2,1)} %bitcast.115), kind=kOutput, calls=%fused_computation.3 | convolution fusion | flops 138932224 | bytes 3227648 | tf_op jit(solution)/shard_map/rnihd,rnjhd->rnhij/dot_general | solution.py:116
  19.0 0.0 collective-permute-done.1
  19.0 0.0 collective-permute-done.3
  19.0 0.2 collective-permute-done.2
  19.3 5.4 %collective-permute-start.5 = (f32[2,33,128]{2,0,1:T(2,128)S(1)}, f32[2,33,128]{2,0,1:T(2,128)S(1)}, u32[]{:S(2)}, u32[]{:S(2)}) collective-permute-start(f32[2,33,128]{2,0,1:T(2,128)S(1)} %get-tuple-element.16), channel_id=1, source_target_pairs={{0,224},{32,0},{64,32},{96,64},{128,96},{160,128},{192,160},{224,1... | collective-permute-start | bytes 101384 | tf_op jit(solution)/shard_map/ppermute | solution.py:22
  24.7 0.0 collective-permute-start.4
  24.7 3.2 %fusion.10 = f32[1,1,256,16,64]{2,4,3,1,0:T(8,128)} fusion(bf16[16,256,256]{1,2,0:T(8,128)(2,1)} %get-tuple-element.32, pred[256,256]{0,1:T(8,128)(4,1)S(1)} %iota_compare_fusion, bf16[1,256,2,16,64]{1,4,3,2,0:T(8,128)(2,1)} %bitcast.116), kind=kOutput, calls=%fused_computation.17 | convolution fusion | flops 135266304 | bytes 3735552 | tf_op jit(solution)/shard_map/rnhij,rnjhd->rnihd/dot_general | solution.py:121
  27.9 0.8 %collective-permute-done.4 = f32[2,33,128]{2,0,1:T(2,128)S(1)} collective-permute-done((f32[2,33,128]{2,0,1:T(2,128)S(1)}, f32[2,33,128]{2,0,1:T(2,128)S(1)}, u32[]{:S(2)}, u32[]{:S(2)}) %collective-permute-start.4) | collective-permute-done | bytes 33824 | tf_op jit(solution)/shard_map/ppermute | solution.py:22
  28.7 0.7 select_add_fusion.6
  29.4 2.8 %collective-permute-start.8 = (f32[2,33,128]{2,0,1:T(2,128)}, f32[2,33,128]{2,0,1:T(2,128)}, u32[]{:S(2)}, u32[]{:S(2)}) collective-permute-start(f32[2,33,128]{2,0,1:T(2,128)} %get-tuple-element.25), channel_id=1, source_target_pairs={{0,192},{32,224},{64,0},{96,32},{128,64},{160,96},{192,128},{224,1... | collective-permute-start | bytes 101384 | tf_op jit(solution)/shard_map/ppermute | solution.py:22
  32.2 0.5 collective-permute-start.7
  32.8 0.0 collective-permute-done.6
  32.8 1.0 %collective-permute-done.8 = f32[2,33,128]{2,0,1:T(2,128)} collective-permute-done((f32[2,33,128]{2,0,1:T(2,128)}, f32[2,33,128]{2,0,1:T(2,128)}, u32[]{:S(2)}, u32[]{:S(2)}) %collective-permute-start.8) | collective-permute-done | bytes 33824 | tf_op jit(solution)/shard_map/ppermute | solution.py:22
  33.8 5.3 %collective-permute-done.7 = f32[2,33,128]{2,0,1:T(2,128)} collective-permute-done((f32[2,33,128]{2,0,1:T(2,128)}, f32[2,33,128]{2,0,1:T(2,128)}, u32[]{:S(2)}, u32[]{:S(2)}) %collective-permute-start.7) | collective-permute-done | bytes 33824 | tf_op jit(solution)/shard_map/ppermute | solution.py:22
  39.1 0.9 %add_bitcast_fusion = (f32[1,2,33,128]{3,1,2,0:T(2,128)S(1)}, f32[2,33,128]{2,0,1:T(2,128)S(1)}) fusion(f32[2,33,128]{2,0,1:T(2,128)S(1)} %collective-permute-done.3, f32[2,33,128]{2,0,1:T(2,128)S(1)} %collective-permute-done.2, f32[2,33,128]{2,0,1:T(2,128)S(1)} %collective-permute-done.1, pred[]{:T(512)S(6)} %lt.193, pred[]{:T(512)S(6)} %lt.191, ...), kind=kLoop, calls=%fused_computation.76 | loop fusion | flops 118272 | bytes 371722 | tf_op jit(solution)/shard_map/stack | solution.py:100
  40.0 0.1 select_add_fusion.5
  40.1 0.7 collective-permute-start.9
  40.8 2.3 %collective-permute-start.11 = (f32[2,33,128]{2,0,1:T(2,128)S(1)}, f32[2,33,128]{2,0,1:T(2,128)}, u32[]{:S(2)}, u32[]{:S(2)}) collective-permute-start(f32[2,33,128]{2,0,1:T(2,128)S(1)} %get-tuple-element.20), channel_id=1, source_target_pairs={{0,24},{8,0},{16,8},{24,16},{1,25},{9,1},{17,9},{25,17},{2,26},{10... | collective-permute-start | bytes 101384 | tf_op jit(solution)/shard_map/ppermute | solution.py:22
  43.0 0.1 collective-permute-start.10
  43.1 1.2 %collective-permute-done.9 = f32[2,33,128]{2,0,1:T(2,128)S(1)} collective-permute-done((f32[2,33,128]{2,0,1:T(2,128)S(1)}, f32[2,33,128]{2,0,1:T(2,128)S(1)}, u32[]{:S(2)}, u32[]{:S(2)}) %collective-permute-start.9) | collective-permute-done | bytes 33824 | tf_op jit(solution)/shard_map/ppermute | solution.py:22
  44.3 0.0 collective-permute-done.11
  44.3 3.0 %collective-permute-done.10 = f32[2,33,128]{2,0,1:T(2,128)S(1)} collective-permute-done((f32[2,33,128]{2,0,1:T(2,128)S(1)}, f32[2,33,128]{2,0,1:T(2,128)S(1)}, u32[]{:S(2)}, u32[]{:S(2)}) %collective-permute-start.10) | collective-permute-done | bytes 33824 | tf_op jit(solution)/shard_map/ppermute | solution.py:22
  47.3 0.6 copy-done.2
  47.9 0.8 %pad_maximum_fusion = f32[4,2,33,128]{3,1,2,0:T(2,128)S(1)} fusion(f32[1,2,33,128]{3,1,2,0:T(2,128)} %bitcast.10, f32[1,2,33,128]{3,1,2,0:T(2,128)} %bitcast.118, f32[1,2,33,128]{3,1,2,0:T(2,128)S(1)} %bitcast.117, f32[1,2,33,128]{3,1,2,0:T(2,128)S(1)} %get-tuple-element.13), kind=kLoop, calls=%fused_computation.69 | loop fusion | flops 101376 | bytes 270336 | tf_op jit(solution)/shard_map/stack | solution.py:100
  48.8 0.7 %gather_fusion = f32[4,2,33,128]{3,1,2,0:T(2,128)S(1)} fusion(f32[4,2,33,128]{3,1,2,0:T(2,128)S(1)} %pad_maximum_fusion, s32[1024]{0:T(1024)S(1)} %pad_clamp_fusion), kind=kCustom, calls=%fused_computation | custom fusion | bytes 270352 | tf_op jit(solution)/shard_map/gather | solution.py:100
  49.5 2.8 %collective-permute-start.12 = (f32[8,33,128]{2,0,1:T(8,128)S(1)}, f32[8,33,128]{2,0,1:T(8,128)S(1)}, u32[]{:S(2)}, u32[]{:S(2)}) collective-permute-start(f32[8,33,128]{2,0,1:T(8,128)S(1)} %select_add_fusion.1), channel_id=1, source_target_pairs={{0,4},{4,0},{1,5},{5,1},{2,6},{6,2},{3,7},{7,3},{8,12},{12,8},{9,1... | collective-permute-start | bytes 405512 | tf_op jit(solution)/shard_map/ppermute | solution.py:22
  52.4 2.6 %collective-permute-done.12 = f32[8,33,128]{2,0,1:T(8,128)S(1)} collective-permute-done((f32[8,33,128]{2,0,1:T(8,128)S(1)}, f32[8,33,128]{2,0,1:T(8,128)S(1)}, u32[]{:S(2)}, u32[]{:S(2)}) %collective-permute-start.12) | collective-permute-done | bytes 135200 | tf_op jit(solution)/shard_map/ppermute | solution.py:22
  55.1 5.0 %collective-permute-start.13 = (f32[8,33,128]{2,1,0:T(8,128)S(1)}, f32[8,33,128]{2,1,0:T(8,128)S(1)}, u32[]{:S(2)}, u32[]{:S(2)}) collective-permute-start(f32[8,33,128]{2,1,0:T(8,128)S(1)} %copy.9), channel_id=1, source_target_pairs={{0,2},{2,0},{1,3},{3,1},{4,6},{6,4},{5,7},{7,5},{8,10},{10,8},{9,1... | collective-permute-start | bytes 405512 | tf_op jit(solution)/shard_map/ppermute | solution.py:22
  60.1 0.1 broadcast_in_dim_broadcast_in_dim_reshape.6
  60.2 0.9 %collective-permute-done.13 = f32[8,33,128]{2,1,0:T(8,128)S(1)} collective-permute-done((f32[8,33,128]{2,1,0:T(8,128)S(1)}, f32[8,33,128]{2,1,0:T(8,128)S(1)}, u32[]{:S(2)}, u32[]{:S(2)}) %collective-permute-start.13) | collective-permute-done | bytes 135200 | tf_op jit(solution)/shard_map/ppermute | solution.py:22
  61.2 0.1 broadcast_in_dim_broadcast_in_dim_reshape.7
  61.3 1.4 %fusion.33 = (f32[256,8]{0,1:T(8,128)S(1)}, f32[256,8]{0,1:T(8,128)S(1)}) fusion(f32[8,64]{1,0:T(8,128)S(1)} %get-tuple-element.30, bf16[1,1,16,64,256]{4,3,2,1,0:T(8,128)(2,1)} %bitcast.108, s32[]{:T(128)S(6)} %select_n.351, f32[8,64]{1,0:T(8,128)S(1)} %get-tuple-element.29, s32[]{:T(128)S(6)} %select_n.350), kind=kLoop, calls=%fused_computation.42 | loop fusion | flops 782336 | bytes 544776 | tf_op jit(solution)/shard_map/reduce_sum | solution.py:135
  62.7 1.6 %fusion.21 = bf16[1,1,256,8,64]{2,4,3,1,0:T(8,128)(2,1)S(1)} fusion(f32[1,1,256,16,64]{2,4,3,1,0:T(8,128)} %fusion.10, s32[]{:T(128)S(6)} %select_n.350, f32[256,8]{0,1:T(8,128)S(1)} %get-tuple-element.28, f32[8,64,64]{2,1,0:T(8,128)S(1)} %broadcast_in_dim_broadcast_in_dim_reshape.6, f32[16,64,64]{2,1,0:T(8,128)S(1)} %fusion.37, ...), kind=kOutput, calls=%fused_computation.29 | convolution fusion | flops 101122048 | bytes 1582592 | tf_op jit(solution)/shard_map/rnihd,rnhde->rnihe/dot_general | solution.py:132
  64.2 1.4 %fusion.20 = bf16[1,1,256,8,64]{2,4,3,1,0:T(8,128)(2,1)S(1)} fusion(f32[1,1,256,16,64]{2,4,3,1,0:T(8,128)S(1)} %copy-done.4, s32[]{:T(128)S(6)} %select_n.351, f32[256,8]{0,1:T(8,128)S(1)} %get-tuple-element.27, f32[8,64,64]{2,1,0:T(8,128)S(1)} %broadcast_in_dim_broadcast_in_dim_reshape.7, f32[16,64,64]{2,1,0:T(8,128)S(1)} %fusion.37, ...), kind=kOutput, calls=%fused_computation.28 | convolution fusion | flops 101122048 | bytes 1582592 | tf_op jit(solution)/shard_map/rnihd,rnhde->rnihe/dot_general | solution.py:132
  65.6 0.5 fusion.29
  66.1 1.3 %fusion.15 = bf16[1,256,1024]{2,1,0:T(8,128)(2,1)} fusion(f32[256,1024]{1,0:T(8,128)S(1)} %fusion.29, bf16[256,512]{0,1:T(8,128)(2,1)S(1)} %bitcast.112, bf16[1024,1024]{1,0:T(8,128)(2,1)S(1)} %copy-done, s32[]{:T(128)S(6)} %select_n.423), kind=kOutput, calls=%fused_computation.21 | convolution fusion | flops 268959744 | bytes 2883588 | tf_op jit(solution)/shard_map/rtd,de->rte/dot_general | solution.py:182
  (28 shorter events, 0.4 us)
Async XLA Ops:
  0.0 65.6 %copy-start = (bf16[1024,1024]{1,0:T(8,128)(2,1)S(1)}, bf16[1024,1024]{1,0:T(8,128)(2,1)}, u32[]{:S(2)}) copy-start(bf16[1024,1024]{1,0:T(8,128)(2,1)} %param.5) | copy-start | bytes 6291460
  3.8 1.0 %copy-start.1 = (bf16[2048,256]{1,0:T(8,128)(2,1)}, bf16[2048,256]{1,0:T(8,128)(2,1)S(1)}, u32[]{:S(2)}) copy-start(bf16[2048,256]{1,0:T(8,128)(2,1)S(1)} %fusion.2) | copy-start | bytes 3145732
  5.5 6.6 %collective-permute-start = (f32[8,33,128]{2,0,1:T(8,128)S(1)}, f32[8,33,128]{2,0,1:T(8,128)S(1)}, u32[]{:S(2)}, u32[]{:S(2)}) collective-permute-start(f32[8,33,128]{2,0,1:T(8,128)S(1)} %fusion.51), channel_id=1, source_target_pairs={{0,2},{2,0},{1,3},{3,1},{4,6},{6,4},{5,7},{7,5},{8,10},{10,8},{9,1... | collective-permute-start | bytes 405512 | tf_op jit(solution)/shard_map/ppermute | solution.py:22
  12.2 6.8 %collective-permute-start.1 = (f32[2,33,128]{2,0,1:T(2,128)S(1)}, f32[2,33,128]{2,0,1:T(2,128)S(1)}, u32[]{:S(2)}, u32[]{:S(2)}) collective-permute-start(f32[2,33,128]{2,0,1:T(2,128)S(1)} %get-tuple-element.22), channel_id=1, source_target_pairs={{0,8},{8,16},{16,24},{24,0},{1,9},{9,17},{17,25},{25,1},{2,10},{10... | collective-permute-start | bytes 101384 | tf_op jit(solution)/shard_map/ppermute | solution.py:22
  12.3 6.7 %collective-permute-start.3 = (f32[2,33,128]{2,0,1:T(2,128)S(1)}, f32[2,33,128]{2,0,1:T(2,128)S(1)}, u32[]{:S(2)}, u32[]{:S(2)}) collective-permute-start(f32[2,33,128]{2,0,1:T(2,128)S(1)} %get-tuple-element.23), channel_id=1, source_target_pairs={{0,24},{8,0},{16,8},{24,16},{1,25},{9,1},{17,9},{25,17},{2,26},{10... | collective-permute-start | bytes 101384 | tf_op jit(solution)/shard_map/ppermute | solution.py:22
  15.0 4.3 %collective-permute-start.2 = (f32[2,33,128]{2,0,1:T(2,128)S(1)}, f32[2,33,128]{2,0,1:T(2,128)S(1)}, u32[]{:S(2)}, u32[]{:S(2)}) collective-permute-start(f32[2,33,128]{2,0,1:T(2,128)S(1)} %get-tuple-element.24), channel_id=1, source_target_pairs={{0,16},{8,24},{16,0},{24,8},{1,17},{9,25},{17,1},{25,9},{2,18},{10... | collective-permute-start | bytes 101384 | tf_op jit(solution)/shard_map/ppermute | solution.py:22
  19.3 8.6 %collective-permute-start.5 = (f32[2,33,128]{2,0,1:T(2,128)S(1)}, f32[2,33,128]{2,0,1:T(2,128)S(1)}, u32[]{:S(2)}, u32[]{:S(2)}) collective-permute-start(f32[2,33,128]{2,0,1:T(2,128)S(1)} %get-tuple-element.16), channel_id=1, source_target_pairs={{0,224},{32,0},{64,32},{96,64},{128,96},{160,128},{192,160},{224,1... | collective-permute-start | bytes 101384 | tf_op jit(solution)/shard_map/ppermute | solution.py:22
  24.7 4.0 %collective-permute-start.4 = (f32[2,33,128]{2,0,1:T(2,128)S(1)}, f32[2,33,128]{2,0,1:T(2,128)S(1)}, u32[]{:S(2)}, u32[]{:S(2)}) collective-permute-start(f32[2,33,128]{2,0,1:T(2,128)S(1)} %get-tuple-element.16), channel_id=1, source_target_pairs={{0,32},{32,64},{64,96},{96,128},{128,160},{160,192},{192,224},{224... | collective-permute-start | bytes 101384 | tf_op jit(solution)/shard_map/ppermute | solution.py:22
  27.9 4.9 %collective-permute-start.6 = (f32[2,33,128]{2,0,1:T(2,128)S(1)}, f32[2,33,128]{2,0,1:T(2,128)S(1)}, u32[]{:S(2)}, u32[]{:S(2)}) collective-permute-start(f32[2,33,128]{2,0,1:T(2,128)S(1)} %get-tuple-element.15), channel_id=1, source_target_pairs={{0,64},{32,96},{64,128},{96,160},{128,192},{160,224},{192,0},{224,... | collective-permute-start | bytes 101384 | tf_op jit(solution)/shard_map/ppermute | solution.py:22
  29.4 4.4 %collective-permute-start.8 = (f32[2,33,128]{2,0,1:T(2,128)}, f32[2,33,128]{2,0,1:T(2,128)}, u32[]{:S(2)}, u32[]{:S(2)}) collective-permute-start(f32[2,33,128]{2,0,1:T(2,128)} %get-tuple-element.25), channel_id=1, source_target_pairs={{0,192},{32,224},{64,0},{96,32},{128,64},{160,96},{192,128},{224,1... | collective-permute-start | bytes 101384 | tf_op jit(solution)/shard_map/ppermute | solution.py:22
  32.2 6.9 %collective-permute-start.7 = (f32[2,33,128]{2,0,1:T(2,128)}, f32[2,33,128]{2,0,1:T(2,128)}, u32[]{:S(2)}, u32[]{:S(2)}) collective-permute-start(f32[2,33,128]{2,0,1:T(2,128)} %get-tuple-element.26), channel_id=1, source_target_pairs={{0,96},{32,128},{64,160},{96,192},{128,224},{160,0},{192,32},{224,... | collective-permute-start | bytes 101384 | tf_op jit(solution)/shard_map/ppermute | solution.py:22
  40.1 4.2 %collective-permute-start.9 = (f32[2,33,128]{2,0,1:T(2,128)S(1)}, f32[2,33,128]{2,0,1:T(2,128)S(1)}, u32[]{:S(2)}, u32[]{:S(2)}) collective-permute-start(f32[2,33,128]{2,0,1:T(2,128)S(1)} %get-tuple-element.19), channel_id=1, source_target_pairs={{0,8},{8,16},{16,24},{24,0},{1,9},{9,17},{17,25},{25,1},{2,10},{10... | collective-permute-start | bytes 101384 | tf_op jit(solution)/shard_map/ppermute | solution.py:22
  40.8 3.6 %collective-permute-start.11 = (f32[2,33,128]{2,0,1:T(2,128)S(1)}, f32[2,33,128]{2,0,1:T(2,128)}, u32[]{:S(2)}, u32[]{:S(2)}) collective-permute-start(f32[2,33,128]{2,0,1:T(2,128)S(1)} %get-tuple-element.20), channel_id=1, source_target_pairs={{0,24},{8,0},{16,8},{24,16},{1,25},{9,1},{17,9},{25,17},{2,26},{10... | collective-permute-start | bytes 101384 | tf_op jit(solution)/shard_map/ppermute | solution.py:22
  43.0 4.3 %collective-permute-start.10 = (f32[2,33,128]{2,0,1:T(2,128)S(1)}, f32[2,33,128]{2,0,1:T(2,128)S(1)}, u32[]{:S(2)}, u32[]{:S(2)}) collective-permute-start(f32[2,33,128]{2,0,1:T(2,128)S(1)} %get-tuple-element.21), channel_id=1, source_target_pairs={{0,16},{8,24},{16,0},{24,8},{1,17},{9,25},{17,1},{25,9},{2,18},{10... | collective-permute-start | bytes 101384 | tf_op jit(solution)/shard_map/ppermute | solution.py:22
  47.3 0.6 copy-start.2
  49.5 13.2 %copy-start.3 = (f32[16,256]{1,0:T(8,128)S(1)}, f32[16,256]{1,0:T(8,128)}, u32[]{:S(2)}) copy-start(f32[16,256]{1,0:T(8,128)} %get-tuple-element.31) | copy-start | bytes 49156
  49.5 5.5 %collective-permute-start.12 = (f32[8,33,128]{2,0,1:T(8,128)S(1)}, f32[8,33,128]{2,0,1:T(8,128)S(1)}, u32[]{:S(2)}, u32[]{:S(2)}) collective-permute-start(f32[8,33,128]{2,0,1:T(8,128)S(1)} %select_add_fusion.1), channel_id=1, source_target_pairs={{0,4},{4,0},{1,5},{5,1},{2,6},{6,2},{3,7},{7,3},{8,12},{12,8},{9,1... | collective-permute-start | bytes 405512 | tf_op jit(solution)/shard_map/ppermute | solution.py:22
  55.1 6.0 %collective-permute-start.13 = (f32[8,33,128]{2,1,0:T(8,128)S(1)}, f32[8,33,128]{2,1,0:T(8,128)S(1)}, u32[]{:S(2)}, u32[]{:S(2)}) collective-permute-start(f32[8,33,128]{2,1,0:T(8,128)S(1)} %copy.9), channel_id=1, source_target_pairs={{0,2},{2,0},{1,3},{3,1},{4,6},{6,4},{5,7},{7,5},{8,10},{10,8},{9,1... | collective-permute-start | bytes 405512 | tf_op jit(solution)/shard_map/ppermute | solution.py:22
  61.3 3.0 %copy-start.4 = (f32[1,1,256,16,64]{2,4,3,1,0:T(8,128)S(1)}, f32[1,1,256,16,64]{2,4,3,1,0:T(8,128)}, u32[]{:S(2)}) copy-start(f32[1,1,256,16,64]{2,4,3,1,0:T(8,128)} %fusion.10) | copy-start | bytes 3145732
